TPU v7x, 256 devices: a whole 4x4x8 slice. The times are simulated.
256 devices in a mesh: az: 16 (over z_lo, x, core), tile: 16 (over y, z_hi).
Axes of the slice: x: 4, y: 4, z: 8 (z_hi: 4, z_lo: 2; z = z_hi * 2 + z_lo), core: 2. Of those that a mesh axis runs over, the one named last changes fastest.
Arguments:
- image: float32 [2, 8192, 2048], P(None, 'tile', 'az'), may hold values from -6 to 6
- tv_dual: float32 [2, 2, 8192, 2048], P(None, None, 'tile', 'az'), may hold values from -3 to 3
- data_dual: float32 [2, 1024, 64, 128], P(None, 'az', 'tile'), may hold values from -3 to 3
- echoes: bfloat16 [2, 1024, 64, 128], P(None, 'az', 'tile'), may hold values from -6 to 6
- row_steer: bfloat16 [2, 1024, 32, 256], P(None, None, 'tile'), may hold values from -0.375 to 0.375
- col_steer: float32 [2, 1024, 32, 16], P(None, None, 'tile'), may hold values from -1.5 to 1.5
- kernels: bfloat16 [8, 128, 128], replicated, may hold values from -0.5 to 0.5
- footprint: int32 [32, 16, 6], P(None, 'az'), may hold values from 0 to 63
- phase: int32 [32, 16, 6], P(None, 'az'), may hold values from 0 to 7
- aperture: int32 [1024], P('az'), may hold values from 0 to 1, as said below
Outputs:
- image_new: float32 [2, 8192, 2048], P(None, 'tile', 'az')
- tv_new: float32 [2, 2, 8192, 2048], P(None, None, 'tile', 'az')
- dual_new: float32 [2, 1024, 64, 128], P(None, 'az', 'tile')
Inputs may be any that keep to these rules, and one draw needn't show every extreme that they name: 0 inside up to three gaps of 64 consecutive pulses each (wrapping around the aperture), 1 elsewhere.
All inputs are finite; a program needn't handle non-finite values.
Results may differ from a plain program's by a relative error of at most 0.0025.
The roundings to bfloat16 on the way count: a program that leaves them out, or rounds other values in their place, can miss the bound.
Values may be sent and summed in bfloat16 or wider, within the bound.
No kernel may reach another device: no remote copies, remote signals or barrier semaphores. Data moves between devices by JAX's collectives and lax.ppermute only.
A program may use at most 64 MiB of HBM per device.

v0:
```python
import jax
import jax.numpy as jnp
from jax import lax
from jax.sharding import PartitionSpec as P

dual_step = 0.5
primal_step = 0.25
edge_limit = 1.5


def padded_2(block, sides, width):
    for axis, dim in sides:
        count = lax.axis_size(axis)
        forward = [(i, i + 1) for i in range(count - 1)]
        backward = [(target, source) for source, target in forward]
        low = lax.ppermute(
            lax.slice_in_dim(block, block.shape[dim] - width, None, axis=dim), axis, forward
        )
        high = lax.ppermute(lax.slice_in_dim(block, 0, width, axis=dim), axis, backward)
        block = jnp.concatenate([low, block, high], axis=dim)
    return block


def on_device(
    image, tv_dual, data_dual, echoes, row_steer, col_steer, kernels, footprint, phase, aperture
):
    highest = lax.Precision.HIGHEST
    az_index = lax.axis_index("az")
    tile_index = lax.axis_index("tile")
    az_count = lax.axis_size("az")
    tile_count = lax.axis_size("tile")
    strip_rows = image.shape[1]
    columns = image.shape[2]
    tiles_dev = row_steer.shape[2]
    tile_rows = row_steer.shape[3]
    rows_dev = data_dual.shape[2]
    range_rows = rows_dev * tile_count
    foot_block = footprint[:, 0, :]
    phase_block = phase[:, 0, :]
    foot_mine = lax.dynamic_slice_in_dim(foot_block, tile_index * tiles_dev, tiles_dev, 0)
    phase_mine = lax.dynamic_slice_in_dim(phase_block, tile_index * tiles_dev, tiles_dev, 0)
    steer_re = row_steer[0]
    steer_im = row_steer[1]
    col_mine = lax.dynamic_slice_in_dim(col_steer, az_index, 1, 3)[..., 0]
    image_b = image.astype(jnp.bfloat16).reshape(2, tiles_dev, tile_rows, columns)
    part_sre = steer_re
    part_sim = steer_im
    weight_re = col_mine[0][..., None]
    weight_im = col_mine[1][..., None]
    prod_re = jnp.einsum("pjh,jhu->pju", part_sre, image_b[0], preferred_element_type=jnp.float32)
    prod_re = prod_re - jnp.einsum(
        "pjh,jhu->pju", part_sim, image_b[1], preferred_element_type=jnp.float32
    )
    prod_im = jnp.einsum("pjh,jhu->pju", part_sre, image_b[1], preferred_element_type=jnp.float32)
    prod_im = prod_im + jnp.einsum(
        "pjh,jhu->pju", part_sim, image_b[0], preferred_element_type=jnp.float32
    )
    real_part = weight_re * prod_re - weight_im * prod_im
    imag_part = weight_re * prod_im + weight_im * prod_re
    summed = lax.psum_scatter(
        jnp.stack([real_part, imag_part], axis=1), "az", scatter_dimension=0, tiled=True
    )
    projection = jnp.transpose(summed, (1, 2, 0, 3))
    projection_b = projection.astype(jnp.bfloat16)
    kern_mine = kernels[phase_mine]
    placed = jnp.einsum(
        "cjpu,jfuv->cjfpv", projection_b, kern_mine, preferred_element_type=jnp.float32
    )
    row_ids = jnp.arange(range_rows, dtype=jnp.int32)
    onehot_rows = (foot_mine[:, :, None] == row_ids[None, None, :]).astype(jnp.float32)
    forward_rows = lax.psum_scatter(
        jnp.einsum("jfk,cjfpv->kcpv", onehot_rows, placed, precision=highest),
        "tile",
        scatter_dimension=0,
        tiled=True,
    )
    forward = jnp.transpose(forward_rows, (1, 2, 0, 3))
    live = (aperture == 1)[None, :, None, None]
    dual_new = jnp.where(
        live,
        (data_dual + dual_step * (forward - echoes.astype(jnp.float32))) / (1.0 + dual_step),
        0.0,
    )
    dual_b = dual_new.astype(jnp.bfloat16)
    all_rows = lax.all_gather(dual_b, "tile", axis=2, tiled=True)
    chosen = jnp.take(all_rows, foot_mine, axis=2)
    back = jnp.einsum("cpjfv,jfuv->cjpu", chosen, kern_mine, preferred_element_type=jnp.float32)
    back_b = back.astype(jnp.bfloat16)
    piece = lax.all_gather(back_b, "az", axis=2, tiled=True)
    weight_re = col_mine[0].T[..., None]
    weight_im = col_mine[1].T[..., None]
    back_re = piece[0].astype(jnp.float32)
    back_im = piece[1].astype(jnp.float32)
    mixed_re = (weight_re * back_re + weight_im * back_im).astype(jnp.bfloat16)
    mixed_im = (weight_re * back_im - weight_im * back_re).astype(jnp.bfloat16)
    part_sre = steer_re
    part_sim = steer_im
    grad_re = jnp.einsum("pjh,jpu->jhu", part_sre, mixed_re, preferred_element_type=jnp.float32)
    grad_re = grad_re + jnp.einsum(
        "pjh,jpu->jhu", part_sim, mixed_im, preferred_element_type=jnp.float32
    )
    grad_im = jnp.einsum("pjh,jpu->jhu", part_sre, mixed_im, preferred_element_type=jnp.float32)
    grad_im = grad_im - jnp.einsum(
        "pjh,jpu->jhu", part_sim, mixed_re, preferred_element_type=jnp.float32
    )
    adjoint = jnp.stack([grad_re, grad_im])
    adjoint = adjoint.reshape(2, strip_rows, columns)
    stacked = jnp.concatenate([image, tv_dual.reshape(4, strip_rows, columns)], axis=0)
    padded = padded_2(stacked, (("az", 2), ("tile", 1)), 1)
    image_pad = padded[:2]
    dual_pad = padded[2:].reshape(2, 2, strip_rows + 2, columns + 2)
    total_rows = tile_count * strip_rows
    total_cols = az_count * columns
    global_row = tile_index * strip_rows - 1 + jnp.arange(strip_rows + 1, dtype=jnp.int32)
    global_col = az_index * columns - 1 + jnp.arange(columns + 1, dtype=jnp.int32)
    centre = image_pad[:, : strip_rows + 1, : columns + 1]
    grad_rows = image_pad[:, 1 : strip_rows + 2, : columns + 1] - centre
    grad_rows = jnp.where((global_row < total_rows - 1)[None, :, None], grad_rows, 0.0)
    grad_cols = image_pad[:, : strip_rows + 1, 1 : columns + 2] - centre
    grad_cols = jnp.where((global_col < total_cols - 1)[None, None, :], grad_cols, 0.0)
    moved = dual_pad[:, :, : strip_rows + 1, : columns + 1] + dual_step * jnp.stack(
        [grad_rows, grad_cols]
    )
    magnitude = jnp.sqrt(jnp.sum(moved * moved, axis=(0, 1)))
    projected = moved / jnp.maximum(1.0, magnitude / edge_limit)
    inside = (global_row >= 0)[:, None] & (global_col >= 0)[None, :]
    projected = jnp.where(inside[None, None], projected, 0.0)
    rows_part = jnp.where((global_row < total_rows - 1)[None, :, None], projected[0], 0.0)
    cols_part = jnp.where((global_col < total_cols - 1)[None, None, :], projected[1], 0.0)
    divergence = (
        rows_part[:, 1:, 1:] - rows_part[:, :-1, 1:] + cols_part[:, 1:, 1:] - cols_part[:, 1:, :-1]
    )
    image_new = image - primal_step * (adjoint - divergence)
    tv_new = projected[:, :, 1:, 1:]
    return (image_new, tv_new, dual_new)


def solution(mesh):
    in_specs = (
        P(None, "tile", "az"),
        P(None, None, "tile", "az"),
        P(None, "az", "tile", None),
        P(None, "az", "tile", None),
        P(None, None, "tile", None),
        P(None, None, "tile", None),
        P(),
        P(None, "az", None),
        P(None, "az", None),
        P("az"),
    )
    out_specs = (P(None, "tile", "az"), P(None, None, "tile", "az"), P(None, "az", "tile", None))
    return jax.shard_map(
        on_device, mesh=mesh, in_specs=in_specs, out_specs=out_specs, check_vma=False
    )
```

profile of v0, /device:TPU:1, one launch (start us, length us, event | category | flops | bytes accessed | tf_op | source)
XLA Modules:
  0.0 316.1 jit_solution(1707536675168299490)
XLA Ops:
  7.2 2.7 fusion.50
  10.1 0.5 fusion.21
  10.6 0.4 copy-done.8
  11.0 1.5 fusion.22
  12.5 0.9 constant_dynamic-slice_fusion
  13.4 0.5 fusion
  13.9 0.7 copy-done.10
  14.6 0.6 subtract_bitcast_fusion
  15.4 2.3 copy.50
  17.8 66.7 %all-reduce.2 = bf16[1024,2,2,128]{3,2,1,0:T(2,128)(2,1)S(1)} all-reduce(f32[1024,2,2,128]{3,2,1,0:T(2,128)} %copy.50), channel_id=2, replica_groups=mesh['az'=16,'tile'=16] {'az'}, use_global_device_ids=true, to_apply=%region_0.0.clone | all-reduce | flops 524288 | bytes 3145728
  85.0 0.6 dynamic-slice.2
  86.3 0.6 gather_fusion
  87.2 2.2 convolution_bitcast_fusion
  89.4 4.4 %copy.53 = f32[64,2,64,128]{3,2,1,0:T(8,128)} copy(f32[64,2,64,128]{3,0,2,1:T(8,128)S(1)} %convolution_bitcast_fusion) | data formatting | bytes 8388608 | tf_op jit(solution)/shard_map/jfk,cjfpv->kcpv/dot_general | solution.py:72
  93.9 0.6 copy-done.20
  94.5 98.1 %reduce-scatter.2.cloned.1.call-done = f32[4,2,64,128]{3,2,1,0:T(8,128)} async-done(((f32[64,2,64,128]{3,2,1,0:T(8,128)}), f32[4,2,64,128]{3,2,1,0:T(8,128)}) %reduce-scatter.2.cloned.1.call-update) | async-done | bytes 262160 | tf_op jit(solution)/shard_map/reduce_scatter | solution.py:71
  192.6 1.8 fusion.48
  194.5 1.7 slice_maximum_fusion
  196.2 1.9 copy.66
  198.1 4.4 %collective-permute-start = (f32[6,512,1]{1,2,0:T(1,128)S(1)}, f32[6,512,1]{1,2,0:T(1,128)S(1)}, u32[]{:S(2)}, u32[]{:S(2)}) collective-permute-start(f32[6,512,1]{1,2,0:T(1,128)S(1)} %copy.66), channel_id=1, source_target_pairs={{0,16},{16,32},{32,48},{48,64},{64,80},{80,96},{96,112},{112,128},... | collective-permute-start | bytes 36872 | tf_op jit(solution)/shard_map/ppermute | solution.py:16
  202.4 0.5 copy.67
  202.9 1.9 collective-permute-start.1
  205.0 0.5 copy.68
  205.5 2.4 collective-permute-done.1
  207.9 0.5 copy.69
  208.4 0.9 pad_maximum_fusion.16
  209.3 2.4 collective-permute-start.2
  211.7 1.5 collective-permute-start.3
  213.2 40.0 %all-gather.3.cloned.1.call-done = bf16[2,64,64,128]{3,1,0,2:T(8,128)(2,1)} async-done(((bf16[2,64,4,128]{3,1,0,2:T(8,128)(2,1)}), bf16[2,64,64,128]{3,1,0,2:T(8,128)(2,1)}) %all-gather.3.cloned.1.call-update) | async-done | bytes 2097168 | tf_op jit(solution)/shard_map/all_gather | solution.py:85
  253.2 3.1 copy.57
  256.4 2.9 gather_fusion.1
  259.3 2.0 fusion.5
  261.6 2.2 pad_maximum_fusion
  263.8 0.6 fusion.10
  264.4 1.0 fusion.13
  265.4 0.4 multiply_reduce_fusion
  266.0 0.4 divide_select_fusion
  266.4 1.3 slice.128
  267.7 1.2 fusion.7
  268.9 0.9 copy.70
  269.8 25.4 %all-gather.5.cloned.1.call-done = bf16[2,2,1024,128]{3,2,0,1:T(8,128)(2,1)} async-done(((bf16[2,2,64,128]{3,2,0,1:T(8,128)(2,1)}), bf16[2,2,1024,128]{3,2,0,1:T(8,128)(2,1)}) %all-gather.5.cloned.1.call-update) | async-done | bytes 1048592 | tf_op jit(solution)/shard_map/all_gather | solution.py:89
  295.2 2.4 fusion.20
  297.6 2.0 fusion.2
  299.6 1.8 copy.62
  301.4 2.4 fusion.19
  303.8 2.0 fusion.3
  305.8 1.1 copy.65
  306.9 2.7 fusion.25
  (71 shorter events, 1.7 us)
Async XLA Ops:
  7.2 79.1 %copy-start = (bf16[8,128,128]{2,1,0:T(8,128)(2,1)S(1)}, bf16[8,128,128]{2,1,0:T(8,128)(2,1)}, u32[]{:S(2)}) copy-start(bf16[8,128,128]{2,1,0:T(8,128)(2,1)} %param.16) | copy-start | bytes 786436
  7.2 185.5 %reduce-scatter.2.cloned.1.call-start = ((), (), s32[]{:S(2)}) async-start(), calls=%async_computation.1 | async-start | bytes 4456448 | tf_op jit(solution)/shard_map/reduce_scatter | solution.py:71
  7.2 2.8 copy-start.3
  10.0 1.0 copy-start.8
  10.0 3.9 %copy-start.6 = (bf16[1,1024,2,256]{3,2,1,0:T(2,128)(2,1)}, bf16[1,1024,2,256]{3,2,1,0:T(2,128)(2,1)S(1)}, u32[]{:S(2)}) copy-start(bf16[1,1024,2,256]{3,2,1,0:T(2,128)(2,1)S(1)} %get-tuple-element.14) | copy-start | bytes 3145732
  13.4 1.2 copy-start.10
  17.8 66.7 %copy-start.16 = (s32[32,1,6]{0,1,2:T(1,128)S(1)}, s32[32,1,6]{0,1,2:T(1,128)}, u32[]{:S(2)}) copy-start(s32[32,1,6]{0,1,2:T(1,128)} %param.17) | copy-start | bytes 2308
  17.8 66.9 %copy-start.17 = (s32[32,1,6]{0,1,2:T(1,128)S(1)}, s32[32,1,6]{0,1,2:T(1,128)}, u32[]{:S(2)}) copy-start(s32[32,1,6]{0,1,2:T(1,128)} %param.18) | copy-start | bytes 2308
  17.8 67.2 %copy-start.21 = (u32[256]{0:T(256)S(1)}, u32[256]{0:T(256)}, u32[]{:S(2)}) copy-start(u32[256]{0:T(256)} %constant.73) | copy-start | bytes 3076
  86.9 2.5 copy-start.11
  93.8 0.7 copy-start.20
  93.8 98.8 %copy-start.14 = (f32[2,64,4,128]{3,2,1,0:T(4,128)S(1)}, f32[2,64,4,128]{3,2,1,0:T(4,128)}, u32[]{:S(2)}) copy-start(f32[2,64,4,128]{3,2,1,0:T(4,128)} %param.12) | copy-start | bytes 786436
  93.8 98.8 %copy-start.15 = (bf16[2,64,4,128]{3,2,1,0:T(4,128)(2,1)S(1)}, bf16[2,64,4,128]{3,2,1,0:T(4,128)(2,1)}, u32[]{:S(2)}) copy-start(bf16[2,64,4,128]{3,2,1,0:T(4,128)(2,1)} %param.13) | copy-start | bytes 393220
  93.9 100.7 %copy-start.1 = (f32[2,2,512,128]{3,2,1,0:T(8,128)S(1)}, f32[2,2,512,128]{3,2,1,0:T(8,128)}, u32[]{:S(2)}) copy-start(f32[2,2,512,128]{3,2,1,0:T(8,128)} %param.11) | copy-start | bytes 3145732
  93.9 159.3 %all-gather.3.cloned.1.call-start = ((), (), s32[]{:S(2)}) async-start(), calls=%async_computation.2 | async-start | bytes 2228224 | tf_op jit(solution)/shard_map/all_gather | solution.py:85
  194.5 100.7 %all-gather.5.cloned.1.call-start = ((), (), s32[]{:S(2)}) async-start(), calls=%async_computation.3 | async-start | bytes 1114112 | tf_op jit(solution)/shard_map/all_gather | solution.py:89
  198.1 6.9 %collective-permute-start = (f32[6,512,1]{1,2,0:T(1,128)S(1)}, f32[6,512,1]{1,2,0:T(1,128)S(1)}, u32[]{:S(2)}, u32[]{:S(2)}) collective-permute-start(f32[6,512,1]{1,2,0:T(1,128)S(1)} %copy.66), channel_id=1, source_target_pairs={{0,16},{16,32},{32,48},{48,64},{64,80},{80,96},{96,112},{112,128},... | collective-permute-start | bytes 36872 | tf_op jit(solution)/shard_map/ppermute | solution.py:16
  202.9 5.0 %collective-permute-start.1 = (f32[6,512,1]{1,2,0:T(1,128)S(1)}, f32[6,512,1]{1,2,0:T(1,128)S(1)}, u32[]{:S(2)}, u32[]{:S(2)}) collective-permute-start(f32[6,512,1]{1,2,0:T(1,128)S(1)} %copy.67), channel_id=1, source_target_pairs={{16,0},{32,16},{48,32},{64,48},{80,64},{96,80},{112,96},{128,112},... | collective-permute-start | bytes 36872 | tf_op jit(solution)/shard_map/ppermute | solution.py:19
  209.3 52.2 %collective-permute-start.2 = (f32[6,1,130]{2,1,0:T(1,128)S(1)}, f32[6,1,130]{2,1,0:T(1,128)S(1)}, u32[]{:S(2)}, u32[]{:S(2)}) collective-permute-start(f32[6,1,130]{2,1,0:T(1,128)S(1)} %get-tuple-element.9), channel_id=1, source_target_pairs={{0,1},{1,2},{2,3},{3,4},{4,5},{5,6},{6,7},{7,8},{8,9},{9,10},{10,1... | collective-permute-start | bytes 9368 | tf_op jit(solution)/shard_map/ppermute | solution.py:16
  211.7 49.8 %collective-permute-start.3 = (f32[6,1,130]{2,1,0:T(1,128)S(1)}, f32[6,1,130]{2,1,0:T(1,128)S(1)}, u32[]{:S(2)}, u32[]{:S(2)}) collective-permute-start(f32[6,1,130]{2,1,0:T(1,128)S(1)} %get-tuple-element.8), channel_id=1, source_target_pairs={{1,0},{2,1},{3,2},{4,3},{5,4},{6,5},{7,6},{8,7},{9,8},{10,9},{11,1... | collective-permute-start | bytes 9368 | tf_op jit(solution)/shard_map/ppermute | solution.py:19
  261.5 2.3 copy-start.2
  261.5 2.3 copy-start.4
  267.7 1.2 copy-start.13
  267.7 27.5 %copy-start.9 = (bf16[1,1024,2,256]{3,2,1,0:T(2,128)(2,1)S(1)}, bf16[1,1024,2,256]{3,2,1,0:T(2,128)(2,1)}, u32[]{:S(2)}) copy-start(bf16[1,1024,2,256]{3,2,1,0:T(2,128)(2,1)} %copy-done.8) | copy-start | bytes 3145732
  295.2 2.5 copy-start.7
  295.2 2.5 copy-start.18
  301.4 2.4 copy-start.19
  303.8 3.1 copy-start.5
  303.8 3.1 copy-start.12
Sparse Core Ops, SparseCore 0:
  94.0 98.6 reduce-scatter.1
  195.9 57.2 all-gather.2
  261.5 33.6 all-gather.4
where the time goes:
time: 317 us; the launch traced here: 316 us
  waiting for transfers between devices  166 us (52%)
  blocking collectives  66.7 us (21%)
  local copies, waits for them, and re-layouts  28.4 us (9%)
  matrix products  16.3 us (5%)
  between operations  14.9 us (5%)
  other arithmetic  13.4 us (4%)
  starting transfers between devices  10.3 us (3%)
    reduce_scatter x1, waiting for transfers between devices, on_device(): lax.psum_scatter(jnp.einsum('jfk,cjfpv->kcpv', onehot_rows, placed, preci...  98.1 us
    unnamed x1, blocking collectives  66.7 us
    all_gather x1, waiting for transfers between devices, on_device(): all_rows = lax.all_gather(dual_b, 'tile', axis=2, tiled=True)  40 us
    all_gather x1, waiting for transfers between devices, on_device(): piece = lax.all_gather(back_b, 'az', axis=2, tiled=True)  25.4 us
    ppermute x2, starting transfers between devices, padded_2(): lax.ppermute(lax.slice_in_dim(block, block.shape[dim] - width, None, axis...  6.78 us
  transfers between devices with their start and end apart: 7, of which 4 were waited for; matrix products, arithmetic and copies ran while one was open for 7% of the time, Pallas kernels for 0%

commit v1 on v0

--- a/solution.py
+++ b/solution.py
@@ -58,23 +58,23 @@
     real_part = weight_re * prod_re - weight_im * prod_im
     imag_part = weight_re * prod_im + weight_im * prod_re
     summed = lax.psum_scatter(
-        jnp.stack([real_part, imag_part], axis=1), "az", scatter_dimension=0, tiled=True
+        jnp.stack([real_part, imag_part], axis=0), "az", scatter_dimension=1, tiled=True
     )
-    projection = jnp.transpose(summed, (1, 2, 0, 3))
-    projection_b = projection.astype(jnp.bfloat16)
+    projection_b = jnp.transpose(summed, (2, 1, 0, 3)).astype(jnp.bfloat16)
+    all_proj = lax.all_gather(projection_b, "tile", axis=0, tiled=True)
+    phase_ids = jnp.arange(kernels.shape[0], dtype=jnp.int32)
+    my_rows = tile_index * rows_dev + jnp.arange(rows_dev, dtype=jnp.int32)
+    hits = (foot_block[:, :, None, None] == my_rows[None, None, :, None]) & (
+        phase_block[:, :, None, None] == phase_ids[None, None, None, :]
+    )
+    counts = jnp.sum(hits.astype(jnp.int32), axis=1).astype(jnp.bfloat16)
+    grouped = jnp.einsum(
+        "jkq,jpcu->kqpcu", counts, all_proj, preferred_element_type=jnp.float32
+    )
+    forward = jnp.einsum(
+        "kqpcu,quv->cpkv", grouped, kernels.astype(jnp.float32), precision=highest
+    )
     kern_mine = kernels[phase_mine]
-    placed = jnp.einsum(
-        "cjpu,jfuv->cjfpv", projection_b, kern_mine, preferred_element_type=jnp.float32
-    )
-    row_ids = jnp.arange(range_rows, dtype=jnp.int32)
-    onehot_rows = (foot_mine[:, :, None] == row_ids[None, None, :]).astype(jnp.float32)
-    forward_rows = lax.psum_scatter(
-        jnp.einsum("jfk,cjfpv->kcpv", onehot_rows, placed, precision=highest),
-        "tile",
-        scatter_dimension=0,
-        tiled=True,
-    )
-    forward = jnp.transpose(forward_rows, (1, 2, 0, 3))
     live = (aperture == 1)[None, :, None, None]
     dual_new = jnp.where(
         live,

time: 317 us -> 265 us (0.84)
  waiting for transfers between devices: 166 us -> 121 us
  local copies, waits for them, and re-layouts: 28.4 us -> 21.7 us
    reduce_scatter x1 -> x0, waiting for transfers between devices: 98.1 us -> none  [on_device(): lax.psum_scatter(jnp.einsum('jfk,cjfpv->kcpv', onehot_rows, placed, preci...]
    all_gather x0 -> x1, waiting for transfers between devices: none -> 56 us  [on_device(): all_proj = lax.all_gather(projection_b, 'tile', axis=0, tiled=True)]
    dot_general x1 -> x0, local copies, waits for them, and re-layouts: 4.4 us -> none  [on_device(): jnp.einsum('jfk,cjfpv->kcpv', onehot_rows, placed, precision=highest)]
  transfers between devices with their start and end apart: 7 -> 7, of which waited for: 4 -> 4; matrix products, arithmetic and copies ran while one was open for 7% -> 8% of each run, Pallas kernels for 0% -> 0%
where the time goes in v1:
time: 265 us
  waiting for transfers between devices  121 us (46%)
  blocking collectives  66.7 us (25%)
  local copies, waits for them, and re-layouts  21.7 us (8%)
  matrix products  18.1 us (7%)
  between operations  15 us (6%)
  other arithmetic  11.7 us (4%)
  starting transfers between devices  10.4 us (4%)
    unnamed x1, blocking collectives  66.7 us
    all_gather x1, waiting for transfers between devices, on_device(): all_proj = lax.all_gather(projection_b, 'tile', axis=0, tiled=True)  56 us
    all_gather x1, waiting for transfers between devices, on_device(): all_rows = lax.all_gather(dual_b, 'tile', axis=2, tiled=True)  38.9 us
    all_gather x1, waiting for transfers between devices, on_device(): piece = lax.all_gather(back_b, 'az', axis=2, tiled=True)  25.4 us
    ppermute x2, starting transfers between devices, padded_2(): lax.ppermute(lax.slice_in_dim(block, block.shape[dim] - width, None, axis...  6.92 us
  transfers between devices with their start and end apart: 7, of which 4 were waited for; matrix products, arithmetic and copies ran while one was open for 8% of the time, Pallas kernels for 0%

profile of v1, /device:TPU:1, one launch (start us, length us, event | category | flops | bytes accessed | tf_op | source)
XLA Modules:
  0.0 264.6 jit_solution(16992743149203517460)
XLA Ops:
  7.3 2.7 %fusion.64 = (bf16[1,1024,2,256]{3,2,1,0:T(2,128)(2,1)S(1)}, bf16[1,1024,2,256]{3,2,1,0:T(2,128)(2,1)S(1)}) fusion(bf16[2,1024,2,256]{3,2,1,0:T(2,128)(2,1)} %param.14), kind=kLoop, calls=%fused_computation.122 | loop fusion | bytes 4194304 | tf_op jit(solution)/shard_map/slice | solution.py:43
  10.1 0.5 fusion.43
  10.6 0.4 copy-done.8
  11.0 1.5 fusion.44
  12.4 0.9 constant_dynamic-slice_fusion
  13.4 0.5 fusion.2
  13.9 0.7 copy-done.10
  14.6 0.6 subtract_bitcast_fusion
  15.2 0.2 pad_maximum_fusion.5
  15.4 2.3 copy.117
  17.8 66.7 %all-reduce.2 = bf16[2,1024,2,128]{3,2,0,1:T(2,128)(2,1)S(1)} all-reduce(f32[2,1024,2,128]{3,2,0,1:T(2,128)} %copy.117), channel_id=2, replica_groups=mesh['az'=16,'tile'=16] {'az'}, use_global_device_ids=true, to_apply=%region_1.0.clone | all-reduce | flops 524288 | bytes 3145728
  84.5 0.6 dynamic-slice.2
  85.8 0.6 copy.118
  86.7 56.0 %all-gather.4.cloned.1.call-done = bf16[32,64,2,128]{3,1,2,0:T(8,128)(2,1)} async-done(((bf16[2,64,2,128]{3,1,2,0:T(8,128)(2,1)}), bf16[32,64,2,128]{3,1,2,0:T(8,128)(2,1)}) %all-gather.4.cloned.1.call-update) | async-done | bytes 1048592 | tf_op jit(solution)/shard_map/all_gather | solution.py:64
  142.7 2.0 fusion.38
  144.8 2.3 fusion.66
  147.2 1.6 slice_maximum_fusion
  148.8 1.9 copy.132
  150.7 5.0 %collective-permute-start = (f32[6,512,1]{1,2,0:T(1,128)S(1)}, f32[6,512,1]{1,2,0:T(1,128)S(1)}, u32[]{:S(2)}, u32[]{:S(2)}) collective-permute-start(f32[6,512,1]{1,2,0:T(1,128)S(1)} %copy.132), channel_id=1, source_target_pairs={{0,16},{16,32},{32,48},{48,64},{64,80},{80,96},{96,112},{112,128},... | collective-permute-start | bytes 36872 | tf_op jit(solution)/shard_map/ppermute | solution.py:16
  155.7 0.5 copy.133
  156.1 1.9 collective-permute-start.1
  158.6 1.4 gather_fusion
  160.0 0.5 copy.134
  160.5 0.6 collective-permute-done.1
  161.2 0.5 copy.135
  161.7 0.9 pad_maximum_fusion.16
  162.5 2.0 collective-permute-start.2
  164.5 1.5 collective-permute-start.3
  166.0 38.9 %all-gather.6.cloned.1.call-done = bf16[2,64,64,128]{3,1,0,2:T(8,128)(2,1)} async-done(((bf16[2,64,4,128]{3,1,0,2:T(8,128)(2,1)}), bf16[2,64,64,128]{3,1,0,2:T(8,128)(2,1)}) %all-gather.6.cloned.1.call-update) | async-done | bytes 2097168 | tf_op jit(solution)/shard_map/all_gather | solution.py:85
  204.9 2.9 %gather_fusion.1 = bf16[12,2,64,128]{3,2,1,0:T(8,128)(2,1)} fusion(bf16[2,64,64,128]{3,1,0,2:T(8,128)(2,1)} %all-gather.6.cloned.1.call-done, s32[1024]{0:T(1024)S(1)} %pad_clamp_fusion), kind=kCustom, calls=%fused_computation.1 | custom fusion | bytes 786480 | tf_op jit(solution)/shard_map/jit(_take)/gather | solution.py:86
  207.8 2.1 fusion.25
  210.1 2.2 pad_maximum_fusion
  212.3 0.6 fusion.30
  213.0 1.0 fusion.33
  213.9 0.4 multiply_reduce_fusion
  214.3 0.2 multiply_maximum_fusion
  214.5 0.4 divide_select_fusion
  214.9 1.3 slice.128
  216.2 1.2 fusion.27
  217.4 0.9 copy.136
  218.3 25.4 %all-gather.8.cloned.1.call-done = bf16[2,2,1024,128]{3,2,0,1:T(8,128)(2,1)} async-done(((bf16[2,2,64,128]{3,2,0,1:T(8,128)(2,1)}), bf16[2,2,1024,128]{3,2,0,1:T(8,128)(2,1)}) %all-gather.8.cloned.1.call-update) | async-done | bytes 1048592 | tf_op jit(solution)/shard_map/all_gather | solution.py:89
  243.7 2.4 fusion.42
  246.2 2.0 fusion.7
  248.1 1.8 copy.128
  249.9 2.4 fusion.41
  252.3 2.0 fusion.8
  254.3 1.1 copy.131
  255.4 2.7 %fusion.47 = f32[2,512,128]{2,1,0:T(8,128)} fusion(f32[2,512,128]{2,1,0:T(8,128)S(1)} %copy-done.5, f32[2,513,129]{2,1,0:T(8,128)} %get-tuple-element.21, f32[2,513,129]{2,1,0:T(8,128)S(1)} %get-tuple-element.20, f32[1,512,128]{2,1,0:T(8,128)S(1)} %bitcast.164, f32[1,512,128]{2,1,0:T(8,128)S(1)} %bitcast.163), kind=kLoop, calls=%fused_computation.75 | loop fusion | flops 917504 | bytes 3670016 | tf_op jit(solution)/shard_map/sub | solution.py:133
  (73 shorter events, 1.2 us)
Async XLA Ops:
  7.2 137.6 %copy-start = (bf16[8,128,128]{2,1,0:T(8,128)(2,1)S(1)}, bf16[8,128,128]{2,1,0:T(8,128)(2,1)}, u32[]{:S(2)}) copy-start(bf16[8,128,128]{2,1,0:T(8,128)(2,1)} %param.16) | copy-start | bytes 786436
  7.2 135.5 %all-gather.4.cloned.1.call-start = ((), (), s32[]{:S(2)}) async-start(), calls=%async_computation | async-start | bytes 1114112 | tf_op jit(solution)/shard_map/all_gather | solution.py:64
  7.2 2.8 %copy-start.3 = (f32[2,512,128]{2,1,0:T(8,128)S(1)}, f32[2,512,128]{2,1,0:T(8,128)}, u32[]{:S(2)}) copy-start(f32[2,512,128]{2,1,0:T(8,128)} %param.10) | copy-start | bytes 1572868
  10.0 1.0 copy-start.8
  10.0 3.8 %copy-start.6 = (bf16[1,1024,2,256]{3,2,1,0:T(2,128)(2,1)}, bf16[1,1024,2,256]{3,2,1,0:T(2,128)(2,1)S(1)}, u32[]{:S(2)}) copy-start(bf16[1,1024,2,256]{3,2,1,0:T(2,128)(2,1)S(1)} %get-tuple-element.24) | copy-start | bytes 3145732
  13.4 1.2 copy-start.10
  17.7 66.8 %copy-start.20 = (u32[256]{0:T(256)S(1)}, u32[256]{0:T(256)}, u32[]{:S(2)}) copy-start(u32[256]{0:T(256)} %constant.75) | copy-start | bytes 3076
  17.7 68.8 %copy-start.15 = (s32[32,1,6]{0,1,2:T(1,128)S(1)}, s32[32,1,6]{0,1,2:T(1,128)}, u32[]{:S(2)}) copy-start(s32[32,1,6]{0,1,2:T(1,128)} %param.17) | copy-start | bytes 2308
  17.7 68.8 %copy-start.16 = (s32[32,1,6]{0,1,2:T(1,128)S(1)}, s32[32,1,6]{0,1,2:T(1,128)}, u32[]{:S(2)}) copy-start(s32[32,1,6]{0,1,2:T(1,128)} %param.18) | copy-start | bytes 2308
  17.7 69.0 %copy-start.19 = (s32[64]{0:T(128)S(1)}, s32[64]{0:T(128)}, u32[]{:S(2)}) copy-start(s32[64]{0:T(128)} %param.19) | copy-start | bytes 772
  86.5 118.4 %all-gather.6.cloned.1.call-start = ((), (), s32[]{:S(2)}) async-start(), calls=%async_computation.1 | async-start | bytes 2228224 | tf_op jit(solution)/shard_map/all_gather | solution.py:85
  86.7 58.0 %copy-start.13 = (f32[2,64,4,128]{3,2,1,0:T(4,128)S(1)}, f32[2,64,4,128]{3,2,1,0:T(4,128)}, u32[]{:S(2)}) copy-start(f32[2,64,4,128]{3,2,1,0:T(4,128)} %param.12) | copy-start | bytes 786436
  86.7 58.0 %copy-start.14 = (bf16[2,64,4,128]{3,2,1,0:T(4,128)(2,1)S(1)}, bf16[2,64,4,128]{3,2,1,0:T(4,128)(2,1)}, u32[]{:S(2)}) copy-start(bf16[2,64,4,128]{3,2,1,0:T(4,128)(2,1)} %param.13) | copy-start | bytes 393220
  144.8 2.4 copy-start.1
  147.1 96.6 %all-gather.8.cloned.1.call-start = ((), (), s32[]{:S(2)}) async-start(), calls=%async_computation.2 | async-start | bytes 1114112 | tf_op jit(solution)/shard_map/all_gather | solution.py:89
  150.7 9.3 %collective-permute-start = (f32[6,512,1]{1,2,0:T(1,128)S(1)}, f32[6,512,1]{1,2,0:T(1,128)S(1)}, u32[]{:S(2)}, u32[]{:S(2)}) collective-permute-start(f32[6,512,1]{1,2,0:T(1,128)S(1)} %copy.132), channel_id=1, source_target_pairs={{0,16},{16,32},{32,48},{48,64},{64,80},{80,96},{96,112},{112,128},... | collective-permute-start | bytes 36872 | tf_op jit(solution)/shard_map/ppermute | solution.py:16
  156.1 5.0 %collective-permute-start.1 = (f32[6,512,1]{1,2,0:T(1,128)S(1)}, f32[6,512,1]{1,2,0:T(1,128)S(1)}, u32[]{:S(2)}, u32[]{:S(2)}) collective-permute-start(f32[6,512,1]{1,2,0:T(1,128)S(1)} %copy.133), channel_id=1, source_target_pairs={{16,0},{32,16},{48,32},{64,48},{80,64},{96,80},{112,96},{128,112},... | collective-permute-start | bytes 36872 | tf_op jit(solution)/shard_map/ppermute | solution.py:19
  162.5 47.5 %collective-permute-start.2 = (f32[6,1,130]{2,1,0:T(1,128)S(1)}, f32[6,1,130]{2,1,0:T(1,128)S(1)}, u32[]{:S(2)}, u32[]{:S(2)}) collective-permute-start(f32[6,1,130]{2,1,0:T(1,128)S(1)} %get-tuple-element.19), channel_id=1, source_target_pairs={{0,1},{1,2},{2,3},{3,4},{4,5},{5,6},{6,7},{7,8},{8,9},{9,10},{10,1... | collective-permute-start | bytes 9368 | tf_op jit(solution)/shard_map/ppermute | solution.py:16
  164.5 45.6 %collective-permute-start.3 = (f32[6,1,130]{2,1,0:T(1,128)S(1)}, f32[6,1,130]{2,1,0:T(1,128)S(1)}, u32[]{:S(2)}, u32[]{:S(2)}) collective-permute-start(f32[6,1,130]{2,1,0:T(1,128)S(1)} %get-tuple-element.18), channel_id=1, source_target_pairs={{1,0},{2,1},{3,2},{4,3},{5,4},{6,5},{7,6},{8,7},{9,8},{10,9},{11,1... | collective-permute-start | bytes 9368 | tf_op jit(solution)/shard_map/ppermute | solution.py:19
  210.0 2.3 copy-start.2
  210.0 2.3 copy-start.4
  216.2 1.2 copy-start.12
  216.2 27.5 %copy-start.9 = (bf16[1,1024,2,256]{3,2,1,0:T(2,128)(2,1)S(1)}, bf16[1,1024,2,256]{3,2,1,0:T(2,128)(2,1)}, u32[]{:S(2)}) copy-start(bf16[1,1024,2,256]{3,2,1,0:T(2,128)(2,1)} %copy-done.8) | copy-start | bytes 3145732
  243.7 2.5 copy-start.7
  243.7 2.5 copy-start.17
  249.9 2.4 copy-start.18
  252.3 3.1 %copy-start.5 = (f32[2,512,128]{2,1,0:T(8,128)S(1)}, f32[2,512,128]{2,1,0:T(8,128)}, u32[]{:S(2)}) copy-start(f32[2,512,128]{2,1,0:T(8,128)} %param.10) | copy-start | bytes 1572868
  252.3 3.1 %copy-start.11 = (f32[2,256,128]{2,1,0:T(8,128)S(1)}, f32[2,256,128]{2,1,0:T(8,128)}, u32[]{:S(2)}) copy-start(f32[2,256,128]{2,1,0:T(8,128)} %copy.128) | copy-start | bytes 786436
Sparse Core Ops, SparseCore 0:
  86.6 56.0 all-gather.3
  147.2 57.5 all-gather.5
  210.0 33.6 all-gather.7

commit v2 on v1

--- a/solution.py
+++ b/solution.py
@@ -19,6 +19,22 @@
         high = lax.ppermute(lax.slice_in_dim(block, 0, width, axis=dim), axis, backward)
         block = jnp.concatenate([low, block, high], axis=dim)
     return block
+
+
+def halving_sum(blocks, axis, bits):
+    me = lax.axis_index(axis)
+    count = lax.axis_size(axis)
+    order = [count >> (level + 1) for level in range(count.bit_length() - 1)]
+    blocks = blocks.reshape(*([2] * len(order)), *blocks.shape[1:])
+    for bit in bits:
+        place = order.index(bit)
+        order.pop(place)
+        mine = (me // bit) % 2
+        keep = lax.dynamic_index_in_dim(blocks, mine, place, keepdims=False)
+        send = lax.dynamic_index_in_dim(blocks, 1 - mine, place, keepdims=False)
+        pairs = [(i, i ^ bit) for i in range(count)]
+        blocks = keep + lax.ppermute(send, axis, pairs)
+    return blocks
 
 
 def on_device(
@@ -57,9 +73,8 @@
     )
     real_part = weight_re * prod_re - weight_im * prod_im
     imag_part = weight_re * prod_im + weight_im * prod_re
-    summed = lax.psum_scatter(
-        jnp.stack([real_part, imag_part], axis=0), "az", scatter_dimension=1, tiled=True
-    )
+    parts = jnp.stack([real_part, imag_part], axis=0).reshape(2, az_count, -1, tiles_dev, columns)
+    summed = halving_sum(jnp.moveaxis(parts, 1, 0), "az", (1, 8, 2, 4))
     projection_b = jnp.transpose(summed, (2, 1, 0, 3)).astype(jnp.bfloat16)
     all_proj = lax.all_gather(projection_b, "tile", axis=0, tiled=True)
     phase_ids = jnp.arange(kernels.shape[0], dtype=jnp.int32)

time: 265 us -> 231 us (0.87)
  blocking collectives: 66.7 us -> 0 us
  waiting for transfers between devices: 121 us -> 147 us
  starting transfers between devices: 10.4 us -> 15.5 us
  other arithmetic: 11.7 us -> 16.7 us
    unnamed x1 -> x0, blocking collectives: 66.7 us -> none
    ppermute x0 -> x4, waiting for transfers between devices: none -> 25.9 us  [halving_sum(): blocks = keep + lax.ppermute(send, axis, pairs)]
    ppermute x0 -> x4, starting transfers between devices: none -> 5.1 us  [halving_sum(): blocks = keep + lax.ppermute(send, axis, pairs)]
    dynamic_slice x0 -> x4, local copies, waits for them, and re-layouts: none -> 2.76 us  [the longest x2 1.71 us: halving_sum(): keep = lax.dynamic_index_in_dim(blocks, mine, place, keepdims=False)]
  transfers between devices with their start and end apart: 7 -> 11, of which waited for: 4 -> 8; matrix products, arithmetic and copies ran while one was open for 8% -> 9% of each run, Pallas kernels for 0% -> 0%
where the time goes in v2:
time: 231 us; the launch traced here: 230 us
  waiting for transfers between devices  147 us (64%)
  local copies, waits for them, and re-layouts  21.2 us (9%)
  other arithmetic  16.7 us (7%)
  matrix products  15.9 us (7%)
  starting transfers between devices  15.5 us (7%)
  between operations  14.5 us (6%)
    all_gather x1, waiting for transfers between devices, on_device(): all_proj = lax.all_gather(projection_b, 'tile', axis=0, tiled=True)  56.1 us
    all_gather x1, waiting for transfers between devices, on_device(): all_rows = lax.all_gather(dual_b, 'tile', axis=2, tiled=True)  38.9 us
    ppermute x4, waiting for transfers between devices, halving_sum(): blocks = keep + lax.ppermute(send, axis, pairs)  25.9 us
    all_gather x1, waiting for transfers between devices, on_device(): piece = lax.all_gather(back_b, 'az', axis=2, tiled=True)  25.1 us
    ppermute x2, starting transfers between devices, padded_2(): lax.ppermute(lax.slice_in_dim(block, block.shape[dim] - width, None, axis...  6.92 us
    ppermute x4, starting transfers between devices, halving_sum(): blocks = keep + lax.ppermute(send, axis, pairs)  5.1 us
  transfers between devices with their start and end apart: 11, of which 8 were waited for; matrix products, arithmetic and copies ran while one was open for 9% of the time, Pallas kernels for 0%

profile of v2, /device:TPU:1, one launch (start us, length us, event | category | flops | bytes accessed | tf_op | source)
XLA Modules:
  0.0 230.3 jit_solution(12319560989316285791)
XLA Ops:
  7.3 2.7 %fusion.65 = (bf16[1,1024,2,256]{3,2,1,0:T(2,128)(2,1)S(1)}, bf16[1,1024,2,256]{3,2,1,0:T(2,128)(2,1)S(1)}) fusion(bf16[2,1024,2,256]{3,2,1,0:T(2,128)(2,1)} %param.14), kind=kLoop, calls=%fused_computation.134 | loop fusion | bytes 4194304 | tf_op jit(solution)/shard_map/slice | solution.py:59
  11.0 0.5 fusion.43
  11.5 0.9 constant_dynamic-slice_fusion
  12.4 0.5 fusion.3
  12.9 0.6 multiply_subtract_fusion
  13.5 1.3 copy.156
  14.8 1.3 copy.157
  16.2 2.8 %pad_maximum_fusion.5 = f32[2,16,64,2,128]{4,2,1,3,0:T(8,128)} fusion(f32[1,16,64,2,128]{4,2,1,3,0:T(8,128)} %bitcast.181, f32[1,16,64,2,128]{4,2,1,3,0:T(8,128)S(1)} %bitcast.180), kind=kLoop, calls=%fused_computation.11 | loop fusion | flops 524288 | bytes 4194304 | tf_op jit(solution)/shard_map/stack | solution.py:76
  18.9 1.7 constant_dynamic-slice_fusion.4
  20.6 1.0 copy.250
  21.7 3.2 %collective-permute-start = (f32[2,2,2,2,64,2,128]{6,4,5,3,2,1,0:T(8,128)}, f32[2,2,2,2,64,2,128]{6,4,5,3,2,1,0:T(8,128)S(1)}, u32[]{:S(2)}, u32[]{:S(2)}) collective-permute-start(f32[2,2,2,2,64,2,128]{6,4,5,3,2,1,0:T(8,128)} %bitcast.168), channel_id=1, source_target_pairs={{0,16},{16,0},{32,48},{48,32},{64,80},{80,64},{96,112},{112,96},{1... | collective-permute-start | bytes 3145736 | tf_op jit(solution)/shard_map/ppermute | solution.py:36
  24.9 2.5 %collective-permute-done = f32[2,2,2,2,64,2,128]{6,4,5,3,2,1,0:T(8,128)S(1)} collective-permute-done((f32[2,2,2,2,64,2,128]{6,4,5,3,2,1,0:T(8,128)}, f32[2,2,2,2,64,2,128]{6,4,5,3,2,1,0:T(8,128)S(1)}, u32[]{:S(2)}, u32[]{:S(2)}) %collective-permute-start) | collective-permute-done | bytes 1048608 | tf_op jit(solution)/shard_map/ppermute | solution.py:36
  27.4 1.0 copy-done.12
  28.4 1.4 bitcast_add_fusion
  29.9 13.1 %collective-permute-done.1 = f32[2,2,2,64,2,128]{5,3,4,2,1,0:T(8,128)S(1)} collective-permute-done((f32[2,2,2,64,2,128]{5,3,4,2,1,0:T(8,128)S(1)}, f32[2,2,2,64,2,128]{5,3,4,2,1,0:T(8,128)S(1)}, u32[]{:S(2)}, u32[]{:S(2)}) %collective-permute-start.1) | collective-permute-done | bytes 524320 | tf_op jit(solution)/shard_map/ppermute | solution.py:36
  43.3 6.5 %collective-permute-done.2 = f32[2,2,64,2,128]{4,2,3,1,0:T(8,128)S(1)} collective-permute-done((f32[2,2,64,2,128]{4,2,3,1,0:T(8,128)S(1)}, f32[2,2,64,2,128]{4,2,3,1,0:T(8,128)S(1)}, u32[]{:S(2)}, u32[]{:S(2)}) %collective-permute-start.2) | collective-permute-done | bytes 262176 | tf_op jit(solution)/shard_map/ppermute | solution.py:36
  49.9 1.7 collective-permute-start.3
  51.6 3.7 %collective-permute-done.3 = f32[2,64,2,128]{3,1,0,2:T(8,128)S(1)} collective-permute-done((f32[2,64,2,128]{3,1,0,2:T(8,128)S(1)}, f32[2,64,2,128]{3,1,0,2:T(8,128)S(1)}, u32[]{:S(2)}, u32[]{:S(2)}) %collective-permute-start.3) | collective-permute-done | bytes 131104 | tf_op jit(solution)/shard_map/ppermute | solution.py:36
  55.3 0.6 fusion.53
  56.3 56.1 %all-gather.4.cloned.1.call-done = bf16[32,64,2,128]{3,1,2,0:T(8,128)(2,1)} async-done(((bf16[2,64,2,128]{3,1,2,0:T(8,128)(2,1)}), bf16[32,64,2,128]{3,1,2,0:T(8,128)(2,1)}) %all-gather.4.cloned.1.call-update) | async-done | bytes 1048592 | tf_op jit(solution)/shard_map/all_gather | solution.py:79
  112.3 2.0 fusion.38
  114.4 2.3 %fusion.67 = (bf16[2,64,4,128]{3,1,0,2:T(8,128)(2,1)}, f32[2,64,4,128]{3,1,0,2:T(8,128)}) fusion(bf16[2,64,4,128]{3,2,1,0:T(4,128)(2,1)S(1)} %copy-done.15, bf16[8,128,128]{2,1,0:T(8,128)(2,1)S(1)} %copy-done, f32[4,8,64,2,128]{4,1,3,2,0:T(8,128)S(1)} %fusion.38, f32[2,64,4,128]{3,2,1,0:T(4,128)S(1)} %copy-done.14, ...), kind=kOutput, calls=%fused_computation.136 | convolution fusion | flops 805765120 | bytes 3145792 | tf_op jit(solution)/shard_map/kqpcu,quv->cpkv/dot_general | solution.py:89
  116.8 1.7 slice_maximum_fusion
  118.5 1.9 copy.175
  120.4 5.0 %collective-permute-start.4 = (f32[6,512,1]{1,2,0:T(1,128)S(1)}, f32[6,512,1]{1,2,0:T(1,128)S(1)}, u32[]{:S(2)}, u32[]{:S(2)}) collective-permute-start(f32[6,512,1]{1,2,0:T(1,128)S(1)} %copy.175), channel_id=1, source_target_pairs={{0,16},{16,32},{32,48},{48,64},{64,80},{80,96},{96,112},{112,128},... | collective-permute-start | bytes 36872 | tf_op jit(solution)/shard_map/ppermute | solution.py:16
  125.8 1.9 collective-permute-start.5
  128.3 1.4 gather_fusion
  129.7 0.5 copy.177
  130.2 0.6 collective-permute-done.5
  130.8 0.5 copy.178
  131.3 0.9 pad_maximum_fusion.16
  132.2 2.0 collective-permute-start.6
  134.2 1.5 collective-permute-start.7
  135.6 38.9 %all-gather.6.cloned.1.call-done = bf16[2,64,64,128]{3,1,0,2:T(8,128)(2,1)} async-done(((bf16[2,64,4,128]{3,1,0,2:T(8,128)(2,1)}), bf16[2,64,64,128]{3,1,0,2:T(8,128)(2,1)}) %all-gather.6.cloned.1.call-update) | async-done | bytes 2097168 | tf_op jit(solution)/shard_map/all_gather | solution.py:100
  174.5 2.9 %gather_fusion.1 = bf16[12,2,64,128]{3,2,1,0:T(8,128)(2,1)} fusion(bf16[2,64,64,128]{3,1,0,2:T(8,128)(2,1)} %all-gather.6.cloned.1.call-done, s32[1024]{0:T(1024)S(1)} %pad_clamp_fusion), kind=kCustom, calls=%fused_computation.1 | custom fusion | bytes 786480 | tf_op jit(solution)/shard_map/jit(_take)/gather | solution.py:101
  177.4 2.1 fusion.25
  179.7 2.2 pad_maximum_fusion
  182.0 0.6 fusion.30
  182.6 1.0 fusion.33
  184.5 1.3 slice.128
  185.8 1.5 fusion.27
  187.4 0.9 copy.179
  188.3 25.1 %all-gather.8.cloned.1.call-done = bf16[2,2,1024,128]{3,2,0,1:T(8,128)(2,1)} async-done(((bf16[2,2,64,128]{3,2,0,1:T(8,128)(2,1)}), bf16[2,2,1024,128]{3,2,0,1:T(8,128)(2,1)}) %all-gather.8.cloned.1.call-update) | async-done | bytes 1048592 | tf_op jit(solution)/shard_map/all_gather | solution.py:104
  213.3 2.4 %fusion.42 = f32[2,128,256]{2,1,0:T(8,128)S(1)} fusion(bf16[1,1024,2,256]{3,2,1,0:T(2,128)(2,1)S(1)} %copy-done.9, f32[2,1024]{1,0:T(2,128)S(1)} %get-tuple-element.42, f32[2,1024]{1,0:T(2,128)S(1)} %get-tuple-element.51, bf16[2,2,1024,128]{3,2,0,1:T(8,128)(2,1)} %all-gather.8.cloned.1.call-done), kind=kOutput, calls=%fused_computation.70 | convolution fusion | flops 135790592 | bytes 2375680 | tf_op jit(solution)/shard_map/pjh,jpu->jhu/dot_general | solution.py:113
  215.8 1.3 fusion.7
  217.2 2.4 %fusion.41 = f32[2,128,256]{2,1,0:T(8,128)S(1)} fusion(bf16[1,1024,2,256]{3,2,1,0:T(2,128)(2,1)S(1)} %copy-done.9, f32[2,1024]{1,0:T(2,128)S(1)} %get-tuple-element.42, f32[2,1024]{1,0:T(2,128)S(1)} %get-tuple-element.51, bf16[2,2,1024,128]{3,2,0,1:T(8,128)(2,1)} %all-gather.8.cloned.1.call-done), kind=kOutput, calls=%fused_computation.69 | convolution fusion | flops 135790592 | bytes 2375680 | tf_op jit(solution)/shard_map/pjh,jpu->jhu/dot_general | solution.py:117
  219.7 1.3 fusion.8
  221.1 2.7 %fusion.47 = f32[2,512,128]{2,1,0:T(8,128)} fusion(f32[2,512,128]{2,1,0:T(8,128)S(1)} %copy-done.5, f32[2,513,129]{2,1,0:T(8,128)} %get-tuple-element.24, f32[2,513,129]{2,1,0:T(8,128)S(1)} %copy-done.10, f32[1,512,128]{2,1,0:T(8,128)S(1)} %bitcast.187, f32[1,512,128]{2,1,0:T(8,128)S(1)} %bitcast.186), kind=kLoop, calls=%fused_computation.77 | loop fusion | flops 917504 | bytes 3670016 | tf_op jit(solution)/shard_map/sub | solution.py:148
  (88 shorter events, 4.1 us)
Async XLA Ops:
  7.2 107.2 %copy-start = (bf16[8,128,128]{2,1,0:T(8,128)(2,1)S(1)}, bf16[8,128,128]{2,1,0:T(8,128)(2,1)}, u32[]{:S(2)}) copy-start(bf16[8,128,128]{2,1,0:T(8,128)(2,1)} %param.16) | copy-start | bytes 786436
  7.2 105.2 %all-gather.4.cloned.1.call-start = ((), (), s32[]{:S(2)}) async-start(), calls=%async_computation | async-start | bytes 1114112 | tf_op jit(solution)/shard_map/all_gather | solution.py:79
  7.2 2.8 %copy-start.3 = (f32[2,512,128]{2,1,0:T(8,128)S(1)}, f32[2,512,128]{2,1,0:T(8,128)}, u32[]{:S(2)}) copy-start(f32[2,512,128]{2,1,0:T(8,128)} %param.10) | copy-start | bytes 1572868
  10.0 1.0 copy-start.8
  10.0 2.9 %copy-start.6 = (bf16[1,1024,2,256]{3,2,1,0:T(2,128)(2,1)}, bf16[1,1024,2,256]{3,2,1,0:T(2,128)(2,1)S(1)}, u32[]{:S(2)}) copy-start(bf16[1,1024,2,256]{3,2,1,0:T(2,128)(2,1)S(1)} %get-tuple-element.29) | copy-start | bytes 3145732
  14.8 1.3 copy-start.11
  21.7 5.7 %collective-permute-start = (f32[2,2,2,2,64,2,128]{6,4,5,3,2,1,0:T(8,128)}, f32[2,2,2,2,64,2,128]{6,4,5,3,2,1,0:T(8,128)S(1)}, u32[]{:S(2)}, u32[]{:S(2)}) collective-permute-start(f32[2,2,2,2,64,2,128]{6,4,5,3,2,1,0:T(8,128)} %bitcast.168), channel_id=1, source_target_pairs={{0,16},{16,0},{32,48},{48,32},{64,80},{80,64},{96,112},{112,96},{1... | collective-permute-start | bytes 3145736 | tf_op jit(solution)/shard_map/ppermute | solution.py:36
  27.4 1.0 copy-start.12
  29.8 13.2 %collective-permute-start.1 = (f32[2,2,2,64,2,128]{5,3,4,2,1,0:T(8,128)S(1)}, f32[2,2,2,64,2,128]{5,3,4,2,1,0:T(8,128)S(1)}, u32[]{:S(2)}, u32[]{:S(2)}) collective-permute-start(f32[2,2,2,64,2,128]{5,3,4,2,1,0:T(8,128)S(1)} %dynamic-slice_bitcast_fusion), channel_id=1, source_target_pairs={{0,128},{16,144},{32,160},{48,176},{64,192},{80,208},{96,224},{112... | collective-permute-start | bytes 1572872 | tf_op jit(solution)/shard_map/ppermute | solution.py:36
  43.1 13.0 %copy-start.16 = (s32[32,1,6]{0,1,2:T(1,128)S(1)}, s32[32,1,6]{0,1,2:T(1,128)}, u32[]{:S(2)}) copy-start(s32[32,1,6]{0,1,2:T(1,128)} %param.17) | copy-start | bytes 2308
  43.1 13.0 %copy-start.17 = (s32[32,1,6]{0,1,2:T(1,128)S(1)}, s32[32,1,6]{0,1,2:T(1,128)}, u32[]{:S(2)}) copy-start(s32[32,1,6]{0,1,2:T(1,128)} %param.18) | copy-start | bytes 2308
  43.1 13.1 %copy-start.20 = (s32[64]{0:T(128)S(1)}, s32[64]{0:T(128)}, u32[]{:S(2)}) copy-start(s32[64]{0:T(128)} %param.19) | copy-start | bytes 772
  43.2 6.7 %collective-permute-start.2 = (f32[2,2,64,2,128]{4,2,3,1,0:T(8,128)S(1)}, f32[2,2,64,2,128]{4,2,3,1,0:T(8,128)S(1)}, u32[]{:S(2)}, u32[]{:S(2)}) collective-permute-start(f32[2,2,64,2,128]{4,2,3,1,0:T(8,128)S(1)} %dynamic-slice_bitcast_fusion.1), channel_id=1, source_target_pairs={{0,32},{16,48},{32,0},{48,16},{64,96},{80,112},{96,64},{112,80},{1... | collective-permute-start | bytes 786440 | tf_op jit(solution)/shard_map/ppermute | solution.py:36
  49.9 5.4 %collective-permute-start.3 = (f32[2,64,2,128]{3,1,0,2:T(8,128)S(1)}, f32[2,64,2,128]{3,1,0,2:T(8,128)S(1)}, u32[]{:S(2)}, u32[]{:S(2)}) collective-permute-start(f32[2,64,2,128]{3,1,0,2:T(8,128)S(1)} %bitcast.190), channel_id=1, source_target_pairs={{0,64},{16,80},{32,96},{48,112},{64,0},{80,16},{96,32},{112,48},{1... | collective-permute-start | bytes 393224 | tf_op jit(solution)/shard_map/ppermute | solution.py:36
  56.0 118.5 %all-gather.6.cloned.1.call-start = ((), (), s32[]{:S(2)}) async-start(), calls=%async_computation.1 | async-start | bytes 2228224 | tf_op jit(solution)/shard_map/all_gather | solution.py:100
  56.3 58.1 %copy-start.14 = (f32[2,64,4,128]{3,2,1,0:T(4,128)S(1)}, f32[2,64,4,128]{3,2,1,0:T(4,128)}, u32[]{:S(2)}) copy-start(f32[2,64,4,128]{3,2,1,0:T(4,128)} %param.12) | copy-start | bytes 786436
  56.3 58.1 %copy-start.15 = (bf16[2,64,4,128]{3,2,1,0:T(4,128)(2,1)S(1)}, bf16[2,64,4,128]{3,2,1,0:T(4,128)(2,1)}, u32[]{:S(2)}) copy-start(bf16[2,64,4,128]{3,2,1,0:T(4,128)(2,1)} %param.13) | copy-start | bytes 393220
  114.4 2.4 %copy-start.1 = (f32[2,2,512,128]{3,2,1,0:T(8,128)S(1)}, f32[2,2,512,128]{3,2,1,0:T(8,128)}, u32[]{:S(2)}) copy-start(f32[2,2,512,128]{3,2,1,0:T(8,128)} %param.11) | copy-start | bytes 3145732
  116.8 96.6 %all-gather.8.cloned.1.call-start = ((), (), s32[]{:S(2)}) async-start(), calls=%async_computation.2 | async-start | bytes 1114112 | tf_op jit(solution)/shard_map/all_gather | solution.py:104
  120.4 9.3 %collective-permute-start.4 = (f32[6,512,1]{1,2,0:T(1,128)S(1)}, f32[6,512,1]{1,2,0:T(1,128)S(1)}, u32[]{:S(2)}, u32[]{:S(2)}) collective-permute-start(f32[6,512,1]{1,2,0:T(1,128)S(1)} %copy.175), channel_id=1, source_target_pairs={{0,16},{16,32},{32,48},{48,64},{64,80},{80,96},{96,112},{112,128},... | collective-permute-start | bytes 36872 | tf_op jit(solution)/shard_map/ppermute | solution.py:16
  125.8 5.0 %collective-permute-start.5 = (f32[6,512,1]{1,2,0:T(1,128)S(1)}, f32[6,512,1]{1,2,0:T(1,128)S(1)}, u32[]{:S(2)}, u32[]{:S(2)}) collective-permute-start(f32[6,512,1]{1,2,0:T(1,128)S(1)} %copy.176), channel_id=1, source_target_pairs={{16,0},{32,16},{48,32},{64,48},{80,64},{96,80},{112,96},{128,112},... | collective-permute-start | bytes 36872 | tf_op jit(solution)/shard_map/ppermute | solution.py:19
  132.2 47.5 %collective-permute-start.6 = (f32[6,1,130]{2,1,0:T(1,128)S(1)}, f32[6,1,130]{2,1,0:T(1,128)S(1)}, u32[]{:S(2)}, u32[]{:S(2)}) collective-permute-start(f32[6,1,130]{2,1,0:T(1,128)S(1)} %get-tuple-element.22), channel_id=1, source_target_pairs={{0,1},{1,2},{2,3},{3,4},{4,5},{5,6},{6,7},{7,8},{8,9},{9,10},{10,1... | collective-permute-start | bytes 9368 | tf_op jit(solution)/shard_map/ppermute | solution.py:16
  134.2 45.5 %collective-permute-start.7 = (f32[6,1,130]{2,1,0:T(1,128)S(1)}, f32[6,1,130]{2,1,0:T(1,128)S(1)}, u32[]{:S(2)}, u32[]{:S(2)}) collective-permute-start(f32[6,1,130]{2,1,0:T(1,128)S(1)} %get-tuple-element.21), channel_id=1, source_target_pairs={{1,0},{2,1},{3,2},{4,3},{5,4},{6,5},{7,6},{8,7},{9,8},{10,9},{11,1... | collective-permute-start | bytes 9368 | tf_op jit(solution)/shard_map/ppermute | solution.py:19
  179.7 2.3 copy-start.2
  179.7 2.3 copy-start.4
  185.8 1.5 copy-start.13
  185.8 27.5 %copy-start.9 = (bf16[1,1024,2,256]{3,2,1,0:T(2,128)(2,1)S(1)}, bf16[1,1024,2,256]{3,2,1,0:T(2,128)(2,1)}, u32[]{:S(2)}) copy-start(bf16[1,1024,2,256]{3,2,1,0:T(2,128)(2,1)} %copy-done.8) | copy-start | bytes 3145732
  213.3 2.5 %copy-start.7 = (bf16[1,1024,2,256]{3,2,1,0:T(2,128)(2,1)S(1)}, bf16[1,1024,2,256]{3,2,1,0:T(2,128)(2,1)}, u32[]{:S(2)}) copy-start(bf16[1,1024,2,256]{3,2,1,0:T(2,128)(2,1)} %copy-done.6) | copy-start | bytes 3145732
  213.3 2.5 %copy-start.18 = (bf16[2,2,1024,128]{3,2,0,1:T(8,128)(2,1)S(1)}, bf16[2,2,1024,128]{3,2,0,1:T(8,128)(2,1)}, u32[]{:S(2)}) copy-start(bf16[2,2,1024,128]{3,2,0,1:T(8,128)(2,1)} %all-gather.8.cloned.1.call-done) | copy-start | bytes 3145732
  217.2 2.4 %copy-start.19 = (bf16[2,2,1024,128]{3,2,0,1:T(8,128)(2,1)S(1)}, bf16[2,2,1024,128]{3,2,0,1:T(8,128)(2,1)}, u32[]{:S(2)}) copy-start(bf16[2,2,1024,128]{3,2,0,1:T(8,128)(2,1)} %all-gather.8.cloned.1.call-done) | copy-start | bytes 3145732
  219.7 1.5 copy-start.5
  219.7 1.5 copy-start.10
Sparse Core Ops, SparseCore 0:
  56.1 56.1 all-gather.3
  116.9 57.5 all-gather.5
  179.6 33.6 all-gather.7

commit v3 on v2

--- a/solution.py
+++ b/solution.py
@@ -35,6 +35,22 @@
         pairs = [(i, i ^ bit) for i in range(count)]
         blocks = keep + lax.ppermute(send, axis, pairs)
     return blocks
+
+
+def doubling_gather(block, axis, bits):
+    me = lax.axis_index(axis)
+    count = lax.axis_size(axis)
+    done = []
+    for bit in bits:
+        mine = (me // bit) % 2
+        pairs = [(i, i ^ bit) for i in range(count)]
+        got = lax.ppermute(block, axis, pairs)
+        place = sum(1 for other in done if other > bit)
+        low = jnp.where(mine == 0, block, got)
+        high = jnp.where(mine == 0, got, block)
+        block = jnp.stack([low, high], axis=place)
+        done.append(bit)
+    return block.reshape(count, *block.shape[len(bits):])
 
 
 def on_device(
@@ -76,7 +92,8 @@
     parts = jnp.stack([real_part, imag_part], axis=0).reshape(2, az_count, -1, tiles_dev, columns)
     summed = halving_sum(jnp.moveaxis(parts, 1, 0), "az", (1, 8, 2, 4))
     projection_b = jnp.transpose(summed, (2, 1, 0, 3)).astype(jnp.bfloat16)
-    all_proj = lax.all_gather(projection_b, "tile", axis=0, tiled=True)
+    all_proj = doubling_gather(projection_b, "tile", (2, 1, 8, 4))
+    all_proj = all_proj.reshape(-1, *all_proj.shape[2:])
     phase_ids = jnp.arange(kernels.shape[0], dtype=jnp.int32)
     my_rows = tile_index * rows_dev + jnp.arange(rows_dev, dtype=jnp.int32)
     hits = (foot_block[:, :, None, None] == my_rows[None, None, :, None]) & (
@@ -97,11 +114,13 @@
         0.0,
     )
     dual_b = dual_new.astype(jnp.bfloat16)
-    all_rows = lax.all_gather(dual_b, "tile", axis=2, tiled=True)
+    all_rows = doubling_gather(jnp.moveaxis(dual_b, 2, 0), "tile", (2, 1, 8, 4))
+    all_rows = jnp.moveaxis(all_rows.reshape(-1, *all_rows.shape[2:]), 0, 2)
     chosen = jnp.take(all_rows, foot_mine, axis=2)
     back = jnp.einsum("cpjfv,jfuv->cjpu", chosen, kern_mine, preferred_element_type=jnp.float32)
     back_b = back.astype(jnp.bfloat16)
-    piece = lax.all_gather(back_b, "az", axis=2, tiled=True)
+    piece = doubling_gather(jnp.moveaxis(back_b, 2, 0), "az", (4, 8, 2, 1))
+    piece = jnp.moveaxis(piece.reshape(-1, *piece.shape[2:]), 0, 2)
     weight_re = col_mine[0].T[..., None]
     weight_im = col_mine[1].T[..., None]
     back_re = piece[0].astype(jnp.float32)

time: 231 us -> 193 us (0.84)
  waiting for transfers between devices: 147 us -> 78.2 us
  starting transfers between devices: 15.5 us -> 51.5 us
  between operations: 14.5 us -> 1.53 us
  other arithmetic: 16.7 us -> 23.3 us
  local copies, waits for them, and re-layouts: 21.2 us -> 24.5 us
  matrix products: 15.9 us -> 13.2 us
    all_gather x3 -> x0, waiting for transfers between devices: 120 us -> none  [the longest x1 56.1 us: on_device(): all_proj = lax.all_gather(projection_b, 'tile', axis=0, tiled=True)]
    ppermute x0 -> x12, waiting for transfers between devices: none -> 48.6 us  [doubling_gather(): got = lax.ppermute(block, axis, pairs)]
    ppermute x0 -> x12, starting transfers between devices: none -> 28.5 us  [doubling_gather(): got = lax.ppermute(block, axis, pairs)]
    ppermute x2, starting transfers between devices: 6.92 us -> 14.7 us  [padded_2(): lax.ppermute(lax.slice_in_dim(block, block.shape[dim] - width, None, axis...]
    another operation x2, other arithmetic: 1.58 us -> 5.12 us  [on_device(): jnp.stack([grad_rows, grad_cols])]
    another operation x0 -> x24, other arithmetic: none -> 3.52 us  [doubling_gather(): block = jnp.stack([low, high], axis=place)]
    ppermute x2, waiting for transfers between devices: 0.64 us -> 3.81 us  [padded_2(): lax.ppermute(lax.slice_in_dim(block, 0, width, axis=dim), axis, backward)]
    unnamed x46 -> x68, local copies, waits for them, and re-layouts: 2.36 us -> 5.42 us
  transfers between devices with their start and end apart: 11 -> 20, of which waited for: 8 -> 15; matrix products, arithmetic and copies ran while one was open for 9% -> 13% of each run, Pallas kernels for 0% -> 0%
where the time goes in v3:
time: 193 us; the launch traced here: 192 us
  waiting for transfers between devices  78.2 us (41%)
  starting transfers between devices  51.5 us (27%)
  local copies, waits for them, and re-layouts  24.5 us (13%)
  other arithmetic  23.3 us (12%)
  matrix products  13.2 us (7%)
    ppermute x12, waiting for transfers between devices, doubling_gather(): got = lax.ppermute(block, axis, pairs)  48.6 us
    ppermute x12, starting transfers between devices, doubling_gather(): got = lax.ppermute(block, axis, pairs)  28.5 us
    ppermute x4, waiting for transfers between devices, halving_sum(): blocks = keep + lax.ppermute(send, axis, pairs)  25.8 us
    ppermute x2, starting transfers between devices, padded_2(): lax.ppermute(lax.slice_in_dim(block, block.shape[dim] - width, None, axis...  14.7 us
    unnamed x68, local copies, waits for them, and re-layouts  5.42 us
    another operation x2, other arithmetic, on_device(): jnp.stack([grad_rows, grad_cols])  5.12 us
    ppermute x4, starting transfers between devices, halving_sum(): blocks = keep + lax.ppermute(send, axis, pairs)  5.11 us
  transfers between devices with their start and end apart: 20, of which 15 were waited for; matrix products, arithmetic and copies ran while one was open for 13% of the time, Pallas kernels for 0%

profile of v3, /device:TPU:1, one launch (start us, length us, event | category | flops | bytes accessed | tf_op | source)
XLA Modules:
  0.0 192.3 jit_solution(12060806445480301277)
XLA Ops:
  0.7 2.7 %fusion.66 = (bf16[1,1024,2,256]{3,2,1,0:T(2,128)(2,1)S(1)}, bf16[1,1024,2,256]{3,2,1,0:T(2,128)(2,1)S(1)}) fusion(bf16[2,1024,2,256]{3,2,1,0:T(2,128)(2,1)} %param.14), kind=kLoop, calls=%fused_computation.171 | loop fusion | bytes 4194304 | tf_op jit(solution)/shard_map/slice | solution.py:75
  7.0 1.6 multiply_subtract_fusion
  8.8 1.6 copy.129
  12.0 3.2 %collective-permute-start = (f32[2,2,2,2,64,2,128]{6,4,5,3,2,1,0:T(8,128)}, f32[2,2,2,2,64,2,128]{6,4,5,3,2,1,0:T(8,128)S(1)}, u32[]{:S(2)}, u32[]{:S(2)}) collective-permute-start(f32[2,2,2,2,64,2,128]{6,4,5,3,2,1,0:T(8,128)} %bitcast.231), channel_id=1, source_target_pairs={{0,16},{16,0},{32,48},{48,32},{64,80},{80,64},{96,112},{112,96},{1... | collective-permute-start | bytes 3145736 | tf_op jit(solution)/shard_map/ppermute | solution.py:36
  15.2 2.5 %collective-permute-done = f32[2,2,2,2,64,2,128]{6,4,5,3,2,1,0:T(8,128)S(1)} collective-permute-done((f32[2,2,2,2,64,2,128]{6,4,5,3,2,1,0:T(8,128)}, f32[2,2,2,2,64,2,128]{6,4,5,3,2,1,0:T(8,128)S(1)}, u32[]{:S(2)}, u32[]{:S(2)}) %collective-permute-start) | collective-permute-done | bytes 1048608 | tf_op jit(solution)/shard_map/ppermute | solution.py:36
  18.7 1.4 bitcast_add_fusion
  20.2 13.1 %collective-permute-done.1 = f32[2,2,2,64,2,128]{5,3,4,2,1,0:T(8,128)S(1)} collective-permute-done((f32[2,2,2,64,2,128]{5,3,4,2,1,0:T(8,128)S(1)}, f32[2,2,2,64,2,128]{5,3,4,2,1,0:T(8,128)S(1)}, u32[]{:S(2)}, u32[]{:S(2)}) %collective-permute-start.1) | collective-permute-done | bytes 524320 | tf_op jit(solution)/shard_map/ppermute | solution.py:36
  33.6 6.5 %collective-permute-done.2 = f32[2,2,64,2,128]{4,2,3,1,0:T(8,128)S(1)} collective-permute-done((f32[2,2,64,2,128]{4,2,3,1,0:T(8,128)S(1)}, f32[2,2,64,2,128]{4,2,3,1,0:T(8,128)S(1)}, u32[]{:S(2)}, u32[]{:S(2)}) %collective-permute-start.2) | collective-permute-done | bytes 262176 | tf_op jit(solution)/shard_map/ppermute | solution.py:36
  40.2 1.7 collective-permute-start.3
  41.9 3.7 %collective-permute-done.3 = f32[2,64,2,128]{3,1,0,2:T(8,128)S(1)} collective-permute-done((f32[2,64,2,128]{3,1,0,2:T(8,128)S(1)}, f32[2,64,2,128]{3,1,0,2:T(8,128)S(1)}, u32[]{:S(2)}, u32[]{:S(2)}) %collective-permute-start.3) | collective-permute-done | bytes 131104 | tf_op jit(solution)/shard_map/ppermute | solution.py:36
  45.7 5.3 %collective-permute-start.4 = (bf16[2,64,2,128]{3,1,2,0:T(8,128)(2,1)S(1)}, bf16[2,64,2,128]{3,1,2,0:T(8,128)(2,1)S(1)}, u32[]{:S(2)}, u32[]{:S(2)}) collective-permute-start(bf16[2,64,2,128]{3,1,2,0:T(8,128)(2,1)S(1)} %fusion.54), channel_id=1, source_target_pairs={{0,2},{1,3},{2,0},{3,1},{4,6},{5,7},{6,4},{7,5},{8,10},{9,11},{10,... | collective-permute-start | bytes 196616 | tf_op jit(solution)/shard_map/ppermute | solution.py:47
  50.9 2.0 %collective-permute-done.4 = bf16[2,64,2,128]{3,1,2,0:T(8,128)(2,1)S(1)} collective-permute-done((bf16[2,64,2,128]{3,1,2,0:T(8,128)(2,1)S(1)}, bf16[2,64,2,128]{3,1,2,0:T(8,128)(2,1)S(1)}, u32[]{:S(2)}, u32[]{:S(2)}) %collective-permute-start.4) | collective-permute-done | bytes 65568 | tf_op jit(solution)/shard_map/ppermute | solution.py:47
  52.9 2.5 %collective-permute-start.5 = (bf16[2,2,64,2,128]{4,2,3,1,0:T(8,128)(2,1)S(1)}, bf16[2,2,64,2,128]{4,2,3,1,0:T(8,128)(2,1)S(1)}, u32[]{:S(2)}, u32[]{:S(2)}) collective-permute-start(bf16[2,2,64,2,128]{4,2,3,1,0:T(8,128)(2,1)S(1)} %pad_maximum_fusion.26), channel_id=1, source_target_pairs={{0,1},{1,0},{2,3},{3,2},{4,5},{5,4},{6,7},{7,6},{8,9},{9,8},{10,11... | collective-permute-start | bytes 393224 | tf_op jit(solution)/shard_map/ppermute | solution.py:47
  55.5 4.5 %collective-permute-done.5 = bf16[2,2,64,2,128]{4,2,3,1,0:T(8,128)(2,1)S(1)} collective-permute-done((bf16[2,2,64,2,128]{4,2,3,1,0:T(8,128)(2,1)S(1)}, bf16[2,2,64,2,128]{4,2,3,1,0:T(8,128)(2,1)S(1)}, u32[]{:S(2)}, u32[]{:S(2)}) %collective-permute-start.5) | collective-permute-done | bytes 131104 | tf_op jit(solution)/shard_map/ppermute | solution.py:47
  60.1 3.0 %collective-permute-start.6 = (bf16[2,2,2,64,2,128]{5,3,4,2,1,0:T(8,128)(2,1)S(1)}, bf16[2,2,2,64,2,128]{5,3,4,2,1,0:T(8,128)(2,1)S(1)}, u32[]{:S(2)}, u32[]{:S(2)}) collective-permute-start(bf16[2,2,2,64,2,128]{5,3,4,2,1,0:T(8,128)(2,1)S(1)} %pad_maximum_fusion.23), channel_id=1, source_target_pairs={{0,8},{1,9},{2,10},{3,11},{4,12},{5,13},{6,14},{7,15},{8,0},{9,1},... | collective-permute-start | bytes 786440 | tf_op jit(solution)/shard_map/ppermute | solution.py:47
  63.1 3.8 %collective-permute-done.6 = bf16[2,2,2,64,2,128]{5,3,4,2,1,0:T(8,128)(2,1)S(1)} collective-permute-done((bf16[2,2,2,64,2,128]{5,3,4,2,1,0:T(8,128)(2,1)S(1)}, bf16[2,2,2,64,2,128]{5,3,4,2,1,0:T(8,128)(2,1)S(1)}, u32[]{:S(2)}, u32[]{:S(2)}) %collective-permute-start.6) | collective-permute-done | bytes 262176 | tf_op jit(solution)/shard_map/ppermute | solution.py:47
  67.0 1.4 collective-permute-start.7
  68.5 10.1 %collective-permute-done.7 = bf16[2,2,2,2,64,2,128]{6,4,5,3,2,1,0:T(8,128)(2,1)S(1)} collective-permute-done((bf16[2,2,2,2,64,2,128]{6,4,5,3,2,1,0:T(8,128)(2,1)S(1)}, bf16[2,2,2,2,64,2,128]{6,4,5,3,2,1,0:T(8,128)(2,1)S(1)}, u32[]{:S(2)}, u32[]{:S(2)}) %collective-permute-start.7) | collective-permute-done | bytes 524320 | tf_op jit(solution)/shard_map/ppermute | solution.py:47
  79.7 1.6 fusion.21
  81.3 4.4 %collective-permute-start.8 = (bf16[4,2,64,128]{3,2,1,0:T(8,128)(2,1)S(1)}, bf16[4,2,64,128]{3,2,1,0:T(8,128)(2,1)S(1)}, u32[]{:S(2)}, u32[]{:S(2)}) collective-permute-start(bf16[4,2,64,128]{3,2,1,0:T(8,128)(2,1)S(1)} %convert_bitcast_fusion), channel_id=1, source_target_pairs={{0,2},{1,3},{2,0},{3,1},{4,6},{5,7},{6,4},{7,5},{8,10},{9,11},{10,... | collective-permute-start | bytes 393224 | tf_op jit(solution)/shard_map/ppermute | solution.py:47
  85.7 3.4 %collective-permute-done.8 = bf16[4,2,64,128]{3,2,1,0:T(8,128)(2,1)S(1)} collective-permute-done((bf16[4,2,64,128]{3,2,1,0:T(8,128)(2,1)S(1)}, bf16[4,2,64,128]{3,2,1,0:T(8,128)(2,1)S(1)}, u32[]{:S(2)}, u32[]{:S(2)}) %collective-permute-start.8) | collective-permute-done | bytes 131104 | tf_op jit(solution)/shard_map/ppermute | solution.py:47
  89.7 1.7 slice_maximum_fusion
  91.4 1.9 copy.150
  93.3 12.5 %collective-permute-start.16 = (f32[6,512,1]{1,2,0:T(1,128)S(1)}, f32[6,512,1]{1,2,0:T(1,128)S(1)}, u32[]{:S(2)}, u32[]{:S(2)}) collective-permute-start(f32[6,512,1]{1,2,0:T(1,128)S(1)} %copy.150), channel_id=1, source_target_pairs={{0,16},{16,32},{32,48},{48,64},{64,80},{80,96},{96,112},{112,128},... | collective-permute-start | bytes 36872 | tf_op jit(solution)/shard_map/ppermute | solution.py:16
  106.3 1.9 collective-permute-start.17
  108.3 2.8 %collective-permute-start.10 = (bf16[2,2,4,2,64,128]{5,4,3,2,0,1:T(8,128)(2,1)S(1)}, bf16[2,2,4,2,64,128]{5,4,3,2,0,1:T(8,128)(2,1)S(1)}, u32[]{:S(2)}, u32[]{:S(2)}) collective-permute-start(bf16[2,2,4,2,64,128]{5,4,3,2,0,1:T(8,128)(2,1)S(1)} %pad_maximum_fusion.21), channel_id=1, source_target_pairs={{0,8},{1,9},{2,10},{3,11},{4,12},{5,13},{6,14},{7,15},{8,0},{9,1},... | collective-permute-start | bytes 1572872 | tf_op jit(solution)/shard_map/ppermute | solution.py:47
  112.1 11.4 %collective-permute-done.10 = bf16[2,2,4,2,64,128]{5,4,3,2,0,1:T(8,128)(2,1)S(1)} collective-permute-done((bf16[2,2,4,2,64,128]{5,4,3,2,0,1:T(8,128)(2,1)S(1)}, bf16[2,2,4,2,64,128]{5,4,3,2,0,1:T(8,128)(2,1)S(1)}, u32[]{:S(2)}, u32[]{:S(2)}) %collective-permute-start.10) | collective-permute-done | bytes 524320 | tf_op jit(solution)/shard_map/ppermute | solution.py:47
  129.1 1.5 pad_maximum_fusion.28
  130.6 2.2 %collective-permute-start.18 = (f32[6,1,130]{2,1,0:T(1,128)}, f32[6,1,130]{2,1,0:T(1,128)S(1)}, u32[]{:S(2)}, u32[]{:S(2)}) collective-permute-start(f32[6,1,130]{2,1,0:T(1,128)} %get-tuple-element.19), channel_id=1, source_target_pairs={{0,1},{1,2},{2,3},{3,4},{4,5},{5,6},{6,7},{7,8},{8,9},{9,10},{10,1... | collective-permute-start | bytes 9368 | tf_op jit(solution)/shard_map/ppermute | solution.py:16
  134.7 1.5 gather_fusion
  136.1 3.8 %collective-permute-done.19 = f32[6,1,130]{2,1,0:T(1,128)} collective-permute-done((f32[6,1,130]{2,1,0:T(1,128)}, f32[6,1,130]{2,1,0:T(1,128)}, u32[]{:S(2)}, u32[]{:S(2)}) %collective-permute-start.19) | collective-permute-done | bytes 3152 | tf_op jit(solution)/shard_map/ppermute | solution.py:19
  140.0 3.2 %fusion.33 = f32[1,2,513,129]{3,2,1,0:T(8,128)} fusion(f32[6,1,130]{2,1,0:T(1,128)} %collective-permute-done.19, f32[6,512,1]{2,1,0:T(8,128)S(1)} %copy.153, f32[6,512,1]{2,1,0:T(8,128)S(1)} %copy.152, f32[4,512,128]{2,1,0:T(8,128)} %bitcast.236, f32[2,512,128]{2,1,0:T(8,128)} %param.10, f32[6,1,130]{2,1,0:T(1,128)S(1)} %collective-permute-done.18, ...), kind=kLoop, calls=%fused_computation.53 | loop fusion | flops 1323540 | bytes 2133609 | tf_op jit(solution)/shard_map/stack | solution.py:155
  143.2 6.6 %collective-permute-done.11 = bf16[2,2,2,4,2,64,128]{6,5,4,3,1,2,0:T(8,128)(2,1)} collective-permute-done((bf16[2,2,2,4,2,64,128]{6,5,4,3,1,2,0:T(8,128)(2,1)}, bf16[2,2,2,4,2,64,128]{6,5,4,3,1,2,0:T(8,128)(2,1)}, u32[]{:S(2)}, u32[]{:S(2)}) %collective-permute-start.11) | collective-permute-done | bytes 1048608 | tf_op jit(solution)/shard_map/ppermute | solution.py:47
  149.8 1.4 select_bitcast_fusion.1
  151.3 1.5 copy.140
  152.8 3.1 %gather_fusion.1 = bf16[12,2,64,128]{3,2,1,0:T(8,128)(2,1)} fusion(bf16[2,64,64,128]{3,1,0,2:T(8,128)(2,1)} %bitcast.246, s32[1024]{0:T(1024)} %pad_clamp_fusion), kind=kCustom, calls=%fused_computation.1 | custom fusion | bytes 786480 | tf_op jit(solution)/shard_map/jit(_take)/gather | solution.py:119
  155.9 1.5 fusion.25
  157.6 1.9 fusion.30
  159.5 2.7 %collective-permute-done.12 = bf16[64,2,2,128]{3,0,1,2:T(8,128)(2,1)S(1)} collective-permute-done((bf16[64,2,2,128]{3,0,1,2:T(8,128)(2,1)S(1)}, bf16[64,2,2,128]{3,0,1,2:T(8,128)(2,1)S(1)}, u32[]{:S(2)}, u32[]{:S(2)}) %collective-permute-start.12) | collective-permute-done | bytes 65568 | tf_op jit(solution)/shard_map/ppermute | solution.py:47
  163.5 1.6 pad_maximum_fusion
  166.2 2.4 %collective-permute-start.14 = (bf16[2,2,64,2,2,128]{5,2,3,4,1,0:T(8,128)(2,1)S(1)}, bf16[2,2,64,2,2,128]{5,2,3,4,1,0:T(8,128)(2,1)S(1)}, u32[]{:S(2)}, u32[]{:S(2)}) collective-permute-start(bf16[2,2,64,2,2,128]{5,2,3,4,1,0:T(8,128)(2,1)S(1)} %pad_maximum_fusion.25), channel_id=1, source_target_pairs={{0,32},{16,48},{32,0},{48,16},{64,96},{80,112},{96,64},{112,80},{1... | collective-permute-start | bytes 786440 | tf_op jit(solution)/shard_map/ppermute | solution.py:47
  169.1 3.2 %collective-permute-done.14 = bf16[2,2,64,2,2,128]{5,2,3,4,1,0:T(8,128)(2,1)S(1)} collective-permute-done((bf16[2,2,64,2,2,128]{5,2,3,4,1,0:T(8,128)(2,1)S(1)}, bf16[2,2,64,2,2,128]{5,2,3,4,1,0:T(8,128)(2,1)S(1)}, u32[]{:S(2)}, u32[]{:S(2)}) %collective-permute-start.14) | collective-permute-done | bytes 262176 | tf_op jit(solution)/shard_map/ppermute | solution.py:47
  172.4 4.9 %collective-permute-start.15 = (bf16[2,2,2,64,2,2,128]{6,3,4,5,1,0,2:T(8,128)(2,1)S(1)}, bf16[2,2,2,64,2,2,128]{6,3,4,5,1,0,2:T(8,128)(2,1)S(1)}, u32[]{:S(2)}, u32[]{:S(2)}) collective-permute-start(bf16[2,2,2,64,2,2,128]{6,3,4,5,1,0,2:T(8,128)(2,1)S(1)} %pad_maximum_fusion.22), channel_id=1, source_target_pairs={{0,16},{16,0},{32,48},{48,32},{64,80},{80,64},{96,112},{112,96},{1... | collective-permute-start | bytes 1572872 | tf_op jit(solution)/shard_map/ppermute | solution.py:47
  177.7 1.3 slice.128
  181.5 1.5 copy-done.11
  184.2 1.3 fusion.41
  187.1 2.4 %fusion.8 = f32[2,256,128]{1,2,0:T(8,128)S(1)} fusion(f32[2,128,256]{2,1,0:T(8,128)S(1)} %fusion.41, bf16[1,1024,2,256]{3,2,1,0:T(2,128)(2,1)S(1)} %copy-done.9, f32[2,1024]{1,0:T(2,128)S(1)} %copy-done.25, f32[2,1024]{1,0:T(2,128)S(1)} %copy-done.26, bf16[2,2,1024,128]{3,2,1,0:T(8,128)(2,1)} %bitcast.256), kind=kOutput, calls=%fused_computation.29 | convolution fusion | flops 135856128 | bytes 2637824 | tf_op jit(solution)/shard_map/pjh,jpu->jhu/dot_general | solution.py:137
  189.6 2.7 %fusion.47 = f32[2,512,128]{2,1,0:T(8,128)} fusion(f32[2,512,128]{2,1,0:T(8,128)S(1)} %copy-done.6, f32[2,513,129]{2,1,0:T(8,128)} %get-tuple-element.21, f32[2,513,129]{2,1,0:T(8,128)S(1)} %get-tuple-element.20, f32[1,512,128]{2,1,0:T(8,128)S(1)} %bitcast.252, f32[1,512,128]{2,1,0:T(8,128)S(1)} %bitcast.251), kind=kLoop, calls=%fused_computation.83 | loop fusion | flops 917504 | bytes 3670016 | tf_op jit(solution)/shard_map/sub | solution.py:167
  (152 shorter events, 26.5 us)
Async XLA Ops:
  0.6 78.9 %copy-start = (bf16[8,128,128]{2,1,0:T(8,128)(2,1)S(1)}, bf16[8,128,128]{2,1,0:T(8,128)(2,1)}, u32[]{:S(2)}) copy-start(bf16[8,128,128]{2,1,0:T(8,128)(2,1)} %param.16) | copy-start | bytes 786436
  0.7 2.8 %copy-start.4 = (f32[2,512,128]{2,1,0:T(8,128)S(1)}, f32[2,512,128]{2,1,0:T(8,128)}, u32[]{:S(2)}) copy-start(f32[2,512,128]{2,1,0:T(8,128)} %param.10) | copy-start | bytes 1572868
  3.4 1.0 copy-start.10
  3.5 3.5 %copy-start.8 = (bf16[1,1024,2,256]{3,2,1,0:T(2,128)(2,1)}, bf16[1,1024,2,256]{3,2,1,0:T(2,128)(2,1)S(1)}, u32[]{:S(2)}) copy-start(bf16[1,1024,2,256]{3,2,1,0:T(2,128)(2,1)S(1)} %get-tuple-element.28) | copy-start | bytes 3145732
  12.0 5.7 %collective-permute-start = (f32[2,2,2,2,64,2,128]{6,4,5,3,2,1,0:T(8,128)}, f32[2,2,2,2,64,2,128]{6,4,5,3,2,1,0:T(8,128)S(1)}, u32[]{:S(2)}, u32[]{:S(2)}) collective-permute-start(f32[2,2,2,2,64,2,128]{6,4,5,3,2,1,0:T(8,128)} %bitcast.231), channel_id=1, source_target_pairs={{0,16},{16,0},{32,48},{48,32},{64,80},{80,64},{96,112},{112,96},{1... | collective-permute-start | bytes 3145736 | tf_op jit(solution)/shard_map/ppermute | solution.py:36
  20.1 13.2 %collective-permute-start.1 = (f32[2,2,2,64,2,128]{5,3,4,2,1,0:T(8,128)S(1)}, f32[2,2,2,64,2,128]{5,3,4,2,1,0:T(8,128)S(1)}, u32[]{:S(2)}, u32[]{:S(2)}) collective-permute-start(f32[2,2,2,64,2,128]{5,3,4,2,1,0:T(8,128)S(1)} %dynamic-slice_bitcast_fusion), channel_id=1, source_target_pairs={{0,128},{16,144},{32,160},{48,176},{64,192},{80,208},{96,224},{112... | collective-permute-start | bytes 1572872 | tf_op jit(solution)/shard_map/ppermute | solution.py:36
  33.4 6.7 %collective-permute-start.2 = (f32[2,2,64,2,128]{4,2,3,1,0:T(8,128)S(1)}, f32[2,2,64,2,128]{4,2,3,1,0:T(8,128)S(1)}, u32[]{:S(2)}, u32[]{:S(2)}) collective-permute-start(f32[2,2,64,2,128]{4,2,3,1,0:T(8,128)S(1)} %dynamic-slice_bitcast_fusion.1), channel_id=1, source_target_pairs={{0,32},{16,48},{32,0},{48,16},{64,96},{80,112},{96,64},{112,80},{1... | collective-permute-start | bytes 786440 | tf_op jit(solution)/shard_map/ppermute | solution.py:36
  40.2 22.9 %copy-start.22 = (s32[32,1,6]{0,1,2:T(1,128)S(1)}, s32[32,1,6]{0,1,2:T(1,128)}, u32[]{:S(2)}) copy-start(s32[32,1,6]{0,1,2:T(1,128)} %param.17) | copy-start | bytes 2308
  40.2 22.9 %copy-start.23 = (s32[32,1,6]{0,1,2:T(1,128)S(1)}, s32[32,1,6]{0,1,2:T(1,128)}, u32[]{:S(2)}) copy-start(s32[32,1,6]{0,1,2:T(1,128)} %param.18) | copy-start | bytes 2308
  40.2 5.4 %collective-permute-start.3 = (f32[2,64,2,128]{3,1,0,2:T(8,128)S(1)}, f32[2,64,2,128]{3,1,0,2:T(8,128)S(1)}, u32[]{:S(2)}, u32[]{:S(2)}) collective-permute-start(f32[2,64,2,128]{3,1,0,2:T(8,128)S(1)} %bitcast.259), channel_id=1, source_target_pairs={{0,64},{16,80},{32,96},{48,112},{64,0},{80,16},{96,32},{112,48},{1... | collective-permute-start | bytes 393224 | tf_op jit(solution)/shard_map/ppermute | solution.py:36
  45.7 7.2 %collective-permute-start.4 = (bf16[2,64,2,128]{3,1,2,0:T(8,128)(2,1)S(1)}, bf16[2,64,2,128]{3,1,2,0:T(8,128)(2,1)S(1)}, u32[]{:S(2)}, u32[]{:S(2)}) collective-permute-start(bf16[2,64,2,128]{3,1,2,0:T(8,128)(2,1)S(1)} %fusion.54), channel_id=1, source_target_pairs={{0,2},{1,3},{2,0},{3,1},{4,6},{5,7},{6,4},{7,5},{8,10},{9,11},{10,... | collective-permute-start | bytes 196616 | tf_op jit(solution)/shard_map/ppermute | solution.py:47
  52.9 7.1 %collective-permute-start.5 = (bf16[2,2,64,2,128]{4,2,3,1,0:T(8,128)(2,1)S(1)}, bf16[2,2,64,2,128]{4,2,3,1,0:T(8,128)(2,1)S(1)}, u32[]{:S(2)}, u32[]{:S(2)}) collective-permute-start(bf16[2,2,64,2,128]{4,2,3,1,0:T(8,128)(2,1)S(1)} %pad_maximum_fusion.26), channel_id=1, source_target_pairs={{0,1},{1,0},{2,3},{3,2},{4,5},{5,4},{6,7},{7,6},{8,9},{9,8},{10,11... | collective-permute-start | bytes 393224 | tf_op jit(solution)/shard_map/ppermute | solution.py:47
  55.5 13.0 %copy-start.30 = (s32[64]{0:T(128)S(1)}, s32[64]{0:T(128)}, u32[]{:S(2)}) copy-start(s32[64]{0:T(128)} %param.19) | copy-start | bytes 772
  60.1 6.8 %collective-permute-start.6 = (bf16[2,2,2,64,2,128]{5,3,4,2,1,0:T(8,128)(2,1)S(1)}, bf16[2,2,2,64,2,128]{5,3,4,2,1,0:T(8,128)(2,1)S(1)}, u32[]{:S(2)}, u32[]{:S(2)}) collective-permute-start(bf16[2,2,2,64,2,128]{5,3,4,2,1,0:T(8,128)(2,1)S(1)} %pad_maximum_fusion.23), channel_id=1, source_target_pairs={{0,8},{1,9},{2,10},{3,11},{4,12},{5,13},{6,14},{7,15},{8,0},{9,1},... | collective-permute-start | bytes 786440 | tf_op jit(solution)/shard_map/ppermute | solution.py:47
  67.0 11.6 %collective-permute-start.7 = (bf16[2,2,2,2,64,2,128]{6,4,5,3,2,1,0:T(8,128)(2,1)S(1)}, bf16[2,2,2,2,64,2,128]{6,4,5,3,2,1,0:T(8,128)(2,1)S(1)}, u32[]{:S(2)}, u32[]{:S(2)}) collective-permute-start(bf16[2,2,2,2,64,2,128]{6,4,5,3,2,1,0:T(8,128)(2,1)S(1)} %pad_maximum_fusion.20), channel_id=1, source_target_pairs={{0,4},{1,5},{2,6},{3,7},{4,0},{5,1},{6,2},{7,3},{8,12},{9,13},{10,... | collective-permute-start | bytes 1572872 | tf_op jit(solution)/shard_map/ppermute | solution.py:47
  79.7 9.9 %copy-start.2 = (f32[2,2,512,128]{3,2,1,0:T(8,128)S(1)}, f32[2,2,512,128]{3,2,1,0:T(8,128)}, u32[]{:S(2)}) copy-start(f32[2,2,512,128]{3,2,1,0:T(8,128)} %param.11) | copy-start | bytes 3145732
  81.3 8.4 %copy-start.16 = (f32[2,64,4,128]{3,1,0,2:T(8,128)}, f32[2,64,4,128]{3,1,0,2:T(8,128)S(1)}, u32[]{:S(2)}) copy-start(f32[2,64,4,128]{3,1,0,2:T(8,128)S(1)} %fusion.21) | copy-start | bytes 786436
  81.3 7.8 %collective-permute-start.8 = (bf16[4,2,64,128]{3,2,1,0:T(8,128)(2,1)S(1)}, bf16[4,2,64,128]{3,2,1,0:T(8,128)(2,1)S(1)}, u32[]{:S(2)}, u32[]{:S(2)}) collective-permute-start(bf16[4,2,64,128]{3,2,1,0:T(8,128)(2,1)S(1)} %convert_bitcast_fusion), channel_id=1, source_target_pairs={{0,2},{1,3},{2,0},{3,1},{4,6},{5,7},{6,4},{7,5},{8,10},{9,11},{10,... | collective-permute-start | bytes 393224 | tf_op jit(solution)/shard_map/ppermute | solution.py:47
  89.2 19.0 %collective-permute-start.9 = (bf16[2,4,2,64,128]{4,3,2,1,0:T(8,128)(2,1)S(1)}, bf16[2,4,2,64,128]{4,3,2,1,0:T(8,128)(2,1)S(1)}, u32[]{:S(2)}, u32[]{:S(2)}) collective-permute-start(bf16[2,4,2,64,128]{4,3,2,1,0:T(8,128)(2,1)S(1)} %pad_maximum_fusion.24), channel_id=1, source_target_pairs={{0,1},{1,0},{2,3},{3,2},{4,5},{5,4},{6,7},{7,6},{8,9},{9,8},{10,11... | collective-permute-start | bytes 786440 | tf_op jit(solution)/shard_map/ppermute | solution.py:47
  93.3 34.8 %collective-permute-start.16 = (f32[6,512,1]{1,2,0:T(1,128)S(1)}, f32[6,512,1]{1,2,0:T(1,128)S(1)}, u32[]{:S(2)}, u32[]{:S(2)}) collective-permute-start(f32[6,512,1]{1,2,0:T(1,128)S(1)} %copy.150), channel_id=1, source_target_pairs={{0,16},{16,32},{32,48},{48,64},{64,80},{80,96},{96,112},{112,128},... | collective-permute-start | bytes 36872 | tf_op jit(solution)/shard_map/ppermute | solution.py:16
  106.3 22.3 %collective-permute-start.17 = (f32[6,512,1]{1,2,0:T(1,128)S(1)}, f32[6,512,1]{1,2,0:T(1,128)S(1)}, u32[]{:S(2)}, u32[]{:S(2)}) collective-permute-start(f32[6,512,1]{1,2,0:T(1,128)S(1)} %copy.151), channel_id=1, source_target_pairs={{16,0},{32,16},{48,32},{64,48},{80,64},{96,80},{112,96},{128,112},... | collective-permute-start | bytes 36872 | tf_op jit(solution)/shard_map/ppermute | solution.py:19
  108.3 15.2 %collective-permute-start.10 = (bf16[2,2,4,2,64,128]{5,4,3,2,0,1:T(8,128)(2,1)S(1)}, bf16[2,2,4,2,64,128]{5,4,3,2,0,1:T(8,128)(2,1)S(1)}, u32[]{:S(2)}, u32[]{:S(2)}) collective-permute-start(bf16[2,2,4,2,64,128]{5,4,3,2,0,1:T(8,128)(2,1)S(1)} %pad_maximum_fusion.21), channel_id=1, source_target_pairs={{0,8},{1,9},{2,10},{3,11},{4,12},{5,13},{6,14},{7,15},{8,0},{9,1},... | collective-permute-start | bytes 1572872 | tf_op jit(solution)/shard_map/ppermute | solution.py:47
  123.6 1.9 copy-start.14
  125.5 24.3 %collective-permute-start.11 = (bf16[2,2,2,4,2,64,128]{6,5,4,3,1,2,0:T(8,128)(2,1)}, bf16[2,2,2,4,2,64,128]{6,5,4,3,1,2,0:T(8,128)(2,1)}, u32[]{:S(2)}, u32[]{:S(2)}) collective-permute-start(bf16[2,2,2,4,2,64,128]{6,5,4,3,1,2,0:T(8,128)(2,1)} %pad_maximum_fusion.18), channel_id=1, source_target_pairs={{0,4},{1,5},{2,6},{3,7},{4,0},{5,1},{6,2},{7,3},{8,12},{9,13},{10,... | collective-permute-start | bytes 3145736 | tf_op jit(solution)/shard_map/ppermute | solution.py:47
  129.1 5.0 %copy-start.29 = (s32[12]{0:T(128)S(1)}, s32[12]{0:T(128)}, u32[]{:S(2)}) copy-start(s32[12]{0:T(128)} %reshape.187) | copy-start | bytes 148
  129.1 10.8 %copy-start.24 = (pred[513]{0:T(1024)(128)(4,1)S(1)}, pred[513]{0:T(1024)(128)(4,1)}, u32[]{:S(2)}) copy-start(pred[513]{0:T(1024)(128)(4,1)} %get-tuple-element.67) | copy-start | bytes 1543
  130.6 5.6 %collective-permute-start.18 = (f32[6,1,130]{2,1,0:T(1,128)}, f32[6,1,130]{2,1,0:T(1,128)S(1)}, u32[]{:S(2)}, u32[]{:S(2)}) collective-permute-start(f32[6,1,130]{2,1,0:T(1,128)} %get-tuple-element.19), channel_id=1, source_target_pairs={{0,1},{1,2},{2,3},{3,4},{4,5},{5,6},{6,7},{7,8},{8,9},{9,10},{10,1... | collective-permute-start | bytes 9368 | tf_op jit(solution)/shard_map/ppermute | solution.py:16
  132.8 7.2 %collective-permute-start.19 = (f32[6,1,130]{2,1,0:T(1,128)}, f32[6,1,130]{2,1,0:T(1,128)}, u32[]{:S(2)}, u32[]{:S(2)}) collective-permute-start(f32[6,1,130]{2,1,0:T(1,128)} %get-tuple-element.18), channel_id=1, source_target_pairs={{1,0},{2,1},{3,2},{4,3},{5,4},{6,5},{7,6},{8,7},{9,8},{10,9},{11,1... | collective-permute-start | bytes 9368 | tf_op jit(solution)/shard_map/ppermute | solution.py:19
  140.0 9.8 %copy-start.13 = (bf16[1,2,2,4,2,64,128]{6,5,4,3,1,2,0:T(8,128)(2,1)S(1)}, bf16[1,2,2,4,2,64,128]{6,5,4,3,1,2,0:T(8,128)(2,1)}, u32[]{:S(2)}) copy-start(bf16[1,2,2,4,2,64,128]{6,5,4,3,1,2,0:T(8,128)(2,1)} %copy-done.12) | copy-start | bytes 1572868
  140.0 9.8 %copy-start.15 = (bf16[1,2,2,4,2,64,128]{6,5,4,3,1,2,0:T(8,128)(2,1)S(1)}, bf16[1,2,2,4,2,64,128]{6,5,4,3,1,2,0:T(8,128)(2,1)}, u32[]{:S(2)}) copy-start(bf16[1,2,2,4,2,64,128]{6,5,4,3,1,2,0:T(8,128)(2,1)} %copy-done.14) | copy-start | bytes 1572868
  151.3 4.6 %copy-start.31 = (pred[2,6]{1,0:T(4,128)(4,1)S(1)}, pred[2,6]{1,0:T(4,128)(4,1)}, u32[]{:S(2)}) copy-start(pred[2,6]{1,0:T(4,128)(4,1)} %compare_and_fusion) | copy-start | bytes 40
  152.8 4.7 %copy-start.27 = (pred[129]{0:T(512)(128)(4,1)S(1)}, pred[129]{0:T(512)(128)(4,1)}, u32[]{:S(2)}) copy-start(pred[129]{0:T(512)(128)(4,1)} %get-tuple-element.64) | copy-start | bytes 391
  155.9 1.6 copy-start.3
  157.4 4.7 %collective-permute-start.12 = (bf16[64,2,2,128]{3,0,1,2:T(8,128)(2,1)S(1)}, bf16[64,2,2,128]{3,0,1,2:T(8,128)(2,1)S(1)}, u32[]{:S(2)}, u32[]{:S(2)}) collective-permute-start(bf16[64,2,2,128]{3,0,1,2:T(8,128)(2,1)S(1)} %fusion.25), channel_id=1, source_target_pairs={{0,64},{16,80},{32,96},{48,112},{64,0},{80,16},{96,32},{112,48},{1... | collective-permute-start | bytes 196616 | tf_op jit(solution)/shard_map/ppermute | solution.py:47
  157.6 5.9 %copy-start.5 = (f32[2,512,128]{2,1,0:T(8,128)S(1)}, f32[2,512,128]{2,1,0:T(8,128)}, u32[]{:S(2)}) copy-start(f32[2,512,128]{2,1,0:T(8,128)} %param.10) | copy-start | bytes 1572868
  162.2 3.9 %collective-permute-start.13 = (bf16[2,64,2,2,128]{4,1,2,3,0:T(8,128)(2,1)S(1)}, bf16[2,64,2,2,128]{4,1,2,3,0:T(8,128)(2,1)S(1)}, u32[]{:S(2)}, u32[]{:S(2)}) collective-permute-start(bf16[2,64,2,2,128]{4,1,2,3,0:T(8,128)(2,1)S(1)} %pad_maximum_fusion.27), channel_id=1, source_target_pairs={{0,128},{16,144},{32,160},{48,176},{64,192},{80,208},{96,224},{112... | collective-permute-start | bytes 393224 | tf_op jit(solution)/shard_map/ppermute | solution.py:47
  163.5 5.0 %copy-start.7 = (f32[1,2,513,129]{3,2,1,0:T(8,128)S(1)}, f32[1,2,513,129]{3,2,1,0:T(8,128)}, u32[]{:S(2)}) copy-start(f32[1,2,513,129]{3,2,1,0:T(8,128)} %fusion.33) | copy-start | bytes 1588252
  166.2 6.1 %collective-permute-start.14 = (bf16[2,2,64,2,2,128]{5,2,3,4,1,0:T(8,128)(2,1)S(1)}, bf16[2,2,64,2,2,128]{5,2,3,4,1,0:T(8,128)(2,1)S(1)}, u32[]{:S(2)}, u32[]{:S(2)}) collective-permute-start(bf16[2,2,64,2,2,128]{5,2,3,4,1,0:T(8,128)(2,1)S(1)} %pad_maximum_fusion.25), channel_id=1, source_target_pairs={{0,32},{16,48},{32,0},{48,16},{64,96},{80,112},{96,64},{112,80},{1... | collective-permute-start | bytes 786440 | tf_op jit(solution)/shard_map/ppermute | solution.py:47
  172.4 8.7 %collective-permute-start.15 = (bf16[2,2,2,64,2,2,128]{6,3,4,5,1,0,2:T(8,128)(2,1)S(1)}, bf16[2,2,2,64,2,2,128]{6,3,4,5,1,0,2:T(8,128)(2,1)S(1)}, u32[]{:S(2)}, u32[]{:S(2)}) collective-permute-start(bf16[2,2,2,64,2,2,128]{6,3,4,5,1,0,2:T(8,128)(2,1)S(1)} %pad_maximum_fusion.22), channel_id=1, source_target_pairs={{0,16},{16,0},{32,48},{48,32},{64,80},{80,64},{96,112},{112,96},{1... | collective-permute-start | bytes 1572872 | tf_op jit(solution)/shard_map/ppermute | solution.py:47
  177.7 1.3 copy-start.28
  179.0 1.2 copy-start.17
  181.3 1.6 copy-start.11
  181.3 1.6 copy-start.25
  181.3 1.6 copy-start.26
  181.4 4.1 %copy-start.19 = (bf16[2,2,2,2,64,2,2,128]{7,4,3,2,1,0,6,5:T(8,128)(2,1)}, bf16[2,2,2,2,64,2,2,128]{7,4,3,2,1,0,6,5:T(8,128)(2,1)S(1)}, u32[]{:S(2)}) copy-start(bf16[2,2,2,2,64,2,2,128]{7,4,3,2,1,0,6,5:T(8,128)(2,1)S(1)} %copy.143) | copy-start | bytes 3145732
  184.2 1.4 copy-start.9
  187.1 2.5 %copy-start.6 = (f32[2,512,128]{2,1,0:T(8,128)S(1)}, f32[2,512,128]{2,1,0:T(8,128)}, u32[]{:S(2)}) copy-start(f32[2,512,128]{2,1,0:T(8,128)} %param.10) | copy-start | bytes 1572868
  189.6 2.7 %copy-start.1 = (bf16[8,128,128]{2,1,0:T(8,128)(2,1)S(1)}, bf16[8,128,128]{2,1,0:T(8,128)(2,1)}, u32[]{:S(2)}) copy-start(bf16[8,128,128]{2,1,0:T(8,128)(2,1)} %param.16) | copy-start | bytes 786436
  (4 other events, 3.7 us)

commit v4 on v3

--- a/solution.py
+++ b/solution.py
@@ -53,6 +53,16 @@
     return block.reshape(count, *block.shape[len(bits):])
 
 
+def swap_sum(blocks, axis):
+    return jnp.sum(lax.all_to_all(blocks, axis, 0, 0, tiled=True), axis=0)
+
+
+def swap_gather(block, axis):
+    count = lax.axis_size(axis)
+    spread = jnp.broadcast_to(block[None], (count, *block.shape))
+    return lax.all_to_all(spread, axis, 0, 0, tiled=True)
+
+
 def on_device(
     image, tv_dual, data_dual, echoes, row_steer, col_steer, kernels, footprint, phase, aperture
 ):
@@ -90,9 +100,9 @@
     real_part = weight_re * prod_re - weight_im * prod_im
     imag_part = weight_re * prod_im + weight_im * prod_re
     parts = jnp.stack([real_part, imag_part], axis=0).reshape(2, az_count, -1, tiles_dev, columns)
-    summed = halving_sum(jnp.moveaxis(parts, 1, 0), "az", (1, 8, 2, 4))
+    summed = swap_sum(jnp.moveaxis(parts, 1, 0), "az")
     projection_b = jnp.transpose(summed, (2, 1, 0, 3)).astype(jnp.bfloat16)
-    all_proj = doubling_gather(projection_b, "tile", (2, 1, 8, 4))
+    all_proj = swap_gather(projection_b, "tile")
     all_proj = all_proj.reshape(-1, *all_proj.shape[2:])
     phase_ids = jnp.arange(kernels.shape[0], dtype=jnp.int32)
     my_rows = tile_index * rows_dev + jnp.arange(rows_dev, dtype=jnp.int32)
@@ -114,12 +124,12 @@
         0.0,
     )
     dual_b = dual_new.astype(jnp.bfloat16)
-    all_rows = doubling_gather(jnp.moveaxis(dual_b, 2, 0), "tile", (2, 1, 8, 4))
+    all_rows = swap_gather(jnp.moveaxis(dual_b, 2, 0), "tile")
     all_rows = jnp.moveaxis(all_rows.reshape(-1, *all_rows.shape[2:]), 0, 2)
     chosen = jnp.take(all_rows, foot_mine, axis=2)
     back = jnp.einsum("cpjfv,jfuv->cjpu", chosen, kern_mine, preferred_element_type=jnp.float32)
     back_b = back.astype(jnp.bfloat16)
-    piece = doubling_gather(jnp.moveaxis(back_b, 2, 0), "az", (4, 8, 2, 1))
+    piece = swap_gather(jnp.moveaxis(back_b, 2, 0), "az")
     piece = jnp.moveaxis(piece.reshape(-1, *piece.shape[2:]), 0, 2)
     weight_re = col_mine[0].T[..., None]
     weight_im = col_mine[1].T[..., None]

time: 193 us -> 197 us (1.021); the launches traced: 192 us -> 194 us
  blocking collectives: 0 us -> 33.6 us
  waiting for transfers between devices: 78.2 us -> 58 us
  other arithmetic: 23.3 us -> 13 us
  starting transfers between devices: 51.5 us -> 45.1 us
  local copies, waits for them, and re-layouts: 24.5 us -> 28.1 us
    ppermute x16 -> x0, waiting for transfers between devices: 74.4 us -> none  [the longest x12 48.6 us: doubling_gather(): got = lax.ppermute(block, axis, pairs)]
    all_to_all x0 -> x3, waiting for transfers between devices: none -> 57 us  [swap_gather(): return lax.all_to_all(spread, axis, 0, 0, tiled=True)]
    all_to_all x0 -> x3, starting transfers between devices: none -> 33.9 us  [swap_gather(): return lax.all_to_all(spread, axis, 0, 0, tiled=True)]
    all_to_all x0 -> x1, blocking collectives: none -> 33.6 us  [swap_sum(): return jnp.sum(lax.all_to_all(blocks, axis, 0, 0, tiled=True), axis=0)]
    ppermute x16 -> x0, starting transfers between devices: 33.6 us -> none  [the longest x12 28.5 us: doubling_gather(): got = lax.ppermute(block, axis, pairs)]
    ppermute x2, starting transfers between devices: 14.7 us -> 8.07 us  [padded_2(): lax.ppermute(lax.slice_in_dim(block, block.shape[dim] - width, None, axis...]
    broadcast_in_dim x0 -> x3, local copies, waits for them, and re-layouts: none -> 4.86 us  [swap_gather(): spread = jnp.broadcast_to(block[None], (count, *block.shape))]
    another operation x25 -> x0, other arithmetic: 3.76 us -> none  [the longest x24 3.52 us: doubling_gather(): block = jnp.stack([low, high], axis=place)]
  transfers between devices with their start and end apart: 20 -> 7, of which waited for: 15 -> 4; matrix products, arithmetic and copies ran while one was open for 13% -> 11% of each run, Pallas kernels for 0% -> 0%
where the time goes in v4:
time: 197 us; the launch traced here: 194 us
  waiting for transfers between devices  58 us (29%)
  starting transfers between devices  45.1 us (23%)
  blocking collectives  33.6 us (17%)
  local copies, waits for them, and re-layouts  28.1 us (14%)
  matrix products  15.1 us (8%)
  other arithmetic  13 us (7%)
    all_to_all x3, waiting for transfers between devices, swap_gather(): return lax.all_to_all(spread, axis, 0, 0, tiled=True)  57 us
    all_to_all x3, starting transfers between devices, swap_gather(): return lax.all_to_all(spread, axis, 0, 0, tiled=True)  33.9 us
    all_to_all x1, blocking collectives, swap_sum(): return jnp.sum(lax.all_to_all(blocks, axis, 0, 0, tiled=True), axis=0)  33.6 us
    ppermute x2, starting transfers between devices, padded_2(): lax.ppermute(lax.slice_in_dim(block, block.shape[dim] - width, None, axis...  8.07 us
    broadcast_in_dim x3, local copies, waits for them, and re-layouts, swap_gather(): spread = jnp.broadcast_to(block[None], (count, *block.shape))  4.86 us
  transfers between devices with their start and end apart: 7, of which 4 were waited for; matrix products, arithmetic and copies ran while one was open for 11% of the time, Pallas kernels for 0%

profile of v4, /device:TPU:1, one launch (start us, length us, event | category | flops | bytes accessed | tf_op | source)
XLA Modules:
  0.0 194.3 jit_solution(4066099123022585519)
XLA Ops:
  0.7 2.8 %fusion.62 = (bf16[1,1024,2,256]{3,2,1,0:T(2,128)(2,1)S(1)}, bf16[1,1024,2,256]{3,2,1,0:T(2,128)(2,1)S(1)}) fusion(bf16[2,1024,2,256]{3,2,1,0:T(2,128)(2,1)} %param.14), kind=kLoop, calls=%fused_computation.120 | loop fusion | bytes 4194304 | tf_op jit(solution)/shard_map/slice | solution.py:85
  4.4 1.5 fusion.40
  5.9 0.9 constant_dynamic-slice_fusion
  7.3 0.7 copy-done.10
  8.0 1.5 multiply_subtract_fusion
  9.6 1.5 copy.125
  11.1 1.3 copy.126
  12.4 1.4 maximum_bitcast_fusion
  14.1 33.6 %all_to_all.20 = f32[16,2,64,2,128]{4,2,3,1,0:T(8,128)S(1)} all-to-all(f32[16,2,64,2,128]{4,2,3,1,0:T(8,128)S(1)} %copy.127), channel_id=1, replica_groups=mesh['az'=16,'tile'=16] {'az'}, dimensions={0} | all-to-all | bytes 4194304 | tf_op jit(solution)/shard_map/all_to_all | solution.py:57
  47.9 1.8 broadcast_in_dim.98
  49.7 10.0 %all-to-all-start.1 = ((bf16[16,2,64,2,128]{4,1,3,2,0:T(2,128)(2,1)}), bf16[16,2,64,2,128]{4,1,3,2,0:T(2,128)(2,1)S(1)}, u32[]{:S(2)}, u32[]{:S(2)}) async-start(bf16[16,2,64,2,128]{4,1,3,2,0:T(2,128)(2,1)} %broadcast_in_dim.98), calls=%async_computation.1 | async-start | bytes 2097152 | tf_op jit(solution)/shard_map/all_to_all | solution.py:63
  60.0 24.8 %all-to-all-done.1 = bf16[16,2,64,2,128]{4,1,3,2,0:T(2,128)(2,1)S(1)} async-done(((bf16[16,2,64,2,128]{4,1,3,2,0:T(2,128)(2,1)}), bf16[16,2,64,2,128]{4,1,3,2,0:T(2,128)(2,1)S(1)}, u32[]{:S(2)}, u32[]{:S(2)}) %all-to-all-start.1) | async-done | bytes 1048608 | tf_op jit(solution)/shard_map/all_to_all | solution.py:63
  84.8 1.1 copy.130
  86.4 0.5 copy-done.14
  86.9 1.6 fusion.21
  88.5 0.7 copy-done.11
  89.2 1.8 broadcast_in_dim.100
  91.0 7.9 %all-to-all-start.2 = ((bf16[16,4,2,64,128]{4,3,2,1,0:T(8,128)(2,1)}), bf16[16,4,2,64,128]{4,3,2,1,0:T(8,128)(2,1)}, u32[]{:S(2)}, u32[]{:S(2)}) async-start(bf16[16,4,2,64,128]{4,3,2,1,0:T(8,128)(2,1)} %broadcast_in_dim.100), calls=%async_computation.2 | async-start | bytes 4194304 | tf_op jit(solution)/shard_map/all_to_all | solution.py:63
  99.0 1.7 slice_maximum_fusion
  100.7 1.9 copy.144
  102.5 3.7 %collective-permute-start = (f32[6,512,1]{1,2,0:T(1,128)S(1)}, f32[6,512,1]{1,2,0:T(1,128)S(1)}, u32[]{:S(2)}, u32[]{:S(2)}) collective-permute-start(f32[6,512,1]{1,2,0:T(1,128)S(1)} %copy.144), channel_id=1, source_target_pairs={{0,16},{16,32},{32,48},{48,64},{64,80},{80,96},{96,112},{112,128},... | collective-permute-start | bytes 36872 | tf_op jit(solution)/shard_map/ppermute | solution.py:16
  106.7 1.9 collective-permute-start.1
  109.2 1.4 gather_fusion
  110.5 0.5 copy.146
  111.1 1.0 collective-permute-done.1
  112.1 0.5 copy.147
  112.6 0.9 pad_maximum_fusion.15
  113.5 4.4 %collective-permute-start.2 = (f32[6,1,130]{2,1,0:T(1,128)S(1)}, f32[6,1,130]{2,1,0:T(1,128)S(1)}, u32[]{:S(2)}, u32[]{:S(2)}) collective-permute-start(f32[6,1,130]{2,1,0:T(1,128)S(1)} %get-tuple-element.19), channel_id=1, source_target_pairs={{0,1},{1,2},{2,3},{3,4},{4,5},{5,6},{6,7},{7,8},{8,9},{9,10},{10,1... | collective-permute-start | bytes 9368 | tf_op jit(solution)/shard_map/ppermute | solution.py:16
  117.9 1.3 collective-permute-start.3
  119.2 24.6 %all-to-all-done.2 = bf16[16,4,2,64,128]{4,3,2,1,0:T(8,128)(2,1)} async-done(((bf16[16,4,2,64,128]{4,3,2,1,0:T(8,128)(2,1)}), bf16[16,4,2,64,128]{4,3,2,1,0:T(8,128)(2,1)}, u32[]{:S(2)}, u32[]{:S(2)}) %all-to-all-start.2) | async-done | bytes 2097184 | tf_op jit(solution)/shard_map/all_to_all | solution.py:63
  143.8 2.9 %gather_fusion.1 = bf16[12,2,64,128]{3,2,1,0:T(8,128)(2,1)} fusion(bf16[2,64,64,128]{3,1,0,2:T(8,128)(2,1)} %bitcast.27, s32[1024]{0:T(1024)S(1)} %pad_clamp_fusion), kind=kCustom, calls=%fused_computation.1 | custom fusion | bytes 786480 | tf_op jit(solution)/shard_map/jit(_take)/gather | solution.py:129
  146.7 1.4 fusion.25
  148.2 1.2 broadcast_in_dim.102
  149.4 15.9 %all-to-all-start.3 = ((bf16[16,64,2,2,128]{4,1,3,2,0:T(8,128)(2,1)}), bf16[16,64,2,2,128]{4,1,3,2,0:T(8,128)(2,1)}, u32[]{:S(2)}, u32[]{:S(2)}) async-start(bf16[16,64,2,2,128]{4,1,3,2,0:T(8,128)(2,1)} %broadcast_in_dim.102), calls=%async_computation.3 | async-start | bytes 2097152 | tf_op jit(solution)/shard_map/all_to_all | solution.py:63
  165.5 2.2 %pad_maximum_fusion = f32[4,514,130]{2,1,0:T(8,128)S(1)} fusion(f32[6,1,130]{2,1,0:T(1,128)S(1)} %collective-permute-done.3, f32[6,1,130]{2,1,0:T(1,128)S(1)} %collective-permute-done.2, f32[6,512,1]{2,1,0:T(8,128)S(1)} %copy.147, f32[6,512,1]{2,1,0:T(8,128)S(1)} %copy.146, f32[4,512,128]{2,1,0:T(8,128)} %bitcast.160, f32[2,512,128]{2,1,0:T(8,128)} %param.10), kind=kLoop, calls=%fused_computation.3 | loop fusion | flops 1336400 | bytes 2672800 | tf_op jit(solution)/shard_map/concatenate | solution.py:20
  167.8 0.6 fusion.30
  168.4 1.0 fusion.33
  170.3 1.3 slice.128
  171.7 1.2 fusion.27
  172.9 0.9 copy.148
  173.7 7.6 %all-to-all-done.3 = bf16[16,64,2,2,128]{4,1,3,2,0:T(8,128)(2,1)} async-done(((bf16[16,64,2,2,128]{4,1,3,2,0:T(8,128)(2,1)}), bf16[16,64,2,2,128]{4,1,3,2,0:T(8,128)(2,1)}, u32[]{:S(2)}, u32[]{:S(2)}) %all-to-all-start.3) | async-done | bytes 1048608 | tf_op jit(solution)/shard_map/all_to_all | solution.py:63
  181.3 1.3 copy.137
  182.6 1.3 fusion.39
  183.9 1.9 %fusion.38 = f32[2,128,256]{2,1,0:T(8,128)} fusion(bf16[1,1024,2,256]{3,2,1,0:T(2,128)(2,1)S(1)} %copy-done.9, f32[2,1024]{1,0:T(2,128)S(1)} %get-tuple-element.35, f32[2,1024]{1,0:T(2,128)S(1)} %get-tuple-element.42, bf16[2,2,1024,128]{3,2,1,0:T(8,128)(2,1)S(1)} %bitcast.176), kind=kOutput, calls=%fused_computation.64 | convolution fusion | flops 135790592 | bytes 2375680 | tf_op jit(solution)/shard_map/pjh,jpu->jhu/dot_general | solution.py:146
  185.9 1.3 fusion.7
  187.3 3.2 %fusion.8 = f32[2,256,128]{1,2,0:T(8,128)} fusion(f32[2,128,256]{2,1,0:T(8,128)} %fusion.38, bf16[1,1024,2,256]{3,2,1,0:T(2,128)(2,1)S(1)} %copy-done.7, f32[2,1024]{1,0:T(2,128)S(1)} %get-tuple-element.35, f32[2,1024]{1,0:T(2,128)S(1)} %get-tuple-element.42, bf16[2,2,1024,128]{3,2,1,0:T(8,128)(2,1)} %bitcast.178), kind=kOutput, calls=%fused_computation.28 | convolution fusion | flops 135856128 | bytes 2637824 | tf_op jit(solution)/shard_map/pjh,jpu->jhu/dot_general | solution.py:147
  190.5 1.1 copy.143
  191.6 2.7 %fusion.44 = f32[2,512,128]{2,1,0:T(8,128)} fusion(f32[2,512,128]{2,1,0:T(8,128)S(1)} %copy-done.5, f32[2,513,129]{2,1,0:T(8,128)} %get-tuple-element.21, f32[2,513,129]{2,1,0:T(8,128)S(1)} %get-tuple-element.20, f32[1,512,128]{2,1,0:T(8,128)S(1)} %bitcast.174, f32[1,512,128]{2,1,0:T(8,128)S(1)} %bitcast.173), kind=kLoop, calls=%fused_computation.72 | loop fusion | flops 917504 | bytes 3670016 | tf_op jit(solution)/shard_map/sub | solution.py:177
  (74 shorter events, 4.8 us)
Async XLA Ops:
  0.6 85.7 %copy-start = (bf16[8,128,128]{2,1,0:T(8,128)(2,1)S(1)}, bf16[8,128,128]{2,1,0:T(8,128)(2,1)}, u32[]{:S(2)}) copy-start(bf16[8,128,128]{2,1,0:T(8,128)(2,1)} %param.16) | copy-start | bytes 786436
  0.7 2.8 %copy-start.3 = (f32[2,512,128]{2,1,0:T(8,128)S(1)}, f32[2,512,128]{2,1,0:T(8,128)}, u32[]{:S(2)}) copy-start(f32[2,512,128]{2,1,0:T(8,128)} %param.10) | copy-start | bytes 1572868
  3.4 1.0 copy-start.8
  3.4 3.9 %copy-start.6 = (bf16[1,1024,2,256]{3,2,1,0:T(2,128)(2,1)}, bf16[1,1024,2,256]{3,2,1,0:T(2,128)(2,1)S(1)}, u32[]{:S(2)}) copy-start(bf16[1,1024,2,256]{3,2,1,0:T(2,128)(2,1)S(1)} %get-tuple-element.24) | copy-start | bytes 3145732
  6.8 1.2 copy-start.10
  47.9 11.9 %copy-start.16 = (s32[32,1,6]{0,1,2:T(1,128)S(1)}, s32[32,1,6]{0,1,2:T(1,128)}, u32[]{:S(2)}) copy-start(s32[32,1,6]{0,1,2:T(1,128)} %param.17) | copy-start | bytes 2308
  47.9 11.9 %copy-start.17 = (s32[32,1,6]{0,1,2:T(1,128)S(1)}, s32[32,1,6]{0,1,2:T(1,128)}, u32[]{:S(2)}) copy-start(s32[32,1,6]{0,1,2:T(1,128)} %param.18) | copy-start | bytes 2308
  47.9 12.0 %copy-start.18 = (s32[64]{0:T(128)S(1)}, s32[64]{0:T(128)}, u32[]{:S(2)}) copy-start(s32[64]{0:T(128)} %param.19) | copy-start | bytes 772
  49.7 35.0 %all-to-all-start.1 = ((bf16[16,2,64,2,128]{4,1,3,2,0:T(2,128)(2,1)}), bf16[16,2,64,2,128]{4,1,3,2,0:T(2,128)(2,1)S(1)}, u32[]{:S(2)}, u32[]{:S(2)}) async-start(bf16[16,2,64,2,128]{4,1,3,2,0:T(2,128)(2,1)} %broadcast_in_dim.98), calls=%async_computation.1 | async-start | bytes 2097152 | tf_op jit(solution)/shard_map/all_to_all | solution.py:63
  85.9 1.0 copy-start.14
  85.9 1.0 copy-start.15
  88.5 0.7 copy-start.11
  91.0 7.9 %copy-start.1 = (f32[2,2,512,128]{3,2,1,0:T(8,128)S(1)}, f32[2,2,512,128]{3,2,1,0:T(8,128)}, u32[]{:S(2)}) copy-start(f32[2,2,512,128]{3,2,1,0:T(8,128)} %param.11) | copy-start | bytes 3145732
  91.0 52.8 %all-to-all-start.2 = ((bf16[16,4,2,64,128]{4,3,2,1,0:T(8,128)(2,1)}), bf16[16,4,2,64,128]{4,3,2,1,0:T(8,128)(2,1)}, u32[]{:S(2)}, u32[]{:S(2)}) async-start(bf16[16,4,2,64,128]{4,3,2,1,0:T(8,128)(2,1)} %broadcast_in_dim.100), calls=%async_computation.2 | async-start | bytes 4194304 | tf_op jit(solution)/shard_map/all_to_all | solution.py:63
  102.5 8.0 %collective-permute-start = (f32[6,512,1]{1,2,0:T(1,128)S(1)}, f32[6,512,1]{1,2,0:T(1,128)S(1)}, u32[]{:S(2)}, u32[]{:S(2)}) collective-permute-start(f32[6,512,1]{1,2,0:T(1,128)S(1)} %copy.144), channel_id=1, source_target_pairs={{0,16},{16,32},{32,48},{48,64},{64,80},{80,96},{96,112},{112,128},... | collective-permute-start | bytes 36872 | tf_op jit(solution)/shard_map/ppermute | solution.py:16
  106.7 5.4 %collective-permute-start.1 = (f32[6,512,1]{1,2,0:T(1,128)S(1)}, f32[6,512,1]{1,2,0:T(1,128)S(1)}, u32[]{:S(2)}, u32[]{:S(2)}) collective-permute-start(f32[6,512,1]{1,2,0:T(1,128)S(1)} %copy.145), channel_id=1, source_target_pairs={{16,0},{32,16},{48,32},{64,48},{80,64},{96,80},{112,96},{128,112},... | collective-permute-start | bytes 36872 | tf_op jit(solution)/shard_map/ppermute | solution.py:19
  113.5 52.1 %collective-permute-start.2 = (f32[6,1,130]{2,1,0:T(1,128)S(1)}, f32[6,1,130]{2,1,0:T(1,128)S(1)}, u32[]{:S(2)}, u32[]{:S(2)}) collective-permute-start(f32[6,1,130]{2,1,0:T(1,128)S(1)} %get-tuple-element.19), channel_id=1, source_target_pairs={{0,1},{1,2},{2,3},{3,4},{4,5},{5,6},{6,7},{7,8},{8,9},{9,10},{10,1... | collective-permute-start | bytes 9368 | tf_op jit(solution)/shard_map/ppermute | solution.py:16
  117.9 47.7 %collective-permute-start.3 = (f32[6,1,130]{2,1,0:T(1,128)S(1)}, f32[6,1,130]{2,1,0:T(1,128)S(1)}, u32[]{:S(2)}, u32[]{:S(2)}) collective-permute-start(f32[6,1,130]{2,1,0:T(1,128)S(1)} %get-tuple-element.18), channel_id=1, source_target_pairs={{1,0},{2,1},{3,2},{4,3},{5,4},{6,5},{7,6},{8,7},{9,8},{10,9},{11,1... | collective-permute-start | bytes 9368 | tf_op jit(solution)/shard_map/ppermute | solution.py:19
  149.4 31.9 %all-to-all-start.3 = ((bf16[16,64,2,2,128]{4,1,3,2,0:T(8,128)(2,1)}), bf16[16,64,2,2,128]{4,1,3,2,0:T(8,128)(2,1)}, u32[]{:S(2)}, u32[]{:S(2)}) async-start(bf16[16,64,2,2,128]{4,1,3,2,0:T(8,128)(2,1)} %broadcast_in_dim.102), calls=%async_computation.3 | async-start | bytes 2097152 | tf_op jit(solution)/shard_map/all_to_all | solution.py:63
  165.5 2.3 %copy-start.2 = (f32[2,2,512,128]{3,2,1,0:T(8,128)S(1)}, f32[2,2,512,128]{3,2,1,0:T(8,128)}, u32[]{:S(2)}) copy-start(f32[2,2,512,128]{3,2,1,0:T(8,128)} %param.11) | copy-start | bytes 3145732
  165.5 2.3 %copy-start.4 = (f32[2,512,128]{2,1,0:T(8,128)S(1)}, f32[2,512,128]{2,1,0:T(8,128)}, u32[]{:S(2)}) copy-start(f32[2,512,128]{2,1,0:T(8,128)} %param.10) | copy-start | bytes 1572868
  171.7 1.2 copy-start.12
  172.9 9.8 %copy-start.9 = (bf16[1,1024,2,256]{3,2,1,0:T(2,128)(2,1)S(1)}, bf16[1,1024,2,256]{3,2,1,0:T(2,128)(2,1)}, u32[]{:S(2)}) copy-start(bf16[1,1024,2,256]{3,2,1,0:T(2,128)(2,1)} %copy-done.8) | copy-start | bytes 3145732
  182.6 3.3 %copy-start.13 = (bf16[16,64,2,2,128]{4,1,0,3,2:T(8,128)(2,1)}, bf16[16,64,2,2,128]{4,1,0,3,2:T(8,128)(2,1)S(1)}, u32[]{:S(2)}) copy-start(bf16[16,64,2,2,128]{4,1,0,3,2:T(8,128)(2,1)S(1)} %copy.137) | copy-start | bytes 3145732
  183.9 2.0 %copy-start.7 = (bf16[1,1024,2,256]{3,2,1,0:T(2,128)(2,1)S(1)}, bf16[1,1024,2,256]{3,2,1,0:T(2,128)(2,1)}, u32[]{:S(2)}) copy-start(bf16[1,1024,2,256]{3,2,1,0:T(2,128)(2,1)} %copy-done.6) | copy-start | bytes 3145732
  187.3 4.3 %copy-start.5 = (f32[2,512,128]{2,1,0:T(8,128)S(1)}, f32[2,512,128]{2,1,0:T(8,128)}, u32[]{:S(2)}) copy-start(f32[2,512,128]{2,1,0:T(8,128)} %param.10) | copy-start | bytes 1572868

commit v5 on v1

--- a/solution.py
+++ b/solution.py
@@ -6,6 +6,7 @@
 dual_step = 0.5
 primal_step = 0.25
 edge_limit = 1.5
+AZ_DIGITS = ((8, 2), (2, 4), (1, 2))
 
 
 def padded_2(block, sides, width):
@@ -19,6 +20,48 @@
         high = lax.ppermute(lax.slice_in_dim(block, 0, width, axis=dim), axis, backward)
         block = jnp.concatenate([low, block, high], axis=dim)
     return block
+
+
+def digit_shift(axis, stride, radix, shift):
+    count = lax.axis_size(axis)
+    pairs = []
+    for source in range(count):
+        digit = (source // stride) % radix
+        pairs.append((source, source + (((digit + shift) % radix) - digit) * stride))
+    return pairs
+
+
+def digits_sum(blocks, axis, digits, stages):
+    me = lax.axis_index(axis)
+    blocks = blocks.reshape(*[radix for _, radix in digits], *blocks.shape[1:])
+    order = [stride for stride, _ in digits]
+    for stride, radix in stages:
+        place = order.index(stride)
+        order.pop(place)
+        mine = (me // stride) % radix
+        total = lax.dynamic_index_in_dim(blocks, mine, place, keepdims=False)
+        for shift in range(1, radix):
+            send = lax.dynamic_index_in_dim(blocks, (mine + shift) % radix, place, keepdims=False)
+            total = total + lax.ppermute(send, axis, digit_shift(axis, stride, radix, shift))
+        blocks = total
+    return blocks
+
+
+def digits_gather(block, axis, stages):
+    me = lax.axis_index(axis)
+    count = lax.axis_size(axis)
+    done = []
+    for stride, radix in stages:
+        mine = (me // stride) % radix
+        got = [block] + [
+            lax.ppermute(block, axis, digit_shift(axis, stride, radix, shift))
+            for shift in range(1, radix)
+        ]
+        place = sum(1 for other in done if other > stride)
+        source = (mine - jnp.arange(radix, dtype=jnp.int32)) % radix
+        block = jnp.take(jnp.stack(got, axis=place), source, axis=place)
+        done.append(stride)
+    return block.reshape(count, *block.shape[len(stages):])
 
 
 def on_device(
@@ -57,11 +100,11 @@
     )
     real_part = weight_re * prod_re - weight_im * prod_im
     imag_part = weight_re * prod_im + weight_im * prod_re
-    summed = lax.psum_scatter(
-        jnp.stack([real_part, imag_part], axis=0), "az", scatter_dimension=1, tiled=True
-    )
+    parts = jnp.stack([real_part, imag_part], axis=0).reshape(2, az_count, -1, tiles_dev, columns)
+    summed = digits_sum(jnp.moveaxis(parts, 1, 0), "az", AZ_DIGITS, ((1, 2), (8, 2), (2, 4)))
     projection_b = jnp.transpose(summed, (2, 1, 0, 3)).astype(jnp.bfloat16)
-    all_proj = lax.all_gather(projection_b, "tile", axis=0, tiled=True)
+    all_proj = digits_gather(projection_b, "tile", ((1, 4), (4, 4)))
+    all_proj = all_proj.reshape(-1, *all_proj.shape[2:])
     phase_ids = jnp.arange(kernels.shape[0], dtype=jnp.int32)
     my_rows = tile_index * rows_dev + jnp.arange(rows_dev, dtype=jnp.int32)
     hits = (foot_block[:, :, None, None] == my_rows[None, None, :, None]) & (
@@ -82,11 +125,13 @@
         0.0,
     )
     dual_b = dual_new.astype(jnp.bfloat16)
-    all_rows = lax.all_gather(dual_b, "tile", axis=2, tiled=True)
+    all_rows = digits_gather(jnp.moveaxis(dual_b, 2, 0), "tile", ((1, 4), (4, 4)))
+    all_rows = jnp.moveaxis(all_rows.reshape(-1, *all_rows.shape[2:]), 0, 2)
     chosen = jnp.take(all_rows, foot_mine, axis=2)
     back = jnp.einsum("cpjfv,jfuv->cjpu", chosen, kern_mine, preferred_element_type=jnp.float32)
     back_b = back.astype(jnp.bfloat16)
-    piece = lax.all_gather(back_b, "az", axis=2, tiled=True)
+    piece = digits_gather(jnp.moveaxis(back_b, 2, 0), "az", ((2, 4), (8, 2), (1, 2)))
+    piece = jnp.moveaxis(piece.reshape(-1, *piece.shape[2:]), 0, 2)
     weight_re = col_mine[0].T[..., None]
     weight_im = col_mine[1].T[..., None]
     back_re = piece[0].astype(jnp.float32)

time: 265 us -> 193 us (0.73)
  waiting for transfers between devices: 121 us -> 39 us
  blocking collectives: 66.7 us -> 0 us
  starting transfers between devices: 10.4 us -> 57.6 us
  other arithmetic: 11.7 us -> 41 us
  local copies, waits for them, and re-layouts: 21.7 us -> 40.5 us
  between operations: 15 us -> 1.73 us
  matrix products: 18.1 us -> 12.1 us
    all_gather x3 -> x0, waiting for transfers between devices: 120 us -> none  [the longest x1 56 us: on_device(): all_proj = lax.all_gather(projection_b, 'tile', axis=0, tiled=True)]
    unnamed x1 -> x0, blocking collectives: 66.7 us -> none
    ppermute x0 -> x22, starting transfers between devices: none -> 48.9 us  [the longest x17 40.8 us: digits_gather(): lax.ppermute(block, axis, digit_shift(axis, stride, radix, shift))]
    ppermute x0 -> x22, waiting for transfers between devices: none -> 39 us  [the longest x17 29.3 us: digits_gather(): lax.ppermute(block, axis, digit_shift(axis, stride, radix, shift))]
    gather x0 -> x8, local copies, waits for them, and re-layouts: none -> 13.7 us  [digits_gather(): block = jnp.take(jnp.stack(got, axis=place), source, axis=place)]
    select_n x0 -> x16, other arithmetic: none -> 6.48 us  [digits_gather(): block = jnp.take(jnp.stack(got, axis=place), source, axis=place)]
    unnamed x47 -> x91, local copies, waits for them, and re-layouts: 2.69 us -> 7.23 us
    another operation x2, other arithmetic: 1.58 us -> 5.6 us  [on_device(): jnp.stack([grad_rows, grad_cols])]
  transfers between devices with their start and end apart: 7 -> 26, of which waited for: 4 -> 11; matrix products, arithmetic and copies ran while one was open for 8% -> 23% of each run, Pallas kernels for 0% -> 0%
where the time goes in v5:
time: 193 us; the launch traced here: 192 us
  starting transfers between devices  57.6 us (30%)
  other arithmetic  41 us (21%)
  local copies, waits for them, and re-layouts  40.5 us (21%)
  waiting for transfers between devices  39 us (20%)
  matrix products  12.1 us (6%)
    ppermute x17, starting transfers between devices, digits_gather(): lax.ppermute(block, axis, digit_shift(axis, stride, radix, shift))  40.8 us
    ppermute x17, waiting for transfers between devices, digits_gather(): lax.ppermute(block, axis, digit_shift(axis, stride, radix, shift))  29.3 us
    gather x8, local copies, waits for them, and re-layouts, digits_gather(): block = jnp.take(jnp.stack(got, axis=place), source, axis=place)  13.7 us
    ppermute x5, waiting for transfers between devices, digits_sum(): lax.ppermute(send, axis, digit_shift(axis, stride, radix, shift))  9.62 us
    ppermute x5, starting transfers between devices, digits_sum(): lax.ppermute(send, axis, digit_shift(axis, stride, radix, shift))  8.09 us
    unnamed x91, local copies, waits for them, and re-layouts  7.23 us
    select_n x16, other arithmetic, digits_gather(): block = jnp.take(jnp.stack(got, axis=place), source, axis=place)  6.48 us
    another operation x2, other arithmetic, on_device(): jnp.stack([grad_rows, grad_cols])  5.6 us
  transfers between devices with their start and end apart: 26, of which 11 were waited for; matrix products, arithmetic and copies ran while one was open for 23% of the time, Pallas kernels for 0%

profile of v5, /device:TPU:1, one launch (start us, length us, event | category | flops | bytes accessed | tf_op | source)
XLA Modules:
  0.0 191.8 jit_solution(2419569643508685756)
XLA Ops:
  0.7 2.7 %fusion.82 = (bf16[1,1024,2,256]{3,2,1,0:T(2,128)(2,1)S(1)}, bf16[1,1024,2,256]{3,2,1,0:T(2,128)(2,1)S(1)}) fusion(bf16[2,1024,2,256]{3,2,1,0:T(2,128)(2,1)} %param.14), kind=kLoop, calls=%fused_computation.229 | loop fusion | bytes 4194304 | tf_op jit(solution)/shard_map/slice | solution.py:86
  7.0 1.6 multiply_subtract_fusion
  8.9 1.6 copy.204
  12.0 3.2 %collective-permute-start = (f32[2,4,2,64,2,128]{5,3,4,2,1,0:T(8,128)}, f32[2,4,2,64,2,128]{5,3,4,2,1,0:T(8,128)}, u32[]{:S(2)}, u32[]{:S(2)}) collective-permute-start(f32[2,4,2,64,2,128]{5,3,4,2,1,0:T(8,128)} %bitcast.221), channel_id=1, source_target_pairs={{0,16},{16,0},{32,48},{48,32},{64,80},{80,64},{96,112},{112,96},{1... | collective-permute-start | bytes 3145736 | tf_op jit(solution)/shard_map/ppermute | solution.py:45
  15.3 1.7 slice_maximum_fusion
  17.0 1.9 copy.224
  18.9 1.9 %collective-permute-start.22 = (f32[6,512,1]{1,2,0:T(1,128)S(1)}, f32[6,512,1]{1,2,0:T(1,128)}, u32[]{:S(2)}, u32[]{:S(2)}) collective-permute-start(f32[6,512,1]{1,2,0:T(1,128)S(1)} %copy.224), channel_id=1, source_target_pairs={{0,16},{16,32},{32,48},{48,64},{64,80},{80,96},{96,112},{112,128},... | collective-permute-start | bytes 36872 | tf_op jit(solution)/shard_map/ppermute | solution.py:17
  21.9 3.0 %collective-permute-start.23 = (f32[6,512,1]{1,2,0:T(1,128)}, f32[6,512,1]{1,2,0:T(1,128)}, u32[]{:S(2)}, u32[]{:S(2)}) collective-permute-start(f32[6,512,1]{1,2,0:T(1,128)} %copy.225), channel_id=1, source_target_pairs={{16,0},{32,16},{48,32},{64,48},{80,64},{96,80},{112,96},{128,112},... | collective-permute-start | bytes 36872 | tf_op jit(solution)/shard_map/ppermute | solution.py:20
  31.0 1.4 fusion.37
  34.9 9.6 %collective-permute-done.1 = f32[4,2,64,2,128]{4,2,3,1,0:T(8,128)S(1)} collective-permute-done((f32[4,2,64,2,128]{4,2,3,1,0:T(8,128)S(1)}, f32[4,2,64,2,128]{4,2,3,1,0:T(8,128)S(1)}, u32[]{:S(2)}, u32[]{:S(2)}) %collective-permute-start.1) | collective-permute-done | bytes 524320 | tf_op jit(solution)/shard_map/ppermute | solution.py:45
  47.1 2.9 %collective-permute-start.3 = (f32[2,64,2,128]{3,1,0,2:T(8,128)}, f32[2,64,2,128]{3,1,0,2:T(8,128)}, u32[]{:S(2)}, u32[]{:S(2)}) collective-permute-start(f32[2,64,2,128]{3,1,0,2:T(8,128)} %bitcast.223), channel_id=1, source_target_pairs={{0,64},{16,80},{32,96},{48,112},{64,0},{80,16},{96,32},{112,48},{1... | collective-permute-start | bytes 393224 | tf_op jit(solution)/shard_map/ppermute | solution.py:45
  54.1 1.4 gather_fusion
  59.0 3.1 %collective-permute-start.5 = (bf16[2,64,2,128]{3,1,2,0:T(8,128)(2,1)S(1)}, bf16[2,64,2,128]{3,1,2,0:T(8,128)(2,1)S(1)}, u32[]{:S(2)}, u32[]{:S(2)}) collective-permute-start(bf16[2,64,2,128]{3,1,2,0:T(8,128)(2,1)S(1)} %bitcast.256), channel_id=1, source_target_pairs={{0,1},{1,2},{2,3},{3,0},{4,5},{5,6},{6,7},{7,4},{8,9},{9,10},{10,1... | collective-permute-start | bytes 196616 | tf_op jit(solution)/shard_map/ppermute | solution.py:57
  62.1 4.7 %collective-permute-start.6 = (bf16[2,64,2,128]{3,1,2,0:T(8,128)(2,1)S(1)}, bf16[2,64,2,128]{3,1,2,0:T(8,128)(2,1)S(1)}, u32[]{:S(2)}, u32[]{:S(2)}) collective-permute-start(bf16[2,64,2,128]{3,1,2,0:T(8,128)(2,1)S(1)} %bitcast.257), channel_id=1, source_target_pairs={{0,2},{1,3},{2,0},{3,1},{4,6},{5,7},{6,4},{7,5},{8,10},{9,11},{10,... | collective-permute-start | bytes 196616 | tf_op jit(solution)/shard_map/ppermute | solution.py:57
  66.8 2.4 %collective-permute-start.7 = (bf16[2,64,2,128]{3,1,2,0:T(8,128)(2,1)S(1)}, bf16[2,64,2,128]{3,1,2,0:T(8,128)(2,1)S(1)}, u32[]{:S(2)}, u32[]{:S(2)}) collective-permute-start(bf16[2,64,2,128]{3,1,2,0:T(8,128)(2,1)S(1)} %bitcast.258), channel_id=1, source_target_pairs={{0,3},{1,0},{2,1},{3,2},{4,7},{5,4},{6,5},{7,6},{8,11},{9,8},{10,9... | collective-permute-start | bytes 196616 | tf_op jit(solution)/shard_map/ppermute | solution.py:57
  69.2 1.5 pad_maximum_fusion.23
  70.6 2.5 %collective-permute-start.24 = (f32[6,1,130]{2,1,0:T(1,128)}, f32[6,1,130]{2,1,0:T(1,128)}, u32[]{:S(2)}, u32[]{:S(2)}) collective-permute-start(f32[6,1,130]{2,1,0:T(1,128)} %get-tuple-element.28), channel_id=1, source_target_pairs={{0,1},{1,2},{2,3},{3,4},{4,5},{5,6},{6,7},{7,8},{8,9},{9,10},{10,1... | collective-permute-start | bytes 9368 | tf_op jit(solution)/shard_map/ppermute | solution.py:17
  75.2 2.4 %gather_fusion.1 = bf16[4,2,64,2,128]{4,2,3,1,0:T(8,128)(2,1)} fusion(bf16[4,2,64,2,128]{4,2,3,1,0:T(8,128)(2,1)} %pad_maximum_fusion.21, s32[1024]{0:T(1024)} %pad_clamp_fusion.5), kind=kCustom, calls=%fused_computation.1 | custom fusion | bytes 524304 | tf_op jit(solution)/shard_map/jit(_take)/gather | solution.py:62
  78.6 6.1 %collective-permute-start.8 = (bf16[4,2,64,2,128]{4,2,3,1,0:T(8,128)(2,1)S(1)}, bf16[4,2,64,2,128]{4,2,3,1,0:T(8,128)(2,1)S(1)}, u32[]{:S(2)}, u32[]{:S(2)}) collective-permute-start(bf16[4,2,64,2,128]{4,2,3,1,0:T(8,128)(2,1)S(1)} %broadcast_select_fusion.3), channel_id=1, source_target_pairs={{0,4},{1,5},{2,6},{3,7},{4,8},{5,9},{6,10},{7,11},{8,12},{9,13},{1... | collective-permute-start | bytes 786440 | tf_op jit(solution)/shard_map/ppermute | solution.py:57
  84.7 2.6 %collective-permute-start.9 = (bf16[4,2,64,2,128]{4,2,3,1,0:T(8,128)(2,1)S(1)}, bf16[4,2,64,2,128]{4,2,3,1,0:T(8,128)(2,1)S(1)}, u32[]{:S(2)}, u32[]{:S(2)}) collective-permute-start(bf16[4,2,64,2,128]{4,2,3,1,0:T(8,128)(2,1)S(1)} %broadcast_select_fusion.3), channel_id=1, source_target_pairs={{0,8},{1,9},{2,10},{3,11},{4,12},{5,13},{6,14},{7,15},{8,0},{9,1},... | collective-permute-start | bytes 786440 | tf_op jit(solution)/shard_map/ppermute | solution.py:57
  88.4 3.2 %fusion.32 = f32[1,2,513,129]{3,2,1,0:T(8,128)} fusion(f32[6,1,130]{2,1,0:T(1,128)} %collective-permute-done.25, f32[6,512,1]{2,1,0:T(8,128)S(1)} %copy.227, f32[6,512,1]{2,1,0:T(8,128)S(1)} %copy.226, f32[4,512,128]{2,1,0:T(8,128)} %bitcast.228, f32[2,512,128]{2,1,0:T(8,128)} %param.10, f32[6,1,130]{2,1,0:T(1,128)} %collective-permute-done.24, ...), kind=kLoop, calls=%fused_computation.60 | loop fusion | flops 1323540 | bytes 2133609 | tf_op jit(solution)/shard_map/stack | solution.py:166
  91.7 3.1 %collective-permute-done.9 = bf16[4,2,64,2,128]{4,2,3,1,0:T(8,128)(2,1)S(1)} collective-permute-done((bf16[4,2,64,2,128]{4,2,3,1,0:T(8,128)(2,1)S(1)}, bf16[4,2,64,2,128]{4,2,3,1,0:T(8,128)(2,1)S(1)}, u32[]{:S(2)}, u32[]{:S(2)}) %collective-permute-start.9) | collective-permute-done | bytes 262176 | tf_op jit(solution)/shard_map/ppermute | solution.py:57
  96.0 3.0 %gather_fusion.2 = bf16[4,4,2,64,2,128]{5,3,4,2,1,0:T(8,128)(2,1)} fusion(bf16[4,4,2,64,2,128]{5,3,4,2,1,0:T(8,128)(2,1)} %pad_maximum_fusion.17, s32[1024]{0:T(1024)} %pad_clamp_fusion.4), kind=kCustom, calls=%fused_computation.2 | custom fusion | bytes 2097168 | tf_op jit(solution)/shard_map/jit(_take)/gather | solution.py:62
  99.0 1.4 bitcast_select_fusion.2
  101.4 1.6 fusion.21
  103.8 1.9 %collective-permute-start.12 = (bf16[4,2,64,128]{3,2,1,0:T(8,128)(2,1)S(1)}, bf16[4,2,64,128]{3,2,1,0:T(8,128)(2,1)S(1)}, u32[]{:S(2)}, u32[]{:S(2)}) collective-permute-start(bf16[4,2,64,128]{3,2,1,0:T(8,128)(2,1)S(1)} %get-tuple-element.44), channel_id=1, source_target_pairs={{0,2},{1,3},{2,0},{3,1},{4,6},{5,7},{6,4},{7,5},{8,10},{9,11},{10,... | collective-permute-start | bytes 393224 | tf_op jit(solution)/shard_map/ppermute | solution.py:57
  105.8 2.0 %collective-permute-start.13 = (bf16[4,2,64,128]{3,2,1,0:T(8,128)(2,1)S(1)}, bf16[4,2,64,128]{3,2,1,0:T(8,128)(2,1)S(1)}, u32[]{:S(2)}, u32[]{:S(2)}) collective-permute-start(bf16[4,2,64,128]{3,2,1,0:T(8,128)(2,1)S(1)} %get-tuple-element.44), channel_id=1, source_target_pairs={{0,3},{1,0},{2,1},{3,2},{4,7},{5,4},{6,5},{7,6},{8,11},{9,8},{10,9... | collective-permute-start | bytes 393224 | tf_op jit(solution)/shard_map/ppermute | solution.py:57
  107.8 2.4 %fusion.29 = f32[1,2,513,129]{3,2,1,0:T(8,128)} fusion(f32[6,1,130]{2,1,0:T(1,128)} %collective-permute-done.24, f32[6,512,1]{2,1,0:T(8,128)S(1)} %copy.227, f32[6,512,1]{2,1,0:T(8,128)S(1)} %copy.226, f32[4,512,128]{2,1,0:T(8,128)S(1)} %bitcast.230, f32[2,512,128]{2,1,0:T(8,128)S(1)} %copy-done.6, pred[129]{0:T(512)(128)(4,1)S(1)} %copy-done.36), kind=kLoop, calls=%fused_computation.52 | loop fusion | flops 1323540 | bytes 2130105 | tf_op jit(solution)/shard_map/stack | solution.py:166
  110.7 1.4 collective-permute-done.12
  112.1 4.3 %collective-permute-done.13 = bf16[4,2,64,128]{3,2,1,0:T(8,128)(2,1)S(1)} collective-permute-done((bf16[4,2,64,128]{3,2,1,0:T(8,128)(2,1)S(1)}, bf16[4,2,64,128]{3,2,1,0:T(8,128)(2,1)S(1)}, u32[]{:S(2)}, u32[]{:S(2)}) %collective-permute-start.13) | collective-permute-done | bytes 131104 | tf_op jit(solution)/shard_map/ppermute | solution.py:57
  117.2 2.6 %gather_fusion.3 = bf16[4,4,2,64,128]{4,3,2,1,0:T(8,128)(2,1)} fusion(bf16[4,4,2,64,128]{4,3,2,1,0:T(8,128)(2,1)} %pad_maximum_fusion.19, s32[1024]{0:T(1024)} %pad_clamp_fusion.5), kind=kCustom, calls=%fused_computation.3 | custom fusion | bytes 1048592 | tf_op jit(solution)/shard_map/jit(_take)/gather | solution.py:62
  121.0 5.5 %collective-permute-start.14 = (bf16[4,4,2,64,128]{4,3,2,1,0:T(8,128)(2,1)S(1)}, bf16[4,4,2,64,128]{4,3,2,1,0:T(8,128)(2,1)S(1)}, u32[]{:S(2)}, u32[]{:S(2)}) collective-permute-start(bf16[4,4,2,64,128]{4,3,2,1,0:T(8,128)(2,1)S(1)} %broadcast_select_fusion.1), channel_id=1, source_target_pairs={{0,4},{1,5},{2,6},{3,7},{4,8},{5,9},{6,10},{7,11},{8,12},{9,13},{1... | collective-permute-start | bytes 1572872 | tf_op jit(solution)/shard_map/ppermute | solution.py:57
  126.5 2.5 %collective-permute-start.16 = (bf16[4,4,2,64,128]{4,3,2,1,0:T(8,128)(2,1)S(1)}, bf16[4,4,2,64,128]{4,3,2,1,0:T(8,128)(2,1)S(1)}, u32[]{:S(2)}, u32[]{:S(2)}) collective-permute-start(bf16[4,4,2,64,128]{4,3,2,1,0:T(8,128)(2,1)S(1)} %broadcast_select_fusion.1), channel_id=1, source_target_pairs={{0,12},{1,13},{2,14},{3,15},{4,0},{5,1},{6,2},{7,3},{8,4},{9,5},{1... | collective-permute-start | bytes 1572872 | tf_op jit(solution)/shard_map/ppermute | solution.py:57
  129.0 1.6 pad_maximum_fusion
  132.2 4.0 %collective-permute-done.14 = bf16[4,4,2,64,128]{4,3,2,1,0:T(8,128)(2,1)S(1)} collective-permute-done((bf16[4,4,2,64,128]{4,3,2,1,0:T(8,128)(2,1)S(1)}, bf16[4,4,2,64,128]{4,3,2,1,0:T(8,128)(2,1)S(1)}, u32[]{:S(2)}, u32[]{:S(2)}) %collective-permute-start.14) | collective-permute-done | bytes 524320 | tf_op jit(solution)/shard_map/ppermute | solution.py:57
  136.2 11.2 %collective-permute-done.15 = bf16[4,4,2,64,128]{4,3,2,1,0:T(8,128)(2,1)S(1)} collective-permute-done((bf16[4,4,2,64,128]{4,3,2,1,0:T(8,128)(2,1)S(1)}, bf16[4,4,2,64,128]{4,3,2,1,0:T(8,128)(2,1)S(1)}, u32[]{:S(2)}, u32[]{:S(2)}) %collective-permute-start.15) | collective-permute-done | bytes 524320 | tf_op jit(solution)/shard_map/ppermute | solution.py:57
  147.4 1.8 collective-permute-done.16
  149.5 2.3 %gather_fusion.4 = bf16[4,4,4,2,64,128]{5,4,3,2,1,0:T(8,128)(2,1)} fusion(bf16[4,4,4,2,64,128]{5,4,3,2,1,0:T(8,128)(2,1)S(1)} %pad_maximum_fusion.6, s32[1024]{0:T(1024)} %pad_clamp_fusion.4), kind=kCustom, calls=%fused_computation.4 | custom fusion | bytes 4194320 | tf_op jit(solution)/shard_map/jit(_take)/gather | solution.py:62
  151.8 1.9 bitcast_select_fusion
  154.9 5.5 %collective-permute-start.18 = (bf16[64,2,2,128]{3,0,1,2:T(8,128)(2,1)S(1)}, bf16[64,2,2,128]{3,0,1,2:T(8,128)(2,1)S(1)}, u32[]{:S(2)}, u32[]{:S(2)}) collective-permute-start(bf16[64,2,2,128]{3,0,1,2:T(8,128)(2,1)S(1)} %bitcast.269), channel_id=1, source_target_pairs={{0,64},{16,80},{32,96},{48,112},{64,0},{80,16},{96,32},{112,48},{1... | collective-permute-start | bytes 196616 | tf_op jit(solution)/shard_map/ppermute | solution.py:57
  160.4 2.0 %multiply_maximum_fusion = f32[513,129]{1,0:T(8,128)} fusion(f32[513,129]{1,0:T(8,128)} %multiply_reduce_fusion), kind=kLoop, calls=%fused_computation.86 | loop fusion | flops 132354 | bytes 529416 | tf_op jit(solution)/shard_map/max | solution.py:170
  162.8 1.6 collective-permute-done.19
  165.1 1.7 gather_fusion.6
  167.0 1.8 divide_select_fusion
  173.7 3.2 %collective-permute-start.21 = (bf16[2,4,64,2,2,128]{5,2,3,4,1,0:T(8,128)(2,1)S(1)}, bf16[2,4,64,2,2,128]{5,2,3,4,1,0:T(8,128)(2,1)S(1)}, u32[]{:S(2)}, u32[]{:S(2)}) collective-permute-start(bf16[2,4,64,2,2,128]{5,2,3,4,1,0:T(8,128)(2,1)S(1)} %broadcast_select_fusion), channel_id=1, source_target_pairs={{0,16},{16,0},{32,48},{48,32},{64,80},{80,64},{96,112},{112,96},{1... | collective-permute-start | bytes 1572872 | tf_op jit(solution)/shard_map/ppermute | solution.py:57
  176.9 1.5 fusion.26
  186.6 2.4 %fusion.8 = f32[2,256,128]{1,2,0:T(8,128)S(1)} fusion(f32[2,128,256]{2,1,0:T(8,128)S(1)} %fusion.41, bf16[1,1024,2,256]{3,2,1,0:T(2,128)(2,1)S(1)} %copy-done.16, f32[2,1024]{1,0:T(2,128)S(1)} %copy-done.32, f32[2,1024]{1,0:T(2,128)S(1)} %copy-done.33, bf16[2,2,1024,128]{3,2,1,0:T(8,128)(2,1)} %bitcast.248), kind=kOutput, calls=%fused_computation.37 | convolution fusion | flops 135856128 | bytes 2637824 | tf_op jit(solution)/shard_map/pjh,jpu->jhu/dot_general | solution.py:148
  189.1 2.7 %fusion.47 = f32[2,512,128]{2,1,0:T(8,128)} fusion(f32[2,512,128]{2,1,0:T(8,128)S(1)} %copy-done.7, f32[2,513,129]{2,1,0:T(8,128)} %get-tuple-element.30, f32[2,513,129]{2,1,0:T(8,128)S(1)} %copy-done.20, f32[1,512,128]{2,1,0:T(8,128)S(1)} %bitcast.244, f32[1,512,128]{2,1,0:T(8,128)S(1)} %bitcast.243), kind=kLoop, calls=%fused_computation.90 | loop fusion | flops 917504 | bytes 3670016 | tf_op jit(solution)/shard_map/sub | solution.py:178
  (205 shorter events, 52.1 us)
Async XLA Ops:
  0.6 53.5 %copy-start = (bf16[8,128,128]{2,1,0:T(8,128)(2,1)S(1)}, bf16[8,128,128]{2,1,0:T(8,128)(2,1)}, u32[]{:S(2)}) copy-start(bf16[8,128,128]{2,1,0:T(8,128)(2,1)} %param.16) | copy-start | bytes 786436
  3.5 3.6 %copy-start.15 = (bf16[1,1024,2,256]{3,2,1,0:T(2,128)(2,1)}, bf16[1,1024,2,256]{3,2,1,0:T(2,128)(2,1)S(1)}, u32[]{:S(2)}) copy-start(bf16[1,1024,2,256]{3,2,1,0:T(2,128)(2,1)S(1)} %get-tuple-element.35) | copy-start | bytes 3145732
  11.0 4.3 %copy-start.2 = (f32[2,2,512,128]{3,2,1,0:T(8,128)S(1)}, f32[2,2,512,128]{3,2,1,0:T(8,128)}, u32[]{:S(2)}) copy-start(f32[2,2,512,128]{3,2,1,0:T(8,128)} %param.11) | copy-start | bytes 3145732
  12.0 19.0 %collective-permute-start = (f32[2,4,2,64,2,128]{5,3,4,2,1,0:T(8,128)}, f32[2,4,2,64,2,128]{5,3,4,2,1,0:T(8,128)}, u32[]{:S(2)}, u32[]{:S(2)}) collective-permute-start(f32[2,4,2,64,2,128]{5,3,4,2,1,0:T(8,128)} %bitcast.221), channel_id=1, source_target_pairs={{0,16},{16,0},{32,48},{48,32},{64,80},{80,64},{96,112},{112,96},{1... | collective-permute-start | bytes 3145736 | tf_op jit(solution)/shard_map/ppermute | solution.py:45
  17.0 9.8 %copy-start.29 = (s32[32,1,6]{0,1,2:T(1,128)S(1)}, s32[32,1,6]{0,1,2:T(1,128)}, u32[]{:S(2)}) copy-start(s32[32,1,6]{0,1,2:T(1,128)} %param.17) | copy-start | bytes 2308
  17.0 9.9 %copy-start.30 = (s32[32,1,6]{0,1,2:T(1,128)S(1)}, s32[32,1,6]{0,1,2:T(1,128)}, u32[]{:S(2)}) copy-start(s32[32,1,6]{0,1,2:T(1,128)} %param.18) | copy-start | bytes 2308
  17.0 13.5 %copy-start.41 = (s32[64]{0:T(128)S(1)}, s32[64]{0:T(128)}, u32[]{:S(2)}) copy-start(s32[64]{0:T(128)} %param.19) | copy-start | bytes 772
  18.9 36.6 %collective-permute-start.22 = (f32[6,512,1]{1,2,0:T(1,128)S(1)}, f32[6,512,1]{1,2,0:T(1,128)}, u32[]{:S(2)}, u32[]{:S(2)}) collective-permute-start(f32[6,512,1]{1,2,0:T(1,128)S(1)} %copy.224), channel_id=1, source_target_pairs={{0,16},{16,32},{32,48},{48,64},{64,80},{80,96},{96,112},{112,128},... | collective-permute-start | bytes 36872 | tf_op jit(solution)/shard_map/ppermute | solution.py:17
  21.9 34.8 %collective-permute-start.23 = (f32[6,512,1]{1,2,0:T(1,128)}, f32[6,512,1]{1,2,0:T(1,128)}, u32[]{:S(2)}, u32[]{:S(2)}) collective-permute-start(f32[6,512,1]{1,2,0:T(1,128)} %copy.225), channel_id=1, source_target_pairs={{16,0},{32,16},{48,32},{64,48},{80,64},{96,80},{112,96},{128,112},... | collective-permute-start | bytes 36872 | tf_op jit(solution)/shard_map/ppermute | solution.py:20
  32.4 12.0 %collective-permute-start.1 = (f32[4,2,64,2,128]{4,2,3,1,0:T(8,128)S(1)}, f32[4,2,64,2,128]{4,2,3,1,0:T(8,128)S(1)}, u32[]{:S(2)}, u32[]{:S(2)}) collective-permute-start(f32[4,2,64,2,128]{4,2,3,1,0:T(8,128)S(1)} %dynamic-slice_bitcast_fusion), channel_id=1, source_target_pairs={{0,128},{16,144},{32,160},{48,176},{64,192},{80,208},{96,224},{112... | collective-permute-start | bytes 1572872 | tf_op jit(solution)/shard_map/ppermute | solution.py:45
  45.3 12.6 %collective-permute-start.2 = (f32[2,64,2,128]{3,1,0,2:T(8,128)}, f32[2,64,2,128]{3,1,0,2:T(8,128)}, u32[]{:S(2)}, u32[]{:S(2)}) collective-permute-start(f32[2,64,2,128]{3,1,0,2:T(8,128)} %bitcast.224), channel_id=1, source_target_pairs={{0,32},{16,48},{32,64},{48,80},{64,96},{80,112},{96,0},{112,16},{1... | collective-permute-start | bytes 393224 | tf_op jit(solution)/shard_map/ppermute | solution.py:45
  47.1 10.8 %collective-permute-start.3 = (f32[2,64,2,128]{3,1,0,2:T(8,128)}, f32[2,64,2,128]{3,1,0,2:T(8,128)}, u32[]{:S(2)}, u32[]{:S(2)}) collective-permute-start(f32[2,64,2,128]{3,1,0,2:T(8,128)} %bitcast.223), channel_id=1, source_target_pairs={{0,64},{16,80},{32,96},{48,112},{64,0},{80,16},{96,32},{112,48},{1... | collective-permute-start | bytes 393224 | tf_op jit(solution)/shard_map/ppermute | solution.py:45
  50.7 7.2 %collective-permute-start.4 = (f32[2,64,2,128]{3,1,0,2:T(8,128)}, f32[2,64,2,128]{3,1,0,2:T(8,128)}, u32[]{:S(2)}, u32[]{:S(2)}) collective-permute-start(f32[2,64,2,128]{3,1,0,2:T(8,128)} %bitcast.222), channel_id=1, source_target_pairs={{0,96},{16,112},{32,0},{48,16},{64,32},{80,48},{96,64},{112,80},{1... | collective-permute-start | bytes 393224 | tf_op jit(solution)/shard_map/ppermute | solution.py:45
  59.0 15.4 %collective-permute-start.5 = (bf16[2,64,2,128]{3,1,2,0:T(8,128)(2,1)S(1)}, bf16[2,64,2,128]{3,1,2,0:T(8,128)(2,1)S(1)}, u32[]{:S(2)}, u32[]{:S(2)}) collective-permute-start(bf16[2,64,2,128]{3,1,2,0:T(8,128)(2,1)S(1)} %bitcast.256), channel_id=1, source_target_pairs={{0,1},{1,2},{2,3},{3,0},{4,5},{5,6},{6,7},{7,4},{8,9},{9,10},{10,1... | collective-permute-start | bytes 196616 | tf_op jit(solution)/shard_map/ppermute | solution.py:57
  62.1 12.3 %collective-permute-start.6 = (bf16[2,64,2,128]{3,1,2,0:T(8,128)(2,1)S(1)}, bf16[2,64,2,128]{3,1,2,0:T(8,128)(2,1)S(1)}, u32[]{:S(2)}, u32[]{:S(2)}) collective-permute-start(bf16[2,64,2,128]{3,1,2,0:T(8,128)(2,1)S(1)} %bitcast.257), channel_id=1, source_target_pairs={{0,2},{1,3},{2,0},{3,1},{4,6},{5,7},{6,4},{7,5},{8,10},{9,11},{10,... | collective-permute-start | bytes 196616 | tf_op jit(solution)/shard_map/ppermute | solution.py:57
  66.8 7.6 %collective-permute-start.7 = (bf16[2,64,2,128]{3,1,2,0:T(8,128)(2,1)S(1)}, bf16[2,64,2,128]{3,1,2,0:T(8,128)(2,1)S(1)}, u32[]{:S(2)}, u32[]{:S(2)}) collective-permute-start(bf16[2,64,2,128]{3,1,2,0:T(8,128)(2,1)S(1)} %bitcast.258), channel_id=1, source_target_pairs={{0,3},{1,0},{2,1},{3,2},{4,7},{5,4},{6,5},{7,6},{8,11},{9,8},{10,9... | collective-permute-start | bytes 196616 | tf_op jit(solution)/shard_map/ppermute | solution.py:57
  70.6 17.7 %collective-permute-start.24 = (f32[6,1,130]{2,1,0:T(1,128)}, f32[6,1,130]{2,1,0:T(1,128)}, u32[]{:S(2)}, u32[]{:S(2)}) collective-permute-start(f32[6,1,130]{2,1,0:T(1,128)} %get-tuple-element.28), channel_id=1, source_target_pairs={{0,1},{1,2},{2,3},{3,4},{4,5},{5,6},{6,7},{7,8},{8,9},{9,10},{10,1... | collective-permute-start | bytes 9368 | tf_op jit(solution)/shard_map/ppermute | solution.py:17
  73.1 15.3 %collective-permute-start.25 = (f32[6,1,130]{2,1,0:T(1,128)}, f32[6,1,130]{2,1,0:T(1,128)}, u32[]{:S(2)}, u32[]{:S(2)}) collective-permute-start(f32[6,1,130]{2,1,0:T(1,128)} %get-tuple-element.27), channel_id=1, source_target_pairs={{1,0},{2,1},{3,2},{4,3},{5,4},{6,5},{7,6},{8,7},{9,8},{10,9},{11,1... | collective-permute-start | bytes 9368 | tf_op jit(solution)/shard_map/ppermute | solution.py:20
  78.6 13.2 %collective-permute-start.8 = (bf16[4,2,64,2,128]{4,2,3,1,0:T(8,128)(2,1)S(1)}, bf16[4,2,64,2,128]{4,2,3,1,0:T(8,128)(2,1)S(1)}, u32[]{:S(2)}, u32[]{:S(2)}) collective-permute-start(bf16[4,2,64,2,128]{4,2,3,1,0:T(8,128)(2,1)S(1)} %broadcast_select_fusion.3), channel_id=1, source_target_pairs={{0,4},{1,5},{2,6},{3,7},{4,8},{5,9},{6,10},{7,11},{8,12},{9,13},{1... | collective-permute-start | bytes 786440 | tf_op jit(solution)/shard_map/ppermute | solution.py:57
  84.7 10.2 %collective-permute-start.9 = (bf16[4,2,64,2,128]{4,2,3,1,0:T(8,128)(2,1)S(1)}, bf16[4,2,64,2,128]{4,2,3,1,0:T(8,128)(2,1)S(1)}, u32[]{:S(2)}, u32[]{:S(2)}) collective-permute-start(bf16[4,2,64,2,128]{4,2,3,1,0:T(8,128)(2,1)S(1)} %broadcast_select_fusion.3), channel_id=1, source_target_pairs={{0,8},{1,9},{2,10},{3,11},{4,12},{5,13},{6,14},{7,15},{8,0},{9,1},... | collective-permute-start | bytes 786440 | tf_op jit(solution)/shard_map/ppermute | solution.py:57
  87.3 7.6 %collective-permute-start.10 = (bf16[4,2,64,2,128]{4,2,3,1,0:T(8,128)(2,1)S(1)}, bf16[4,2,64,2,128]{4,2,3,1,0:T(8,128)(2,1)S(1)}, u32[]{:S(2)}, u32[]{:S(2)}) collective-permute-start(bf16[4,2,64,2,128]{4,2,3,1,0:T(8,128)(2,1)S(1)} %broadcast_select_fusion.3), channel_id=1, source_target_pairs={{0,12},{1,13},{2,14},{3,15},{4,0},{5,1},{6,2},{7,3},{8,4},{9,5},{1... | collective-permute-start | bytes 786440 | tf_op jit(solution)/shard_map/ppermute | solution.py:57
  88.4 3.3 %copy-start.23 = (bf16[4,2,64,2,128]{4,2,3,1,0:T(8,128)(2,1)S(1)}, bf16[4,2,64,2,128]{4,2,3,1,0:T(8,128)(2,1)}, u32[]{:S(2)}) copy-start(bf16[4,2,64,2,128]{4,2,3,1,0:T(8,128)(2,1)} %gather_fusion.1) | copy-start | bytes 786436
  88.4 3.3 %copy-start.28 = (pred[4]{0:T(512)(128)(4,1)S(1)}, pred[4]{0:T(512)(128)(4,1)}, u32[]{:S(2)}) copy-start(pred[4]{0:T(512)(128)(4,1)} %get-tuple-element.59) | copy-start | bytes 16
  96.0 3.0 %copy-start.39 = (pred[32]{0:T(512)(128)(4,1)S(1)}, pred[32]{0:T(512)(128)(4,1)}, u32[]{:S(2)}) copy-start(pred[32]{0:T(512)(128)(4,1)} %broadcast_in_dim.188) | copy-start | bytes 100
  101.4 6.4 %copy-start.3 = (f32[2,2,512,128]{3,2,1,0:T(8,128)S(1)}, f32[2,2,512,128]{3,2,1,0:T(8,128)}, u32[]{:S(2)}) copy-start(f32[2,2,512,128]{3,2,1,0:T(8,128)} %param.11) | copy-start | bytes 3145732
  101.4 6.4 %copy-start.6 = (f32[2,512,128]{2,1,0:T(8,128)S(1)}, f32[2,512,128]{2,1,0:T(8,128)}, u32[]{:S(2)}) copy-start(f32[2,512,128]{2,1,0:T(8,128)} %param.10) | copy-start | bytes 1572868
  101.4 6.4 %copy-start.36 = (pred[129]{0:T(512)(128)(4,1)S(1)}, pred[129]{0:T(512)(128)(4,1)}, u32[]{:S(2)}) copy-start(pred[129]{0:T(512)(128)(4,1)} %get-tuple-element.53) | copy-start | bytes 391
  103.7 6.9 %collective-permute-start.11 = (bf16[4,2,64,128]{3,2,1,0:T(8,128)(2,1)S(1)}, bf16[4,2,64,128]{3,2,1,0:T(8,128)(2,1)S(1)}, u32[]{:S(2)}, u32[]{:S(2)}) collective-permute-start(bf16[4,2,64,128]{3,2,1,0:T(8,128)(2,1)S(1)} %get-tuple-element.44), channel_id=1, source_target_pairs={{0,1},{1,2},{2,3},{3,0},{4,5},{5,6},{6,7},{7,4},{8,9},{9,10},{10,1... | collective-permute-start | bytes 393224 | tf_op jit(solution)/shard_map/ppermute | solution.py:57
  103.8 8.2 %collective-permute-start.12 = (bf16[4,2,64,128]{3,2,1,0:T(8,128)(2,1)S(1)}, bf16[4,2,64,128]{3,2,1,0:T(8,128)(2,1)S(1)}, u32[]{:S(2)}, u32[]{:S(2)}) collective-permute-start(bf16[4,2,64,128]{3,2,1,0:T(8,128)(2,1)S(1)} %get-tuple-element.44), channel_id=1, source_target_pairs={{0,2},{1,3},{2,0},{3,1},{4,6},{5,7},{6,4},{7,5},{8,10},{9,11},{10,... | collective-permute-start | bytes 393224 | tf_op jit(solution)/shard_map/ppermute | solution.py:57
  105.8 10.6 %collective-permute-start.13 = (bf16[4,2,64,128]{3,2,1,0:T(8,128)(2,1)S(1)}, bf16[4,2,64,128]{3,2,1,0:T(8,128)(2,1)S(1)}, u32[]{:S(2)}, u32[]{:S(2)}) collective-permute-start(bf16[4,2,64,128]{3,2,1,0:T(8,128)(2,1)S(1)} %get-tuple-element.44), channel_id=1, source_target_pairs={{0,3},{1,0},{2,1},{3,2},{4,7},{5,4},{6,5},{7,6},{8,11},{9,8},{10,9... | collective-permute-start | bytes 393224 | tf_op jit(solution)/shard_map/ppermute | solution.py:57
  119.8 9.3 %copy-start.4 = (f32[2,2,512,128]{3,2,1,0:T(8,128)S(1)}, f32[2,2,512,128]{3,2,1,0:T(8,128)}, u32[]{:S(2)}) copy-start(f32[2,2,512,128]{3,2,1,0:T(8,128)} %param.11) | copy-start | bytes 3145732
  121.0 9.6 %copy-start.12 = (f32[1,2,513,129]{3,2,1,0:T(8,128)S(1)}, f32[1,2,513,129]{3,2,1,0:T(8,128)}, u32[]{:S(2)}) copy-start(f32[1,2,513,129]{3,2,1,0:T(8,128)} %fusion.29) | copy-start | bytes 1588252
  121.0 9.6 %copy-start.14 = (f32[1,2,513,129]{3,2,1,0:T(8,128)S(1)}, f32[1,2,513,129]{3,2,1,0:T(8,128)}, u32[]{:S(2)}) copy-start(f32[1,2,513,129]{3,2,1,0:T(8,128)} %fusion.32) | copy-start | bytes 1588252
  121.0 15.1 %collective-permute-start.14 = (bf16[4,4,2,64,128]{4,3,2,1,0:T(8,128)(2,1)S(1)}, bf16[4,4,2,64,128]{4,3,2,1,0:T(8,128)(2,1)S(1)}, u32[]{:S(2)}, u32[]{:S(2)}) collective-permute-start(bf16[4,4,2,64,128]{4,3,2,1,0:T(8,128)(2,1)S(1)} %broadcast_select_fusion.1), channel_id=1, source_target_pairs={{0,4},{1,5},{2,6},{3,7},{4,8},{5,9},{6,10},{7,11},{8,12},{9,13},{1... | collective-permute-start | bytes 1572872 | tf_op jit(solution)/shard_map/ppermute | solution.py:57
  126.5 20.9 %collective-permute-start.15 = (bf16[4,4,2,64,128]{4,3,2,1,0:T(8,128)(2,1)S(1)}, bf16[4,4,2,64,128]{4,3,2,1,0:T(8,128)(2,1)S(1)}, u32[]{:S(2)}, u32[]{:S(2)}) collective-permute-start(bf16[4,4,2,64,128]{4,3,2,1,0:T(8,128)(2,1)S(1)} %broadcast_select_fusion.1), channel_id=1, source_target_pairs={{0,8},{1,9},{2,10},{3,11},{4,12},{5,13},{6,14},{7,15},{8,0},{9,1},... | collective-permute-start | bytes 1572872 | tf_op jit(solution)/shard_map/ppermute | solution.py:57
  126.5 22.7 %collective-permute-start.16 = (bf16[4,4,2,64,128]{4,3,2,1,0:T(8,128)(2,1)S(1)}, bf16[4,4,2,64,128]{4,3,2,1,0:T(8,128)(2,1)S(1)}, u32[]{:S(2)}, u32[]{:S(2)}) collective-permute-start(bf16[4,4,2,64,128]{4,3,2,1,0:T(8,128)(2,1)S(1)} %broadcast_select_fusion.1), channel_id=1, source_target_pairs={{0,12},{1,13},{2,14},{3,15},{4,0},{5,1},{6,2},{7,3},{8,4},{9,5},{1... | collective-permute-start | bytes 1572872 | tf_op jit(solution)/shard_map/ppermute | solution.py:57
  154.5 12.3 %copy-start.37 = (pred[4]{0:T(512)(128)(4,1)S(1)}, pred[4]{0:T(512)(128)(4,1)}, u32[]{:S(2)}) copy-start(pred[4]{0:T(512)(128)(4,1)} %compare_and_fusion.3) | copy-start | bytes 16
  154.5 12.5 %copy-start.13 = (f32[1,2,513,129]{3,2,1,0:T(8,128)S(1)}, f32[1,2,513,129]{3,2,1,0:T(8,128)}, u32[]{:S(2)}) copy-start(f32[1,2,513,129]{3,2,1,0:T(8,128)} %fusion.29) | copy-start | bytes 1588252
  154.8 12.2 %copy-start.9 = (f32[4,514,130]{2,1,0:T(8,128)S(1)}, f32[4,514,130]{2,1,0:T(8,128)}, u32[]{:S(2)}) copy-start(f32[4,514,130]{2,1,0:T(8,128)} %copy-done.8) | copy-start | bytes 3207364
  154.8 7.5 %collective-permute-start.17 = (bf16[64,2,2,128]{3,0,1,2:T(8,128)(2,1)S(1)}, bf16[64,2,2,128]{3,0,1,2:T(8,128)(2,1)S(1)}, u32[]{:S(2)}, u32[]{:S(2)}) collective-permute-start(bf16[64,2,2,128]{3,0,1,2:T(8,128)(2,1)S(1)} %bitcast.268), channel_id=1, source_target_pairs={{0,32},{16,48},{32,64},{48,80},{64,96},{80,112},{96,0},{112,16},{1... | collective-permute-start | bytes 196616 | tf_op jit(solution)/shard_map/ppermute | solution.py:57
  154.9 7.9 %collective-permute-start.18 = (bf16[64,2,2,128]{3,0,1,2:T(8,128)(2,1)S(1)}, bf16[64,2,2,128]{3,0,1,2:T(8,128)(2,1)S(1)}, u32[]{:S(2)}, u32[]{:S(2)}) collective-permute-start(bf16[64,2,2,128]{3,0,1,2:T(8,128)(2,1)S(1)} %bitcast.269), channel_id=1, source_target_pairs={{0,64},{16,80},{32,96},{48,112},{64,0},{80,16},{96,32},{112,48},{1... | collective-permute-start | bytes 196616 | tf_op jit(solution)/shard_map/ppermute | solution.py:57
  160.4 4.0 %collective-permute-start.19 = (bf16[64,2,2,128]{3,0,1,2:T(8,128)(2,1)S(1)}, bf16[64,2,2,128]{3,0,1,2:T(8,128)(2,1)S(1)}, u32[]{:S(2)}, u32[]{:S(2)}) collective-permute-start(bf16[64,2,2,128]{3,0,1,2:T(8,128)(2,1)S(1)} %bitcast.270), channel_id=1, source_target_pairs={{0,96},{16,112},{32,0},{48,16},{64,32},{80,48},{96,64},{112,80},{1... | collective-permute-start | bytes 196616 | tf_op jit(solution)/shard_map/ppermute | solution.py:57
  166.9 5.7 %collective-permute-start.20 = (bf16[4,64,2,2,128]{4,1,2,3,0:T(8,128)(2,1)S(1)}, bf16[4,64,2,2,128]{4,1,2,3,0:T(8,128)(2,1)S(1)}, u32[]{:S(2)}, u32[]{:S(2)}) collective-permute-start(bf16[4,64,2,2,128]{4,1,2,3,0:T(8,128)(2,1)S(1)} %broadcast_select_fusion.2), channel_id=1, source_target_pairs={{0,128},{16,144},{32,160},{48,176},{64,192},{80,208},{96,224},{112... | collective-permute-start | bytes 786440 | tf_op jit(solution)/shard_map/ppermute | solution.py:57
  172.6 4.3 %copy-start.11 = (f32[2,2,513,129]{3,2,1,0:T(8,128)S(1)}, f32[2,2,513,129]{3,2,1,0:T(8,128)}, u32[]{:S(2)}) copy-start(f32[2,2,513,129]{3,2,1,0:T(8,128)} %copy-done.10) | copy-start | bytes 3176500
  172.6 4.3 %copy-start.31 = (pred[513]{0:T(1024)(128)(4,1)S(1)}, pred[513]{0:T(1024)(128)(4,1)}, u32[]{:S(2)}) copy-start(pred[513]{0:T(1024)(128)(4,1)} %get-tuple-element.56) | copy-start | bytes 1543
  173.7 4.8 %copy-start.22 = (f32[2,64,4,128]{3,1,0,2:T(8,128)S(1)}, f32[2,64,4,128]{3,1,0,2:T(8,128)}, u32[]{:S(2)}) copy-start(f32[2,64,4,128]{3,1,0,2:T(8,128)} %copy-done.21) | copy-start | bytes 786436
  173.7 5.8 %collective-permute-start.21 = (bf16[2,4,64,2,2,128]{5,2,3,4,1,0:T(8,128)(2,1)S(1)}, bf16[2,4,64,2,2,128]{5,2,3,4,1,0:T(8,128)(2,1)S(1)}, u32[]{:S(2)}, u32[]{:S(2)}) collective-permute-start(bf16[2,4,64,2,2,128]{5,2,3,4,1,0:T(8,128)(2,1)S(1)} %broadcast_select_fusion), channel_id=1, source_target_pairs={{0,16},{16,0},{32,48},{48,32},{64,80},{80,64},{96,112},{112,96},{1... | collective-permute-start | bytes 1572872 | tf_op jit(solution)/shard_map/ppermute | solution.py:57
  181.3 3.8 %copy-start.24 = (bf16[1024,2,2,128]{3,0,2,1:T(8,128)(2,1)}, bf16[1024,2,2,128]{3,0,2,1:T(8,128)(2,1)S(1)}, u32[]{:S(2)}) copy-start(bf16[1024,2,2,128]{3,0,2,1:T(8,128)(2,1)S(1)} %bitcast_select_fusion.1) | copy-start | bytes 3145732
  (21 other events, 35.3 us)

commit v6 on v3

--- a/solution.py
+++ b/solution.py
@@ -114,8 +114,7 @@
         0.0,
     )
     dual_b = dual_new.astype(jnp.bfloat16)
-    all_rows = doubling_gather(jnp.moveaxis(dual_b, 2, 0), "tile", (2, 1, 8, 4))
-    all_rows = jnp.moveaxis(all_rows.reshape(-1, *all_rows.shape[2:]), 0, 2)
+    all_rows = lax.all_gather(dual_b, "tile", axis=2, tiled=True)
     chosen = jnp.take(all_rows, foot_mine, axis=2)
     back = jnp.einsum("cpjfv,jfuv->cjpu", chosen, kern_mine, preferred_element_type=jnp.float32)
     back_b = back.astype(jnp.bfloat16)

time: 193 us -> 202 us (1.047)
  between operations: 1.53 us -> 14.8 us
  starting transfers between devices: 51.5 us -> 41.1 us
  waiting for transfers between devices: 78.2 us -> 87.2 us
  other arithmetic: 23.3 us -> 20.1 us
    all_gather x0 -> x1, waiting for transfers between devices: none -> 30.8 us  [on_device(): all_rows = lax.all_gather(dual_b, 'tile', axis=2, tiled=True)]
    ppermute x12 -> x8, waiting for transfers between devices: 48.6 us -> 25.8 us  [doubling_gather(): got = lax.ppermute(block, axis, pairs)]
    ppermute x12 -> x8, starting transfers between devices: 28.5 us -> 21 us  [doubling_gather(): got = lax.ppermute(block, axis, pairs)]
    ppermute x2, starting transfers between devices: 14.7 us -> 11.8 us  [padded_2(): lax.ppermute(lax.slice_in_dim(block, block.shape[dim] - width, None, axis...]
    another operation x24 -> x16, other arithmetic: 3.52 us -> 0.68 us  [doubling_gather(): block = jnp.stack([low, high], axis=place)]
    unnamed x68 -> x52, local copies, waits for them, and re-layouts: 5.42 us -> 4.58 us
  transfers between devices with their start and end apart: 20 -> 17, of which waited for: 15 -> 13; matrix products, arithmetic and copies ran while one was open for 13% -> 12% of each run, Pallas kernels for 0% -> 0%
where the time goes in v6:
time: 202 us; the launch traced here: 201 us
  waiting for transfers between devices  87.2 us (43%)
  starting transfers between devices  41.1 us (20%)
  local copies, waits for them, and re-layouts  23.4 us (12%)
  other arithmetic  20.1 us (10%)
  between operations  14.8 us (7%)
  matrix products  14.7 us (7%)
    all_gather x1, waiting for transfers between devices, on_device(): all_rows = lax.all_gather(dual_b, 'tile', axis=2, tiled=True)  30.8 us
    ppermute x4, waiting for transfers between devices, halving_sum(): blocks = keep + lax.ppermute(send, axis, pairs)  25.9 us
    ppermute x8, waiting for transfers between devices, doubling_gather(): got = lax.ppermute(block, axis, pairs)  25.8 us
    ppermute x8, starting transfers between devices, doubling_gather(): got = lax.ppermute(block, axis, pairs)  21 us
    ppermute x2, starting transfers between devices, padded_2(): lax.ppermute(lax.slice_in_dim(block, block.shape[dim] - width, None, axis...  11.8 us
    ppermute x4, starting transfers between devices, halving_sum(): blocks = keep + lax.ppermute(send, axis, pairs)  5.09 us
    another operation x2, other arithmetic, on_device(): jnp.stack([grad_rows, grad_cols])  5.05 us
    ppermute x2, waiting for transfers between devices, padded_2(): lax.ppermute(lax.slice_in_dim(block, 0, width, axis=dim), axis, backward)  4.67 us
  transfers between devices with their start and end apart: 17, of which 13 were waited for; matrix products, arithmetic and copies ran while one was open for 12% of the time, Pallas kernels for 0%

profile of v6, /device:TPU:1, one launch (start us, length us, event | category | flops | bytes accessed | tf_op | source)
XLA Modules:
  0.0 201.3 jit_solution(14505943858660390414)
XLA Ops:
  7.3 2.7 %fusion.65 = (bf16[1,1024,2,256]{3,2,1,0:T(2,128)(2,1)S(1)}, bf16[1,1024,2,256]{3,2,1,0:T(2,128)(2,1)S(1)}) fusion(bf16[2,1024,2,256]{3,2,1,0:T(2,128)(2,1)} %param.14), kind=kLoop, calls=%fused_computation.158 | loop fusion | bytes 4194304 | tf_op jit(solution)/shard_map/slice | solution.py:75
  13.5 1.5 multiply_subtract_fusion
  15.4 1.6 copy.127
  18.5 3.2 %collective-permute-start = (f32[2,2,2,2,64,2,128]{6,4,5,3,2,1,0:T(8,128)}, f32[2,2,2,2,64,2,128]{6,4,5,3,2,1,0:T(8,128)S(1)}, u32[]{:S(2)}, u32[]{:S(2)}) collective-permute-start(f32[2,2,2,2,64,2,128]{6,4,5,3,2,1,0:T(8,128)} %bitcast.206), channel_id=1, source_target_pairs={{0,16},{16,0},{32,48},{48,32},{64,80},{80,64},{96,112},{112,96},{1... | collective-permute-start | bytes 3145736 | tf_op jit(solution)/shard_map/ppermute | solution.py:36
  21.7 2.5 %collective-permute-done = f32[2,2,2,2,64,2,128]{6,4,5,3,2,1,0:T(8,128)S(1)} collective-permute-done((f32[2,2,2,2,64,2,128]{6,4,5,3,2,1,0:T(8,128)}, f32[2,2,2,2,64,2,128]{6,4,5,3,2,1,0:T(8,128)S(1)}, u32[]{:S(2)}, u32[]{:S(2)}) %collective-permute-start) | collective-permute-done | bytes 1048608 | tf_op jit(solution)/shard_map/ppermute | solution.py:36
  25.2 1.4 bitcast_add_fusion
  26.8 13.1 %collective-permute-done.1 = f32[2,2,2,64,2,128]{5,3,4,2,1,0:T(8,128)S(1)} collective-permute-done((f32[2,2,2,64,2,128]{5,3,4,2,1,0:T(8,128)S(1)}, f32[2,2,2,64,2,128]{5,3,4,2,1,0:T(8,128)S(1)}, u32[]{:S(2)}, u32[]{:S(2)}) %collective-permute-start.1) | collective-permute-done | bytes 524320 | tf_op jit(solution)/shard_map/ppermute | solution.py:36
  40.1 6.5 %collective-permute-done.2 = f32[2,2,64,2,128]{4,2,3,1,0:T(8,128)S(1)} collective-permute-done((f32[2,2,64,2,128]{4,2,3,1,0:T(8,128)S(1)}, f32[2,2,64,2,128]{4,2,3,1,0:T(8,128)S(1)}, u32[]{:S(2)}, u32[]{:S(2)}) %collective-permute-start.2) | collective-permute-done | bytes 262176 | tf_op jit(solution)/shard_map/ppermute | solution.py:36
  46.8 1.7 collective-permute-start.3
  48.4 3.8 %collective-permute-done.3 = f32[2,64,2,128]{3,1,0,2:T(8,128)S(1)} collective-permute-done((f32[2,64,2,128]{3,1,0,2:T(8,128)S(1)}, f32[2,64,2,128]{3,1,0,2:T(8,128)S(1)}, u32[]{:S(2)}, u32[]{:S(2)}) %collective-permute-start.3) | collective-permute-done | bytes 131104 | tf_op jit(solution)/shard_map/ppermute | solution.py:36
  52.2 5.3 %collective-permute-start.4 = (bf16[2,64,2,128]{3,1,2,0:T(8,128)(2,1)S(1)}, bf16[2,64,2,128]{3,1,2,0:T(8,128)(2,1)S(1)}, u32[]{:S(2)}, u32[]{:S(2)}) collective-permute-start(bf16[2,64,2,128]{3,1,2,0:T(8,128)(2,1)S(1)} %fusion.53), channel_id=1, source_target_pairs={{0,2},{1,3},{2,0},{3,1},{4,6},{5,7},{6,4},{7,5},{8,10},{9,11},{10,... | collective-permute-start | bytes 196616 | tf_op jit(solution)/shard_map/ppermute | solution.py:47
  57.5 1.9 collective-permute-done.4
  59.4 2.5 %collective-permute-start.5 = (bf16[2,2,64,2,128]{4,2,3,1,0:T(8,128)(2,1)S(1)}, bf16[2,2,64,2,128]{4,2,3,1,0:T(8,128)(2,1)S(1)}, u32[]{:S(2)}, u32[]{:S(2)}) collective-permute-start(bf16[2,2,64,2,128]{4,2,3,1,0:T(8,128)(2,1)S(1)} %pad_maximum_fusion.22), channel_id=1, source_target_pairs={{0,1},{1,0},{2,3},{3,2},{4,5},{5,4},{6,7},{7,6},{8,9},{9,8},{10,11... | collective-permute-start | bytes 393224 | tf_op jit(solution)/shard_map/ppermute | solution.py:47
  62.0 4.6 %collective-permute-done.5 = bf16[2,2,64,2,128]{4,2,3,1,0:T(8,128)(2,1)S(1)} collective-permute-done((bf16[2,2,64,2,128]{4,2,3,1,0:T(8,128)(2,1)S(1)}, bf16[2,2,64,2,128]{4,2,3,1,0:T(8,128)(2,1)S(1)}, u32[]{:S(2)}, u32[]{:S(2)}) %collective-permute-start.5) | collective-permute-done | bytes 131104 | tf_op jit(solution)/shard_map/ppermute | solution.py:47
  66.6 3.0 %collective-permute-start.6 = (bf16[2,2,2,64,2,128]{5,3,4,2,1,0:T(8,128)(2,1)S(1)}, bf16[2,2,2,64,2,128]{5,3,4,2,1,0:T(8,128)(2,1)S(1)}, u32[]{:S(2)}, u32[]{:S(2)}) collective-permute-start(bf16[2,2,2,64,2,128]{5,3,4,2,1,0:T(8,128)(2,1)S(1)} %pad_maximum_fusion.20), channel_id=1, source_target_pairs={{0,8},{1,9},{2,10},{3,11},{4,12},{5,13},{6,14},{7,15},{8,0},{9,1},... | collective-permute-start | bytes 786440 | tf_op jit(solution)/shard_map/ppermute | solution.py:47
  69.6 3.8 %collective-permute-done.6 = bf16[2,2,2,64,2,128]{5,3,4,2,1,0:T(8,128)(2,1)S(1)} collective-permute-done((bf16[2,2,2,64,2,128]{5,3,4,2,1,0:T(8,128)(2,1)S(1)}, bf16[2,2,2,64,2,128]{5,3,4,2,1,0:T(8,128)(2,1)S(1)}, u32[]{:S(2)}, u32[]{:S(2)}) %collective-permute-start.6) | collective-permute-done | bytes 262176 | tf_op jit(solution)/shard_map/ppermute | solution.py:47
  73.5 1.6 collective-permute-start.7
  75.2 9.8 %collective-permute-done.7 = bf16[2,2,2,2,64,2,128]{6,4,5,3,2,1,0:T(8,128)(2,1)S(1)} collective-permute-done((bf16[2,2,2,2,64,2,128]{6,4,5,3,2,1,0:T(8,128)(2,1)S(1)}, bf16[2,2,2,2,64,2,128]{6,4,5,3,2,1,0:T(8,128)(2,1)S(1)}, u32[]{:S(2)}, u32[]{:S(2)}) %collective-permute-start.7) | collective-permute-done | bytes 524320 | tf_op jit(solution)/shard_map/ppermute | solution.py:47
  86.2 2.3 %fusion.67 = (bf16[2,64,4,128]{3,1,0,2:T(8,128)(2,1)}, f32[2,64,4,128]{3,1,0,2:T(8,128)}) fusion(bf16[2,64,4,128]{3,2,1,0:T(4,128)(2,1)S(1)} %copy-done.15, bf16[8,128,128]{2,1,0:T(8,128)(2,1)S(1)} %copy-done, f32[4,8,64,2,128]{4,1,3,2,0:T(8,128)S(1)} %fusion.38, f32[2,64,4,128]{3,2,1,0:T(4,128)S(1)} %copy-done.14, ...), kind=kOutput, calls=%fused_computation.160 | convolution fusion | flops 805765120 | bytes 3145792 | tf_op jit(solution)/shard_map/kqpcu,quv->cpkv/dot_general | solution.py:106
  88.5 1.6 slice_maximum_fusion
  90.2 1.9 copy.147
  92.1 8.7 %collective-permute-start.12 = (f32[6,512,1]{1,2,0:T(1,128)S(1)}, f32[6,512,1]{1,2,0:T(1,128)S(1)}, u32[]{:S(2)}, u32[]{:S(2)}) collective-permute-start(f32[6,512,1]{1,2,0:T(1,128)S(1)} %copy.147), channel_id=1, source_target_pairs={{0,16},{16,32},{32,48},{48,64},{64,80},{80,96},{96,112},{112,128},... | collective-permute-start | bytes 36872 | tf_op jit(solution)/shard_map/ppermute | solution.py:16
  101.8 1.9 collective-permute-start.13
  107.7 1.2 copy.150
  108.9 1.5 pad_maximum_fusion.24
  110.4 3.1 %collective-permute-start.14 = (f32[6,1,130]{2,1,0:T(1,128)}, f32[6,1,130]{2,1,0:T(1,128)S(1)}, u32[]{:S(2)}, u32[]{:S(2)}) collective-permute-start(f32[6,1,130]{2,1,0:T(1,128)} %get-tuple-element.19), channel_id=1, source_target_pairs={{0,1},{1,2},{2,3},{3,4},{4,5},{5,6},{6,7},{7,8},{8,9},{9,10},{10,1... | collective-permute-start | bytes 9368 | tf_op jit(solution)/shard_map/ppermute | solution.py:16
  113.5 1.3 collective-permute-start.15
  115.4 1.5 gather_fusion
  116.8 4.7 %collective-permute-done.15 = f32[6,1,130]{2,1,0:T(1,128)} collective-permute-done((f32[6,1,130]{2,1,0:T(1,128)}, f32[6,1,130]{2,1,0:T(1,128)}, u32[]{:S(2)}, u32[]{:S(2)}) %collective-permute-start.15) | collective-permute-done | bytes 3152 | tf_op jit(solution)/shard_map/ppermute | solution.py:19
  121.5 3.2 %fusion.33 = f32[1,2,513,129]{3,2,1,0:T(8,128)} fusion(f32[6,1,130]{2,1,0:T(1,128)} %collective-permute-done.15, f32[6,512,1]{2,1,0:T(8,128)S(1)} %copy.150, f32[6,512,1]{2,1,0:T(8,128)S(1)} %copy.149, f32[4,512,128]{2,1,0:T(8,128)} %bitcast.211, f32[2,512,128]{2,1,0:T(8,128)} %param.10, f32[6,1,130]{2,1,0:T(1,128)S(1)} %collective-permute-done.14, ...), kind=kLoop, calls=%fused_computation.52 | loop fusion | flops 1323540 | bytes 2133609 | tf_op jit(solution)/shard_map/stack | solution.py:154
  124.7 30.8 %all-gather.2.cloned.1.call-done = bf16[2,64,64,128]{3,1,0,2:T(8,128)(2,1)} async-done(((bf16[2,64,4,128]{3,1,0,2:T(8,128)(2,1)}), bf16[2,64,64,128]{3,1,0,2:T(8,128)(2,1)}) %all-gather.2.cloned.1.call-update) | async-done | bytes 2097168 | tf_op jit(solution)/shard_map/all_gather | solution.py:117
  155.5 3.1 %gather_fusion.1 = bf16[12,2,64,128]{3,2,1,0:T(8,128)(2,1)} fusion(bf16[2,64,64,128]{3,1,0,2:T(8,128)(2,1)} %all-gather.2.cloned.1.call-done, s32[1024]{0:T(1024)} %pad_clamp_fusion), kind=kCustom, calls=%fused_computation.1 | custom fusion | bytes 786480 | tf_op jit(solution)/shard_map/jit(_take)/gather | solution.py:118
  158.5 1.5 fusion.25
  160.1 2.7 %collective-permute-start.8 = (bf16[64,2,2,128]{3,0,1,2:T(8,128)(2,1)S(1)}, bf16[64,2,2,128]{3,0,1,2:T(8,128)(2,1)S(1)}, u32[]{:S(2)}, u32[]{:S(2)}) collective-permute-start(bf16[64,2,2,128]{3,0,1,2:T(8,128)(2,1)S(1)} %fusion.25), channel_id=1, source_target_pairs={{0,64},{16,80},{32,96},{48,112},{64,0},{80,16},{96,32},{112,48},{1... | collective-permute-start | bytes 196616 | tf_op jit(solution)/shard_map/ppermute | solution.py:47
  162.7 1.9 fusion.30
  165.0 1.6 pad_maximum_fusion
  166.7 2.0 %collective-permute-done.9 = bf16[2,64,2,2,128]{4,1,2,3,0:T(8,128)(2,1)S(1)} collective-permute-done((bf16[2,64,2,2,128]{4,1,2,3,0:T(8,128)(2,1)S(1)}, bf16[2,64,2,2,128]{4,1,2,3,0:T(8,128)(2,1)S(1)}, u32[]{:S(2)}, u32[]{:S(2)}) %collective-permute-start.9) | collective-permute-done | bytes 131104 | tf_op jit(solution)/shard_map/ppermute | solution.py:47
  168.8 1.2 collective-permute-start.10
  170.5 3.6 %collective-permute-done.10 = bf16[2,2,64,2,2,128]{5,2,3,4,1,0:T(8,128)(2,1)S(1)} collective-permute-done((bf16[2,2,64,2,2,128]{5,2,3,4,1,0:T(8,128)(2,1)S(1)}, bf16[2,2,64,2,2,128]{5,2,3,4,1,0:T(8,128)(2,1)S(1)}, u32[]{:S(2)}, u32[]{:S(2)}) %collective-permute-start.10) | collective-permute-done | bytes 262176 | tf_op jit(solution)/shard_map/ppermute | solution.py:47
  174.2 4.6 %collective-permute-start.11 = (bf16[2,2,2,64,2,2,128]{6,3,4,5,1,0,2:T(8,128)(2,1)S(1)}, bf16[2,2,2,64,2,2,128]{6,3,4,5,1,0,2:T(8,128)(2,1)S(1)}, u32[]{:S(2)}, u32[]{:S(2)}) collective-permute-start(bf16[2,2,2,64,2,2,128]{6,3,4,5,1,0,2:T(8,128)(2,1)S(1)} %pad_maximum_fusion.19), channel_id=1, source_target_pairs={{0,16},{16,0},{32,48},{48,32},{64,80},{80,64},{96,112},{112,96},{1... | collective-permute-start | bytes 1572872 | tf_op jit(solution)/shard_map/ppermute | solution.py:47
  179.1 1.3 slice.128
  180.5 1.2 fusion.27
  182.9 1.5 copy-done.10
  184.4 1.3 fusion.42
  185.7 2.0 fusion.41
  187.7 1.3 fusion.7
  189.1 2.5 %fusion.8 = f32[2,256,128]{1,2,0:T(8,128)S(1)} fusion(f32[2,128,256]{2,1,0:T(8,128)} %fusion.41, bf16[1,1024,2,256]{3,2,1,0:T(2,128)(2,1)S(1)} %copy-done.8, f32[2,1024]{1,0:T(2,128)S(1)} %copy-done.19, f32[2,1024]{1,0:T(2,128)S(1)} %copy-done.20, bf16[2,2,1024,128]{3,2,1,0:T(8,128)(2,1)} %bitcast.230), kind=kOutput, calls=%fused_computation.28 | convolution fusion | flops 135856128 | bytes 2637824 | tf_op jit(solution)/shard_map/pjh,jpu->jhu/dot_general | solution.py:136
  191.8 2.7 %fusion.47 = f32[2,512,128]{2,1,0:T(8,128)} fusion(f32[2,512,128]{2,1,0:T(8,128)S(1)} %copy-done.5, f32[2,513,129]{2,1,0:T(8,128)} %get-tuple-element.21, f32[2,513,129]{2,1,0:T(8,128)S(1)} %get-tuple-element.20, f32[1,512,128]{2,1,0:T(8,128)S(1)} %bitcast.226, f32[1,512,128]{2,1,0:T(8,128)S(1)} %bitcast.225), kind=kLoop, calls=%fused_computation.79 | loop fusion | flops 917504 | bytes 3670016 | tf_op jit(solution)/shard_map/sub | solution.py:166
  (121 shorter events, 16.6 us)
Async XLA Ops:
  7.2 78.9 %copy-start = (bf16[8,128,128]{2,1,0:T(8,128)(2,1)S(1)}, bf16[8,128,128]{2,1,0:T(8,128)(2,1)}, u32[]{:S(2)}) copy-start(bf16[8,128,128]{2,1,0:T(8,128)(2,1)} %param.16) | copy-start | bytes 786436
  7.2 148.3 %all-gather.2.cloned.1.call-start = ((), (), s32[]{:S(2)}) async-start(), calls=%async_computation | async-start | bytes 2228224 | tf_op jit(solution)/shard_map/all_gather | solution.py:117
  7.2 2.8 %copy-start.3 = (f32[2,512,128]{2,1,0:T(8,128)S(1)}, f32[2,512,128]{2,1,0:T(8,128)}, u32[]{:S(2)}) copy-start(f32[2,512,128]{2,1,0:T(8,128)} %param.10) | copy-start | bytes 1572868
  10.0 1.0 copy-start.9
  10.0 3.5 %copy-start.7 = (bf16[1,1024,2,256]{3,2,1,0:T(2,128)(2,1)}, bf16[1,1024,2,256]{3,2,1,0:T(2,128)(2,1)S(1)}, u32[]{:S(2)}) copy-start(bf16[1,1024,2,256]{3,2,1,0:T(2,128)(2,1)S(1)} %get-tuple-element.26) | copy-start | bytes 3145732
  18.5 5.7 %collective-permute-start = (f32[2,2,2,2,64,2,128]{6,4,5,3,2,1,0:T(8,128)}, f32[2,2,2,2,64,2,128]{6,4,5,3,2,1,0:T(8,128)S(1)}, u32[]{:S(2)}, u32[]{:S(2)}) collective-permute-start(f32[2,2,2,2,64,2,128]{6,4,5,3,2,1,0:T(8,128)} %bitcast.206), channel_id=1, source_target_pairs={{0,16},{16,0},{32,48},{48,32},{64,80},{80,64},{96,112},{112,96},{1... | collective-permute-start | bytes 3145736 | tf_op jit(solution)/shard_map/ppermute | solution.py:36
  24.2 1.0 copy-start.11
  26.6 13.2 %collective-permute-start.1 = (f32[2,2,2,64,2,128]{5,3,4,2,1,0:T(8,128)S(1)}, f32[2,2,2,64,2,128]{5,3,4,2,1,0:T(8,128)S(1)}, u32[]{:S(2)}, u32[]{:S(2)}) collective-permute-start(f32[2,2,2,64,2,128]{5,3,4,2,1,0:T(8,128)S(1)} %dynamic-slice_bitcast_fusion), channel_id=1, source_target_pairs={{0,128},{16,144},{32,160},{48,176},{64,192},{80,208},{96,224},{112... | collective-permute-start | bytes 1572872 | tf_op jit(solution)/shard_map/ppermute | solution.py:36
  40.0 6.7 %collective-permute-start.2 = (f32[2,2,64,2,128]{4,2,3,1,0:T(8,128)S(1)}, f32[2,2,64,2,128]{4,2,3,1,0:T(8,128)S(1)}, u32[]{:S(2)}, u32[]{:S(2)}) collective-permute-start(f32[2,2,64,2,128]{4,2,3,1,0:T(8,128)S(1)} %dynamic-slice_bitcast_fusion.1), channel_id=1, source_target_pairs={{0,32},{16,48},{32,0},{48,16},{64,96},{80,112},{96,64},{112,80},{1... | collective-permute-start | bytes 786440 | tf_op jit(solution)/shard_map/ppermute | solution.py:36
  46.7 22.9 %copy-start.16 = (s32[32,1,6]{0,1,2:T(1,128)S(1)}, s32[32,1,6]{0,1,2:T(1,128)}, u32[]{:S(2)}) copy-start(s32[32,1,6]{0,1,2:T(1,128)} %param.17) | copy-start | bytes 2308
  46.7 22.9 %copy-start.17 = (s32[32,1,6]{0,1,2:T(1,128)S(1)}, s32[32,1,6]{0,1,2:T(1,128)}, u32[]{:S(2)}) copy-start(s32[32,1,6]{0,1,2:T(1,128)} %param.18) | copy-start | bytes 2308
  46.8 5.4 %collective-permute-start.3 = (f32[2,64,2,128]{3,1,0,2:T(8,128)S(1)}, f32[2,64,2,128]{3,1,0,2:T(8,128)S(1)}, u32[]{:S(2)}, u32[]{:S(2)}) collective-permute-start(f32[2,64,2,128]{3,1,0,2:T(8,128)S(1)} %bitcast.233), channel_id=1, source_target_pairs={{0,64},{16,80},{32,96},{48,112},{64,0},{80,16},{96,32},{112,48},{1... | collective-permute-start | bytes 393224 | tf_op jit(solution)/shard_map/ppermute | solution.py:36
  52.2 7.2 %collective-permute-start.4 = (bf16[2,64,2,128]{3,1,2,0:T(8,128)(2,1)S(1)}, bf16[2,64,2,128]{3,1,2,0:T(8,128)(2,1)S(1)}, u32[]{:S(2)}, u32[]{:S(2)}) collective-permute-start(bf16[2,64,2,128]{3,1,2,0:T(8,128)(2,1)S(1)} %fusion.53), channel_id=1, source_target_pairs={{0,2},{1,3},{2,0},{3,1},{4,6},{5,7},{6,4},{7,5},{8,10},{9,11},{10,... | collective-permute-start | bytes 196616 | tf_op jit(solution)/shard_map/ppermute | solution.py:47
  59.4 7.1 %collective-permute-start.5 = (bf16[2,2,64,2,128]{4,2,3,1,0:T(8,128)(2,1)S(1)}, bf16[2,2,64,2,128]{4,2,3,1,0:T(8,128)(2,1)S(1)}, u32[]{:S(2)}, u32[]{:S(2)}) collective-permute-start(bf16[2,2,64,2,128]{4,2,3,1,0:T(8,128)(2,1)S(1)} %pad_maximum_fusion.22), channel_id=1, source_target_pairs={{0,1},{1,0},{2,3},{3,2},{4,5},{5,4},{6,7},{7,6},{8,9},{9,8},{10,11... | collective-permute-start | bytes 393224 | tf_op jit(solution)/shard_map/ppermute | solution.py:47
  62.0 13.2 %copy-start.23 = (s32[64]{0:T(128)S(1)}, s32[64]{0:T(128)}, u32[]{:S(2)}) copy-start(s32[64]{0:T(128)} %param.19) | copy-start | bytes 772
  66.6 6.8 %collective-permute-start.6 = (bf16[2,2,2,64,2,128]{5,3,4,2,1,0:T(8,128)(2,1)S(1)}, bf16[2,2,2,64,2,128]{5,3,4,2,1,0:T(8,128)(2,1)S(1)}, u32[]{:S(2)}, u32[]{:S(2)}) collective-permute-start(bf16[2,2,2,64,2,128]{5,3,4,2,1,0:T(8,128)(2,1)S(1)} %pad_maximum_fusion.20), channel_id=1, source_target_pairs={{0,8},{1,9},{2,10},{3,11},{4,12},{5,13},{6,14},{7,15},{8,0},{9,1},... | collective-permute-start | bytes 786440 | tf_op jit(solution)/shard_map/ppermute | solution.py:47
  73.5 11.5 %collective-permute-start.7 = (bf16[2,2,2,2,64,2,128]{6,4,5,3,2,1,0:T(8,128)(2,1)S(1)}, bf16[2,2,2,2,64,2,128]{6,4,5,3,2,1,0:T(8,128)(2,1)S(1)}, u32[]{:S(2)}, u32[]{:S(2)}) collective-permute-start(bf16[2,2,2,2,64,2,128]{6,4,5,3,2,1,0:T(8,128)(2,1)S(1)} %pad_maximum_fusion.18), channel_id=1, source_target_pairs={{0,4},{1,5},{2,6},{3,7},{4,0},{5,1},{6,2},{7,3},{8,12},{9,13},{10,... | collective-permute-start | bytes 1572872 | tf_op jit(solution)/shard_map/ppermute | solution.py:47
  85.2 1.0 copy-start.14
  85.2 1.0 copy-start.15
  86.2 2.4 %copy-start.1 = (f32[2,2,512,128]{3,2,1,0:T(8,128)S(1)}, f32[2,2,512,128]{3,2,1,0:T(8,128)}, u32[]{:S(2)}) copy-start(f32[2,2,512,128]{3,2,1,0:T(8,128)} %param.11) | copy-start | bytes 3145732
  92.1 15.1 %collective-permute-start.12 = (f32[6,512,1]{1,2,0:T(1,128)S(1)}, f32[6,512,1]{1,2,0:T(1,128)S(1)}, u32[]{:S(2)}, u32[]{:S(2)}) collective-permute-start(f32[6,512,1]{1,2,0:T(1,128)S(1)} %copy.147), channel_id=1, source_target_pairs={{0,16},{16,32},{32,48},{48,64},{64,80},{80,96},{96,112},{112,128},... | collective-permute-start | bytes 36872 | tf_op jit(solution)/shard_map/ppermute | solution.py:16
  101.8 5.9 %collective-permute-start.13 = (f32[6,512,1]{1,2,0:T(1,128)}, f32[6,512,1]{1,2,0:T(1,128)}, u32[]{:S(2)}, u32[]{:S(2)}) collective-permute-start(f32[6,512,1]{1,2,0:T(1,128)} %copy.148), channel_id=1, source_target_pairs={{16,0},{32,16},{48,32},{64,48},{80,64},{96,80},{112,96},{128,112},... | collective-permute-start | bytes 36872 | tf_op jit(solution)/shard_map/ppermute | solution.py:19
  108.9 5.9 %copy-start.22 = (s32[12]{0:T(128)S(1)}, s32[12]{0:T(128)}, u32[]{:S(2)}) copy-start(s32[12]{0:T(128)} %reshape.187) | copy-start | bytes 148
  108.9 12.6 %copy-start.18 = (pred[513]{0:T(1024)(128)(4,1)S(1)}, pred[513]{0:T(1024)(128)(4,1)}, u32[]{:S(2)}) copy-start(pred[513]{0:T(1024)(128)(4,1)} %get-tuple-element.61) | copy-start | bytes 1543
  110.4 6.5 %collective-permute-start.14 = (f32[6,1,130]{2,1,0:T(1,128)}, f32[6,1,130]{2,1,0:T(1,128)S(1)}, u32[]{:S(2)}, u32[]{:S(2)}) collective-permute-start(f32[6,1,130]{2,1,0:T(1,128)} %get-tuple-element.19), channel_id=1, source_target_pairs={{0,1},{1,2},{2,3},{3,4},{4,5},{5,6},{6,7},{7,8},{8,9},{9,10},{10,1... | collective-permute-start | bytes 9368 | tf_op jit(solution)/shard_map/ppermute | solution.py:16
  113.5 8.1 %collective-permute-start.15 = (f32[6,1,130]{2,1,0:T(1,128)}, f32[6,1,130]{2,1,0:T(1,128)}, u32[]{:S(2)}, u32[]{:S(2)}) collective-permute-start(f32[6,1,130]{2,1,0:T(1,128)} %get-tuple-element.18), channel_id=1, source_target_pairs={{1,0},{2,1},{3,2},{4,3},{5,4},{6,5},{7,6},{8,7},{9,8},{10,9},{11,1... | collective-permute-start | bytes 9368 | tf_op jit(solution)/shard_map/ppermute | solution.py:19
  158.5 4.2 %copy-start.2 = (f32[2,2,512,128]{3,2,1,0:T(8,128)S(1)}, f32[2,2,512,128]{3,2,1,0:T(8,128)}, u32[]{:S(2)}) copy-start(f32[2,2,512,128]{3,2,1,0:T(8,128)} %param.11) | copy-start | bytes 3145732
  160.1 4.7 %collective-permute-start.8 = (bf16[64,2,2,128]{3,0,1,2:T(8,128)(2,1)S(1)}, bf16[64,2,2,128]{3,0,1,2:T(8,128)(2,1)S(1)}, u32[]{:S(2)}, u32[]{:S(2)}) collective-permute-start(bf16[64,2,2,128]{3,0,1,2:T(8,128)(2,1)S(1)} %fusion.25), channel_id=1, source_target_pairs={{0,64},{16,80},{32,96},{48,112},{64,0},{80,16},{96,32},{112,48},{1... | collective-permute-start | bytes 196616 | tf_op jit(solution)/shard_map/ppermute | solution.py:47
  162.7 2.3 %copy-start.4 = (f32[2,512,128]{2,1,0:T(8,128)S(1)}, f32[2,512,128]{2,1,0:T(8,128)}, u32[]{:S(2)}) copy-start(f32[2,512,128]{2,1,0:T(8,128)} %param.10) | copy-start | bytes 1572868
  164.8 3.9 %collective-permute-start.9 = (bf16[2,64,2,2,128]{4,1,2,3,0:T(8,128)(2,1)S(1)}, bf16[2,64,2,2,128]{4,1,2,3,0:T(8,128)(2,1)S(1)}, u32[]{:S(2)}, u32[]{:S(2)}) collective-permute-start(bf16[2,64,2,2,128]{4,1,2,3,0:T(8,128)(2,1)S(1)} %pad_maximum_fusion.23), channel_id=1, source_target_pairs={{0,128},{16,144},{32,160},{48,176},{64,192},{80,208},{96,224},{112... | collective-permute-start | bytes 393224 | tf_op jit(solution)/shard_map/ppermute | solution.py:47
  165.0 4.9 %copy-start.6 = (f32[1,2,513,129]{3,2,1,0:T(8,128)S(1)}, f32[1,2,513,129]{3,2,1,0:T(8,128)}, u32[]{:S(2)}) copy-start(f32[1,2,513,129]{3,2,1,0:T(8,128)} %fusion.33) | copy-start | bytes 1588252
  168.8 5.3 %collective-permute-start.10 = (bf16[2,2,64,2,2,128]{5,2,3,4,1,0:T(8,128)(2,1)S(1)}, bf16[2,2,64,2,2,128]{5,2,3,4,1,0:T(8,128)(2,1)S(1)}, u32[]{:S(2)}, u32[]{:S(2)}) collective-permute-start(bf16[2,2,64,2,2,128]{5,2,3,4,1,0:T(8,128)(2,1)S(1)} %pad_maximum_fusion.21), channel_id=1, source_target_pairs={{0,32},{16,48},{32,0},{48,16},{64,96},{80,112},{96,64},{112,80},{1... | collective-permute-start | bytes 786440 | tf_op jit(solution)/shard_map/ppermute | solution.py:47
  174.2 8.4 %collective-permute-start.11 = (bf16[2,2,2,64,2,2,128]{6,3,4,5,1,0,2:T(8,128)(2,1)S(1)}, bf16[2,2,2,64,2,2,128]{6,3,4,5,1,0,2:T(8,128)(2,1)S(1)}, u32[]{:S(2)}, u32[]{:S(2)}) collective-permute-start(bf16[2,2,2,64,2,2,128]{6,3,4,5,1,0,2:T(8,128)(2,1)S(1)} %pad_maximum_fusion.19), channel_id=1, source_target_pairs={{0,16},{16,0},{32,48},{48,32},{64,80},{80,64},{96,112},{112,96},{1... | collective-permute-start | bytes 1572872 | tf_op jit(solution)/shard_map/ppermute | solution.py:47
  179.1 1.3 copy-start.21
  180.5 1.2 copy-start.13
  182.8 1.6 copy-start.10
  182.8 1.6 copy-start.19
  182.8 1.6 copy-start.20
  182.9 4.8 %copy-start.12 = (bf16[2,2,2,2,64,2,2,128]{7,4,3,2,1,0,6,5:T(8,128)(2,1)}, bf16[2,2,2,2,64,2,2,128]{7,4,3,2,1,0,6,5:T(8,128)(2,1)S(1)}, u32[]{:S(2)}) copy-start(bf16[2,2,2,2,64,2,2,128]{7,4,3,2,1,0,6,5:T(8,128)(2,1)S(1)} %copy.140) | copy-start | bytes 3145732
  185.7 2.0 copy-start.8
  189.1 2.7 %copy-start.5 = (f32[2,512,128]{2,1,0:T(8,128)S(1)}, f32[2,512,128]{2,1,0:T(8,128)}, u32[]{:S(2)}) copy-start(f32[2,512,128]{2,1,0:T(8,128)} %param.10) | copy-start | bytes 1572868
Sparse Core Ops, SparseCore 0:
  88.6 66.7 all-gather.1

commit v7 on v3

--- a/solution.py
+++ b/solution.py
@@ -92,6 +92,9 @@
     parts = jnp.stack([real_part, imag_part], axis=0).reshape(2, az_count, -1, tiles_dev, columns)
     summed = halving_sum(jnp.moveaxis(parts, 1, 0), "az", (1, 8, 2, 4))
     projection_b = jnp.transpose(summed, (2, 1, 0, 3)).astype(jnp.bfloat16)
+    stacked = jnp.concatenate([image, tv_dual.reshape(4, strip_rows, columns)], axis=0)
+    padded = padded_2(stacked, (("az", 2), ("tile", 1)), 1)
+    padded, projection_b = lax.optimization_barrier((padded, projection_b))
     all_proj = doubling_gather(projection_b, "tile", (2, 1, 8, 4))
     all_proj = all_proj.reshape(-1, *all_proj.shape[2:])
     phase_ids = jnp.arange(kernels.shape[0], dtype=jnp.int32)
@@ -139,8 +142,6 @@
     )
     adjoint = jnp.stack([grad_re, grad_im])
     adjoint = adjoint.reshape(2, strip_rows, columns)
-    stacked = jnp.concatenate([image, tv_dual.reshape(4, strip_rows, columns)], axis=0)
-    padded = padded_2(stacked, (("az", 2), ("tile", 1)), 1)
     image_pad = padded[:2]
     dual_pad = padded[2:].reshape(2, 2, strip_rows + 2, columns + 2)
     total_rows = tile_count * strip_rows

time: 193 us -> 222 us (1.15)
  waiting for transfers between devices: 78.2 us -> 91.7 us
  starting transfers between devices: 51.5 us -> 62.7 us
    ppermute x12, waiting for transfers between devices: 48.6 us -> 71.3 us  [doubling_gather(): got = lax.ppermute(block, axis, pairs)]
    ppermute x12, starting transfers between devices: 28.5 us -> 45.3 us  [doubling_gather(): got = lax.ppermute(block, axis, pairs)]
    ppermute x4, waiting for transfers between devices: 25.8 us -> 15.8 us  [halving_sum(): blocks = keep + lax.ppermute(send, axis, pairs)]
    ppermute x2, starting transfers between devices: 14.7 us -> 8.13 us  [padded_2(): lax.ppermute(lax.slice_in_dim(block, block.shape[dim] - width, None, axis...]
    another operation x24, other arithmetic: 3.52 us -> 9.97 us  [doubling_gather(): block = jnp.stack([low, high], axis=place)]
    another operation x2 -> x1, other arithmetic: 5.12 us -> 0.41 us  [on_device(): jnp.stack([grad_rows, grad_cols])]
    unnamed x68 -> x71, local copies, waits for them, and re-layouts: 5.42 us -> 6.18 us
  transfers between devices with their start and end apart: 20 -> 20, of which waited for: 15 -> 15; matrix products, arithmetic and copies ran while one was open for 13% -> 8% of each run, Pallas kernels for 0% -> 0%
where the time goes in v7:
time: 222 us; the launch traced here: 220 us
  waiting for transfers between devices  91.7 us (41%)
  starting transfers between devices  62.7 us (28%)
  local copies, waits for them, and re-layouts  26.1 us (12%)
  other arithmetic  24.5 us (11%)
  matrix products  13.9 us (6%)
    ppermute x12, waiting for transfers between devices, doubling_gather(): got = lax.ppermute(block, axis, pairs)  71.3 us
    ppermute x12, starting transfers between devices, doubling_gather(): got = lax.ppermute(block, axis, pairs)  45.3 us
    ppermute x4, waiting for transfers between devices, halving_sum(): blocks = keep + lax.ppermute(send, axis, pairs)  15.8 us
    another operation x24, other arithmetic, doubling_gather(): block = jnp.stack([low, high], axis=place)  9.97 us
    ppermute x2, starting transfers between devices, padded_2(): lax.ppermute(lax.slice_in_dim(block, block.shape[dim] - width, None, axis...  8.13 us
    unnamed x71, local copies, waits for them, and re-layouts  6.18 us
    ppermute x4, starting transfers between devices, halving_sum(): blocks = keep + lax.ppermute(send, axis, pairs)  6.07 us
    ppermute x2, waiting for transfers between devices, padded_2(): lax.ppermute(lax.slice_in_dim(block, 0, width, axis=dim), axis, backward)  4.53 us
  transfers between devices with their start and end apart: 20, of which 15 were waited for; matrix products, arithmetic and copies ran while one was open for 8% of the time, Pallas kernels for 0%

profile of v7, /device:TPU:1, one launch (start us, length us, event | category | flops | bytes accessed | tf_op | source)
XLA Modules:
  0.0 220.5 jit_solution(15022365610935344980)
XLA Ops:
  0.7 2.7 %fusion.60 = (bf16[1,1024,2,256]{3,2,1,0:T(2,128)(2,1)S(1)}, bf16[1,1024,2,256]{3,2,1,0:T(2,128)(2,1)S(1)}) fusion(bf16[2,1024,2,256]{3,2,1,0:T(2,128)(2,1)} %param.14), kind=kLoop, calls=%fused_computation.154 | loop fusion | bytes 4194304 | tf_op jit(solution)/shard_map/slice | solution.py:75
  6.0 1.6 multiply_subtract_fusion
  7.9 1.6 copy.133
  11.0 3.2 %collective-permute-start.4 = (f32[2,2,2,2,64,2,128]{6,4,5,3,2,1,0:T(8,128)}, f32[2,2,2,2,64,2,128]{6,4,5,3,2,1,0:T(8,128)S(1)}, u32[]{:S(2)}, u32[]{:S(2)}) collective-permute-start(f32[2,2,2,2,64,2,128]{6,4,5,3,2,1,0:T(8,128)} %bitcast.231), channel_id=1, source_target_pairs={{0,16},{16,0},{32,48},{48,32},{64,80},{80,64},{96,112},{112,96},{1... | collective-permute-start | bytes 3145736 | tf_op jit(solution)/shard_map/ppermute | solution.py:36
  14.2 2.5 %collective-permute-done.4 = f32[2,2,2,2,64,2,128]{6,4,5,3,2,1,0:T(8,128)S(1)} collective-permute-done((f32[2,2,2,2,64,2,128]{6,4,5,3,2,1,0:T(8,128)}, f32[2,2,2,2,64,2,128]{6,4,5,3,2,1,0:T(8,128)S(1)}, u32[]{:S(2)}, u32[]{:S(2)}) %collective-permute-start.4) | collective-permute-done | bytes 1048608 | tf_op jit(solution)/shard_map/ppermute | solution.py:36
  17.7 1.4 bitcast_add_fusion
  19.9 13.3 %collective-permute-done.5 = f32[2,2,2,64,2,128]{5,3,4,2,1,0:T(8,128)S(1)} collective-permute-done((f32[2,2,2,64,2,128]{5,3,4,2,1,0:T(8,128)}, f32[2,2,2,64,2,128]{5,3,4,2,1,0:T(8,128)S(1)}, u32[]{:S(2)}, u32[]{:S(2)}) %collective-permute-start.5) | collective-permute-done | bytes 524320 | tf_op jit(solution)/shard_map/ppermute | solution.py:36
  34.2 1.7 slice_maximum_fusion
  35.9 1.9 copy.122
  37.8 4.7 %collective-permute-start = (f32[6,512,1]{1,2,0:T(1,128)S(1)}, f32[6,512,1]{1,2,0:T(1,128)S(1)}, u32[]{:S(2)}, u32[]{:S(2)}) collective-permute-start(f32[6,512,1]{1,2,0:T(1,128)S(1)} %copy.122), channel_id=1, source_target_pairs={{0,16},{16,32},{32,48},{48,64},{64,80},{80,96},{96,112},{112,128},... | collective-permute-start | bytes 36872 | tf_op jit(solution)/shard_map/ppermute | solution.py:16
  42.9 1.9 collective-permute-start.1
  45.4 2.5 %collective-permute-done.1 = f32[6,512,1]{1,2,0:T(1,128)S(1)} collective-permute-done((f32[6,512,1]{1,2,0:T(1,128)S(1)}, f32[6,512,1]{1,2,0:T(1,128)S(1)}, u32[]{:S(2)}, u32[]{:S(2)}) %collective-permute-start.1) | collective-permute-done | bytes 12320 | tf_op jit(solution)/shard_map/ppermute | solution.py:19
  49.7 3.5 %collective-permute-start.2 = (f32[6,1,130]{2,1,0:T(1,128)S(1)}, f32[6,1,130]{2,1,0:T(1,128)S(1)}, u32[]{:S(2)}, u32[]{:S(2)}) collective-permute-start(f32[6,1,130]{2,1,0:T(1,128)S(1)} %get-tuple-element.22), channel_id=1, source_target_pairs={{0,1},{1,2},{2,3},{3,4},{4,5},{5,6},{6,7},{7,8},{8,9},{9,10},{10,1... | collective-permute-start | bytes 9368 | tf_op jit(solution)/shard_map/ppermute | solution.py:16
  53.2 1.3 collective-permute-start.3
  55.6 2.8 %collective-permute-start.7 = (f32[2,64,2,128]{3,1,0,2:T(8,128)S(1)}, f32[2,64,2,128]{3,1,0,2:T(8,128)S(1)}, u32[]{:S(2)}, u32[]{:S(2)}) collective-permute-start(f32[2,64,2,128]{3,1,0,2:T(8,128)S(1)} %bitcast.257), channel_id=1, source_target_pairs={{0,64},{16,80},{32,96},{48,112},{64,0},{80,16},{96,32},{112,48},{1... | collective-permute-start | bytes 393224 | tf_op jit(solution)/shard_map/ppermute | solution.py:36
  58.4 2.0 collective-permute-done.3
  60.4 2.7 %pad_maximum_fusion = f32[6,514,130]{2,1,0:T(8,128)S(1)} fusion(f32[6,1,130]{2,1,0:T(1,128)S(1)} %collective-permute-done.3, f32[6,512,1]{2,1,0:T(8,128)} %copy-done.4, f32[4,512,128]{2,1,0:T(8,128)S(1)} %bitcast.239, f32[2,512,128]{2,1,0:T(8,128)S(1)} %copy-done.6, f32[6,512,1]{2,1,0:T(8,128)S(1)} %copy-done.3, f32[6,1,130]{2,1,0:T(1,128)S(1)} %collective-permute-done.2), kind=kLoop, calls=%fused_computation.2 | loop fusion | flops 2004600 | bytes 3207360 | tf_op jit(solution)/shard_map/concatenate | solution.py:20
  63.2 7.4 %collective-permute-start.8 = (bf16[2,64,2,128]{3,1,2,0:T(8,128)(2,1)S(1)}, bf16[2,64,2,128]{3,1,2,0:T(8,128)(2,1)}, u32[]{:S(2)}, u32[]{:S(2)}) collective-permute-start(bf16[2,64,2,128]{3,1,2,0:T(8,128)(2,1)S(1)} %fusion.48), channel_id=1, source_target_pairs={{0,2},{1,3},{2,0},{3,1},{4,6},{5,7},{6,4},{7,5},{8,10},{9,11},{10,... | collective-permute-start | bytes 196616 | tf_op jit(solution)/shard_map/ppermute | solution.py:47
  70.6 2.1 collective-permute-done.8
  74.9 3.6 %collective-permute-start.9 = (bf16[2,2,64,2,128]{4,2,3,1,0:T(8,128)(2,1)}, bf16[2,2,64,2,128]{4,2,3,1,0:T(8,128)(2,1)}, u32[]{:S(2)}, u32[]{:S(2)}) collective-permute-start(bf16[2,2,64,2,128]{4,2,3,1,0:T(8,128)(2,1)} %pad_maximum_fusion.13), channel_id=1, source_target_pairs={{0,1},{1,0},{2,3},{3,2},{4,5},{5,4},{6,7},{7,6},{8,9},{9,8},{10,11... | collective-permute-start | bytes 393224 | tf_op jit(solution)/shard_map/ppermute | solution.py:47
  78.5 3.4 %collective-permute-done.9 = bf16[2,2,64,2,128]{4,2,3,1,0:T(8,128)(2,1)} collective-permute-done((bf16[2,2,64,2,128]{4,2,3,1,0:T(8,128)(2,1)}, bf16[2,2,64,2,128]{4,2,3,1,0:T(8,128)(2,1)}, u32[]{:S(2)}, u32[]{:S(2)}) %collective-permute-start.9) | collective-permute-done | bytes 131104 | tf_op jit(solution)/shard_map/ppermute | solution.py:47
  84.3 2.5 %collective-permute-start.10 = (bf16[2,2,2,64,2,128]{5,3,4,2,1,0:T(8,128)(2,1)}, bf16[2,2,2,64,2,128]{5,3,4,2,1,0:T(8,128)(2,1)}, u32[]{:S(2)}, u32[]{:S(2)}) collective-permute-start(bf16[2,2,2,64,2,128]{5,3,4,2,1,0:T(8,128)(2,1)} %pad_maximum_fusion.10), channel_id=1, source_target_pairs={{0,8},{1,9},{2,10},{3,11},{4,12},{5,13},{6,14},{7,15},{8,0},{9,1},... | collective-permute-start | bytes 786440 | tf_op jit(solution)/shard_map/ppermute | solution.py:47
  86.8 4.5 %collective-permute-done.10 = bf16[2,2,2,64,2,128]{5,3,4,2,1,0:T(8,128)(2,1)} collective-permute-done((bf16[2,2,2,64,2,128]{5,3,4,2,1,0:T(8,128)(2,1)}, bf16[2,2,2,64,2,128]{5,3,4,2,1,0:T(8,128)(2,1)}, u32[]{:S(2)}, u32[]{:S(2)}) %collective-permute-start.10) | collective-permute-done | bytes 262176 | tf_op jit(solution)/shard_map/ppermute | solution.py:47
  92.4 2.2 %collective-permute-start.11 = (bf16[2,2,2,2,64,2,128]{6,4,5,3,2,1,0:T(8,128)(2,1)S(1)}, bf16[2,2,2,2,64,2,128]{6,4,5,3,2,1,0:T(8,128)(2,1)S(1)}, u32[]{:S(2)}, u32[]{:S(2)}) collective-permute-start(bf16[2,2,2,2,64,2,128]{6,4,5,3,2,1,0:T(8,128)(2,1)S(1)} %pad_maximum_fusion.7), channel_id=1, source_target_pairs={{0,4},{1,5},{2,6},{3,7},{4,0},{5,1},{6,2},{7,3},{8,12},{9,13},{10,... | collective-permute-start | bytes 1572872 | tf_op jit(solution)/shard_map/ppermute | solution.py:47
  94.8 8.6 %collective-permute-done.11 = bf16[2,2,2,2,64,2,128]{6,4,5,3,2,1,0:T(8,128)(2,1)S(1)} collective-permute-done((bf16[2,2,2,2,64,2,128]{6,4,5,3,2,1,0:T(8,128)(2,1)S(1)}, bf16[2,2,2,2,64,2,128]{6,4,5,3,2,1,0:T(8,128)(2,1)S(1)}, u32[]{:S(2)}, u32[]{:S(2)}) %collective-permute-start.11) | collective-permute-done | bytes 524320 | tf_op jit(solution)/shard_map/ppermute | solution.py:47
  104.6 1.6 fusion.21
  106.2 3.3 %collective-permute-start.12 = (bf16[4,2,64,128]{3,2,1,0:T(8,128)(2,1)S(1)}, bf16[4,2,64,128]{3,2,1,0:T(8,128)(2,1)S(1)}, u32[]{:S(2)}, u32[]{:S(2)}) collective-permute-start(bf16[4,2,64,128]{3,2,1,0:T(8,128)(2,1)S(1)} %convert_bitcast_fusion), channel_id=1, source_target_pairs={{0,2},{1,3},{2,0},{3,1},{4,6},{5,7},{6,4},{7,5},{8,10},{9,11},{10,... | collective-permute-start | bytes 393224 | tf_op jit(solution)/shard_map/ppermute | solution.py:47
  109.5 4.6 %collective-permute-done.12 = bf16[4,2,64,128]{3,2,1,0:T(8,128)(2,1)S(1)} collective-permute-done((bf16[4,2,64,128]{3,2,1,0:T(8,128)(2,1)S(1)}, bf16[4,2,64,128]{3,2,1,0:T(8,128)(2,1)S(1)}, u32[]{:S(2)}, u32[]{:S(2)}) %collective-permute-start.12) | collective-permute-done | bytes 131104 | tf_op jit(solution)/shard_map/ppermute | solution.py:47
  114.1 3.6 %collective-permute-start.13 = (bf16[2,4,2,64,128]{4,3,2,1,0:T(8,128)(2,1)S(1)}, bf16[2,4,2,64,128]{4,3,2,1,0:T(8,128)(2,1)S(1)}, u32[]{:S(2)}, u32[]{:S(2)}) collective-permute-start(bf16[2,4,2,64,128]{4,3,2,1,0:T(8,128)(2,1)S(1)} %pad_maximum_fusion.11), channel_id=1, source_target_pairs={{0,1},{1,0},{2,3},{3,2},{4,5},{5,4},{6,7},{7,6},{8,9},{9,8},{10,11... | collective-permute-start | bytes 786440 | tf_op jit(solution)/shard_map/ppermute | solution.py:47
  117.7 9.8 %collective-permute-done.13 = bf16[2,4,2,64,128]{4,3,2,1,0:T(8,128)(2,1)S(1)} collective-permute-done((bf16[2,4,2,64,128]{4,3,2,1,0:T(8,128)(2,1)S(1)}, bf16[2,4,2,64,128]{4,3,2,1,0:T(8,128)(2,1)S(1)}, u32[]{:S(2)}, u32[]{:S(2)}) %collective-permute-start.13) | collective-permute-done | bytes 262176 | tf_op jit(solution)/shard_map/ppermute | solution.py:47
  129.1 12.5 %collective-permute-done.14 = bf16[2,2,4,2,64,128]{5,4,3,2,0,1:T(8,128)(2,1)} collective-permute-done((bf16[2,2,4,2,64,128]{5,4,3,2,0,1:T(8,128)(2,1)}, bf16[2,2,4,2,64,128]{5,4,3,2,0,1:T(8,128)(2,1)}, u32[]{:S(2)}, u32[]{:S(2)}) %collective-permute-start.14) | collective-permute-done | bytes 524320 | tf_op jit(solution)/shard_map/ppermute | solution.py:47
  145.8 1.4 gather_fusion
  147.2 18.8 %collective-permute-done.15 = bf16[2,2,2,4,2,64,128]{6,5,4,3,1,2,0:T(8,128)(2,1)} collective-permute-done((bf16[2,2,2,4,2,64,128]{6,5,4,3,1,2,0:T(8,128)(2,1)}, bf16[2,2,2,4,2,64,128]{6,5,4,3,1,2,0:T(8,128)(2,1)}, u32[]{:S(2)}, u32[]{:S(2)}) %collective-permute-start.15) | collective-permute-done | bytes 1048608 | tf_op jit(solution)/shard_map/ppermute | solution.py:47
  166.0 1.7 select_bitcast_fusion.3
  167.8 1.5 copy.144
  169.3 2.9 %gather_fusion.1 = bf16[12,2,64,128]{3,2,1,0:T(8,128)(2,1)} fusion(bf16[2,64,64,128]{3,1,0,2:T(8,128)(2,1)} %bitcast.244, s32[1024]{0:T(1024)S(1)} %pad_clamp_fusion), kind=kCustom, calls=%fused_computation.1 | custom fusion | bytes 786480 | tf_op jit(solution)/shard_map/jit(_take)/gather | solution.py:122
  172.3 1.4 fusion.25
  173.7 10.2 %collective-permute-start.16 = (bf16[64,2,2,128]{3,0,1,2:T(8,128)(2,1)S(1)}, bf16[64,2,2,128]{3,0,1,2:T(8,128)(2,1)S(1)}, u32[]{:S(2)}, u32[]{:S(2)}) collective-permute-start(bf16[64,2,2,128]{3,0,1,2:T(8,128)(2,1)S(1)} %fusion.25), channel_id=1, source_target_pairs={{0,64},{16,80},{32,96},{48,112},{64,0},{80,16},{96,32},{112,48},{1... | collective-permute-start | bytes 196616 | tf_op jit(solution)/shard_map/ppermute | solution.py:47
  186.4 3.1 %collective-permute-done.17 = bf16[2,64,2,2,128]{4,1,2,3,0:T(8,128)(2,1)S(1)} collective-permute-done((bf16[2,64,2,2,128]{4,1,2,3,0:T(8,128)(2,1)S(1)}, bf16[2,64,2,2,128]{4,1,2,3,0:T(8,128)(2,1)S(1)}, u32[]{:S(2)}, u32[]{:S(2)}) %collective-permute-start.17) | collective-permute-done | bytes 131104 | tf_op jit(solution)/shard_map/ppermute | solution.py:47
  189.6 5.3 %collective-permute-start.18 = (bf16[2,2,64,2,2,128]{5,2,3,4,1,0:T(8,128)(2,1)S(1)}, bf16[2,2,64,2,2,128]{5,2,3,4,1,0:T(8,128)(2,1)S(1)}, u32[]{:S(2)}, u32[]{:S(2)}) collective-permute-start(bf16[2,2,64,2,2,128]{5,2,3,4,1,0:T(8,128)(2,1)S(1)} %pad_maximum_fusion.12), channel_id=1, source_target_pairs={{0,32},{16,48},{32,0},{48,16},{64,96},{80,112},{96,64},{112,80},{1... | collective-permute-start | bytes 786440 | tf_op jit(solution)/shard_map/ppermute | solution.py:47
  195.4 3.2 %collective-permute-done.18 = bf16[2,2,64,2,2,128]{5,2,3,4,1,0:T(8,128)(2,1)S(1)} collective-permute-done((bf16[2,2,64,2,2,128]{5,2,3,4,1,0:T(8,128)(2,1)S(1)}, bf16[2,2,64,2,2,128]{5,2,3,4,1,0:T(8,128)(2,1)S(1)}, u32[]{:S(2)}, u32[]{:S(2)}) %collective-permute-start.18) | collective-permute-done | bytes 262176 | tf_op jit(solution)/shard_map/ppermute | solution.py:47
  198.7 6.4 %collective-permute-start.19 = (bf16[2,2,2,64,2,2,128]{6,3,4,5,1,0,2:T(8,128)(2,1)S(1)}, bf16[2,2,2,64,2,2,128]{6,3,4,5,1,0,2:T(8,128)(2,1)S(1)}, u32[]{:S(2)}, u32[]{:S(2)}) collective-permute-start(bf16[2,2,2,64,2,2,128]{6,3,4,5,1,0,2:T(8,128)(2,1)S(1)} %pad_maximum_fusion.9), channel_id=1, source_target_pairs={{0,16},{16,0},{32,48},{48,32},{64,80},{80,64},{96,112},{112,96},{1... | collective-permute-start | bytes 1572872 | tf_op jit(solution)/shard_map/ppermute | solution.py:47
  205.5 1.3 slice.125
  210.4 1.3 fusion.36
  211.7 2.0 fusion.35
  213.7 1.3 fusion.7
  215.1 2.5 %fusion.8 = f32[2,256,128]{1,2,0:T(8,128)S(1)} fusion(f32[2,128,256]{2,1,0:T(8,128)} %fusion.35, bf16[1,1024,2,256]{3,2,1,0:T(2,128)(2,1)S(1)} %copy-done.11, f32[2,1024]{1,0:T(2,128)S(1)} %get-tuple-element.68, f32[2,1024]{1,0:T(2,128)S(1)} %get-tuple-element.73, bf16[2,2,1024,128]{3,2,1,0:T(8,128)(2,1)} %bitcast.254), kind=kOutput, calls=%fused_computation.25 | convolution fusion | flops 135856128 | bytes 2637824 | tf_op jit(solution)/shard_map/pjh,jpu->jhu/dot_general | solution.py:140
  217.8 2.7 %fusion.41 = f32[2,512,128]{2,1,0:T(8,128)} fusion(f32[2,512,128]{2,1,0:T(8,128)S(1)} %copy-done.7, f32[2,513,129]{2,1,0:T(8,128)} %get-tuple-element.27, f32[2,513,129]{2,1,0:T(8,128)S(1)} %get-tuple-element.26, f32[1,512,128]{2,1,0:T(8,128)S(1)} %bitcast.250, f32[1,512,128]{2,1,0:T(8,128)S(1)} %bitcast.249), kind=kLoop, calls=%fused_computation.66 | loop fusion | flops 917504 | bytes 3670016 | tf_op jit(solution)/shard_map/sub | solution.py:168
  (156 shorter events, 31.2 us)
Async XLA Ops:
  0.6 103.8 %copy-start = (bf16[8,128,128]{2,1,0:T(8,128)(2,1)S(1)}, bf16[8,128,128]{2,1,0:T(8,128)(2,1)}, u32[]{:S(2)}) copy-start(bf16[8,128,128]{2,1,0:T(8,128)(2,1)} %param.16) | copy-start | bytes 786436
  0.7 2.8 %copy-start.5 = (f32[2,512,128]{2,1,0:T(8,128)S(1)}, f32[2,512,128]{2,1,0:T(8,128)}, u32[]{:S(2)}) copy-start(f32[2,512,128]{2,1,0:T(8,128)} %param.10) | copy-start | bytes 1572868
  3.4 1.1 copy-start.12
  3.5 2.5 %copy-start.10 = (bf16[1,1024,2,256]{3,2,1,0:T(2,128)(2,1)}, bf16[1,1024,2,256]{3,2,1,0:T(2,128)(2,1)S(1)}, u32[]{:S(2)}) copy-start(bf16[1,1024,2,256]{3,2,1,0:T(2,128)(2,1)S(1)} %get-tuple-element.34) | copy-start | bytes 3145732
  11.0 5.7 %collective-permute-start.4 = (f32[2,2,2,2,64,2,128]{6,4,5,3,2,1,0:T(8,128)}, f32[2,2,2,2,64,2,128]{6,4,5,3,2,1,0:T(8,128)S(1)}, u32[]{:S(2)}, u32[]{:S(2)}) collective-permute-start(f32[2,2,2,2,64,2,128]{6,4,5,3,2,1,0:T(8,128)} %bitcast.231), channel_id=1, source_target_pairs={{0,16},{16,0},{32,48},{48,32},{64,80},{80,64},{96,112},{112,96},{1... | collective-permute-start | bytes 3145736 | tf_op jit(solution)/shard_map/ppermute | solution.py:36
  16.7 1.0 copy-start.24
  19.0 15.2 %copy-start.8 = (f32[2,2,512,128]{3,2,1,0:T(8,128)S(1)}, f32[2,2,512,128]{3,2,1,0:T(8,128)}, u32[]{:S(2)}) copy-start(f32[2,2,512,128]{3,2,1,0:T(8,128)} %param.11) | copy-start | bytes 3145732
  19.9 13.3 %collective-permute-start.5 = (f32[2,2,2,64,2,128]{5,3,4,2,1,0:T(8,128)}, f32[2,2,2,64,2,128]{5,3,4,2,1,0:T(8,128)S(1)}, u32[]{:S(2)}, u32[]{:S(2)}) collective-permute-start(f32[2,2,2,64,2,128]{5,3,4,2,1,0:T(8,128)} %dynamic-slice_bitcast_fusion), channel_id=1, source_target_pairs={{0,128},{16,144},{32,160},{48,176},{64,192},{80,208},{96,224},{112... | collective-permute-start | bytes 1572872 | tf_op jit(solution)/shard_map/ppermute | solution.py:36
  34.1 20.3 %collective-permute-start.6 = (f32[2,2,64,2,128]{4,2,3,1,0:T(8,128)}, f32[2,2,64,2,128]{4,2,3,1,0:T(8,128)}, u32[]{:S(2)}, u32[]{:S(2)}) collective-permute-start(f32[2,2,64,2,128]{4,2,3,1,0:T(8,128)} %dynamic-slice_bitcast_fusion.1), channel_id=1, source_target_pairs={{0,32},{16,48},{32,0},{48,16},{64,96},{80,112},{96,64},{112,80},{1... | collective-permute-start | bytes 786440 | tf_op jit(solution)/shard_map/ppermute | solution.py:36
  37.8 7.1 %collective-permute-start = (f32[6,512,1]{1,2,0:T(1,128)S(1)}, f32[6,512,1]{1,2,0:T(1,128)S(1)}, u32[]{:S(2)}, u32[]{:S(2)}) collective-permute-start(f32[6,512,1]{1,2,0:T(1,128)S(1)} %copy.122), channel_id=1, source_target_pairs={{0,16},{16,32},{32,48},{48,64},{64,80},{80,96},{96,112},{112,128},... | collective-permute-start | bytes 36872 | tf_op jit(solution)/shard_map/ppermute | solution.py:16
  42.9 5.0 %collective-permute-start.1 = (f32[6,512,1]{1,2,0:T(1,128)S(1)}, f32[6,512,1]{1,2,0:T(1,128)S(1)}, u32[]{:S(2)}, u32[]{:S(2)}) collective-permute-start(f32[6,512,1]{1,2,0:T(1,128)S(1)} %copy.123), channel_id=1, source_target_pairs={{16,0},{32,16},{48,32},{64,48},{80,64},{96,80},{112,96},{128,112},... | collective-permute-start | bytes 36872 | tf_op jit(solution)/shard_map/ppermute | solution.py:19
  45.4 4.2 %copy-start.2 = (f32[6,512,1]{2,1,0:T(8,128)}, f32[6,512,1]{2,1,0:T(8,128)S(1)}, u32[]{:S(2)}) copy-start(f32[6,512,1]{2,1,0:T(8,128)S(1)} %copy.124) | copy-start | bytes 36868
  48.5 1.2 copy-start.4
  48.5 6.0 %copy-start.21 = (f32[2,2,2,64,2,128]{5,3,4,2,1,0:T(8,128)S(1)}, f32[2,2,2,64,2,128]{5,3,4,2,1,0:T(8,128)}, u32[]{:S(2)}) copy-start(f32[2,2,2,64,2,128]{5,3,4,2,1,0:T(8,128)} %copy-done.20) | copy-start | bytes 1572868
  48.5 11.9 %copy-start.6 = (f32[2,512,128]{2,1,0:T(8,128)S(1)}, f32[2,512,128]{2,1,0:T(8,128)}, u32[]{:S(2)}) copy-start(f32[2,512,128]{2,1,0:T(8,128)} %param.10) | copy-start | bytes 1572868
  48.5 11.9 %copy-start.9 = (f32[2,2,512,128]{3,2,1,0:T(8,128)S(1)}, f32[2,2,512,128]{3,2,1,0:T(8,128)}, u32[]{:S(2)}) copy-start(f32[2,2,512,128]{3,2,1,0:T(8,128)} %param.11) | copy-start | bytes 3145732
  49.7 10.7 %copy-start.3 = (f32[6,512,1]{2,1,0:T(8,128)S(1)}, f32[6,512,1]{2,1,0:T(8,128)}, u32[]{:S(2)}) copy-start(f32[6,512,1]{2,1,0:T(8,128)} %copy-done.2) | copy-start | bytes 36868
  49.7 8.7 %collective-permute-start.2 = (f32[6,1,130]{2,1,0:T(1,128)S(1)}, f32[6,1,130]{2,1,0:T(1,128)S(1)}, u32[]{:S(2)}, u32[]{:S(2)}) collective-permute-start(f32[6,1,130]{2,1,0:T(1,128)S(1)} %get-tuple-element.22), channel_id=1, source_target_pairs={{0,1},{1,2},{2,3},{3,4},{4,5},{5,6},{6,7},{7,8},{8,9},{9,10},{10,1... | collective-permute-start | bytes 9368 | tf_op jit(solution)/shard_map/ppermute | solution.py:16
  53.2 7.2 %collective-permute-start.3 = (f32[6,1,130]{2,1,0:T(1,128)S(1)}, f32[6,1,130]{2,1,0:T(1,128)S(1)}, u32[]{:S(2)}, u32[]{:S(2)}) collective-permute-start(f32[6,1,130]{2,1,0:T(1,128)S(1)} %get-tuple-element.23), channel_id=1, source_target_pairs={{1,0},{2,1},{3,2},{4,3},{5,4},{6,5},{7,6},{8,7},{9,8},{10,9},{11,1... | collective-permute-start | bytes 9368 | tf_op jit(solution)/shard_map/ppermute | solution.py:19
  55.5 31.3 %copy-start.31 = (s32[32,1,6]{0,1,2:T(1,128)S(1)}, s32[32,1,6]{0,1,2:T(1,128)}, u32[]{:S(2)}) copy-start(s32[32,1,6]{0,1,2:T(1,128)} %param.17) | copy-start | bytes 2308
  55.6 31.3 %copy-start.32 = (s32[32,1,6]{0,1,2:T(1,128)S(1)}, s32[32,1,6]{0,1,2:T(1,128)}, u32[]{:S(2)}) copy-start(s32[32,1,6]{0,1,2:T(1,128)} %param.18) | copy-start | bytes 2308
  55.6 7.6 %collective-permute-start.7 = (f32[2,64,2,128]{3,1,0,2:T(8,128)S(1)}, f32[2,64,2,128]{3,1,0,2:T(8,128)S(1)}, u32[]{:S(2)}, u32[]{:S(2)}) collective-permute-start(f32[2,64,2,128]{3,1,0,2:T(8,128)S(1)} %bitcast.257), channel_id=1, source_target_pairs={{0,64},{16,80},{32,96},{48,112},{64,0},{80,16},{96,32},{112,48},{1... | collective-permute-start | bytes 393224 | tf_op jit(solution)/shard_map/ppermute | solution.py:36
  63.2 31.6 %copy-start.33 = (s32[64]{0:T(128)S(1)}, s32[64]{0:T(128)}, u32[]{:S(2)}) copy-start(s32[64]{0:T(128)} %param.19) | copy-start | bytes 772
  63.2 7.4 %copy-start.29 = (bf16[2,64,2,128]{3,1,2,0:T(8,128)(2,1)}, bf16[2,64,2,128]{3,1,2,0:T(8,128)(2,1)S(1)}, u32[]{:S(2)}) copy-start(bf16[2,64,2,128]{3,1,2,0:T(8,128)(2,1)S(1)} %fusion.48) | copy-start | bytes 196612
  63.2 9.5 %collective-permute-start.8 = (bf16[2,64,2,128]{3,1,2,0:T(8,128)(2,1)S(1)}, bf16[2,64,2,128]{3,1,2,0:T(8,128)(2,1)}, u32[]{:S(2)}, u32[]{:S(2)}) collective-permute-start(bf16[2,64,2,128]{3,1,2,0:T(8,128)(2,1)S(1)} %fusion.48), channel_id=1, source_target_pairs={{0,2},{1,3},{2,0},{3,1},{4,6},{5,7},{6,4},{7,5},{8,10},{9,11},{10,... | collective-permute-start | bytes 196616 | tf_op jit(solution)/shard_map/ppermute | solution.py:47
  74.9 7.0 %collective-permute-start.9 = (bf16[2,2,64,2,128]{4,2,3,1,0:T(8,128)(2,1)}, bf16[2,2,64,2,128]{4,2,3,1,0:T(8,128)(2,1)}, u32[]{:S(2)}, u32[]{:S(2)}) collective-permute-start(bf16[2,2,64,2,128]{4,2,3,1,0:T(8,128)(2,1)} %pad_maximum_fusion.13), channel_id=1, source_target_pairs={{0,1},{1,0},{2,3},{3,2},{4,5},{5,4},{6,7},{7,6},{8,9},{9,8},{10,11... | collective-permute-start | bytes 393224 | tf_op jit(solution)/shard_map/ppermute | solution.py:47
  82.9 1.4 copy-start.23
  84.3 7.0 %collective-permute-start.10 = (bf16[2,2,2,64,2,128]{5,3,4,2,1,0:T(8,128)(2,1)}, bf16[2,2,2,64,2,128]{5,3,4,2,1,0:T(8,128)(2,1)}, u32[]{:S(2)}, u32[]{:S(2)}) collective-permute-start(bf16[2,2,2,64,2,128]{5,3,4,2,1,0:T(8,128)(2,1)} %pad_maximum_fusion.10), channel_id=1, source_target_pairs={{0,8},{1,9},{2,10},{3,11},{4,12},{5,13},{6,14},{7,15},{8,0},{9,1},... | collective-permute-start | bytes 786440 | tf_op jit(solution)/shard_map/ppermute | solution.py:47
  92.4 11.0 %collective-permute-start.11 = (bf16[2,2,2,2,64,2,128]{6,4,5,3,2,1,0:T(8,128)(2,1)S(1)}, bf16[2,2,2,2,64,2,128]{6,4,5,3,2,1,0:T(8,128)(2,1)S(1)}, u32[]{:S(2)}, u32[]{:S(2)}) collective-permute-start(bf16[2,2,2,2,64,2,128]{6,4,5,3,2,1,0:T(8,128)(2,1)S(1)} %pad_maximum_fusion.7), channel_id=1, source_target_pairs={{0,4},{1,5},{2,6},{3,7},{4,0},{5,1},{6,2},{7,3},{8,12},{9,13},{10,... | collective-permute-start | bytes 1572872 | tf_op jit(solution)/shard_map/ppermute | solution.py:47
  103.6 1.0 copy-start.30
  106.2 7.9 %copy-start.16 = (f32[2,64,4,128]{3,1,0,2:T(8,128)}, f32[2,64,4,128]{3,1,0,2:T(8,128)S(1)}, u32[]{:S(2)}) copy-start(f32[2,64,4,128]{3,1,0,2:T(8,128)S(1)} %fusion.21) | copy-start | bytes 786436
  106.2 7.9 %collective-permute-start.12 = (bf16[4,2,64,128]{3,2,1,0:T(8,128)(2,1)S(1)}, bf16[4,2,64,128]{3,2,1,0:T(8,128)(2,1)S(1)}, u32[]{:S(2)}, u32[]{:S(2)}) collective-permute-start(bf16[4,2,64,128]{3,2,1,0:T(8,128)(2,1)S(1)} %convert_bitcast_fusion), channel_id=1, source_target_pairs={{0,2},{1,3},{2,0},{3,1},{4,6},{5,7},{6,4},{7,5},{8,10},{9,11},{10,... | collective-permute-start | bytes 393224 | tf_op jit(solution)/shard_map/ppermute | solution.py:47
  114.1 13.3 %collective-permute-start.13 = (bf16[2,4,2,64,128]{4,3,2,1,0:T(8,128)(2,1)S(1)}, bf16[2,4,2,64,128]{4,3,2,1,0:T(8,128)(2,1)S(1)}, u32[]{:S(2)}, u32[]{:S(2)}) collective-permute-start(bf16[2,4,2,64,128]{4,3,2,1,0:T(8,128)(2,1)S(1)} %pad_maximum_fusion.11), channel_id=1, source_target_pairs={{0,1},{1,0},{2,3},{3,2},{4,5},{5,4},{6,7},{7,6},{8,9},{9,8},{10,11... | collective-permute-start | bytes 786440 | tf_op jit(solution)/shard_map/ppermute | solution.py:47
  127.5 1.5 copy-start.19
  129.1 12.5 %collective-permute-start.14 = (bf16[2,2,4,2,64,128]{5,4,3,2,0,1:T(8,128)(2,1)}, bf16[2,2,4,2,64,128]{5,4,3,2,0,1:T(8,128)(2,1)}, u32[]{:S(2)}, u32[]{:S(2)}) collective-permute-start(bf16[2,2,4,2,64,128]{5,4,3,2,0,1:T(8,128)(2,1)} %pad_maximum_fusion.8), channel_id=1, source_target_pairs={{0,8},{1,9},{2,10},{3,11},{4,12},{5,13},{6,14},{7,15},{8,0},{9,1},... | collective-permute-start | bytes 1572872 | tf_op jit(solution)/shard_map/ppermute | solution.py:47
  142.8 1.9 copy-start.15
  144.7 21.3 %collective-permute-start.15 = (bf16[2,2,2,4,2,64,128]{6,5,4,3,1,2,0:T(8,128)(2,1)}, bf16[2,2,2,4,2,64,128]{6,5,4,3,1,2,0:T(8,128)(2,1)}, u32[]{:S(2)}, u32[]{:S(2)}) collective-permute-start(bf16[2,2,2,4,2,64,128]{6,5,4,3,1,2,0:T(8,128)(2,1)} %pad_maximum_fusion.5), channel_id=1, source_target_pairs={{0,4},{1,5},{2,6},{3,7},{4,0},{5,1},{6,2},{7,3},{8,12},{9,13},{10,... | collective-permute-start | bytes 3145736 | tf_op jit(solution)/shard_map/ppermute | solution.py:47
  173.7 11.9 %collective-permute-start.16 = (bf16[64,2,2,128]{3,0,1,2:T(8,128)(2,1)S(1)}, bf16[64,2,2,128]{3,0,1,2:T(8,128)(2,1)S(1)}, u32[]{:S(2)}, u32[]{:S(2)}) collective-permute-start(bf16[64,2,2,128]{3,0,1,2:T(8,128)(2,1)S(1)} %fusion.25), channel_id=1, source_target_pairs={{0,64},{16,80},{32,96},{48,112},{64,0},{80,16},{96,32},{112,48},{1... | collective-permute-start | bytes 196616 | tf_op jit(solution)/shard_map/ppermute | solution.py:47
  185.6 3.9 %collective-permute-start.17 = (bf16[2,64,2,2,128]{4,1,2,3,0:T(8,128)(2,1)S(1)}, bf16[2,64,2,2,128]{4,1,2,3,0:T(8,128)(2,1)S(1)}, u32[]{:S(2)}, u32[]{:S(2)}) collective-permute-start(bf16[2,64,2,2,128]{4,1,2,3,0:T(8,128)(2,1)S(1)} %pad_maximum_fusion.14), channel_id=1, source_target_pairs={{0,128},{16,144},{32,160},{48,176},{64,192},{80,208},{96,224},{112... | collective-permute-start | bytes 393224 | tf_op jit(solution)/shard_map/ppermute | solution.py:47
  189.6 9.0 %collective-permute-start.18 = (bf16[2,2,64,2,2,128]{5,2,3,4,1,0:T(8,128)(2,1)S(1)}, bf16[2,2,64,2,2,128]{5,2,3,4,1,0:T(8,128)(2,1)S(1)}, u32[]{:S(2)}, u32[]{:S(2)}) collective-permute-start(bf16[2,2,64,2,2,128]{5,2,3,4,1,0:T(8,128)(2,1)S(1)} %pad_maximum_fusion.12), channel_id=1, source_target_pairs={{0,32},{16,48},{32,0},{48,16},{64,96},{80,112},{96,64},{112,80},{1... | collective-permute-start | bytes 786440 | tf_op jit(solution)/shard_map/ppermute | solution.py:47
  195.2 9.8 %copy-start.27 = (pred[513,129]{1,0:T(8,128)(4,1)S(1)}, pred[513,129]{1,0:T(8,128)(4,1)}, u32[]{:S(2)}) copy-start(pred[513,129]{1,0:T(8,128)(4,1)} %broadcast_and_fusion) | copy-start | bytes 198535
  198.7 10.2 %collective-permute-start.19 = (bf16[2,2,2,64,2,2,128]{6,3,4,5,1,0,2:T(8,128)(2,1)S(1)}, bf16[2,2,2,64,2,2,128]{6,3,4,5,1,0,2:T(8,128)(2,1)S(1)}, u32[]{:S(2)}, u32[]{:S(2)}) collective-permute-start(bf16[2,2,2,64,2,2,128]{6,3,4,5,1,0,2:T(8,128)(2,1)S(1)} %pad_maximum_fusion.9), channel_id=1, source_target_pairs={{0,16},{16,0},{32,48},{48,32},{64,80},{80,64},{96,112},{112,96},{1... | collective-permute-start | bytes 1572872 | tf_op jit(solution)/shard_map/ppermute | solution.py:47
  206.8 1.2 copy-start.17
  209.0 1.4 copy-start.13
  209.2 4.5 %copy-start.25 = (bf16[2,2,2,2,64,2,2,128]{7,4,3,2,1,0,6,5:T(8,128)(2,1)}, bf16[2,2,2,2,64,2,2,128]{7,4,3,2,1,0,6,5:T(8,128)(2,1)S(1)}, u32[]{:S(2)}) copy-start(bf16[2,2,2,2,64,2,2,128]{7,4,3,2,1,0,6,5:T(8,128)(2,1)S(1)} %copy.147) | copy-start | bytes 3145732
  211.7 2.0 copy-start.11
  215.0 2.8 %copy-start.7 = (f32[2,512,128]{2,1,0:T(8,128)S(1)}, f32[2,512,128]{2,1,0:T(8,128)}, u32[]{:S(2)}) copy-start(f32[2,512,128]{2,1,0:T(8,128)} %param.10) | copy-start | bytes 1572868
  215.1 5.3 %copy-start.1 = (bf16[8,128,128]{2,1,0:T(8,128)(2,1)S(1)}, bf16[8,128,128]{2,1,0:T(8,128)(2,1)}, u32[]{:S(2)}) copy-start(bf16[8,128,128]{2,1,0:T(8,128)(2,1)} %param.16) | copy-start | bytes 786436
  (6 other events, 4.6 us)

commit v8 on v3

--- a/solution.py
+++ b/solution.py
@@ -75,23 +75,19 @@
     steer_im = row_steer[1]
     col_mine = lax.dynamic_slice_in_dim(col_steer, az_index, 1, 3)[..., 0]
     image_b = image.astype(jnp.bfloat16).reshape(2, tiles_dev, tile_rows, columns)
-    part_sre = steer_re
-    part_sim = steer_im
+    image_pair = jnp.stack(
+        [jnp.stack([image_b[0], image_b[1]], axis=2), jnp.stack([-image_b[1], image_b[0]], axis=2)]
+    )
+    prod = jnp.einsum(
+        "cpjh,cjhou->pjou", row_steer, image_pair, preferred_element_type=jnp.float32
+    )
     weight_re = col_mine[0][..., None]
     weight_im = col_mine[1][..., None]
-    prod_re = jnp.einsum("pjh,jhu->pju", part_sre, image_b[0], preferred_element_type=jnp.float32)
-    prod_re = prod_re - jnp.einsum(
-        "pjh,jhu->pju", part_sim, image_b[1], preferred_element_type=jnp.float32
-    )
-    prod_im = jnp.einsum("pjh,jhu->pju", part_sre, image_b[1], preferred_element_type=jnp.float32)
-    prod_im = prod_im + jnp.einsum(
-        "pjh,jhu->pju", part_sim, image_b[0], preferred_element_type=jnp.float32
-    )
-    real_part = weight_re * prod_re - weight_im * prod_im
-    imag_part = weight_re * prod_im + weight_im * prod_re
-    parts = jnp.stack([real_part, imag_part], axis=0).reshape(2, az_count, -1, tiles_dev, columns)
-    summed = halving_sum(jnp.moveaxis(parts, 1, 0), "az", (1, 8, 2, 4))
-    projection_b = jnp.transpose(summed, (2, 1, 0, 3)).astype(jnp.bfloat16)
+    real_part = weight_re * prod[:, :, 0] - weight_im * prod[:, :, 1]
+    imag_part = weight_re * prod[:, :, 1] + weight_im * prod[:, :, 0]
+    parts = jnp.stack([real_part, imag_part], axis=2).reshape(az_count, -1, tiles_dev, 2, columns)
+    summed = halving_sum(parts, "az", (1, 8, 2, 4))
+    projection_b = jnp.transpose(summed, (1, 0, 2, 3)).astype(jnp.bfloat16)
     all_proj = doubling_gather(projection_b, "tile", (2, 1, 8, 4))
     all_proj = all_proj.reshape(-1, *all_proj.shape[2:])
     phase_ids = jnp.arange(kernels.shape[0], dtype=jnp.int32)
@@ -127,17 +123,12 @@
     back_im = piece[1].astype(jnp.float32)
     mixed_re = (weight_re * back_re + weight_im * back_im).astype(jnp.bfloat16)
     mixed_im = (weight_re * back_im - weight_im * back_re).astype(jnp.bfloat16)
-    part_sre = steer_re
-    part_sim = steer_im
-    grad_re = jnp.einsum("pjh,jpu->jhu", part_sre, mixed_re, preferred_element_type=jnp.float32)
-    grad_re = grad_re + jnp.einsum(
-        "pjh,jpu->jhu", part_sim, mixed_im, preferred_element_type=jnp.float32
+    mixed = jnp.stack(
+        [jnp.stack([mixed_re, mixed_im], axis=2), jnp.stack([mixed_im, -mixed_re], axis=2)]
     )
-    grad_im = jnp.einsum("pjh,jpu->jhu", part_sre, mixed_im, preferred_element_type=jnp.float32)
-    grad_im = grad_im - jnp.einsum(
-        "pjh,jpu->jhu", part_sim, mixed_re, preferred_element_type=jnp.float32
+    adjoint = jnp.einsum(
+        "cpjh,cjpou->ojhu", row_steer, mixed, preferred_element_type=jnp.float32
     )
-    adjoint = jnp.stack([grad_re, grad_im])
     adjoint = adjoint.reshape(2, strip_rows, columns)
     stacked = jnp.concatenate([image, tv_dual.reshape(4, strip_rows, columns)], axis=0)
     padded = padded_2(stacked, (("az", 2), ("tile", 1)), 1)

time: 193 us -> 206 us (1.067)
  other arithmetic: 23.3 us -> 37.2 us
  waiting for transfers between devices: 78.2 us -> 65 us
  local copies, waits for them, and re-layouts: 24.5 us -> 35.1 us
  starting transfers between devices: 51.5 us -> 58.9 us
  matrix products: 13.2 us -> 6.18 us
    ppermute x12, waiting for transfers between devices: 48.6 us -> 36.9 us  [doubling_gather(): got = lax.ppermute(block, axis, pairs)]
    dot_general x8 -> x2, matrix products: 9.32 us -> 2.3 us  [the longest x1 1.53 us: on_device(): jnp.einsum('cpjh,cjpou->ojhu', row_steer, mixed, preferred_element_type=j...]
    ppermute x12, starting transfers between devices: 28.5 us -> 33.6 us  [doubling_gather(): got = lax.ppermute(block, axis, pairs)]
    another operation x24, other arithmetic: 3.52 us -> 7.19 us  [doubling_gather(): block = jnp.stack([low, high], axis=place)]
    slice x1 -> x0, local copies, waits for them, and re-layouts: 2.75 us -> none  [on_device(): steer_im = row_steer[1]]
    ppermute x2, starting transfers between devices: 14.7 us -> 17.1 us  [padded_2(): lax.ppermute(lax.slice_in_dim(block, block.shape[dim] - width, None, axis...]
    sub x2 -> x1, local copies, waits for them, and re-layouts: 0.44 us -> 2.58 us  [on_device(): real_part = weight_re * prod[:, :, 0] - weight_im * prod[:, :, 1]]
    unnamed x68 -> x53, local copies, waits for them, and re-layouts: 5.42 us -> 4.27 us
  transfers between devices with their start and end apart: 20 -> 20, of which waited for: 15 -> 13; matrix products, arithmetic and copies ran while one was open for 13% -> 20% of each run, Pallas kernels for 0% -> 0%
where the time goes in v8:
time: 206 us; the launch traced here: 204 us
  waiting for transfers between devices  65 us (32%)
  starting transfers between devices  58.9 us (29%)
  other arithmetic  37.2 us (18%)
  local copies, waits for them, and re-layouts  35.1 us (17%)
  matrix products  6.18 us (3%)
    ppermute x12, waiting for transfers between devices, doubling_gather(): got = lax.ppermute(block, axis, pairs)  36.9 us
    ppermute x12, starting transfers between devices, doubling_gather(): got = lax.ppermute(block, axis, pairs)  33.6 us
    ppermute x4, waiting for transfers between devices, halving_sum(): blocks = keep + lax.ppermute(send, axis, pairs)  26 us
    ppermute x2, starting transfers between devices, padded_2(): lax.ppermute(lax.slice_in_dim(block, block.shape[dim] - width, None, axis...  17.1 us
    another operation x24, other arithmetic, doubling_gather(): block = jnp.stack([low, high], axis=place)  7.19 us
    another operation x2, other arithmetic, on_device(): jnp.stack([grad_rows, grad_cols])  6.28 us
    ppermute x4, starting transfers between devices, halving_sum(): blocks = keep + lax.ppermute(send, axis, pairs)  5.1 us
    unnamed x53, local copies, waits for them, and re-layouts  4.27 us
  transfers between devices with their start and end apart: 20, of which 13 were waited for; matrix products, arithmetic and copies ran while one was open for 20% of the time, Pallas kernels for 0%

profile of v8, /device:TPU:1, one launch (start us, length us, event | category | flops | bytes accessed | tf_op | source)
XLA Modules:
  0.0 203.8 jit_solution(4446175566089555324)
XLA Ops:
  5.8 2.6 %copy.142 = f32[1024,2,1,128]{3,0,1,2:T(8,128)} copy(f32[1024,2,1,128]{0,3,2,1:T(8,128)} %get-tuple-element.28) | data formatting | bytes 2097152 | tf_op jit(solution)/shard_map/sub | solution.py:86
  9.7 1.7 fusion.50
  12.4 3.2 %collective-permute-start = (f32[2,2,2,64,2,2,128]{6,3,5,4,2,1,0:T(8,128)}, f32[2,2,2,64,2,2,128]{6,3,5,4,2,1,0:T(8,128)}, u32[]{:S(2)}, u32[]{:S(2)}) collective-permute-start(f32[2,2,2,64,2,2,128]{6,3,5,4,2,1,0:T(8,128)} %bitcast.217), channel_id=1, source_target_pairs={{0,16},{16,0},{32,48},{48,32},{64,80},{80,64},{96,112},{112,96},{1... | collective-permute-start | bytes 3145736 | tf_op jit(solution)/shard_map/ppermute | solution.py:36
  15.7 2.6 %collective-permute-done = f32[2,2,2,64,2,2,128]{6,3,5,4,2,1,0:T(8,128)} collective-permute-done((f32[2,2,2,64,2,2,128]{6,3,5,4,2,1,0:T(8,128)}, f32[2,2,2,64,2,2,128]{6,3,5,4,2,1,0:T(8,128)}, u32[]{:S(2)}, u32[]{:S(2)}) %collective-permute-start) | collective-permute-done | bytes 1048608 | tf_op jit(solution)/shard_map/ppermute | solution.py:36
  20.8 13.1 %collective-permute-done.1 = f32[2,2,64,2,2,128]{5,2,4,3,1,0:T(8,128)S(1)} collective-permute-done((f32[2,2,64,2,2,128]{5,2,4,3,1,0:T(8,128)S(1)}, f32[2,2,64,2,2,128]{5,2,4,3,1,0:T(8,128)S(1)}, u32[]{:S(2)}, u32[]{:S(2)}) %collective-permute-start.1) | collective-permute-done | bytes 524320 | tf_op jit(solution)/shard_map/ppermute | solution.py:36
  35.2 6.5 %collective-permute-done.2 = f32[2,64,2,2,128]{4,1,3,2,0:T(8,128)S(1)} collective-permute-done((f32[2,64,2,2,128]{4,1,3,2,0:T(8,128)S(1)}, f32[2,64,2,2,128]{4,1,3,2,0:T(8,128)S(1)}, u32[]{:S(2)}, u32[]{:S(2)}) %collective-permute-start.2) | collective-permute-done | bytes 262176 | tf_op jit(solution)/shard_map/ppermute | solution.py:36
  41.8 1.7 collective-permute-start.3
  43.5 3.7 %collective-permute-done.3 = f32[64,2,2,128]{3,0,2,1:T(8,128)S(1)} collective-permute-done((f32[64,2,2,128]{3,0,2,1:T(8,128)S(1)}, f32[64,2,2,128]{3,0,2,1:T(8,128)S(1)}, u32[]{:S(2)}, u32[]{:S(2)}) %collective-permute-start.3) | collective-permute-done | bytes 131104 | tf_op jit(solution)/shard_map/ppermute | solution.py:36
  47.2 5.3 %collective-permute-start.4 = (bf16[2,64,2,128]{3,1,2,0:T(8,128)(2,1)S(1)}, bf16[2,64,2,128]{3,1,2,0:T(8,128)(2,1)S(1)}, u32[]{:S(2)}, u32[]{:S(2)}) collective-permute-start(bf16[2,64,2,128]{3,1,2,0:T(8,128)(2,1)S(1)} %fusion.66), channel_id=1, source_target_pairs={{0,2},{1,3},{2,0},{3,1},{4,6},{5,7},{6,4},{7,5},{8,10},{9,11},{10,... | collective-permute-start | bytes 196616 | tf_op jit(solution)/shard_map/ppermute | solution.py:47
  52.5 2.0 collective-permute-done.4
  54.5 2.5 %collective-permute-start.5 = (bf16[2,2,64,2,128]{4,2,3,1,0:T(8,128)(2,1)S(1)}, bf16[2,2,64,2,128]{4,2,3,1,0:T(8,128)(2,1)S(1)}, u32[]{:S(2)}, u32[]{:S(2)}) collective-permute-start(bf16[2,2,64,2,128]{4,2,3,1,0:T(8,128)(2,1)S(1)} %pad_maximum_fusion.25), channel_id=1, source_target_pairs={{0,1},{1,0},{2,3},{3,2},{4,5},{5,4},{6,7},{7,6},{8,9},{9,8},{10,11... | collective-permute-start | bytes 393224 | tf_op jit(solution)/shard_map/ppermute | solution.py:47
  57.0 4.5 %collective-permute-done.5 = bf16[2,2,64,2,128]{4,2,3,1,0:T(8,128)(2,1)S(1)} collective-permute-done((bf16[2,2,64,2,128]{4,2,3,1,0:T(8,128)(2,1)S(1)}, bf16[2,2,64,2,128]{4,2,3,1,0:T(8,128)(2,1)S(1)}, u32[]{:S(2)}, u32[]{:S(2)}) %collective-permute-start.5) | collective-permute-done | bytes 131104 | tf_op jit(solution)/shard_map/ppermute | solution.py:47
  61.6 3.0 %collective-permute-start.6 = (bf16[2,2,2,64,2,128]{5,3,4,2,1,0:T(8,128)(2,1)S(1)}, bf16[2,2,2,64,2,128]{5,3,4,2,1,0:T(8,128)(2,1)S(1)}, u32[]{:S(2)}, u32[]{:S(2)}) collective-permute-start(bf16[2,2,2,64,2,128]{5,3,4,2,1,0:T(8,128)(2,1)S(1)} %pad_maximum_fusion.22), channel_id=1, source_target_pairs={{0,8},{1,9},{2,10},{3,11},{4,12},{5,13},{6,14},{7,15},{8,0},{9,1},... | collective-permute-start | bytes 786440 | tf_op jit(solution)/shard_map/ppermute | solution.py:47
  64.7 3.8 %collective-permute-done.6 = bf16[2,2,2,64,2,128]{5,3,4,2,1,0:T(8,128)(2,1)S(1)} collective-permute-done((bf16[2,2,2,64,2,128]{5,3,4,2,1,0:T(8,128)(2,1)S(1)}, bf16[2,2,2,64,2,128]{5,3,4,2,1,0:T(8,128)(2,1)S(1)}, u32[]{:S(2)}, u32[]{:S(2)}) %collective-permute-start.6) | collective-permute-done | bytes 262176 | tf_op jit(solution)/shard_map/ppermute | solution.py:47
  68.5 1.4 collective-permute-start.7
  70.0 10.1 %collective-permute-done.7 = bf16[2,2,2,2,64,2,128]{6,4,5,3,2,1,0:T(8,128)(2,1)S(1)} collective-permute-done((bf16[2,2,2,2,64,2,128]{6,4,5,3,2,1,0:T(8,128)(2,1)S(1)}, bf16[2,2,2,2,64,2,128]{6,4,5,3,2,1,0:T(8,128)(2,1)S(1)}, u32[]{:S(2)}, u32[]{:S(2)}) %collective-permute-start.7) | collective-permute-done | bytes 524320 | tf_op jit(solution)/shard_map/ppermute | solution.py:47
  81.4 1.6 fusion.32
  83.0 4.4 %collective-permute-start.8 = (bf16[4,2,64,128]{3,2,1,0:T(8,128)(2,1)S(1)}, bf16[4,2,64,128]{3,2,1,0:T(8,128)(2,1)S(1)}, u32[]{:S(2)}, u32[]{:S(2)}) collective-permute-start(bf16[4,2,64,128]{3,2,1,0:T(8,128)(2,1)S(1)} %convert_bitcast_fusion), channel_id=1, source_target_pairs={{0,2},{1,3},{2,0},{3,1},{4,6},{5,7},{6,4},{7,5},{8,10},{9,11},{10,... | collective-permute-start | bytes 393224 | tf_op jit(solution)/shard_map/ppermute | solution.py:47
  87.3 3.4 %collective-permute-done.8 = bf16[4,2,64,128]{3,2,1,0:T(8,128)(2,1)S(1)} collective-permute-done((bf16[4,2,64,128]{3,2,1,0:T(8,128)(2,1)S(1)}, bf16[4,2,64,128]{3,2,1,0:T(8,128)(2,1)S(1)}, u32[]{:S(2)}, u32[]{:S(2)}) %collective-permute-start.8) | collective-permute-done | bytes 131104 | tf_op jit(solution)/shard_map/ppermute | solution.py:47
  92.4 2.2 %slice_maximum_fusion = (f32[6,512,1]{2,1,0:T(8,128)}, f32[6,512,1]{2,1,0:T(8,128)}) fusion(f32[4,512,128]{2,1,0:T(8,128)S(1)} %bitcast.222, f32[2,512,128]{2,1,0:T(8,128)S(1)} %copy-done.4), kind=kLoop, calls=%fused_computation.27 | loop fusion | flops 6144 | bytes 1597440 | tf_op jit(solution)/shard_map/concatenate | solution.py:133
  94.6 2.5 %copy.160 = f32[6,512,1]{1,2,0:T(1,128)} copy(f32[6,512,1]{2,1,0:T(8,128)} %get-tuple-element.33) | data formatting | bytes 24576 | tf_op jit(solution)/shard_map/slice | solution.py:17
  97.0 12.6 %collective-permute-start.16 = (f32[6,512,1]{1,2,0:T(1,128)}, f32[6,512,1]{1,2,0:T(1,128)}, u32[]{:S(2)}, u32[]{:S(2)}) collective-permute-start(f32[6,512,1]{1,2,0:T(1,128)} %copy.160), channel_id=1, source_target_pairs={{0,16},{16,32},{32,48},{48,64},{64,80},{80,96},{96,112},{112,128},... | collective-permute-start | bytes 36872 | tf_op jit(solution)/shard_map/ppermute | solution.py:16
  109.7 2.5 %copy.161 = f32[6,512,1]{1,2,0:T(1,128)} copy(f32[6,512,1]{2,1,0:T(8,128)} %get-tuple-element.34) | data formatting | bytes 24576 | tf_op jit(solution)/shard_map/slice | solution.py:19
  112.2 1.9 collective-permute-start.17
  116.7 3.7 %collective-permute-start.10 = (bf16[2,2,4,2,64,128]{5,4,3,2,0,1:T(8,128)(2,1)}, bf16[2,2,4,2,64,128]{5,4,3,2,0,1:T(8,128)(2,1)}, u32[]{:S(2)}, u32[]{:S(2)}) collective-permute-start(bf16[2,2,4,2,64,128]{5,4,3,2,0,1:T(8,128)(2,1)} %pad_maximum_fusion.20), channel_id=1, source_target_pairs={{0,8},{1,9},{2,10},{3,11},{4,12},{5,13},{6,14},{7,15},{8,0},{9,1},... | collective-permute-start | bytes 1572872 | tf_op jit(solution)/shard_map/ppermute | solution.py:47
  121.9 9.2 %collective-permute-done.10 = bf16[2,2,4,2,64,128]{5,4,3,2,0,1:T(8,128)(2,1)} collective-permute-done((bf16[2,2,4,2,64,128]{5,4,3,2,0,1:T(8,128)(2,1)}, bf16[2,2,4,2,64,128]{5,4,3,2,0,1:T(8,128)(2,1)}, u32[]{:S(2)}, u32[]{:S(2)}) %collective-permute-start.10) | collective-permute-done | bytes 524320 | tf_op jit(solution)/shard_map/ppermute | solution.py:47
  139.4 2.4 %copy.162 = f32[6,512,1]{2,1,0:T(8,128)} copy(f32[6,512,1]{1,2,0:T(1,128)} %collective-permute-done.16) | data formatting | bytes 24576 | tf_op jit(solution)/shard_map/ppermute | solution.py:16
  141.7 2.4 %copy.163 = f32[6,512,1]{2,1,0:T(8,128)} copy(f32[6,512,1]{1,2,0:T(1,128)} %collective-permute-done.17) | data formatting | bytes 24576 | tf_op jit(solution)/shard_map/ppermute | solution.py:19
  144.1 1.5 pad_maximum_fusion.27
  145.6 4.4 %collective-permute-start.18 = (f32[6,1,130]{2,1,0:T(1,128)}, f32[6,1,130]{2,1,0:T(1,128)}, u32[]{:S(2)}, u32[]{:S(2)}) collective-permute-start(f32[6,1,130]{2,1,0:T(1,128)} %get-tuple-element.24), channel_id=1, source_target_pairs={{0,1},{1,2},{2,3},{3,4},{4,5},{5,6},{6,7},{7,8},{8,9},{9,10},{10,1... | collective-permute-start | bytes 9368 | tf_op jit(solution)/shard_map/ppermute | solution.py:16
  151.9 2.4 %gather_fusion = bf16[12,128,128]{2,1,0:T(8,128)(2,1)} fusion(bf16[8,128,128]{2,1,0:T(8,128)(2,1)} %param.16, s32[1024]{0:T(1024)} %pad_clamp_fusion.1), kind=kCustom, calls=%fused_computation | custom fusion | bytes 786480 | tf_op jit(solution)/shard_map/gather | solution.py:105
  154.3 2.2 %collective-permute-done.19 = f32[6,1,130]{2,1,0:T(1,128)} collective-permute-done((f32[6,1,130]{2,1,0:T(1,128)}, f32[6,1,130]{2,1,0:T(1,128)}, u32[]{:S(2)}, u32[]{:S(2)}) %collective-permute-start.19) | collective-permute-done | bytes 3152 | tf_op jit(solution)/shard_map/ppermute | solution.py:19
  156.5 4.0 %fusion.44 = f32[1,2,513,129]{3,2,1,0:T(8,128)} fusion(f32[6,1,130]{2,1,0:T(1,128)} %collective-permute-done.19, f32[6,512,1]{2,1,0:T(8,128)} %copy.163, f32[6,512,1]{2,1,0:T(8,128)} %copy.162, f32[4,512,128]{2,1,0:T(8,128)S(1)} %bitcast.224, f32[2,512,128]{2,1,0:T(8,128)} %param.10, f32[6,1,130]{2,1,0:T(1,128)} %collective-permute-done.18, ...), kind=kLoop, calls=%fused_computation.57 | loop fusion | flops 1323540 | bytes 2133609 | tf_op jit(solution)/shard_map/stack | solution.py:146
  160.5 1.4 select_bitcast_fusion.1
  162.0 1.5 copy.152
  163.6 3.1 %gather_fusion.1 = bf16[12,2,64,128]{3,2,1,0:T(8,128)(2,1)} fusion(bf16[2,64,64,128]{3,1,0,2:T(8,128)(2,1)} %bitcast.235, s32[1024]{0:T(1024)} %pad_clamp_fusion), kind=kCustom, calls=%fused_computation.1 | custom fusion | bytes 786480 | tf_op jit(solution)/shard_map/jit(_take)/gather | solution.py:115
  166.6 1.5 fusion.36
  168.1 2.7 %collective-permute-start.12 = (bf16[64,2,2,128]{3,0,1,2:T(8,128)(2,1)S(1)}, bf16[64,2,2,128]{3,0,1,2:T(8,128)(2,1)S(1)}, u32[]{:S(2)}, u32[]{:S(2)}) collective-permute-start(bf16[64,2,2,128]{3,0,1,2:T(8,128)(2,1)S(1)} %fusion.36), channel_id=1, source_target_pairs={{0,64},{16,80},{32,96},{48,112},{64,0},{80,16},{96,32},{112,48},{1... | collective-permute-start | bytes 196616 | tf_op jit(solution)/shard_map/ppermute | solution.py:47
  170.8 2.3 %fusion.41 = f32[1,2,513,129]{3,2,1,0:T(8,128)S(1)} fusion(f32[6,1,130]{2,1,0:T(1,128)} %collective-permute-done.18, f32[6,512,1]{2,1,0:T(8,128)} %copy.163, f32[6,512,1]{2,1,0:T(8,128)} %copy.162, f32[4,512,128]{2,1,0:T(8,128)S(1)} %bitcast.225, f32[2,512,128]{2,1,0:T(8,128)S(1)} %copy-done.5, pred[129]{0:T(512)(128)(4,1)} %get-tuple-element.69), kind=kLoop, calls=%fused_computation.49 | loop fusion | flops 1323540 | bytes 2130105 | tf_op jit(solution)/shard_map/stack | solution.py:146
  173.2 2.3 %collective-permute-start.13 = (bf16[2,64,2,2,128]{4,1,2,3,0:T(8,128)(2,1)S(1)}, bf16[2,64,2,2,128]{4,1,2,3,0:T(8,128)(2,1)S(1)}, u32[]{:S(2)}, u32[]{:S(2)}) collective-permute-start(bf16[2,64,2,2,128]{4,1,2,3,0:T(8,128)(2,1)S(1)} %pad_maximum_fusion.26), channel_id=1, source_target_pairs={{0,128},{16,144},{32,160},{48,176},{64,192},{80,208},{96,224},{112... | collective-permute-start | bytes 393224 | tf_op jit(solution)/shard_map/ppermute | solution.py:47
  175.5 1.7 pad_maximum_fusion
  178.0 2.2 %collective-permute-start.14 = (bf16[2,2,64,2,2,128]{5,2,3,4,1,0:T(8,128)(2,1)S(1)}, bf16[2,2,64,2,2,128]{5,2,3,4,1,0:T(8,128)(2,1)S(1)}, u32[]{:S(2)}, u32[]{:S(2)}) collective-permute-start(bf16[2,2,64,2,2,128]{5,2,3,4,1,0:T(8,128)(2,1)S(1)} %pad_maximum_fusion.24), channel_id=1, source_target_pairs={{0,32},{16,48},{32,0},{48,16},{64,96},{80,112},{96,64},{112,80},{1... | collective-permute-start | bytes 786440 | tf_op jit(solution)/shard_map/ppermute | solution.py:47
  180.7 3.2 %collective-permute-done.14 = bf16[2,2,64,2,2,128]{5,2,3,4,1,0:T(8,128)(2,1)S(1)} collective-permute-done((bf16[2,2,64,2,2,128]{5,2,3,4,1,0:T(8,128)(2,1)S(1)}, bf16[2,2,64,2,2,128]{5,2,3,4,1,0:T(8,128)(2,1)S(1)}, u32[]{:S(2)}, u32[]{:S(2)}) %collective-permute-start.14) | collective-permute-done | bytes 262176 | tf_op jit(solution)/shard_map/ppermute | solution.py:47
  184.0 5.9 %collective-permute-start.15 = (bf16[2,2,2,64,2,2,128]{6,3,4,5,1,0,2:T(8,128)(2,1)S(1)}, bf16[2,2,2,64,2,2,128]{6,3,4,5,1,0,2:T(8,128)(2,1)S(1)}, u32[]{:S(2)}, u32[]{:S(2)}) collective-permute-start(bf16[2,2,2,64,2,2,128]{6,3,4,5,1,0,2:T(8,128)(2,1)S(1)} %pad_maximum_fusion.21), channel_id=1, source_target_pairs={{0,16},{16,0},{32,48},{48,32},{64,80},{80,64},{96,112},{112,96},{1... | collective-permute-start | bytes 1572872 | tf_op jit(solution)/shard_map/ppermute | solution.py:47
  191.7 1.5 fusion.38
  195.3 1.5 copy.156
  197.5 1.5 fusion.12
  200.3 3.4 %fusion.56 = f32[2,512,128]{2,1,0:T(8,128)} fusion(f32[2,512,128]{2,1,0:T(8,128)S(1)} %copy-done.6, f32[2,513,129]{2,1,0:T(8,128)} %get-tuple-element.26, f32[2,513,129]{2,1,0:T(8,128)} %get-tuple-element.25, f32[2,2,256,128]{3,2,1,0:T(8,128)S(1)} %copy.159), kind=kLoop, calls=%fused_computation.85 | loop fusion | flops 786432 | bytes 3670016 | tf_op jit(solution)/shard_map/sub | solution.py:158
  (137 shorter events, 35.8 us)
Async XLA Ops:
  0.6 3.1 %copy-start = (bf16[2,1024,2,256]{3,2,1,0:T(2,128)(2,1)S(1)}, bf16[2,1024,2,256]{3,2,1,0:T(2,128)(2,1)}, u32[]{:S(2)}) copy-start(bf16[2,1024,2,256]{3,2,1,0:T(2,128)(2,1)} %param.14) | copy-start | bytes 6291460
  12.4 5.9 %collective-permute-start = (f32[2,2,2,64,2,2,128]{6,3,5,4,2,1,0:T(8,128)}, f32[2,2,2,64,2,2,128]{6,3,5,4,2,1,0:T(8,128)}, u32[]{:S(2)}, u32[]{:S(2)}) collective-permute-start(f32[2,2,2,64,2,2,128]{6,3,5,4,2,1,0:T(8,128)} %bitcast.217), channel_id=1, source_target_pairs={{0,16},{16,0},{32,48},{48,32},{64,80},{80,64},{96,112},{112,96},{1... | collective-permute-start | bytes 3145736 | tf_op jit(solution)/shard_map/ppermute | solution.py:36
  19.7 1.0 copy-start.12
  20.7 13.2 %collective-permute-start.1 = (f32[2,2,64,2,2,128]{5,2,4,3,1,0:T(8,128)S(1)}, f32[2,2,64,2,2,128]{5,2,4,3,1,0:T(8,128)S(1)}, u32[]{:S(2)}, u32[]{:S(2)}) collective-permute-start(f32[2,2,64,2,2,128]{5,2,4,3,1,0:T(8,128)S(1)} %dynamic-slice_bitcast_fusion), channel_id=1, source_target_pairs={{0,128},{16,144},{32,160},{48,176},{64,192},{80,208},{96,224},{112... | collective-permute-start | bytes 1572872 | tf_op jit(solution)/shard_map/ppermute | solution.py:36
  35.0 6.7 %collective-permute-start.2 = (f32[2,64,2,2,128]{4,1,3,2,0:T(8,128)S(1)}, f32[2,64,2,2,128]{4,1,3,2,0:T(8,128)S(1)}, u32[]{:S(2)}, u32[]{:S(2)}) collective-permute-start(f32[2,64,2,2,128]{4,1,3,2,0:T(8,128)S(1)} %dynamic-slice_bitcast_fusion.1), channel_id=1, source_target_pairs={{0,32},{16,48},{32,0},{48,16},{64,96},{80,112},{96,64},{112,80},{1... | collective-permute-start | bytes 786440 | tf_op jit(solution)/shard_map/ppermute | solution.py:36
  35.2 29.5 %copy-start.20 = (s32[32,1,6]{0,1,2:T(1,128)S(1)}, s32[32,1,6]{0,1,2:T(1,128)}, u32[]{:S(2)}) copy-start(s32[32,1,6]{0,1,2:T(1,128)} %param.17) | copy-start | bytes 2308
  35.2 29.4 %copy-start.21 = (s32[32,1,6]{0,1,2:T(1,128)S(1)}, s32[32,1,6]{0,1,2:T(1,128)}, u32[]{:S(2)}) copy-start(s32[32,1,6]{0,1,2:T(1,128)} %param.18) | copy-start | bytes 2308
  41.8 5.4 %collective-permute-start.3 = (f32[64,2,2,128]{3,0,2,1:T(8,128)S(1)}, f32[64,2,2,128]{3,0,2,1:T(8,128)S(1)}, u32[]{:S(2)}, u32[]{:S(2)}) collective-permute-start(f32[64,2,2,128]{3,0,2,1:T(8,128)S(1)} %dynamic-slice_bitcast_fusion.2), channel_id=1, source_target_pairs={{0,64},{16,80},{32,96},{48,112},{64,0},{80,16},{96,32},{112,48},{1... | collective-permute-start | bytes 393224 | tf_op jit(solution)/shard_map/ppermute | solution.py:36
  47.2 7.2 %collective-permute-start.4 = (bf16[2,64,2,128]{3,1,2,0:T(8,128)(2,1)S(1)}, bf16[2,64,2,128]{3,1,2,0:T(8,128)(2,1)S(1)}, u32[]{:S(2)}, u32[]{:S(2)}) collective-permute-start(bf16[2,64,2,128]{3,1,2,0:T(8,128)(2,1)S(1)} %fusion.66), channel_id=1, source_target_pairs={{0,2},{1,3},{2,0},{3,1},{4,6},{5,7},{6,4},{7,5},{8,10},{9,11},{10,... | collective-permute-start | bytes 196616 | tf_op jit(solution)/shard_map/ppermute | solution.py:47
  54.5 7.1 %collective-permute-start.5 = (bf16[2,2,64,2,128]{4,2,3,1,0:T(8,128)(2,1)S(1)}, bf16[2,2,64,2,128]{4,2,3,1,0:T(8,128)(2,1)S(1)}, u32[]{:S(2)}, u32[]{:S(2)}) collective-permute-start(bf16[2,2,64,2,128]{4,2,3,1,0:T(8,128)(2,1)S(1)} %pad_maximum_fusion.25), channel_id=1, source_target_pairs={{0,1},{1,0},{2,3},{3,2},{4,5},{5,4},{6,7},{7,6},{8,9},{9,8},{10,11... | collective-permute-start | bytes 393224 | tf_op jit(solution)/shard_map/ppermute | solution.py:47
  57.0 13.0 %copy-start.24 = (s32[64]{0:T(128)S(1)}, s32[64]{0:T(128)}, u32[]{:S(2)}) copy-start(s32[64]{0:T(128)} %param.19) | copy-start | bytes 772
  61.6 6.8 %collective-permute-start.6 = (bf16[2,2,2,64,2,128]{5,3,4,2,1,0:T(8,128)(2,1)S(1)}, bf16[2,2,2,64,2,128]{5,3,4,2,1,0:T(8,128)(2,1)S(1)}, u32[]{:S(2)}, u32[]{:S(2)}) collective-permute-start(bf16[2,2,2,64,2,128]{5,3,4,2,1,0:T(8,128)(2,1)S(1)} %pad_maximum_fusion.22), channel_id=1, source_target_pairs={{0,8},{1,9},{2,10},{3,11},{4,12},{5,13},{6,14},{7,15},{8,0},{9,1},... | collective-permute-start | bytes 786440 | tf_op jit(solution)/shard_map/ppermute | solution.py:47
  68.5 11.6 %collective-permute-start.7 = (bf16[2,2,2,2,64,2,128]{6,4,5,3,2,1,0:T(8,128)(2,1)S(1)}, bf16[2,2,2,2,64,2,128]{6,4,5,3,2,1,0:T(8,128)(2,1)S(1)}, u32[]{:S(2)}, u32[]{:S(2)}) collective-permute-start(bf16[2,2,2,2,64,2,128]{6,4,5,3,2,1,0:T(8,128)(2,1)S(1)} %pad_maximum_fusion.19), channel_id=1, source_target_pairs={{0,4},{1,5},{2,6},{3,7},{4,0},{5,1},{6,2},{7,3},{8,12},{9,13},{10,... | collective-permute-start | bytes 1572872 | tf_op jit(solution)/shard_map/ppermute | solution.py:47
  80.3 1.0 copy-start.15
  80.3 1.0 copy-start.17
  80.3 1.0 copy-start.18
  81.4 11.0 %copy-start.3 = (f32[2,2,512,128]{3,2,1,0:T(8,128)S(1)}, f32[2,2,512,128]{3,2,1,0:T(8,128)}, u32[]{:S(2)}) copy-start(f32[2,2,512,128]{3,2,1,0:T(8,128)} %param.11) | copy-start | bytes 3145732
  81.4 11.0 %copy-start.4 = (f32[2,512,128]{2,1,0:T(8,128)S(1)}, f32[2,512,128]{2,1,0:T(8,128)}, u32[]{:S(2)}) copy-start(f32[2,512,128]{2,1,0:T(8,128)} %param.10) | copy-start | bytes 1572868
  83.0 7.8 %collective-permute-start.8 = (bf16[4,2,64,128]{3,2,1,0:T(8,128)(2,1)S(1)}, bf16[4,2,64,128]{3,2,1,0:T(8,128)(2,1)S(1)}, u32[]{:S(2)}, u32[]{:S(2)}) collective-permute-start(bf16[4,2,64,128]{3,2,1,0:T(8,128)(2,1)S(1)} %convert_bitcast_fusion), channel_id=1, source_target_pairs={{0,2},{1,3},{2,0},{3,1},{4,6},{5,7},{6,4},{7,5},{8,10},{9,11},{10,... | collective-permute-start | bytes 393224 | tf_op jit(solution)/shard_map/ppermute | solution.py:47
  90.8 0.7 copy-start.16
  92.2 21.9 %collective-permute-start.9 = (bf16[2,4,2,64,128]{4,3,2,1,0:T(8,128)(2,1)}, bf16[2,4,2,64,128]{4,3,2,1,0:T(8,128)(2,1)}, u32[]{:S(2)}, u32[]{:S(2)}) collective-permute-start(bf16[2,4,2,64,128]{4,3,2,1,0:T(8,128)(2,1)} %pad_maximum_fusion.23), channel_id=1, source_target_pairs={{0,1},{1,0},{2,3},{3,2},{4,5},{5,4},{6,7},{7,6},{8,9},{9,8},{10,11... | collective-permute-start | bytes 786440 | tf_op jit(solution)/shard_map/ppermute | solution.py:47
  97.0 42.3 %collective-permute-start.16 = (f32[6,512,1]{1,2,0:T(1,128)}, f32[6,512,1]{1,2,0:T(1,128)}, u32[]{:S(2)}, u32[]{:S(2)}) collective-permute-start(f32[6,512,1]{1,2,0:T(1,128)} %copy.160), channel_id=1, source_target_pairs={{0,16},{16,32},{32,48},{48,64},{64,80},{80,96},{96,112},{112,128},... | collective-permute-start | bytes 36872 | tf_op jit(solution)/shard_map/ppermute | solution.py:16
  112.2 29.6 %collective-permute-start.17 = (f32[6,512,1]{1,2,0:T(1,128)}, f32[6,512,1]{1,2,0:T(1,128)}, u32[]{:S(2)}, u32[]{:S(2)}) collective-permute-start(f32[6,512,1]{1,2,0:T(1,128)} %copy.161), channel_id=1, source_target_pairs={{16,0},{32,16},{48,32},{64,48},{80,64},{96,80},{112,96},{128,112},... | collective-permute-start | bytes 36872 | tf_op jit(solution)/shard_map/ppermute | solution.py:19
  115.1 0.7 copy-start.13
  115.1 1.5 copy-start.14
  116.7 14.5 %collective-permute-start.10 = (bf16[2,2,4,2,64,128]{5,4,3,2,0,1:T(8,128)(2,1)}, bf16[2,2,4,2,64,128]{5,4,3,2,0,1:T(8,128)(2,1)}, u32[]{:S(2)}, u32[]{:S(2)}) collective-permute-start(bf16[2,2,4,2,64,128]{5,4,3,2,0,1:T(8,128)(2,1)} %pad_maximum_fusion.20), channel_id=1, source_target_pairs={{0,8},{1,9},{2,10},{3,11},{4,12},{5,13},{6,14},{7,15},{8,0},{9,1},... | collective-permute-start | bytes 1572872 | tf_op jit(solution)/shard_map/ppermute | solution.py:47
  132.4 0.8 copy-start.8
  132.4 1.8 copy-start.10
  134.3 26.2 %collective-permute-start.11 = (bf16[2,2,2,4,2,64,128]{6,5,4,3,1,2,0:T(8,128)(2,1)}, bf16[2,2,2,4,2,64,128]{6,5,4,3,1,2,0:T(8,128)(2,1)}, u32[]{:S(2)}, u32[]{:S(2)}) collective-permute-start(bf16[2,2,2,4,2,64,128]{6,5,4,3,1,2,0:T(8,128)(2,1)} %pad_maximum_fusion.17), channel_id=1, source_target_pairs={{0,4},{1,5},{2,6},{3,7},{4,0},{5,1},{6,2},{7,3},{8,12},{9,13},{10,... | collective-permute-start | bytes 3145736 | tf_op jit(solution)/shard_map/ppermute | solution.py:47
  144.1 7.2 %copy-start.23 = (s32[12]{0:T(128)S(1)}, s32[12]{0:T(128)}, u32[]{:S(2)}) copy-start(s32[12]{0:T(128)} %reshape.265) | copy-start | bytes 148
  145.6 8.7 %collective-permute-start.18 = (f32[6,1,130]{2,1,0:T(1,128)}, f32[6,1,130]{2,1,0:T(1,128)}, u32[]{:S(2)}, u32[]{:S(2)}) collective-permute-start(f32[6,1,130]{2,1,0:T(1,128)} %get-tuple-element.24), channel_id=1, source_target_pairs={{0,1},{1,2},{2,3},{3,4},{4,5},{5,6},{6,7},{7,8},{8,9},{9,10},{10,1... | collective-permute-start | bytes 9368 | tf_op jit(solution)/shard_map/ppermute | solution.py:16
  150.0 6.5 %collective-permute-start.19 = (f32[6,1,130]{2,1,0:T(1,128)}, f32[6,1,130]{2,1,0:T(1,128)}, u32[]{:S(2)}, u32[]{:S(2)}) collective-permute-start(f32[6,1,130]{2,1,0:T(1,128)} %get-tuple-element.23), channel_id=1, source_target_pairs={{1,0},{2,1},{3,2},{4,3},{5,4},{6,5},{7,6},{8,7},{9,8},{10,9},{11,1... | collective-permute-start | bytes 9368 | tf_op jit(solution)/shard_map/ppermute | solution.py:19
  156.5 4.0 %copy-start.9 = (bf16[1,2,2,4,2,64,128]{6,5,4,3,1,2,0:T(8,128)(2,1)S(1)}, bf16[1,2,2,4,2,64,128]{6,5,4,3,1,2,0:T(8,128)(2,1)}, u32[]{:S(2)}) copy-start(bf16[1,2,2,4,2,64,128]{6,5,4,3,1,2,0:T(8,128)(2,1)} %copy-done.8) | copy-start | bytes 1572868
  156.5 4.0 %copy-start.11 = (bf16[1,2,2,4,2,64,128]{6,5,4,3,1,2,0:T(8,128)(2,1)S(1)}, bf16[1,2,2,4,2,64,128]{6,5,4,3,1,2,0:T(8,128)(2,1)}, u32[]{:S(2)}) copy-start(bf16[1,2,2,4,2,64,128]{6,5,4,3,1,2,0:T(8,128)(2,1)} %copy-done.10) | copy-start | bytes 1572868
  166.6 4.2 %copy-start.5 = (f32[2,512,128]{2,1,0:T(8,128)S(1)}, f32[2,512,128]{2,1,0:T(8,128)}, u32[]{:S(2)}) copy-start(f32[2,512,128]{2,1,0:T(8,128)} %param.10) | copy-start | bytes 1572868
  168.1 5.0 %collective-permute-start.12 = (bf16[64,2,2,128]{3,0,1,2:T(8,128)(2,1)S(1)}, bf16[64,2,2,128]{3,0,1,2:T(8,128)(2,1)S(1)}, u32[]{:S(2)}, u32[]{:S(2)}) collective-permute-start(bf16[64,2,2,128]{3,0,1,2:T(8,128)(2,1)S(1)} %fusion.36), channel_id=1, source_target_pairs={{0,64},{16,80},{32,96},{48,112},{64,0},{80,16},{96,32},{112,48},{1... | collective-permute-start | bytes 196616 | tf_op jit(solution)/shard_map/ppermute | solution.py:47
  170.8 4.7 %copy-start.1 = (f32[6,512,1]{2,1,0:T(8,128)S(1)}, f32[6,512,1]{2,1,0:T(8,128)}, u32[]{:S(2)}) copy-start(f32[6,512,1]{2,1,0:T(8,128)} %copy.162) | copy-start | bytes 36868
  170.8 4.7 %copy-start.2 = (f32[6,512,1]{2,1,0:T(8,128)S(1)}, f32[6,512,1]{2,1,0:T(8,128)}, u32[]{:S(2)}) copy-start(f32[6,512,1]{2,1,0:T(8,128)} %copy.163) | copy-start | bytes 36868
  173.2 4.7 %collective-permute-start.13 = (bf16[2,64,2,2,128]{4,1,2,3,0:T(8,128)(2,1)S(1)}, bf16[2,64,2,2,128]{4,1,2,3,0:T(8,128)(2,1)S(1)}, u32[]{:S(2)}, u32[]{:S(2)}) collective-permute-start(bf16[2,64,2,2,128]{4,1,2,3,0:T(8,128)(2,1)S(1)} %pad_maximum_fusion.26), channel_id=1, source_target_pairs={{0,128},{16,144},{32,160},{48,176},{64,192},{80,208},{96,224},{112... | collective-permute-start | bytes 393224 | tf_op jit(solution)/shard_map/ppermute | solution.py:47
  175.5 4.6 %copy-start.7 = (f32[1,2,513,129]{3,2,1,0:T(8,128)S(1)}, f32[1,2,513,129]{3,2,1,0:T(8,128)}, u32[]{:S(2)}) copy-start(f32[1,2,513,129]{3,2,1,0:T(8,128)} %fusion.44) | copy-start | bytes 1588252
  178.0 5.9 %collective-permute-start.14 = (bf16[2,2,64,2,2,128]{5,2,3,4,1,0:T(8,128)(2,1)S(1)}, bf16[2,2,64,2,2,128]{5,2,3,4,1,0:T(8,128)(2,1)S(1)}, u32[]{:S(2)}, u32[]{:S(2)}) collective-permute-start(bf16[2,2,64,2,2,128]{5,2,3,4,1,0:T(8,128)(2,1)S(1)} %pad_maximum_fusion.24), channel_id=1, source_target_pairs={{0,32},{16,48},{32,0},{48,16},{64,96},{80,112},{96,64},{112,80},{1... | collective-permute-start | bytes 786440 | tf_op jit(solution)/shard_map/ppermute | solution.py:47
  184.0 10.1 %collective-permute-start.15 = (bf16[2,2,2,64,2,2,128]{6,3,4,5,1,0,2:T(8,128)(2,1)S(1)}, bf16[2,2,2,64,2,2,128]{6,3,4,5,1,0,2:T(8,128)(2,1)S(1)}, u32[]{:S(2)}, u32[]{:S(2)}) collective-permute-start(bf16[2,2,2,64,2,2,128]{6,3,4,5,1,0,2:T(8,128)(2,1)S(1)} %pad_maximum_fusion.21), channel_id=1, source_target_pairs={{0,16},{16,0},{32,48},{48,32},{64,80},{80,64},{96,112},{112,96},{1... | collective-permute-start | bytes 1572872 | tf_op jit(solution)/shard_map/ppermute | solution.py:47
  190.3 1.3 copy-start.22
  195.3 1.5 copy-start.19
  197.5 2.8 %copy-start.6 = (f32[2,512,128]{2,1,0:T(8,128)S(1)}, f32[2,512,128]{2,1,0:T(8,128)}, u32[]{:S(2)}) copy-start(f32[2,512,128]{2,1,0:T(8,128)} %param.10) | copy-start | bytes 1572868

commit v9 on v3

--- a/solution.py
+++ b/solution.py
@@ -50,7 +50,7 @@
         high = jnp.where(mine == 0, got, block)
         block = jnp.stack([low, high], axis=place)
         done.append(bit)
-    return block.reshape(count, *block.shape[len(bits):])
+    return block.reshape(-1, *block.shape[len(bits):])
 
 
 def on_device(
@@ -119,25 +119,32 @@
     chosen = jnp.take(all_rows, foot_mine, axis=2)
     back = jnp.einsum("cpjfv,jfuv->cjpu", chosen, kern_mine, preferred_element_type=jnp.float32)
     back_b = back.astype(jnp.bfloat16)
-    piece = doubling_gather(jnp.moveaxis(back_b, 2, 0), "az", (4, 8, 2, 1))
-    piece = jnp.moveaxis(piece.reshape(-1, *piece.shape[2:]), 0, 2)
-    weight_re = col_mine[0].T[..., None]
-    weight_im = col_mine[1].T[..., None]
-    back_re = piece[0].astype(jnp.float32)
-    back_im = piece[1].astype(jnp.float32)
-    mixed_re = (weight_re * back_re + weight_im * back_im).astype(jnp.bfloat16)
-    mixed_im = (weight_re * back_im - weight_im * back_re).astype(jnp.bfloat16)
-    part_sre = steer_re
-    part_sim = steer_im
-    grad_re = jnp.einsum("pjh,jpu->jhu", part_sre, mixed_re, preferred_element_type=jnp.float32)
-    grad_re = grad_re + jnp.einsum(
-        "pjh,jpu->jhu", part_sim, mixed_im, preferred_element_type=jnp.float32
-    )
-    grad_im = jnp.einsum("pjh,jpu->jhu", part_sre, mixed_im, preferred_element_type=jnp.float32)
-    grad_im = grad_im - jnp.einsum(
-        "pjh,jpu->jhu", part_sim, mixed_re, preferred_element_type=jnp.float32
-    )
-    adjoint = jnp.stack([grad_re, grad_im])
+    near = doubling_gather(jnp.moveaxis(back_b, 2, 0), "az", (4, 8, 2))
+    core = az_index % 2
+    far = lax.ppermute(near, "az", [(i, i ^ 1) for i in range(az_count)])
+    block_pulses = back_b.shape[2]
+    steer_split = row_steer.reshape(2, az_count // 2, 2, block_pulses, tiles_dev, tile_rows)
+    col_split = col_mine.reshape(2, az_count // 2, 2, block_pulses, tiles_dev)
+
+    def partial_adjoint(blocks, side):
+        piece = jnp.transpose(blocks, (2, 3, 0, 1, 4))
+        steer = lax.dynamic_index_in_dim(steer_split, side, 2, keepdims=False)
+        cols = lax.dynamic_index_in_dim(col_split, side, 2, keepdims=False)
+        weight_re = jnp.transpose(cols[0], (2, 0, 1))[..., None]
+        weight_im = jnp.transpose(cols[1], (2, 0, 1))[..., None]
+        back_re = piece[0].astype(jnp.float32)
+        back_im = piece[1].astype(jnp.float32)
+        mixed_re = (weight_re * back_re + weight_im * back_im).astype(jnp.bfloat16)
+        mixed_im = (weight_re * back_im - weight_im * back_re).astype(jnp.bfloat16)
+        grad_re = jnp.einsum(
+            "bpjh,jbpu->jhu", steer[0], mixed_re, preferred_element_type=jnp.float32
+        ) + jnp.einsum("bpjh,jbpu->jhu", steer[1], mixed_im, preferred_element_type=jnp.float32)
+        grad_im = jnp.einsum(
+            "bpjh,jbpu->jhu", steer[0], mixed_im, preferred_element_type=jnp.float32
+        ) - jnp.einsum("bpjh,jbpu->jhu", steer[1], mixed_re, preferred_element_type=jnp.float32)
+        return jnp.stack([grad_re, grad_im])
+
+    adjoint = partial_adjoint(near, core) + partial_adjoint(far, 1 - core)
     adjoint = adjoint.reshape(2, strip_rows, columns)
     stacked = jnp.concatenate([image, tv_dual.reshape(4, strip_rows, columns)], axis=0)
     padded = padded_2(stacked, (("az", 2), ("tile", 1)), 1)

time: 193 us -> 228 us (1.18)
  local copies, waits for them, and re-layouts: 24.5 us -> 47 us
  other arithmetic: 23.3 us -> 37.3 us
  starting transfers between devices: 51.5 us -> 40.5 us
  waiting for transfers between devices: 78.2 us -> 83 us
  matrix products: 13.2 us -> 15.9 us
    ppermute x2, waiting for transfers between devices: 0.01 us -> 11.7 us  [padded_2(): lax.ppermute(lax.slice_in_dim(block, block.shape[dim] - width, None, axis...]
    ppermute x12 -> x11, starting transfers between devices: 28.5 us -> 17.2 us  [doubling_gather(): got = lax.ppermute(block, axis, pairs)]
    unnamed x68 -> x103, local copies, waits for them, and re-layouts: 5.42 us -> 14.8 us
    another operation x24 -> x22, other arithmetic: 3.52 us -> 10.3 us  [doubling_gather(): block = jnp.stack([low, high], axis=place)]
    ppermute x12 -> x11, waiting for transfers between devices: 48.6 us -> 42.4 us  [doubling_gather(): got = lax.ppermute(block, axis, pairs)]
    another operation x0 -> x5, local copies, waits for them, and re-layouts: none -> 5.51 us  [the longest x4 4.08 us: partial_adjoint(): return jnp.stack([grad_re, grad_im])]
    ppermute x0 -> x1, starting transfers between devices: none -> 5.13 us  [on_device(): far = lax.ppermute(near, 'az', [(i, i ^ 1) for i in range(az_count)])]
    ppermute x2, starting transfers between devices: 14.7 us -> 10 us  [padded_2(): lax.ppermute(lax.slice_in_dim(block, block.shape[dim] - width, None, axis...]
  transfers between devices with their start and end apart: 20 -> 20, of which waited for: 15 -> 14; matrix products, arithmetic and copies ran while one was open for 13% -> 24% of each run, Pallas kernels for 0% -> 0%
where the time goes in v9:
time: 228 us; the launch traced here: 225 us
  waiting for transfers between devices  83 us (36%)
  local copies, waits for them, and re-layouts  47 us (21%)
  starting transfers between devices  40.5 us (18%)
  other arithmetic  37.3 us (16%)
  matrix products  15.9 us (7%)
    ppermute x11, waiting for transfers between devices, doubling_gather(): got = lax.ppermute(block, axis, pairs)  42.4 us
    ppermute x4, waiting for transfers between devices, halving_sum(): blocks = keep + lax.ppermute(send, axis, pairs)  24.2 us
    ppermute x11, starting transfers between devices, doubling_gather(): got = lax.ppermute(block, axis, pairs)  17.2 us
    unnamed x103, local copies, waits for them, and re-layouts  14.8 us
    ppermute x2, waiting for transfers between devices, padded_2(): lax.ppermute(lax.slice_in_dim(block, block.shape[dim] - width, None, axis...  11.7 us
    another operation x22, other arithmetic, doubling_gather(): block = jnp.stack([low, high], axis=place)  10.3 us
    ppermute x2, starting transfers between devices, padded_2(): lax.ppermute(lax.slice_in_dim(block, block.shape[dim] - width, None, axis...  10 us
    ppermute x1, starting transfers between devices, on_device(): far = lax.ppermute(near, 'az', [(i, i ^ 1) for i in range(az_count)])  5.13 us
  transfers between devices with their start and end apart: 20, of which 14 were waited for; matrix products, arithmetic and copies ran while one was open for 24% of the time, Pallas kernels for 0%

profile of v9, /device:TPU:1, one launch (start us, length us, event | category | flops | bytes accessed | tf_op | source)
XLA Modules:
  0.0 225.1 jit_solution(10606522486569916732)
XLA Ops:
  0.7 1.9 copy.158
  5.1 1.9 multiply_subtract_fusion
  7.0 1.5 copy.169
  8.5 2.5 %copy.170 = f32[1024,2,128]{2,0,1:T(8,128)} copy(f32[1024,2,128]{0,2,1:T(8,128)} %get-tuple-element.19) | data formatting | bytes 2097152 | tf_op jit(solution)/shard_map/add | solution.py:91
  11.1 1.4 pad_maximum_fusion
  13.8 3.2 %collective-permute-start = (f32[2,2,2,2,64,2,128]{6,4,5,3,2,1,0:T(8,128)}, f32[2,2,2,2,64,2,128]{6,4,5,3,2,1,0:T(8,128)}, u32[]{:S(2)}, u32[]{:S(2)}) collective-permute-start(f32[2,2,2,2,64,2,128]{6,4,5,3,2,1,0:T(8,128)} %bitcast.299), channel_id=1, source_target_pairs={{0,16},{16,0},{32,48},{48,32},{64,80},{80,64},{96,112},{112,96},{1... | collective-permute-start | bytes 3145736 | tf_op jit(solution)/shard_map/ppermute | solution.py:36
  17.0 2.6 %collective-permute-done = f32[2,2,2,2,64,2,128]{6,4,5,3,2,1,0:T(8,128)} collective-permute-done((f32[2,2,2,2,64,2,128]{6,4,5,3,2,1,0:T(8,128)}, f32[2,2,2,2,64,2,128]{6,4,5,3,2,1,0:T(8,128)}, u32[]{:S(2)}, u32[]{:S(2)}) %collective-permute-start) | collective-permute-done | bytes 1048608 | tf_op jit(solution)/shard_map/ppermute | solution.py:36
  22.2 13.2 %collective-permute-done.1 = f32[2,2,2,64,2,128]{5,3,4,2,1,0:T(8,128)} collective-permute-done((f32[2,2,2,64,2,128]{5,3,4,2,1,0:T(8,128)S(1)}, f32[2,2,2,64,2,128]{5,3,4,2,1,0:T(8,128)}, u32[]{:S(2)}, u32[]{:S(2)}) %collective-permute-start.1) | collective-permute-done | bytes 524320 | tf_op jit(solution)/shard_map/ppermute | solution.py:36
  37.4 6.9 %collective-permute-done.2 = f32[2,2,64,2,128]{4,2,3,1,0:T(8,128)} collective-permute-done((f32[2,2,64,2,128]{4,2,3,1,0:T(8,128)}, f32[2,2,64,2,128]{4,2,3,1,0:T(8,128)}, u32[]{:S(2)}, u32[]{:S(2)}) %collective-permute-start.2) | collective-permute-done | bytes 262176 | tf_op jit(solution)/shard_map/ppermute | solution.py:36
  46.0 1.6 collective-permute-start.3
  48.5 1.6 copy.203
  50.1 1.5 collective-permute-done.3
  51.6 1.5 fusion.66
  53.1 5.2 %collective-permute-start.4 = (bf16[2,64,2,128]{3,1,2,0:T(8,128)(2,1)}, bf16[2,64,2,128]{3,1,2,0:T(8,128)(2,1)S(1)}, u32[]{:S(2)}, u32[]{:S(2)}) collective-permute-start(bf16[2,64,2,128]{3,1,2,0:T(8,128)(2,1)} %fusion.66), channel_id=1, source_target_pairs={{0,2},{1,3},{2,0},{3,1},{4,6},{5,7},{6,4},{7,5},{8,10},{9,11},{10,... | collective-permute-start | bytes 196616 | tf_op jit(solution)/shard_map/ppermute | solution.py:47
  58.3 1.4 pad_maximum_fusion.31
  59.7 6.5 %collective-permute-start.16 = (f32[6,512,1]{1,2,0:T(1,128)}, f32[6,512,1]{1,2,0:T(1,128)S(1)}, u32[]{:S(2)}, u32[]{:S(2)}) collective-permute-start(f32[6,512,1]{1,2,0:T(1,128)} %get-tuple-element.26), channel_id=1, source_target_pairs={{0,16},{16,32},{32,48},{48,64},{64,80},{80,96},{96,112},{112,128},... | collective-permute-start | bytes 36872 | tf_op jit(solution)/shard_map/ppermute | solution.py:16
  66.3 1.9 collective-permute-start.17
  73.1 3.0 %collective-permute-done.5 = bf16[2,2,64,2,128]{4,2,3,1,0:T(8,128)(2,1)} collective-permute-done((bf16[2,2,64,2,128]{4,2,3,1,0:T(8,128)(2,1)S(1)}, bf16[2,2,64,2,128]{4,2,3,1,0:T(8,128)(2,1)}, u32[]{:S(2)}, u32[]{:S(2)}) %collective-permute-start.5) | collective-permute-done | bytes 131104 | tf_op jit(solution)/shard_map/ppermute | solution.py:47
  78.4 2.9 %collective-permute-start.6 = (bf16[2,2,2,64,2,128]{5,3,4,2,1,0:T(8,128)(2,1)}, bf16[2,2,2,64,2,128]{5,3,4,2,1,0:T(8,128)(2,1)}, u32[]{:S(2)}, u32[]{:S(2)}) collective-permute-start(bf16[2,2,2,64,2,128]{5,3,4,2,1,0:T(8,128)(2,1)} %pad_maximum_fusion.25), channel_id=1, source_target_pairs={{0,8},{1,9},{2,10},{3,11},{4,12},{5,13},{6,14},{7,15},{8,0},{9,1},... | collective-permute-start | bytes 786440 | tf_op jit(solution)/shard_map/ppermute | solution.py:47
  87.2 1.4 collective-permute-start.7
  88.7 11.2 %collective-permute-done.7 = bf16[2,2,2,2,64,2,128]{6,4,5,3,2,1,0:T(8,128)(2,1)S(1)} collective-permute-done((bf16[2,2,2,2,64,2,128]{6,4,5,3,2,1,0:T(8,128)(2,1)S(1)}, bf16[2,2,2,2,64,2,128]{6,4,5,3,2,1,0:T(8,128)(2,1)S(1)}, u32[]{:S(2)}, u32[]{:S(2)}) %collective-permute-start.7) | collective-permute-done | bytes 524320 | tf_op jit(solution)/shard_map/ppermute | solution.py:47
  101.1 1.6 fusion.19
  103.6 11.5 %collective-permute-done.8 = bf16[4,2,64,128]{3,2,1,0:T(8,128)(2,1)S(1)} collective-permute-done((bf16[4,2,64,128]{3,2,1,0:T(8,128)(2,1)S(1)}, bf16[4,2,64,128]{3,2,1,0:T(8,128)(2,1)S(1)}, u32[]{:S(2)}, u32[]{:S(2)}) %collective-permute-start.8) | collective-permute-done | bytes 131104 | tf_op jit(solution)/shard_map/ppermute | solution.py:47
  116.5 1.9 collective-permute-start.9
  121.6 1.6 dynamic-slice_reduce_fusion
  123.1 1.4 reshape_squeeze.3
  125.8 1.4 constant_dynamic-slice_fusion
  128.3 2.9 %collective-permute-start.10 = (bf16[2,2,4,2,64,128]{5,4,3,2,0,1:T(8,128)(2,1)S(1)}, bf16[2,2,4,2,64,128]{5,4,3,2,0,1:T(8,128)(2,1)S(1)}, u32[]{:S(2)}, u32[]{:S(2)}) collective-permute-start(bf16[2,2,4,2,64,128]{5,4,3,2,0,1:T(8,128)(2,1)S(1)} %pad_maximum_fusion.19), channel_id=1, source_target_pairs={{0,8},{1,9},{2,10},{3,11},{4,12},{5,13},{6,14},{7,15},{8,0},{9,1},... | collective-permute-start | bytes 1572872 | tf_op jit(solution)/shard_map/ppermute | solution.py:47
  132.6 9.8 %collective-permute-done.10 = bf16[2,2,4,2,64,128]{5,4,3,2,0,1:T(8,128)(2,1)S(1)} collective-permute-done((bf16[2,2,4,2,64,128]{5,4,3,2,0,1:T(8,128)(2,1)S(1)}, bf16[2,2,4,2,64,128]{5,4,3,2,0,1:T(8,128)(2,1)S(1)}, u32[]{:S(2)}, u32[]{:S(2)}) %collective-permute-start.10) | collective-permute-done | bytes 524320 | tf_op jit(solution)/shard_map/ppermute | solution.py:47
  144.8 1.8 pad_maximum_fusion.21
  146.6 3.5 %collective-permute-start.18 = (f32[6,1,130]{1,2,0:T(8,128)}, f32[6,1,130]{1,2,0:T(8,128)}, u32[]{:S(2)}, u32[]{:S(2)}) collective-permute-start(f32[6,1,130]{1,2,0:T(8,128)} %get-tuple-element.25), channel_id=1, source_target_pairs={{0,1},{1,2},{2,3},{3,4},{4,5},{5,6},{6,7},{7,8},{8,9},{9,10},{10,1... | collective-permute-start | bytes 9368 | tf_op jit(solution)/shard_map/ppermute | solution.py:16
  155.2 11.7 %collective-permute-done.18 = f32[6,1,130]{1,2,0:T(8,128)} collective-permute-done((f32[6,1,130]{1,2,0:T(8,128)}, f32[6,1,130]{1,2,0:T(8,128)}, u32[]{:S(2)}, u32[]{:S(2)}) %collective-permute-start.18) | collective-permute-done | bytes 3152 | tf_op jit(solution)/shard_map/ppermute | solution.py:16
  166.9 4.7 %collective-permute-done.19 = f32[6,1,130]{1,2,0:T(8,128)} collective-permute-done((f32[6,1,130]{1,2,0:T(8,128)}, f32[6,1,130]{1,2,0:T(8,128)}, u32[]{:S(2)}, u32[]{:S(2)}) %collective-permute-start.19) | collective-permute-done | bytes 3152 | tf_op jit(solution)/shard_map/ppermute | solution.py:19
  171.5 1.6 pad_maximum_fusion.2
  173.2 1.8 fusion.37
  175.0 1.5 fusion.40
  178.0 1.5 select_bitcast_fusion.1
  179.7 1.5 copy.181
  181.2 3.1 %gather_fusion.1 = bf16[12,2,64,128]{3,2,1,0:T(8,128)(2,1)} fusion(bf16[2,64,64,128]{3,1,0,2:T(8,128)(2,1)} %bitcast.322, s32[1024]{0:T(1024)} %pad_clamp_fusion), kind=kCustom, calls=%fused_computation.1 | custom fusion | bytes 786480 | tf_op jit(solution)/shard_map/jit(_take)/gather | solution.py:119
  184.3 1.6 fusion.27
  186.1 4.5 %collective-permute-done.12 = bf16[64,2,2,128]{3,0,1,2:T(8,128)(2,1)S(1)} collective-permute-done((bf16[64,2,2,128]{3,0,1,2:T(8,128)(2,1)S(1)}, bf16[64,2,2,128]{3,0,1,2:T(8,128)(2,1)S(1)}, u32[]{:S(2)}, u32[]{:S(2)}) %collective-permute-start.12) | collective-permute-done | bytes 65568 | tf_op jit(solution)/shard_map/ppermute | solution.py:47
  196.5 2.4 %fusion.34 = (f32[2,513,129]{1,2,0:T(8,128)}, f32[2,513,129]{1,2,0:T(8,128)}) fusion(f32[2,2,513,129]{2,3,1,0:T(8,128)} %copy-done.6, pred[513]{0:T(1024)(128)(4,1)S(1)} %get-tuple-element.67, pred[129]{0:T(512)(128)(4,1)S(1)} %copy-done.43), kind=kLoop, calls=%fused_computation.58 | loop fusion | flops 264708 | bytes 2118306 | tf_op jit(solution)/shard_map/jit(_where)/select_n | solution.py:169
  199.8 1.9 collective-permute-done.14
  201.8 5.1 %collective-permute-start.15 = (bf16[8,64,2,2,128]{4,1,3,2,0:T(8,128)(2,1)S(1)}, bf16[8,64,2,2,128]{4,1,3,2,0:T(8,128)(2,1)}, u32[]{:S(2)}, u32[]{:S(2)}) collective-permute-start(bf16[8,64,2,2,128]{4,1,3,2,0:T(8,128)(2,1)S(1)} %bitcast.323), channel_id=1, source_target_pairs={{0,16},{16,0},{32,48},{48,32},{64,80},{80,64},{96,112},{112,96},{1... | collective-permute-start | bytes 1572872 | tf_op jit(solution)/shard_map/ppermute | solution.py:124
  209.6 2.0 fusion.23
  216.9 1.8 copy.201
  218.7 2.1 fusion.25
  221.9 2.2 fusion.51
  (195 shorter events, 60.1 us)
Async XLA Ops:
  0.6 100.3 %copy-start = (bf16[8,128,128]{2,1,0:T(8,128)(2,1)S(1)}, bf16[8,128,128]{2,1,0:T(8,128)(2,1)}, u32[]{:S(2)}) copy-start(bf16[8,128,128]{2,1,0:T(8,128)(2,1)} %param.16) | copy-start | bytes 786436
  13.8 5.9 %collective-permute-start = (f32[2,2,2,2,64,2,128]{6,4,5,3,2,1,0:T(8,128)}, f32[2,2,2,2,64,2,128]{6,4,5,3,2,1,0:T(8,128)}, u32[]{:S(2)}, u32[]{:S(2)}) collective-permute-start(f32[2,2,2,2,64,2,128]{6,4,5,3,2,1,0:T(8,128)} %bitcast.299), channel_id=1, source_target_pairs={{0,16},{16,0},{32,48},{48,32},{64,80},{80,64},{96,112},{112,96},{1... | collective-permute-start | bytes 3145736 | tf_op jit(solution)/shard_map/ppermute | solution.py:36
  22.0 25.5 %copy-start.19 = (f32[2,512,128]{2,1,0:T(8,128)S(1)}, f32[2,512,128]{2,1,0:T(8,128)}, u32[]{:S(2)}) copy-start(f32[2,512,128]{2,1,0:T(8,128)} %param.10) | copy-start | bytes 1572868
  22.0 13.3 %collective-permute-start.1 = (f32[2,2,2,64,2,128]{5,3,4,2,1,0:T(8,128)S(1)}, f32[2,2,2,64,2,128]{5,3,4,2,1,0:T(8,128)}, u32[]{:S(2)}, u32[]{:S(2)}) collective-permute-start(f32[2,2,2,64,2,128]{5,3,4,2,1,0:T(8,128)S(1)} %dynamic-slice_bitcast_fusion.4), channel_id=1, source_target_pairs={{0,128},{16,144},{32,160},{48,176},{64,192},{80,208},{96,224},{112... | collective-permute-start | bytes 1572872 | tf_op jit(solution)/shard_map/ppermute | solution.py:36
  37.4 6.9 %collective-permute-start.2 = (f32[2,2,64,2,128]{4,2,3,1,0:T(8,128)}, f32[2,2,64,2,128]{4,2,3,1,0:T(8,128)}, u32[]{:S(2)}, u32[]{:S(2)}) collective-permute-start(f32[2,2,64,2,128]{4,2,3,1,0:T(8,128)} %dynamic-slice_bitcast_fusion.13), channel_id=1, source_target_pairs={{0,32},{16,48},{32,0},{48,16},{64,96},{80,112},{96,64},{112,80},{1... | collective-permute-start | bytes 786440 | tf_op jit(solution)/shard_map/ppermute | solution.py:36
  46.0 5.6 %collective-permute-start.3 = (f32[2,64,2,128]{3,1,0,2:T(8,128)}, f32[2,64,2,128]{3,1,0,2:T(8,128)}, u32[]{:S(2)}, u32[]{:S(2)}) collective-permute-start(f32[2,64,2,128]{3,1,0,2:T(8,128)} %bitcast.300), channel_id=1, source_target_pairs={{0,64},{16,80},{32,96},{48,112},{64,0},{80,16},{96,32},{112,48},{1... | collective-permute-start | bytes 393224 | tf_op jit(solution)/shard_map/ppermute | solution.py:36
  48.5 22.5 %copy-start.38 = (s32[32,1,6]{0,1,2:T(1,128)S(1)}, s32[32,1,6]{0,1,2:T(1,128)}, u32[]{:S(2)}) copy-start(s32[32,1,6]{0,1,2:T(1,128)} %param.17) | copy-start | bytes 2308
  53.1 15.1 %collective-permute-start.4 = (bf16[2,64,2,128]{3,1,2,0:T(8,128)(2,1)}, bf16[2,64,2,128]{3,1,2,0:T(8,128)(2,1)S(1)}, u32[]{:S(2)}, u32[]{:S(2)}) collective-permute-start(bf16[2,64,2,128]{3,1,2,0:T(8,128)(2,1)} %fusion.66), channel_id=1, source_target_pairs={{0,2},{1,3},{2,0},{3,1},{4,6},{5,7},{6,4},{7,5},{8,10},{9,11},{10,... | collective-permute-start | bytes 196616 | tf_op jit(solution)/shard_map/ppermute | solution.py:47
  59.7 85.1 %collective-permute-start.16 = (f32[6,512,1]{1,2,0:T(1,128)}, f32[6,512,1]{1,2,0:T(1,128)S(1)}, u32[]{:S(2)}, u32[]{:S(2)}) collective-permute-start(f32[6,512,1]{1,2,0:T(1,128)} %get-tuple-element.26), channel_id=1, source_target_pairs={{0,16},{16,32},{32,48},{48,64},{64,80},{80,96},{96,112},{112,128},... | collective-permute-start | bytes 36872 | tf_op jit(solution)/shard_map/ppermute | solution.py:16
  66.3 78.6 %collective-permute-start.17 = (f32[6,512,1]{1,2,0:T(1,128)}, f32[6,512,1]{1,2,0:T(1,128)}, u32[]{:S(2)}, u32[]{:S(2)}) collective-permute-start(f32[6,512,1]{1,2,0:T(1,128)} %get-tuple-element.27), channel_id=1, source_target_pairs={{16,0},{32,16},{48,32},{64,48},{80,64},{96,80},{112,96},{128,112},... | collective-permute-start | bytes 36872 | tf_op jit(solution)/shard_map/ppermute | solution.py:19
  69.8 6.3 %collective-permute-start.5 = (bf16[2,2,64,2,128]{4,2,3,1,0:T(8,128)(2,1)S(1)}, bf16[2,2,64,2,128]{4,2,3,1,0:T(8,128)(2,1)}, u32[]{:S(2)}, u32[]{:S(2)}) collective-permute-start(bf16[2,2,64,2,128]{4,2,3,1,0:T(8,128)(2,1)S(1)} %pad_maximum_fusion.28), channel_id=1, source_target_pairs={{0,1},{1,0},{2,3},{3,2},{4,5},{5,4},{6,7},{7,6},{8,9},{9,8},{10,11... | collective-permute-start | bytes 393224 | tf_op jit(solution)/shard_map/ppermute | solution.py:47
  78.4 7.7 %collective-permute-start.6 = (bf16[2,2,2,64,2,128]{5,3,4,2,1,0:T(8,128)(2,1)}, bf16[2,2,2,64,2,128]{5,3,4,2,1,0:T(8,128)(2,1)}, u32[]{:S(2)}, u32[]{:S(2)}) collective-permute-start(bf16[2,2,2,64,2,128]{5,3,4,2,1,0:T(8,128)(2,1)} %pad_maximum_fusion.25), channel_id=1, source_target_pairs={{0,8},{1,9},{2,10},{3,11},{4,12},{5,13},{6,14},{7,15},{8,0},{9,1},... | collective-permute-start | bytes 786440 | tf_op jit(solution)/shard_map/ppermute | solution.py:47
  85.8 2.8 %copy-start.37 = (s32[32,1,6]{0,2,1:T(8,128)S(1)}, s32[32,1,6]{0,2,1:T(8,128)}, u32[]{:S(2)}) copy-start(s32[32,1,6]{0,2,1:T(8,128)} %copy.287) | copy-start | bytes 2308
  85.8 2.8 %copy-start.45 = (s32[4]{0:T(128)S(1)}, s32[4]{0:T(128)}, u32[]{:S(2)}) copy-start(s32[4]{0:T(128)} %iota_add_fusion.2) | copy-start | bytes 52
  85.8 2.9 %copy-start.46 = (s32[64]{0:T(128)S(1)}, s32[64]{0:T(128)}, u32[]{:S(2)}) copy-start(s32[64]{0:T(128)} %param.19) | copy-start | bytes 772
  87.2 12.7 %collective-permute-start.7 = (bf16[2,2,2,2,64,2,128]{6,4,5,3,2,1,0:T(8,128)(2,1)S(1)}, bf16[2,2,2,2,64,2,128]{6,4,5,3,2,1,0:T(8,128)(2,1)S(1)}, u32[]{:S(2)}, u32[]{:S(2)}) collective-permute-start(bf16[2,2,2,2,64,2,128]{6,4,5,3,2,1,0:T(8,128)(2,1)S(1)} %pad_maximum_fusion.18), channel_id=1, source_target_pairs={{0,4},{1,5},{2,6},{3,7},{4,0},{5,1},{6,2},{7,3},{8,12},{9,13},{10,... | collective-permute-start | bytes 1572872 | tf_op jit(solution)/shard_map/ppermute | solution.py:47
  102.7 12.5 %copy-start.16 = (f32[2,64,4,128]{3,1,0,2:T(8,128)}, f32[2,64,4,128]{3,1,0,2:T(8,128)S(1)}, u32[]{:S(2)}) copy-start(f32[2,64,4,128]{3,1,0,2:T(8,128)S(1)} %fusion.19) | copy-start | bytes 786436
  102.7 12.4 %collective-permute-start.8 = (bf16[4,2,64,128]{3,2,1,0:T(8,128)(2,1)S(1)}, bf16[4,2,64,128]{3,2,1,0:T(8,128)(2,1)S(1)}, u32[]{:S(2)}, u32[]{:S(2)}) collective-permute-start(bf16[4,2,64,128]{3,2,1,0:T(8,128)(2,1)S(1)} %convert_bitcast_fusion), channel_id=1, source_target_pairs={{0,2},{1,3},{2,0},{3,1},{4,6},{5,7},{6,4},{7,5},{8,10},{9,11},{10,... | collective-permute-start | bytes 393224 | tf_op jit(solution)/shard_map/ppermute | solution.py:47
  116.5 10.6 %collective-permute-start.9 = (bf16[2,4,2,64,128]{4,3,2,1,0:T(8,128)(2,1)}, bf16[2,4,2,64,128]{4,3,2,1,0:T(8,128)(2,1)}, u32[]{:S(2)}, u32[]{:S(2)}) collective-permute-start(bf16[2,4,2,64,128]{4,3,2,1,0:T(8,128)(2,1)} %pad_maximum_fusion.26), channel_id=1, source_target_pairs={{0,1},{1,0},{2,3},{3,2},{4,5},{5,4},{6,7},{7,6},{8,9},{9,8},{10,11... | collective-permute-start | bytes 786440 | tf_op jit(solution)/shard_map/ppermute | solution.py:47
  124.6 7.3 %copy-start.39 = (pred[513]{0:T(1024)(128)(4,1)S(1)}, pred[513]{0:T(1024)(128)(4,1)}, u32[]{:S(2)}) copy-start(pred[513]{0:T(1024)(128)(4,1)} %get-tuple-element.66) | copy-start | bytes 1543
  128.3 14.1 %collective-permute-start.10 = (bf16[2,2,4,2,64,128]{5,4,3,2,0,1:T(8,128)(2,1)S(1)}, bf16[2,2,4,2,64,128]{5,4,3,2,0,1:T(8,128)(2,1)S(1)}, u32[]{:S(2)}, u32[]{:S(2)}) collective-permute-start(bf16[2,2,4,2,64,128]{5,4,3,2,0,1:T(8,128)(2,1)S(1)} %pad_maximum_fusion.19), channel_id=1, source_target_pairs={{0,8},{1,9},{2,10},{3,11},{4,12},{5,13},{6,14},{7,15},{8,0},{9,1},... | collective-permute-start | bytes 1572872 | tf_op jit(solution)/shard_map/ppermute | solution.py:47
  131.2 42.0 %copy-start.42 = (pred[129]{0:T(512)(128)(4,1)}, pred[129]{0:T(512)(128)(4,1)S(1)}, u32[]{:S(2)}) copy-start(pred[129]{0:T(512)(128)(4,1)S(1)} %get-tuple-element.64) | copy-start | bytes 391
  132.6 12.2 %copy-start.1 = (f32[2,512,128]{1,2,0:T(8,128)S(1)}, f32[2,512,128]{1,2,0:T(8,128)}, u32[]{:S(2)}) copy-start(f32[2,512,128]{1,2,0:T(8,128)} %copy.205) | copy-start | bytes 1572868
  142.5 4.1 %copy-start.11 = (bf16[1,2,2,4,2,64,128]{6,5,4,3,1,2,0:T(8,128)(2,1)}, bf16[1,2,2,4,2,64,128]{6,5,4,3,1,2,0:T(8,128)(2,1)S(1)}, u32[]{:S(2)}) copy-start(bf16[1,2,2,4,2,64,128]{6,5,4,3,1,2,0:T(8,128)(2,1)S(1)} %get-tuple-element.30) | copy-start | bytes 1572868
  142.5 4.1 %copy-start.13 = (bf16[1,2,2,4,2,64,128]{6,5,4,3,1,2,0:T(8,128)(2,1)}, bf16[1,2,2,4,2,64,128]{6,5,4,3,1,2,0:T(8,128)(2,1)S(1)}, u32[]{:S(2)}) copy-start(bf16[1,2,2,4,2,64,128]{6,5,4,3,1,2,0:T(8,128)(2,1)S(1)} %get-tuple-element.31) | copy-start | bytes 1572868
  142.5 8.9 %copy-start.44 = (s32[12]{0:T(128)S(1)}, s32[12]{0:T(128)}, u32[]{:S(2)}) copy-start(s32[12]{0:T(128)} %reshape.221) | copy-start | bytes 148
  143.7 9.1 %copy-start.36 = (f32[1,8,1,64,2]{3,2,1,4,0:T(1,128)S(1)}, f32[1,8,1,64,2]{3,2,1,4,0:T(1,128)}, u32[]{:S(2)}) copy-start(f32[1,8,1,64,2]{3,2,1,4,0:T(1,128)} %get-tuple-element.60) | copy-start | bytes 12292
  143.7 9.7 %copy-start.35 = (f32[1,8,1,64,2]{3,2,1,4,0:T(1,128)S(1)}, f32[1,8,1,64,2]{3,2,1,4,0:T(1,128)}, u32[]{:S(2)}) copy-start(f32[1,8,1,64,2]{3,2,1,4,0:T(1,128)} %get-tuple-element.62) | copy-start | bytes 12292
  143.7 10.3 %copy-start.34 = (f32[1,8,1,64,2]{3,2,1,4,0:T(1,128)S(1)}, f32[1,8,1,64,2]{3,2,1,4,0:T(1,128)}, u32[]{:S(2)}) copy-start(f32[1,8,1,64,2]{3,2,1,4,0:T(1,128)} %get-tuple-element.61) | copy-start | bytes 12292
  143.7 10.9 %copy-start.33 = (f32[1,8,1,64,2]{3,2,1,4,0:T(1,128)S(1)}, f32[1,8,1,64,2]{3,2,1,4,0:T(1,128)}, u32[]{:S(2)}) copy-start(f32[1,8,1,64,2]{3,2,1,4,0:T(1,128)} %get-tuple-element.63) | copy-start | bytes 12292
  143.7 33.7 %collective-permute-start.11 = (bf16[2,2,2,4,2,64,128]{6,5,4,3,1,2,0:T(8,128)(2,1)}, bf16[2,2,2,4,2,64,128]{6,5,4,3,1,2,0:T(8,128)(2,1)}, u32[]{:S(2)}, u32[]{:S(2)}) collective-permute-start(bf16[2,2,2,4,2,64,128]{6,5,4,3,1,2,0:T(8,128)(2,1)} %pad_maximum_fusion.8), channel_id=1, source_target_pairs={{0,4},{1,5},{2,6},{3,7},{4,0},{5,1},{6,2},{7,3},{8,12},{9,13},{10,... | collective-permute-start | bytes 3145736 | tf_op jit(solution)/shard_map/ppermute | solution.py:47
  146.6 20.3 %collective-permute-start.18 = (f32[6,1,130]{1,2,0:T(8,128)}, f32[6,1,130]{1,2,0:T(8,128)}, u32[]{:S(2)}, u32[]{:S(2)}) collective-permute-start(f32[6,1,130]{1,2,0:T(8,128)} %get-tuple-element.25), channel_id=1, source_target_pairs={{0,1},{1,2},{2,3},{3,4},{4,5},{5,6},{6,7},{7,8},{8,9},{9,10},{10,1... | collective-permute-start | bytes 9368 | tf_op jit(solution)/shard_map/ppermute | solution.py:16
  150.1 21.4 %collective-permute-start.19 = (f32[6,1,130]{1,2,0:T(8,128)}, f32[6,1,130]{1,2,0:T(8,128)}, u32[]{:S(2)}, u32[]{:S(2)}) collective-permute-start(f32[6,1,130]{1,2,0:T(8,128)} %get-tuple-element.24), channel_id=1, source_target_pairs={{1,0},{2,1},{3,2},{4,3},{5,4},{6,5},{7,6},{8,7},{9,8},{10,9},{11,1... | collective-permute-start | bytes 9368 | tf_op jit(solution)/shard_map/ppermute | solution.py:19
  152.8 20.4 %copy-start.2 = (f32[2,512,128]{1,2,0:T(8,128)S(1)}, f32[2,512,128]{1,2,0:T(8,128)}, u32[]{:S(2)}) copy-start(f32[2,512,128]{1,2,0:T(8,128)} %copy.205) | copy-start | bytes 1572868
  173.2 3.4 %copy-start.4 = (f32[4,514,130]{1,2,0:T(8,128)}, f32[4,514,130]{1,2,0:T(8,128)S(1)}, u32[]{:S(2)}) copy-start(f32[4,514,130]{1,2,0:T(8,128)S(1)} %pad_maximum_fusion.2) | copy-start | bytes 3207364
  181.2 10.1 %copy-start.8 = (f32[1,2,513,129]{2,3,1,0:T(8,128)S(1)}, f32[1,2,513,129]{2,3,1,0:T(8,128)}, u32[]{:S(2)}) copy-start(f32[1,2,513,129]{2,3,1,0:T(8,128)} %copy-done.7) | copy-start | bytes 1588252
  184.3 7.0 %copy-start.5 = (f32[4,514,130]{1,2,0:T(8,128)S(1)}, f32[4,514,130]{1,2,0:T(8,128)}, u32[]{:S(2)}) copy-start(f32[4,514,130]{1,2,0:T(8,128)} %copy-done.4) | copy-start | bytes 3207364
  184.3 7.0 %copy-start.10 = (f32[1,2,513,129]{2,3,1,0:T(8,128)S(1)}, f32[1,2,513,129]{2,3,1,0:T(8,128)}, u32[]{:S(2)}) copy-start(f32[1,2,513,129]{2,3,1,0:T(8,128)} %copy-done.9) | copy-start | bytes 1588252
  185.9 4.7 %collective-permute-start.12 = (bf16[64,2,2,128]{3,0,1,2:T(8,128)(2,1)S(1)}, bf16[64,2,2,128]{3,0,1,2:T(8,128)(2,1)S(1)}, u32[]{:S(2)}, u32[]{:S(2)}) collective-permute-start(bf16[64,2,2,128]{3,0,1,2:T(8,128)(2,1)S(1)} %fusion.27), channel_id=1, source_target_pairs={{0,64},{16,80},{32,96},{48,112},{64,0},{80,16},{96,32},{112,48},{1... | collective-permute-start | bytes 196616 | tf_op jit(solution)/shard_map/ppermute | solution.py:47
  191.3 4.1 %collective-permute-start.13 = (bf16[2,64,2,2,128]{4,1,2,3,0:T(8,128)(2,1)}, bf16[2,64,2,2,128]{4,1,2,3,0:T(8,128)(2,1)}, u32[]{:S(2)}, u32[]{:S(2)}) collective-permute-start(bf16[2,64,2,2,128]{4,1,2,3,0:T(8,128)(2,1)} %pad_maximum_fusion.29), channel_id=1, source_target_pairs={{0,128},{16,144},{32,160},{48,176},{64,192},{80,208},{96,224},{112... | collective-permute-start | bytes 393224 | tf_op jit(solution)/shard_map/ppermute | solution.py:47
  195.3 3.7 %copy-start.17 = (f32[2,64,4,128]{3,1,0,2:T(8,128)S(1)}, f32[2,64,4,128]{3,1,0,2:T(8,128)}, u32[]{:S(2)}) copy-start(f32[2,64,4,128]{3,1,0,2:T(8,128)} %copy-done.16) | copy-start | bytes 786436
  196.4 5.3 %collective-permute-start.14 = (bf16[2,2,64,2,2,128]{5,2,3,4,1,0:T(8,128)(2,1)S(1)}, bf16[2,2,64,2,2,128]{5,2,3,4,1,0:T(8,128)(2,1)S(1)}, u32[]{:S(2)}, u32[]{:S(2)}) collective-permute-start(bf16[2,2,64,2,2,128]{5,2,3,4,1,0:T(8,128)(2,1)S(1)} %pad_maximum_fusion.27), channel_id=1, source_target_pairs={{0,32},{16,48},{32,0},{48,16},{64,96},{80,112},{96,64},{112,80},{1... | collective-permute-start | bytes 786440 | tf_op jit(solution)/shard_map/ppermute | solution.py:47
  198.9 8.0 %copy-start.31 = (f32[2,8,64]{2,0,1:T(2,128)S(1)}, f32[2,8,64]{2,0,1:T(2,128)}, u32[]{:S(2)}) copy-start(f32[2,8,64]{2,0,1:T(2,128)} %copy.160) | copy-start | bytes 12292
  198.9 8.0 %copy-start.32 = (f32[2,8,64]{2,0,1:T(2,128)S(1)}, f32[2,8,64]{2,0,1:T(2,128)}, u32[]{:S(2)}) copy-start(f32[2,8,64]{2,0,1:T(2,128)} %copy.186) | copy-start | bytes 12292
  201.8 10.8 %collective-permute-start.15 = (bf16[8,64,2,2,128]{4,1,3,2,0:T(8,128)(2,1)S(1)}, bf16[8,64,2,2,128]{4,1,3,2,0:T(8,128)(2,1)}, u32[]{:S(2)}, u32[]{:S(2)}) collective-permute-start(bf16[8,64,2,2,128]{4,1,3,2,0:T(8,128)(2,1)S(1)} %bitcast.323), channel_id=1, source_target_pairs={{0,16},{16,0},{32,48},{48,32},{64,80},{80,64},{96,112},{112,96},{1... | collective-permute-start | bytes 1572872 | tf_op jit(solution)/shard_map/ppermute | solution.py:124
  207.7 5.0 %copy-start.29 = (f32[2,8,64]{2,0,1:T(2,128)S(1)}, f32[2,8,64]{2,0,1:T(2,128)}, u32[]{:S(2)}) copy-start(f32[2,8,64]{2,0,1:T(2,128)} %copy.194) | copy-start | bytes 12292
  207.7 5.0 %copy-start.30 = (f32[2,8,64]{2,0,1:T(2,128)S(1)}, f32[2,8,64]{2,0,1:T(2,128)}, u32[]{:S(2)}) copy-start(f32[2,8,64]{2,0,1:T(2,128)} %copy.196) | copy-start | bytes 12292
  215.8 6.0 %copy-start.3 = (f32[2,512,128]{1,2,0:T(8,128)S(1)}, f32[2,512,128]{1,2,0:T(8,128)}, u32[]{:S(2)}) copy-start(f32[2,512,128]{1,2,0:T(8,128)} %copy.205) | copy-start | bytes 1572868
  (19 other events, 22.6 us)

commit v10 on v3

--- a/solution.py
+++ b/solution.py
@@ -90,6 +90,9 @@
     real_part = weight_re * prod_re - weight_im * prod_im
     imag_part = weight_re * prod_im + weight_im * prod_re
     parts = jnp.stack([real_part, imag_part], axis=0).reshape(2, az_count, -1, tiles_dev, columns)
+    stacked = jnp.concatenate([image, tv_dual.reshape(4, strip_rows, columns)], axis=0)
+    padded = padded_2(stacked, (("az", 2), ("tile", 1)), 1)
+    padded, parts = lax.optimization_barrier((padded, parts))
     summed = halving_sum(jnp.moveaxis(parts, 1, 0), "az", (1, 8, 2, 4))
     projection_b = jnp.transpose(summed, (2, 1, 0, 3)).astype(jnp.bfloat16)
     all_proj = doubling_gather(projection_b, "tile", (2, 1, 8, 4))
@@ -139,8 +142,6 @@
     )
     adjoint = jnp.stack([grad_re, grad_im])
     adjoint = adjoint.reshape(2, strip_rows, columns)
-    stacked = jnp.concatenate([image, tv_dual.reshape(4, strip_rows, columns)], axis=0)
-    padded = padded_2(stacked, (("az", 2), ("tile", 1)), 1)
     image_pad = padded[:2]
     dual_pad = padded[2:].reshape(2, 2, strip_rows + 2, columns + 2)
     total_rows = tile_count * strip_rows

time: 193 us -> 235 us (1.22)
  waiting for transfers between devices: 78.2 us -> 104 us
  other arithmetic: 23.3 us -> 30.4 us
  local copies, waits for them, and re-layouts: 24.5 us -> 31.4 us
  matrix products: 13.2 us -> 15.7 us
    ppermute x12, waiting for transfers between devices: 48.6 us -> 72 us  [doubling_gather(): got = lax.ppermute(block, axis, pairs)]
    another operation x24, other arithmetic: 3.52 us -> 9.96 us  [doubling_gather(): block = jnp.stack([low, high], axis=place)]
    ppermute x12, starting transfers between devices: 28.5 us -> 33.7 us  [doubling_gather(): got = lax.ppermute(block, axis, pairs)]
    ppermute x2, starting transfers between devices: 14.7 us -> 9.52 us  [padded_2(): lax.ppermute(lax.slice_in_dim(block, block.shape[dim] - width, None, axis...]
    another operation x2 -> x1, other arithmetic: 5.12 us -> 0.41 us  [on_device(): jnp.stack([grad_rows, grad_cols])]
    add x3, other arithmetic: 1.46 us -> 3.99 us  [halving_sum(): blocks = keep + lax.ppermute(send, axis, pairs)]
    unnamed x68 -> x77, local copies, waits for them, and re-layouts: 5.42 us -> 7.6 us
  transfers between devices with their start and end apart: 20 -> 20, of which waited for: 15 -> 16; matrix products, arithmetic and copies ran while one was open for 13% -> 10% of each run, Pallas kernels for 0% -> 0%
where the time goes in v10:
time: 235 us; the launch traced here: 234 us
  waiting for transfers between devices  104 us (44%)
  starting transfers between devices  51.5 us (22%)
  local copies, waits for them, and re-layouts  31.4 us (13%)
  other arithmetic  30.4 us (13%)
  matrix products  15.7 us (7%)
    ppermute x12, waiting for transfers between devices, doubling_gather(): got = lax.ppermute(block, axis, pairs)  72 us
    ppermute x12, starting transfers between devices, doubling_gather(): got = lax.ppermute(block, axis, pairs)  33.7 us
    ppermute x4, waiting for transfers between devices, halving_sum(): blocks = keep + lax.ppermute(send, axis, pairs)  27.2 us
    another operation x24, other arithmetic, doubling_gather(): block = jnp.stack([low, high], axis=place)  9.96 us
    ppermute x2, starting transfers between devices, padded_2(): lax.ppermute(lax.slice_in_dim(block, block.shape[dim] - width, None, axis...  9.52 us
    unnamed x77, local copies, waits for them, and re-layouts  7.6 us
    ppermute x4, starting transfers between devices, halving_sum(): blocks = keep + lax.ppermute(send, axis, pairs)  5.05 us
  transfers between devices with their start and end apart: 20, of which 16 were waited for; matrix products, arithmetic and copies ran while one was open for 10% of the time, Pallas kernels for 0%

profile of v10, /device:TPU:1, one launch (start us, length us, event | category | flops | bytes accessed | tf_op | source)
XLA Modules:
  0.0 234.1 jit_solution(11078274197865597366)
XLA Ops:
  0.6 3.6 %slice_maximum_fusion = (f32[6,512,1]{2,1,0:T(8,128)}, f32[6,512,1]{2,1,0:T(8,128)S(1)}) fusion(f32[4,512,128]{2,1,0:T(8,128)} %bitcast.237, f32[2,512,128]{2,1,0:T(8,128)} %param.10), kind=kLoop, calls=%fused_computation.12 | loop fusion | flops 6144 | bytes 1597440 | tf_op jit(solution)/shard_map/concatenate | solution.py:93
  4.3 1.9 copy.122
  6.2 4.5 %collective-permute-start = (f32[6,512,1]{1,2,0:T(1,128)S(1)}, f32[6,512,1]{1,2,0:T(1,128)S(1)}, u32[]{:S(2)}, u32[]{:S(2)}) collective-permute-start(f32[6,512,1]{1,2,0:T(1,128)S(1)} %copy.122), channel_id=1, source_target_pairs={{0,16},{16,32},{32,48},{48,64},{64,80},{80,96},{96,112},{112,128},... | collective-permute-start | bytes 36872 | tf_op jit(solution)/shard_map/ppermute | solution.py:16
  11.2 1.9 collective-permute-start.1
  13.2 2.7 %fusion.60 = (bf16[1,1024,2,256]{3,2,1,0:T(2,128)(2,1)S(1)}, bf16[1,1024,2,256]{3,2,1,0:T(2,128)(2,1)S(1)}) fusion(bf16[2,1024,2,256]{3,2,1,0:T(2,128)(2,1)} %param.14), kind=kLoop, calls=%fused_computation.154 | loop fusion | bytes 4194304 | tf_op jit(solution)/shard_map/slice | solution.py:75
  17.2 1.5 fusion.37
  19.7 1.4 fusion.3
  21.1 1.5 multiply_subtract_fusion
  22.6 2.6 %copy.132 = f32[1024,2,128]{2,0,1:T(8,128)} copy(f32[1024,2,128]{0,2,1:T(8,128)} %get-tuple-element.28) | data formatting | bytes 2097152 | tf_op jit(solution)/shard_map/sub | solution.py:90
  28.7 5.0 %collective-permute-start.2 = (f32[6,1,130]{2,1,0:T(1,128)S(1)}, f32[6,1,130]{2,1,0:T(1,128)S(1)}, u32[]{:S(2)}, u32[]{:S(2)}) collective-permute-start(f32[6,1,130]{2,1,0:T(1,128)S(1)} %get-tuple-element.22), channel_id=1, source_target_pairs={{0,1},{1,2},{2,3},{3,4},{4,5},{5,6},{6,7},{7,8},{8,9},{9,10},{10,1... | collective-permute-start | bytes 9368 | tf_op jit(solution)/shard_map/ppermute | solution.py:16
  35.1 1.4 pad_maximum_fusion.1
  36.5 4.4 %collective-permute-done.3 = f32[6,1,130]{2,1,0:T(1,128)S(1)} collective-permute-done((f32[6,1,130]{2,1,0:T(1,128)S(1)}, f32[6,1,130]{2,1,0:T(1,128)S(1)}, u32[]{:S(2)}, u32[]{:S(2)}) %collective-permute-start.3) | collective-permute-done | bytes 3152 | tf_op jit(solution)/shard_map/ppermute | solution.py:19
  40.9 3.7 %pad_maximum_fusion = f32[6,514,130]{2,1,0:T(8,128)S(1)} fusion(f32[6,1,130]{2,1,0:T(1,128)S(1)} %collective-permute-done.3, f32[6,512,1]{2,1,0:T(8,128)} %copy-done.3, f32[4,512,128]{2,1,0:T(8,128)} %bitcast.239, f32[2,512,128]{2,1,0:T(8,128)} %param.10, f32[6,512,1]{2,1,0:T(8,128)} %copy-done.2, f32[6,1,130]{2,1,0:T(1,128)S(1)} %collective-permute-done.2), kind=kLoop, calls=%fused_computation.2 | loop fusion | flops 2004600 | bytes 3207360 | tf_op jit(solution)/shard_map/concatenate | solution.py:20
  46.8 3.0 %collective-permute-done.4 = f32[2,2,2,2,64,2,128]{6,4,5,3,2,1,0:T(8,128)} collective-permute-done((f32[2,2,2,2,64,2,128]{6,4,5,3,2,1,0:T(8,128)}, f32[2,2,2,2,64,2,128]{6,4,5,3,2,1,0:T(8,128)}, u32[]{:S(2)}, u32[]{:S(2)}) %collective-permute-start.4) | collective-permute-done | bytes 1048608 | tf_op jit(solution)/shard_map/ppermute | solution.py:36
  49.8 1.7 bitcast_add_fusion
  53.3 4.3 %collective-permute-start.5 = (f32[2,2,2,64,2,128]{5,3,4,2,1,0:T(8,128)}, f32[2,2,2,64,2,128]{5,3,4,2,1,0:T(8,128)}, u32[]{:S(2)}, u32[]{:S(2)}) collective-permute-start(f32[2,2,2,64,2,128]{5,3,4,2,1,0:T(8,128)} %dynamic-slice_bitcast_fusion), channel_id=1, source_target_pairs={{0,128},{16,144},{32,160},{48,176},{64,192},{80,208},{96,224},{112... | collective-permute-start | bytes 1572872 | tf_op jit(solution)/shard_map/ppermute | solution.py:36
  57.6 12.3 %collective-permute-done.5 = f32[2,2,2,64,2,128]{5,3,4,2,1,0:T(8,128)} collective-permute-done((f32[2,2,2,64,2,128]{5,3,4,2,1,0:T(8,128)}, f32[2,2,2,64,2,128]{5,3,4,2,1,0:T(8,128)}, u32[]{:S(2)}, u32[]{:S(2)}) %collective-permute-start.5) | collective-permute-done | bytes 524320 | tf_op jit(solution)/shard_map/ppermute | solution.py:36
  72.6 7.3 %collective-permute-done.6 = f32[2,2,64,2,128]{4,2,3,1,0:T(8,128)} collective-permute-done((f32[2,2,64,2,128]{4,2,3,1,0:T(8,128)}, f32[2,2,64,2,128]{4,2,3,1,0:T(8,128)}, u32[]{:S(2)}, u32[]{:S(2)}) %collective-permute-start.6) | collective-permute-done | bytes 262176 | tf_op jit(solution)/shard_map/ppermute | solution.py:36
  81.8 4.6 %collective-permute-done.7 = f32[2,64,2,128]{3,1,0,2:T(8,128)S(1)} collective-permute-done((f32[2,64,2,128]{3,1,0,2:T(8,128)S(1)}, f32[2,64,2,128]{3,1,0,2:T(8,128)S(1)}, u32[]{:S(2)}, u32[]{:S(2)}) %collective-permute-start.7) | collective-permute-done | bytes 131104 | tf_op jit(solution)/shard_map/ppermute | solution.py:36
  86.5 3.8 %collective-permute-start.8 = (bf16[2,64,2,128]{3,1,2,0:T(8,128)(2,1)S(1)}, bf16[2,64,2,128]{3,1,2,0:T(8,128)(2,1)}, u32[]{:S(2)}, u32[]{:S(2)}) collective-permute-start(bf16[2,64,2,128]{3,1,2,0:T(8,128)(2,1)S(1)} %fusion.48), channel_id=1, source_target_pairs={{0,2},{1,3},{2,0},{3,1},{4,6},{5,7},{6,4},{7,5},{8,10},{9,11},{10,... | collective-permute-start | bytes 196616 | tf_op jit(solution)/shard_map/ppermute | solution.py:47
  90.3 3.4 %collective-permute-done.8 = bf16[2,64,2,128]{3,1,2,0:T(8,128)(2,1)} collective-permute-done((bf16[2,64,2,128]{3,1,2,0:T(8,128)(2,1)S(1)}, bf16[2,64,2,128]{3,1,2,0:T(8,128)(2,1)}, u32[]{:S(2)}, u32[]{:S(2)}) %collective-permute-start.8) | collective-permute-done | bytes 65568 | tf_op jit(solution)/shard_map/ppermute | solution.py:47
  95.9 3.9 %collective-permute-start.9 = (bf16[2,2,64,2,128]{4,2,3,1,0:T(8,128)(2,1)}, bf16[2,2,64,2,128]{4,2,3,1,0:T(8,128)(2,1)}, u32[]{:S(2)}, u32[]{:S(2)}) collective-permute-start(bf16[2,2,64,2,128]{4,2,3,1,0:T(8,128)(2,1)} %pad_maximum_fusion.13), channel_id=1, source_target_pairs={{0,1},{1,0},{2,3},{3,2},{4,5},{5,4},{6,7},{7,6},{8,9},{9,8},{10,11... | collective-permute-start | bytes 393224 | tf_op jit(solution)/shard_map/ppermute | solution.py:47
  99.7 4.1 %collective-permute-done.9 = bf16[2,2,64,2,128]{4,2,3,1,0:T(8,128)(2,1)} collective-permute-done((bf16[2,2,64,2,128]{4,2,3,1,0:T(8,128)(2,1)}, bf16[2,2,64,2,128]{4,2,3,1,0:T(8,128)(2,1)}, u32[]{:S(2)}, u32[]{:S(2)}) %collective-permute-start.9) | collective-permute-done | bytes 131104 | tf_op jit(solution)/shard_map/ppermute | solution.py:47
  106.1 2.9 %collective-permute-start.10 = (bf16[2,2,2,64,2,128]{5,3,4,2,1,0:T(8,128)(2,1)}, bf16[2,2,2,64,2,128]{5,3,4,2,1,0:T(8,128)(2,1)}, u32[]{:S(2)}, u32[]{:S(2)}) collective-permute-start(bf16[2,2,2,64,2,128]{5,3,4,2,1,0:T(8,128)(2,1)} %pad_maximum_fusion.10), channel_id=1, source_target_pairs={{0,8},{1,9},{2,10},{3,11},{4,12},{5,13},{6,14},{7,15},{8,0},{9,1},... | collective-permute-start | bytes 786440 | tf_op jit(solution)/shard_map/ppermute | solution.py:47
  109.1 4.1 %collective-permute-done.10 = bf16[2,2,2,64,2,128]{5,3,4,2,1,0:T(8,128)(2,1)} collective-permute-done((bf16[2,2,2,64,2,128]{5,3,4,2,1,0:T(8,128)(2,1)}, bf16[2,2,2,64,2,128]{5,3,4,2,1,0:T(8,128)(2,1)}, u32[]{:S(2)}, u32[]{:S(2)}) %collective-permute-start.10) | collective-permute-done | bytes 262176 | tf_op jit(solution)/shard_map/ppermute | solution.py:47
  114.3 1.6 collective-permute-start.11
  116.0 8.1 %collective-permute-done.11 = bf16[2,2,2,2,64,2,128]{6,4,5,3,2,1,0:T(8,128)(2,1)S(1)} collective-permute-done((bf16[2,2,2,2,64,2,128]{6,4,5,3,2,1,0:T(8,128)(2,1)S(1)}, bf16[2,2,2,2,64,2,128]{6,4,5,3,2,1,0:T(8,128)(2,1)S(1)}, u32[]{:S(2)}, u32[]{:S(2)}) %collective-permute-start.11) | collective-permute-done | bytes 524320 | tf_op jit(solution)/shard_map/ppermute | solution.py:47
  125.3 1.6 fusion.21
  126.9 3.3 %collective-permute-start.12 = (bf16[4,2,64,128]{3,2,1,0:T(8,128)(2,1)S(1)}, bf16[4,2,64,128]{3,2,1,0:T(8,128)(2,1)S(1)}, u32[]{:S(2)}, u32[]{:S(2)}) collective-permute-start(bf16[4,2,64,128]{3,2,1,0:T(8,128)(2,1)S(1)} %convert_bitcast_fusion), channel_id=1, source_target_pairs={{0,2},{1,3},{2,0},{3,1},{4,6},{5,7},{6,4},{7,5},{8,10},{9,11},{10,... | collective-permute-start | bytes 393224 | tf_op jit(solution)/shard_map/ppermute | solution.py:47
  130.2 5.9 %collective-permute-done.12 = bf16[4,2,64,128]{3,2,1,0:T(8,128)(2,1)S(1)} collective-permute-done((bf16[4,2,64,128]{3,2,1,0:T(8,128)(2,1)S(1)}, bf16[4,2,64,128]{3,2,1,0:T(8,128)(2,1)S(1)}, u32[]{:S(2)}, u32[]{:S(2)}) %collective-permute-start.12) | collective-permute-done | bytes 131104 | tf_op jit(solution)/shard_map/ppermute | solution.py:47
  137.2 11.3 %collective-permute-done.13 = bf16[2,4,2,64,128]{4,3,2,1,0:T(8,128)(2,1)S(1)} collective-permute-done((bf16[2,4,2,64,128]{4,3,2,1,0:T(8,128)(2,1)S(1)}, bf16[2,4,2,64,128]{4,3,2,1,0:T(8,128)(2,1)S(1)}, u32[]{:S(2)}, u32[]{:S(2)}) %collective-permute-start.13) | collective-permute-done | bytes 262176 | tf_op jit(solution)/shard_map/ppermute | solution.py:47
  151.2 8.7 %collective-permute-done.14 = bf16[2,2,4,2,64,128]{5,4,3,2,0,1:T(8,128)(2,1)} collective-permute-done((bf16[2,2,4,2,64,128]{5,4,3,2,0,1:T(8,128)(2,1)}, bf16[2,2,4,2,64,128]{5,4,3,2,0,1:T(8,128)(2,1)}, u32[]{:S(2)}, u32[]{:S(2)}) %collective-permute-start.14) | collective-permute-done | bytes 524320 | tf_op jit(solution)/shard_map/ppermute | solution.py:47
  163.1 1.3 collective-permute-start.15
  164.9 1.4 gather_fusion
  166.3 17.7 %collective-permute-done.15 = bf16[2,2,2,4,2,64,128]{6,5,4,3,1,2,0:T(8,128)(2,1)} collective-permute-done((bf16[2,2,2,4,2,64,128]{6,5,4,3,1,2,0:T(8,128)(2,1)}, bf16[2,2,2,4,2,64,128]{6,5,4,3,1,2,0:T(8,128)(2,1)}, u32[]{:S(2)}, u32[]{:S(2)}) %collective-permute-start.15) | collective-permute-done | bytes 1048608 | tf_op jit(solution)/shard_map/ppermute | solution.py:47
  184.0 1.7 select_bitcast_fusion.3
  185.9 1.5 copy.144
  187.4 2.9 %gather_fusion.1 = bf16[12,2,64,128]{3,2,1,0:T(8,128)(2,1)} fusion(bf16[2,64,64,128]{3,1,0,2:T(8,128)(2,1)} %bitcast.244, s32[1024]{0:T(1024)S(1)} %pad_clamp_fusion), kind=kCustom, calls=%fused_computation.1 | custom fusion | bytes 786480 | tf_op jit(solution)/shard_map/jit(_take)/gather | solution.py:122
  190.3 1.4 fusion.25
  192.6 3.8 %collective-permute-done.16 = bf16[64,2,2,128]{3,0,1,2:T(8,128)(2,1)S(1)} collective-permute-done((bf16[64,2,2,128]{3,0,1,2:T(8,128)(2,1)S(1)}, bf16[64,2,2,128]{3,0,1,2:T(8,128)(2,1)S(1)}, u32[]{:S(2)}, u32[]{:S(2)}) %collective-permute-start.16) | collective-permute-done | bytes 65568 | tf_op jit(solution)/shard_map/ppermute | solution.py:47
  196.5 4.2 %collective-permute-start.17 = (bf16[2,64,2,2,128]{4,1,2,3,0:T(8,128)(2,1)S(1)}, bf16[2,64,2,2,128]{4,1,2,3,0:T(8,128)(2,1)S(1)}, u32[]{:S(2)}, u32[]{:S(2)}) collective-permute-start(bf16[2,64,2,2,128]{4,1,2,3,0:T(8,128)(2,1)S(1)} %pad_maximum_fusion.14), channel_id=1, source_target_pairs={{0,128},{16,144},{32,160},{48,176},{64,192},{80,208},{96,224},{112... | collective-permute-start | bytes 393224 | tf_op jit(solution)/shard_map/ppermute | solution.py:47
  201.3 1.8 collective-permute-done.17
  203.2 3.1 %collective-permute-start.18 = (bf16[2,2,64,2,2,128]{5,2,3,4,1,0:T(8,128)(2,1)S(1)}, bf16[2,2,64,2,2,128]{5,2,3,4,1,0:T(8,128)(2,1)S(1)}, u32[]{:S(2)}, u32[]{:S(2)}) collective-permute-start(bf16[2,2,64,2,2,128]{5,2,3,4,1,0:T(8,128)(2,1)S(1)} %pad_maximum_fusion.12), channel_id=1, source_target_pairs={{0,32},{16,48},{32,0},{48,16},{64,96},{80,112},{96,64},{112,80},{1... | collective-permute-start | bytes 786440 | tf_op jit(solution)/shard_map/ppermute | solution.py:47
  206.8 3.2 %collective-permute-done.18 = bf16[2,2,64,2,2,128]{5,2,3,4,1,0:T(8,128)(2,1)S(1)} collective-permute-done((bf16[2,2,64,2,2,128]{5,2,3,4,1,0:T(8,128)(2,1)S(1)}, bf16[2,2,64,2,2,128]{5,2,3,4,1,0:T(8,128)(2,1)S(1)}, u32[]{:S(2)}, u32[]{:S(2)}) %collective-permute-start.18) | collective-permute-done | bytes 262176 | tf_op jit(solution)/shard_map/ppermute | solution.py:47
  210.1 7.3 %collective-permute-start.19 = (bf16[2,2,2,64,2,2,128]{6,3,4,5,1,0,2:T(8,128)(2,1)S(1)}, bf16[2,2,2,64,2,2,128]{6,3,4,5,1,0,2:T(8,128)(2,1)S(1)}, u32[]{:S(2)}, u32[]{:S(2)}) collective-permute-start(bf16[2,2,2,64,2,2,128]{6,3,4,5,1,0,2:T(8,128)(2,1)S(1)} %pad_maximum_fusion.9), channel_id=1, source_target_pairs={{0,16},{16,0},{32,48},{48,32},{64,80},{80,64},{96,112},{112,96},{1... | collective-permute-start | bytes 1572872 | tf_op jit(solution)/shard_map/ppermute | solution.py:47
  219.1 1.5 fusion.27
  227.1 3.1 %fusion.8 = f32[2,256,128]{1,2,0:T(8,128)} fusion(f32[2,128,256]{2,1,0:T(8,128)S(1)} %fusion.35, bf16[1,1024,2,256]{3,2,1,0:T(2,128)(2,1)S(1)} %copy-done.7, f32[2,1024]{1,0:T(2,128)S(1)} %get-tuple-element.68, f32[2,1024]{1,0:T(2,128)S(1)} %get-tuple-element.73, bf16[2,2,1024,128]{3,2,1,0:T(8,128)(2,1)} %bitcast.254), kind=kOutput, calls=%fused_computation.25 | convolution fusion | flops 135856128 | bytes 2637824 | tf_op jit(solution)/shard_map/pjh,jpu->jhu/dot_general | solution.py:140
  231.4 2.7 %fusion.41 = f32[2,512,128]{2,1,0:T(8,128)} fusion(f32[2,512,128]{2,1,0:T(8,128)S(1)} %copy-done.5, f32[2,513,129]{2,1,0:T(8,128)} %get-tuple-element.27, f32[2,513,129]{2,1,0:T(8,128)S(1)} %copy-done.13, f32[1,512,128]{2,1,0:T(8,128)S(1)} %bitcast.250, f32[1,512,128]{2,1,0:T(8,128)S(1)} %bitcast.249), kind=kLoop, calls=%fused_computation.66 | loop fusion | flops 917504 | bytes 3670016 | tf_op jit(solution)/shard_map/sub | solution.py:168
  (162 shorter events, 42.1 us)
Async XLA Ops:
  0.6 124.5 %copy-start = (bf16[8,128,128]{2,1,0:T(8,128)(2,1)S(1)}, bf16[8,128,128]{2,1,0:T(8,128)(2,1)}, u32[]{:S(2)}) copy-start(bf16[8,128,128]{2,1,0:T(8,128)(2,1)} %param.16) | copy-start | bytes 786436
  4.3 8.9 %copy-start.4 = (f32[2,512,128]{2,1,0:T(8,128)S(1)}, f32[2,512,128]{2,1,0:T(8,128)}, u32[]{:S(2)}) copy-start(f32[2,512,128]{2,1,0:T(8,128)} %param.10) | copy-start | bytes 1572868
  6.2 20.3 %collective-permute-start = (f32[6,512,1]{1,2,0:T(1,128)S(1)}, f32[6,512,1]{1,2,0:T(1,128)S(1)}, u32[]{:S(2)}, u32[]{:S(2)}) collective-permute-start(f32[6,512,1]{1,2,0:T(1,128)S(1)} %copy.122), channel_id=1, source_target_pairs={{0,16},{16,32},{32,48},{48,64},{64,80},{80,96},{96,112},{112,128},... | collective-permute-start | bytes 36872 | tf_op jit(solution)/shard_map/ppermute | solution.py:16
  11.2 15.8 %collective-permute-start.1 = (f32[6,512,1]{1,2,0:T(1,128)S(1)}, f32[6,512,1]{1,2,0:T(1,128)S(1)}, u32[]{:S(2)}, u32[]{:S(2)}) collective-permute-start(f32[6,512,1]{1,2,0:T(1,128)S(1)} %copy.123), channel_id=1, source_target_pairs={{16,0},{32,16},{48,32},{64,48},{80,64},{96,80},{112,96},{128,112},... | collective-permute-start | bytes 36872 | tf_op jit(solution)/shard_map/ppermute | solution.py:19
  15.9 2.7 %copy-start.8 = (bf16[1,1024,2,256]{3,2,1,0:T(2,128)(2,1)}, bf16[1,1024,2,256]{3,2,1,0:T(2,128)(2,1)S(1)}, u32[]{:S(2)}) copy-start(bf16[1,1024,2,256]{3,2,1,0:T(2,128)(2,1)S(1)} %get-tuple-element.35) | copy-start | bytes 3145732
  15.9 5.1 %copy-start.6 = (bf16[1,1024,2,256]{3,2,1,0:T(2,128)(2,1)}, bf16[1,1024,2,256]{3,2,1,0:T(2,128)(2,1)S(1)}, u32[]{:S(2)}) copy-start(bf16[1,1024,2,256]{3,2,1,0:T(2,128)(2,1)S(1)} %get-tuple-element.34) | copy-start | bytes 3145732
  16.0 1.2 copy-start.23
  18.7 2.4 %copy-start.19 = (f32[2,128,1024]{2,1,0:T(8,128)S(1)}, f32[2,128,1024]{2,1,0:T(8,128)}, u32[]{:S(2)}) copy-start(f32[2,128,1024]{2,1,0:T(8,128)} %fusion.37) | copy-start | bytes 3145732
  18.7 2.4 %copy-start.27 = (bf16[1,512,128]{2,1,0:T(8,128)(2,1)S(1)}, bf16[1,512,128]{2,1,0:T(8,128)(2,1)}, u32[]{:S(2)}) copy-start(bf16[1,512,128]{2,1,0:T(8,128)(2,1)} %copy-done.26) | copy-start | bytes 393220
  27.0 1.7 copy-start.2
  27.5 1.2 copy-start.3
  27.6 7.5 %copy-start.17 = (f32[1024,2,128]{2,0,1:T(8,128)S(1)}, f32[1024,2,128]{2,0,1:T(8,128)}, u32[]{:S(2)}) copy-start(f32[1024,2,128]{2,0,1:T(8,128)} %copy.132) | copy-start | bytes 3145732
  27.6 7.5 %copy-start.18 = (f32[1024,2,128]{2,0,1:T(8,128)S(1)}, f32[1024,2,128]{2,0,1:T(8,128)}, u32[]{:S(2)}) copy-start(f32[1024,2,128]{2,0,1:T(8,128)} %copy.133) | copy-start | bytes 3145732
  28.7 7.8 %collective-permute-start.2 = (f32[6,1,130]{2,1,0:T(1,128)S(1)}, f32[6,1,130]{2,1,0:T(1,128)S(1)}, u32[]{:S(2)}, u32[]{:S(2)}) collective-permute-start(f32[6,1,130]{2,1,0:T(1,128)S(1)} %get-tuple-element.22), channel_id=1, source_target_pairs={{0,1},{1,2},{2,3},{3,4},{4,5},{5,6},{6,7},{7,8},{8,9},{9,10},{10,1... | collective-permute-start | bytes 9368 | tf_op jit(solution)/shard_map/ppermute | solution.py:16
  33.8 7.1 %collective-permute-start.3 = (f32[6,1,130]{2,1,0:T(1,128)S(1)}, f32[6,1,130]{2,1,0:T(1,128)S(1)}, u32[]{:S(2)}, u32[]{:S(2)}) collective-permute-start(f32[6,1,130]{2,1,0:T(1,128)S(1)} %get-tuple-element.23), channel_id=1, source_target_pairs={{1,0},{2,1},{3,2},{4,3},{5,4},{6,5},{7,6},{8,7},{9,8},{10,9},{11,1... | collective-permute-start | bytes 9368 | tf_op jit(solution)/shard_map/ppermute | solution.py:19
  36.5 8.0 %copy-start.10 = (f32[2,16,64,2,128]{4,2,1,3,0:T(8,128)S(1)}, f32[2,16,64,2,128]{4,2,1,3,0:T(8,128)}, u32[]{:S(2)}) copy-start(f32[2,16,64,2,128]{4,2,1,3,0:T(8,128)} %pad_maximum_fusion.1) | copy-start | bytes 6291460
  46.8 3.0 %collective-permute-start.4 = (f32[2,2,2,2,64,2,128]{6,4,5,3,2,1,0:T(8,128)}, f32[2,2,2,2,64,2,128]{6,4,5,3,2,1,0:T(8,128)}, u32[]{:S(2)}, u32[]{:S(2)}) collective-permute-start(f32[2,2,2,2,64,2,128]{6,4,5,3,2,1,0:T(8,128)} %bitcast.231), channel_id=1, source_target_pairs={{0,16},{16,0},{32,48},{48,32},{64,80},{80,64},{96,112},{112,96},{1... | collective-permute-start | bytes 3145736 | tf_op jit(solution)/shard_map/ppermute | solution.py:36
  53.3 16.6 %collective-permute-start.5 = (f32[2,2,2,64,2,128]{5,3,4,2,1,0:T(8,128)}, f32[2,2,2,64,2,128]{5,3,4,2,1,0:T(8,128)}, u32[]{:S(2)}, u32[]{:S(2)}) collective-permute-start(f32[2,2,2,64,2,128]{5,3,4,2,1,0:T(8,128)} %dynamic-slice_bitcast_fusion), channel_id=1, source_target_pairs={{0,128},{16,144},{32,160},{48,176},{64,192},{80,208},{96,224},{112... | collective-permute-start | bytes 1572872 | tf_op jit(solution)/shard_map/ppermute | solution.py:36
  71.9 37.1 %copy-start.34 = (s32[32,1,6]{0,1,2:T(1,128)S(1)}, s32[32,1,6]{0,1,2:T(1,128)}, u32[]{:S(2)}) copy-start(s32[32,1,6]{0,1,2:T(1,128)} %param.17) | copy-start | bytes 2308
  71.9 37.2 %copy-start.35 = (s32[32,1,6]{0,1,2:T(1,128)S(1)}, s32[32,1,6]{0,1,2:T(1,128)}, u32[]{:S(2)}) copy-start(s32[32,1,6]{0,1,2:T(1,128)} %param.18) | copy-start | bytes 2308
  72.6 7.3 %collective-permute-start.6 = (f32[2,2,64,2,128]{4,2,3,1,0:T(8,128)}, f32[2,2,64,2,128]{4,2,3,1,0:T(8,128)}, u32[]{:S(2)}, u32[]{:S(2)}) collective-permute-start(f32[2,2,64,2,128]{4,2,3,1,0:T(8,128)} %dynamic-slice_bitcast_fusion.1), channel_id=1, source_target_pairs={{0,32},{16,48},{32,0},{48,16},{64,96},{80,112},{96,64},{112,80},{1... | collective-permute-start | bytes 786440 | tf_op jit(solution)/shard_map/ppermute | solution.py:36
  81.0 5.4 %collective-permute-start.7 = (f32[2,64,2,128]{3,1,0,2:T(8,128)S(1)}, f32[2,64,2,128]{3,1,0,2:T(8,128)S(1)}, u32[]{:S(2)}, u32[]{:S(2)}) collective-permute-start(f32[2,64,2,128]{3,1,0,2:T(8,128)S(1)} %bitcast.257), channel_id=1, source_target_pairs={{0,64},{16,80},{32,96},{48,112},{64,0},{80,16},{96,32},{112,48},{1... | collective-permute-start | bytes 393224 | tf_op jit(solution)/shard_map/ppermute | solution.py:36
  86.4 29.6 %copy-start.36 = (s32[64]{0:T(128)S(1)}, s32[64]{0:T(128)}, u32[]{:S(2)}) copy-start(s32[64]{0:T(128)} %param.19) | copy-start | bytes 772
  86.4 3.8 %copy-start.32 = (bf16[2,64,2,128]{3,1,2,0:T(8,128)(2,1)}, bf16[2,64,2,128]{3,1,2,0:T(8,128)(2,1)S(1)}, u32[]{:S(2)}) copy-start(bf16[2,64,2,128]{3,1,2,0:T(8,128)(2,1)S(1)} %fusion.48) | copy-start | bytes 196612
  86.5 7.2 %collective-permute-start.8 = (bf16[2,64,2,128]{3,1,2,0:T(8,128)(2,1)S(1)}, bf16[2,64,2,128]{3,1,2,0:T(8,128)(2,1)}, u32[]{:S(2)}, u32[]{:S(2)}) collective-permute-start(bf16[2,64,2,128]{3,1,2,0:T(8,128)(2,1)S(1)} %fusion.48), channel_id=1, source_target_pairs={{0,2},{1,3},{2,0},{3,1},{4,6},{5,7},{6,4},{7,5},{8,10},{9,11},{10,... | collective-permute-start | bytes 196616 | tf_op jit(solution)/shard_map/ppermute | solution.py:47
  95.9 8.0 %collective-permute-start.9 = (bf16[2,2,64,2,128]{4,2,3,1,0:T(8,128)(2,1)}, bf16[2,2,64,2,128]{4,2,3,1,0:T(8,128)(2,1)}, u32[]{:S(2)}, u32[]{:S(2)}) collective-permute-start(bf16[2,2,64,2,128]{4,2,3,1,0:T(8,128)(2,1)} %pad_maximum_fusion.13), channel_id=1, source_target_pairs={{0,1},{1,0},{2,3},{3,2},{4,5},{5,4},{6,7},{7,6},{8,9},{9,8},{10,11... | collective-permute-start | bytes 393224 | tf_op jit(solution)/shard_map/ppermute | solution.py:47
  104.8 1.4 copy-start.25
  106.1 7.0 %collective-permute-start.10 = (bf16[2,2,2,64,2,128]{5,3,4,2,1,0:T(8,128)(2,1)}, bf16[2,2,2,64,2,128]{5,3,4,2,1,0:T(8,128)(2,1)}, u32[]{:S(2)}, u32[]{:S(2)}) collective-permute-start(bf16[2,2,2,64,2,128]{5,3,4,2,1,0:T(8,128)(2,1)} %pad_maximum_fusion.10), channel_id=1, source_target_pairs={{0,8},{1,9},{2,10},{3,11},{4,12},{5,13},{6,14},{7,15},{8,0},{9,1},... | collective-permute-start | bytes 786440 | tf_op jit(solution)/shard_map/ppermute | solution.py:47
  114.3 9.8 %collective-permute-start.11 = (bf16[2,2,2,2,64,2,128]{6,4,5,3,2,1,0:T(8,128)(2,1)S(1)}, bf16[2,2,2,2,64,2,128]{6,4,5,3,2,1,0:T(8,128)(2,1)S(1)}, u32[]{:S(2)}, u32[]{:S(2)}) collective-permute-start(bf16[2,2,2,2,64,2,128]{6,4,5,3,2,1,0:T(8,128)(2,1)S(1)} %pad_maximum_fusion.7), channel_id=1, source_target_pairs={{0,4},{1,5},{2,6},{3,7},{4,0},{5,1},{6,2},{7,3},{8,12},{9,13},{10,... | collective-permute-start | bytes 1572872 | tf_op jit(solution)/shard_map/ppermute | solution.py:47
  126.9 9.3 %copy-start.15 = (f32[2,64,4,128]{3,1,0,2:T(8,128)}, f32[2,64,4,128]{3,1,0,2:T(8,128)S(1)}, u32[]{:S(2)}) copy-start(f32[2,64,4,128]{3,1,0,2:T(8,128)S(1)} %fusion.21) | copy-start | bytes 786436
  126.9 9.2 %collective-permute-start.12 = (bf16[4,2,64,128]{3,2,1,0:T(8,128)(2,1)S(1)}, bf16[4,2,64,128]{3,2,1,0:T(8,128)(2,1)S(1)}, u32[]{:S(2)}, u32[]{:S(2)}) collective-permute-start(bf16[4,2,64,128]{3,2,1,0:T(8,128)(2,1)S(1)} %convert_bitcast_fusion), channel_id=1, source_target_pairs={{0,2},{1,3},{2,0},{3,1},{4,6},{5,7},{6,4},{7,5},{8,10},{9,11},{10,... | collective-permute-start | bytes 393224 | tf_op jit(solution)/shard_map/ppermute | solution.py:47
  136.2 12.3 %collective-permute-start.13 = (bf16[2,4,2,64,128]{4,3,2,1,0:T(8,128)(2,1)S(1)}, bf16[2,4,2,64,128]{4,3,2,1,0:T(8,128)(2,1)S(1)}, u32[]{:S(2)}, u32[]{:S(2)}) collective-permute-start(bf16[2,4,2,64,128]{4,3,2,1,0:T(8,128)(2,1)S(1)} %pad_maximum_fusion.11), channel_id=1, source_target_pairs={{0,1},{1,0},{2,3},{3,2},{4,5},{5,4},{6,7},{7,6},{8,9},{9,8},{10,11... | collective-permute-start | bytes 786440 | tf_op jit(solution)/shard_map/ppermute | solution.py:47
  148.5 1.5 copy-start.21
  150.1 9.9 %collective-permute-start.14 = (bf16[2,2,4,2,64,128]{5,4,3,2,0,1:T(8,128)(2,1)}, bf16[2,2,4,2,64,128]{5,4,3,2,0,1:T(8,128)(2,1)}, u32[]{:S(2)}, u32[]{:S(2)}) collective-permute-start(bf16[2,2,4,2,64,128]{5,4,3,2,0,1:T(8,128)(2,1)} %pad_maximum_fusion.8), channel_id=1, source_target_pairs={{0,8},{1,9},{2,10},{3,11},{4,12},{5,13},{6,14},{7,15},{8,0},{9,1},... | collective-permute-start | bytes 1572872 | tf_op jit(solution)/shard_map/ppermute | solution.py:47
  161.2 1.9 copy-start.12
  163.1 21.0 %collective-permute-start.15 = (bf16[2,2,2,4,2,64,128]{6,5,4,3,1,2,0:T(8,128)(2,1)}, bf16[2,2,2,4,2,64,128]{6,5,4,3,1,2,0:T(8,128)(2,1)}, u32[]{:S(2)}, u32[]{:S(2)}) collective-permute-start(bf16[2,2,2,4,2,64,128]{6,5,4,3,1,2,0:T(8,128)(2,1)} %pad_maximum_fusion.5), channel_id=1, source_target_pairs={{0,4},{1,5},{2,6},{3,7},{4,0},{5,1},{6,2},{7,3},{8,12},{9,13},{10,... | collective-permute-start | bytes 3145736 | tf_op jit(solution)/shard_map/ppermute | solution.py:47
  191.7 4.7 %collective-permute-start.16 = (bf16[64,2,2,128]{3,0,1,2:T(8,128)(2,1)S(1)}, bf16[64,2,2,128]{3,0,1,2:T(8,128)(2,1)S(1)}, u32[]{:S(2)}, u32[]{:S(2)}) collective-permute-start(bf16[64,2,2,128]{3,0,1,2:T(8,128)(2,1)S(1)} %fusion.25), channel_id=1, source_target_pairs={{0,64},{16,80},{32,96},{48,112},{64,0},{80,16},{96,32},{112,48},{1... | collective-permute-start | bytes 196616 | tf_op jit(solution)/shard_map/ppermute | solution.py:47
  196.5 6.6 %collective-permute-start.17 = (bf16[2,64,2,2,128]{4,1,2,3,0:T(8,128)(2,1)S(1)}, bf16[2,64,2,2,128]{4,1,2,3,0:T(8,128)(2,1)S(1)}, u32[]{:S(2)}, u32[]{:S(2)}) collective-permute-start(bf16[2,64,2,2,128]{4,1,2,3,0:T(8,128)(2,1)S(1)} %pad_maximum_fusion.14), channel_id=1, source_target_pairs={{0,128},{16,144},{32,160},{48,176},{64,192},{80,208},{96,224},{112... | collective-permute-start | bytes 393224 | tf_op jit(solution)/shard_map/ppermute | solution.py:47
  203.2 6.9 %collective-permute-start.18 = (bf16[2,2,64,2,2,128]{5,2,3,4,1,0:T(8,128)(2,1)S(1)}, bf16[2,2,64,2,2,128]{5,2,3,4,1,0:T(8,128)(2,1)S(1)}, u32[]{:S(2)}, u32[]{:S(2)}) collective-permute-start(bf16[2,2,64,2,2,128]{5,2,3,4,1,0:T(8,128)(2,1)S(1)} %pad_maximum_fusion.12), channel_id=1, source_target_pairs={{0,32},{16,48},{32,0},{48,16},{64,96},{80,112},{96,64},{112,80},{1... | collective-permute-start | bytes 786440 | tf_op jit(solution)/shard_map/ppermute | solution.py:47
  206.6 10.8 %copy-start.30 = (pred[513,129]{1,0:T(8,128)(4,1)S(1)}, pred[513,129]{1,0:T(8,128)(4,1)}, u32[]{:S(2)}) copy-start(pred[513,129]{1,0:T(8,128)(4,1)} %broadcast_and_fusion) | copy-start | bytes 198535
  210.1 11.4 %collective-permute-start.19 = (bf16[2,2,2,64,2,2,128]{6,3,4,5,1,0,2:T(8,128)(2,1)S(1)}, bf16[2,2,2,64,2,2,128]{6,3,4,5,1,0,2:T(8,128)(2,1)S(1)}, u32[]{:S(2)}, u32[]{:S(2)}) collective-permute-start(bf16[2,2,2,64,2,2,128]{6,3,4,5,1,0,2:T(8,128)(2,1)S(1)} %pad_maximum_fusion.9), channel_id=1, source_target_pairs={{0,16},{16,0},{32,48},{48,32},{64,80},{80,64},{96,112},{112,96},{1... | collective-permute-start | bytes 1572872 | tf_op jit(solution)/shard_map/ppermute | solution.py:47
  219.1 1.5 copy-start.16
  221.6 1.4 copy-start.9
  221.8 3.8 %copy-start.28 = (bf16[2,2,2,2,64,2,2,128]{7,4,3,2,1,0,6,5:T(8,128)(2,1)}, bf16[2,2,2,2,64,2,2,128]{7,4,3,2,1,0,6,5:T(8,128)(2,1)S(1)}, u32[]{:S(2)}) copy-start(bf16[2,2,2,2,64,2,2,128]{7,4,3,2,1,0,6,5:T(8,128)(2,1)S(1)} %copy.147) | copy-start | bytes 3145732
  224.3 1.3 copy-start.7
  227.0 4.4 %copy-start.5 = (f32[2,512,128]{2,1,0:T(8,128)S(1)}, f32[2,512,128]{2,1,0:T(8,128)}, u32[]{:S(2)}) copy-start(f32[2,512,128]{2,1,0:T(8,128)} %param.10) | copy-start | bytes 1572868
  227.0 4.4 %copy-start.13 = (f32[2,513,129]{2,1,0:T(8,128)S(1)}, f32[2,513,129]{2,1,0:T(8,128)}, u32[]{:S(2)}) copy-start(f32[2,513,129]{2,1,0:T(8,128)} %get-tuple-element.26) | copy-start | bytes 1588252
  227.1 6.9 %copy-start.1 = (bf16[8,128,128]{2,1,0:T(8,128)(2,1)S(1)}, bf16[8,128,128]{2,1,0:T(8,128)(2,1)}, u32[]{:S(2)}) copy-start(bf16[8,128,128]{2,1,0:T(8,128)(2,1)} %param.16) | copy-start | bytes 786436
  (9 other events, 7.2 us)

commit v11 on v3

--- a/solution.py
+++ b/solution.py
@@ -116,7 +116,12 @@
     dual_b = dual_new.astype(jnp.bfloat16)
     all_rows = doubling_gather(jnp.moveaxis(dual_b, 2, 0), "tile", (2, 1, 8, 4))
     all_rows = jnp.moveaxis(all_rows.reshape(-1, *all_rows.shape[2:]), 0, 2)
-    chosen = jnp.take(all_rows, foot_mine, axis=2)
+    row_pick = (foot_mine[:, :, None] == jnp.arange(range_rows, dtype=jnp.int32)).astype(
+        jnp.bfloat16
+    )
+    chosen = jnp.einsum(
+        "jfk,cpkv->cpjfv", row_pick, all_rows, preferred_element_type=jnp.float32
+    ).astype(jnp.bfloat16)
     back = jnp.einsum("cpjfv,jfuv->cjpu", chosen, kern_mine, preferred_element_type=jnp.float32)
     back_b = back.astype(jnp.bfloat16)
     piece = doubling_gather(jnp.moveaxis(back_b, 2, 0), "az", (4, 8, 2, 1))

time: 193 us -> 188 us (0.974)
  starting transfers between devices: 51.5 us -> 42.4 us
  waiting for transfers between devices: 78.2 us -> 86.4 us
  other arithmetic: 23.3 us -> 20.5 us
    ppermute x12, waiting for transfers between devices: 48.6 us -> 56.5 us  [doubling_gather(): got = lax.ppermute(block, axis, pairs)]
    ppermute x12, starting transfers between devices: 28.5 us -> 22.6 us  [doubling_gather(): got = lax.ppermute(block, axis, pairs)]
    ppermute x2, starting transfers between devices: 14.7 us -> 11.5 us  [padded_2(): lax.ppermute(lax.slice_in_dim(block, block.shape[dim] - width, None, axis...]
    gather x1 -> x0, local copies, waits for them, and re-layouts: 3.07 us -> none  [on_device(): chosen = jnp.take(all_rows, foot_mine, axis=2)]
    another operation x2, other arithmetic: 5.12 us -> 2.87 us  [on_device(): jnp.stack([grad_rows, grad_cols])]
  transfers between devices with their start and end apart: 20 -> 20, of which waited for: 15 -> 15; matrix products, arithmetic and copies ran while one was open for 13% -> 12% of each run, Pallas kernels for 0% -> 0%
where the time goes in v11:
time: 188 us; the launch traced here: 187 us
  waiting for transfers between devices  86.4 us (46%)
  starting transfers between devices  42.4 us (23%)
  local copies, waits for them, and re-layouts  22.8 us (12%)
  other arithmetic  20.5 us (11%)
  matrix products  13.2 us (7%)
    ppermute x12, waiting for transfers between devices, doubling_gather(): got = lax.ppermute(block, axis, pairs)  56.5 us
    ppermute x4, waiting for transfers between devices, halving_sum(): blocks = keep + lax.ppermute(send, axis, pairs)  25.9 us
    ppermute x12, starting transfers between devices, doubling_gather(): got = lax.ppermute(block, axis, pairs)  22.6 us
    ppermute x2, starting transfers between devices, padded_2(): lax.ppermute(lax.slice_in_dim(block, block.shape[dim] - width, None, axis...  11.5 us
    unnamed x68, local copies, waits for them, and re-layouts  5.75 us
    ppermute x4, starting transfers between devices, halving_sum(): blocks = keep + lax.ppermute(send, axis, pairs)  5.1 us
    another operation x24, other arithmetic, doubling_gather(): block = jnp.stack([low, high], axis=place)  4.32 us
    ppermute x2, waiting for transfers between devices, padded_2(): lax.ppermute(lax.slice_in_dim(block, 0, width, axis=dim), axis, backward)  4.05 us
  transfers between devices with their start and end apart: 20, of which 15 were waited for; matrix products, arithmetic and copies ran while one was open for 12% of the time, Pallas kernels for 0%

profile of v11, /device:TPU:1, one launch (start us, length us, event | category | flops | bytes accessed | tf_op | source)
XLA Modules:
  0.0 186.8 jit_solution(4471187351331160619)
XLA Ops:
  0.7 2.7 %fusion.74 = (bf16[1,1024,2,256]{3,2,1,0:T(2,128)(2,1)S(1)}, bf16[1,1024,2,256]{3,2,1,0:T(2,128)(2,1)S(1)}) fusion(bf16[2,1024,2,256]{3,2,1,0:T(2,128)(2,1)} %param.14), kind=kLoop, calls=%fused_computation.170 | loop fusion | bytes 4194304 | tf_op jit(solution)/shard_map/slice | solution.py:75
  6.9 1.6 multiply_subtract_fusion
  8.8 1.6 copy.125
  11.9 3.2 %collective-permute-start = (f32[2,2,2,2,64,2,128]{6,4,5,3,2,1,0:T(8,128)}, f32[2,2,2,2,64,2,128]{6,4,5,3,2,1,0:T(8,128)S(1)}, u32[]{:S(2)}, u32[]{:S(2)}) collective-permute-start(f32[2,2,2,2,64,2,128]{6,4,5,3,2,1,0:T(8,128)} %bitcast.234), channel_id=1, source_target_pairs={{0,16},{16,0},{32,48},{48,32},{64,80},{80,64},{96,112},{112,96},{1... | collective-permute-start | bytes 3145736 | tf_op jit(solution)/shard_map/ppermute | solution.py:36
  15.2 2.5 %collective-permute-done = f32[2,2,2,2,64,2,128]{6,4,5,3,2,1,0:T(8,128)S(1)} collective-permute-done((f32[2,2,2,2,64,2,128]{6,4,5,3,2,1,0:T(8,128)}, f32[2,2,2,2,64,2,128]{6,4,5,3,2,1,0:T(8,128)S(1)}, u32[]{:S(2)}, u32[]{:S(2)}) %collective-permute-start) | collective-permute-done | bytes 1048608 | tf_op jit(solution)/shard_map/ppermute | solution.py:36
  18.7 1.4 bitcast_add_fusion
  20.2 13.1 %collective-permute-done.1 = f32[2,2,2,64,2,128]{5,3,4,2,1,0:T(8,128)S(1)} collective-permute-done((f32[2,2,2,64,2,128]{5,3,4,2,1,0:T(8,128)S(1)}, f32[2,2,2,64,2,128]{5,3,4,2,1,0:T(8,128)S(1)}, u32[]{:S(2)}, u32[]{:S(2)}) %collective-permute-start.1) | collective-permute-done | bytes 524320 | tf_op jit(solution)/shard_map/ppermute | solution.py:36
  33.6 6.5 %collective-permute-done.2 = f32[2,2,64,2,128]{4,2,3,1,0:T(8,128)S(1)} collective-permute-done((f32[2,2,64,2,128]{4,2,3,1,0:T(8,128)S(1)}, f32[2,2,64,2,128]{4,2,3,1,0:T(8,128)S(1)}, u32[]{:S(2)}, u32[]{:S(2)}) %collective-permute-start.2) | collective-permute-done | bytes 262176 | tf_op jit(solution)/shard_map/ppermute | solution.py:36
  40.2 1.7 collective-permute-start.3
  41.9 3.7 %collective-permute-done.3 = f32[2,64,2,128]{3,1,0,2:T(8,128)S(1)} collective-permute-done((f32[2,64,2,128]{3,1,0,2:T(8,128)S(1)}, f32[2,64,2,128]{3,1,0,2:T(8,128)S(1)}, u32[]{:S(2)}, u32[]{:S(2)}) %collective-permute-start.3) | collective-permute-done | bytes 131104 | tf_op jit(solution)/shard_map/ppermute | solution.py:36
  45.6 5.3 %collective-permute-start.4 = (bf16[2,64,2,128]{3,1,2,0:T(8,128)(2,1)S(1)}, bf16[2,64,2,128]{3,1,2,0:T(8,128)(2,1)S(1)}, u32[]{:S(2)}, u32[]{:S(2)}) collective-permute-start(bf16[2,64,2,128]{3,1,2,0:T(8,128)(2,1)S(1)} %fusion.60), channel_id=1, source_target_pairs={{0,2},{1,3},{2,0},{3,1},{4,6},{5,7},{6,4},{7,5},{8,10},{9,11},{10,... | collective-permute-start | bytes 196616 | tf_op jit(solution)/shard_map/ppermute | solution.py:47
  50.9 2.0 %collective-permute-done.4 = bf16[2,64,2,128]{3,1,2,0:T(8,128)(2,1)S(1)} collective-permute-done((bf16[2,64,2,128]{3,1,2,0:T(8,128)(2,1)S(1)}, bf16[2,64,2,128]{3,1,2,0:T(8,128)(2,1)S(1)}, u32[]{:S(2)}, u32[]{:S(2)}) %collective-permute-start.4) | collective-permute-done | bytes 65568 | tf_op jit(solution)/shard_map/ppermute | solution.py:47
  52.9 2.5 %collective-permute-start.5 = (bf16[2,2,64,2,128]{4,2,3,1,0:T(8,128)(2,1)S(1)}, bf16[2,2,64,2,128]{4,2,3,1,0:T(8,128)(2,1)S(1)}, u32[]{:S(2)}, u32[]{:S(2)}) collective-permute-start(bf16[2,2,64,2,128]{4,2,3,1,0:T(8,128)(2,1)S(1)} %pad_maximum_fusion.26), channel_id=1, source_target_pairs={{0,1},{1,0},{2,3},{3,2},{4,5},{5,4},{6,7},{7,6},{8,9},{9,8},{10,11... | collective-permute-start | bytes 393224 | tf_op jit(solution)/shard_map/ppermute | solution.py:47
  55.4 4.6 %collective-permute-done.5 = bf16[2,2,64,2,128]{4,2,3,1,0:T(8,128)(2,1)S(1)} collective-permute-done((bf16[2,2,64,2,128]{4,2,3,1,0:T(8,128)(2,1)S(1)}, bf16[2,2,64,2,128]{4,2,3,1,0:T(8,128)(2,1)S(1)}, u32[]{:S(2)}, u32[]{:S(2)}) %collective-permute-start.5) | collective-permute-done | bytes 131104 | tf_op jit(solution)/shard_map/ppermute | solution.py:47
  60.0 3.0 %collective-permute-start.6 = (bf16[2,2,2,64,2,128]{5,3,4,2,1,0:T(8,128)(2,1)S(1)}, bf16[2,2,2,64,2,128]{5,3,4,2,1,0:T(8,128)(2,1)S(1)}, u32[]{:S(2)}, u32[]{:S(2)}) collective-permute-start(bf16[2,2,2,64,2,128]{5,3,4,2,1,0:T(8,128)(2,1)S(1)} %pad_maximum_fusion.23), channel_id=1, source_target_pairs={{0,8},{1,9},{2,10},{3,11},{4,12},{5,13},{6,14},{7,15},{8,0},{9,1},... | collective-permute-start | bytes 786440 | tf_op jit(solution)/shard_map/ppermute | solution.py:47
  63.1 3.8 %collective-permute-done.6 = bf16[2,2,2,64,2,128]{5,3,4,2,1,0:T(8,128)(2,1)S(1)} collective-permute-done((bf16[2,2,2,64,2,128]{5,3,4,2,1,0:T(8,128)(2,1)S(1)}, bf16[2,2,2,64,2,128]{5,3,4,2,1,0:T(8,128)(2,1)S(1)}, u32[]{:S(2)}, u32[]{:S(2)}) %collective-permute-start.6) | collective-permute-done | bytes 262176 | tf_op jit(solution)/shard_map/ppermute | solution.py:47
  66.9 1.4 collective-permute-start.7
  68.5 10.1 %collective-permute-done.7 = bf16[2,2,2,2,64,2,128]{6,4,5,3,2,1,0:T(8,128)(2,1)S(1)} collective-permute-done((bf16[2,2,2,2,64,2,128]{6,4,5,3,2,1,0:T(8,128)(2,1)S(1)}, bf16[2,2,2,2,64,2,128]{6,4,5,3,2,1,0:T(8,128)(2,1)S(1)}, u32[]{:S(2)}, u32[]{:S(2)}) %collective-permute-start.7) | collective-permute-done | bytes 524320 | tf_op jit(solution)/shard_map/ppermute | solution.py:47
  79.7 1.6 fusion.30
  81.3 4.4 %collective-permute-start.8 = (bf16[4,2,64,128]{3,2,1,0:T(8,128)(2,1)S(1)}, bf16[4,2,64,128]{3,2,1,0:T(8,128)(2,1)S(1)}, u32[]{:S(2)}, u32[]{:S(2)}) collective-permute-start(bf16[4,2,64,128]{3,2,1,0:T(8,128)(2,1)S(1)} %convert_bitcast_fusion), channel_id=1, source_target_pairs={{0,2},{1,3},{2,0},{3,1},{4,6},{5,7},{6,4},{7,5},{8,10},{9,11},{10,... | collective-permute-start | bytes 393224 | tf_op jit(solution)/shard_map/ppermute | solution.py:47
  85.7 3.4 %collective-permute-done.8 = bf16[4,2,64,128]{3,2,1,0:T(8,128)(2,1)S(1)} collective-permute-done((bf16[4,2,64,128]{3,2,1,0:T(8,128)(2,1)S(1)}, bf16[4,2,64,128]{3,2,1,0:T(8,128)(2,1)S(1)}, u32[]{:S(2)}, u32[]{:S(2)}) %collective-permute-start.8) | collective-permute-done | bytes 131104 | tf_op jit(solution)/shard_map/ppermute | solution.py:47
  89.6 15.5 %collective-permute-done.9 = bf16[2,4,2,64,128]{4,3,2,1,0:T(8,128)(2,1)S(1)} collective-permute-done((bf16[2,4,2,64,128]{4,3,2,1,0:T(8,128)(2,1)S(1)}, bf16[2,4,2,64,128]{4,3,2,1,0:T(8,128)(2,1)S(1)}, u32[]{:S(2)}, u32[]{:S(2)}) %collective-permute-start.9) | collective-permute-done | bytes 262176 | tf_op jit(solution)/shard_map/ppermute | solution.py:47
  106.1 1.7 slice_maximum_fusion
  107.8 1.9 %copy.147 = f32[6,512,1]{1,2,0:T(1,128)S(1)} copy(f32[6,512,1]{2,1,0:T(8,128)} %get-tuple-element.30) | data formatting | bytes 24576 | tf_op jit(solution)/shard_map/slice | solution.py:17
  109.6 10.2 %collective-permute-start.16 = (f32[6,512,1]{1,2,0:T(1,128)S(1)}, f32[6,512,1]{1,2,0:T(1,128)S(1)}, u32[]{:S(2)}, u32[]{:S(2)}) collective-permute-start(f32[6,512,1]{1,2,0:T(1,128)S(1)} %copy.147), channel_id=1, source_target_pairs={{0,16},{16,32},{32,48},{48,64},{64,80},{80,96},{96,112},{112,128},... | collective-permute-start | bytes 36872 | tf_op jit(solution)/shard_map/ppermute | solution.py:16
  120.9 1.9 %collective-permute-start.17 = (f32[6,512,1]{1,2,0:T(1,128)}, f32[6,512,1]{1,2,0:T(1,128)}, u32[]{:S(2)}, u32[]{:S(2)}) collective-permute-start(f32[6,512,1]{1,2,0:T(1,128)} %copy.148), channel_id=1, source_target_pairs={{16,0},{32,16},{48,32},{64,48},{80,64},{96,80},{112,96},{128,112},... | collective-permute-start | bytes 36872 | tf_op jit(solution)/shard_map/ppermute | solution.py:19
  129.2 1.5 pad_maximum_fusion.28
  130.6 1.3 collective-permute-start.18
  131.9 1.3 collective-permute-start.19
  134.5 1.5 gather_fusion
  136.0 4.0 %collective-permute-done.19 = f32[6,1,130]{2,1,0:T(1,128)} collective-permute-done((f32[6,1,130]{2,1,0:T(1,128)}, f32[6,1,130]{2,1,0:T(1,128)}, u32[]{:S(2)}, u32[]{:S(2)}) %collective-permute-start.19) | collective-permute-done | bytes 3152 | tf_op jit(solution)/shard_map/ppermute | solution.py:19
  140.0 2.2 %fusion.42 = f32[1,2,513,129]{3,2,1,0:T(8,128)S(1)} fusion(f32[6,1,130]{2,1,0:T(1,128)} %collective-permute-done.19, f32[6,512,1]{2,1,0:T(8,128)S(1)} %copy.150, f32[6,512,1]{2,1,0:T(8,128)S(1)} %copy.149, f32[4,512,128]{2,1,0:T(8,128)} %bitcast.239, f32[2,512,128]{2,1,0:T(8,128)} %param.10, f32[6,1,130]{2,1,0:T(1,128)S(1)} %collective-permute-done.18, ...), kind=kLoop, calls=%fused_computation.57 | loop fusion | flops 1323540 | bytes 2133609 | tf_op jit(solution)/shard_map/stack | solution.py:160
  142.3 7.4 %collective-permute-done.11 = bf16[2,2,2,4,2,64,128]{6,5,4,3,1,2,0:T(8,128)(2,1)} collective-permute-done((bf16[2,2,2,4,2,64,128]{6,5,4,3,1,2,0:T(8,128)(2,1)}, bf16[2,2,2,4,2,64,128]{6,5,4,3,1,2,0:T(8,128)(2,1)}, u32[]{:S(2)}, u32[]{:S(2)}) %collective-permute-start.11) | collective-permute-done | bytes 1048608 | tf_op jit(solution)/shard_map/ppermute | solution.py:47
  149.7 1.4 select_bitcast_fusion.1
  152.0 1.3 fusion.10
  153.5 1.7 collective-permute-start.12
  155.8 2.8 %collective-permute-done.12 = bf16[64,2,2,128]{3,0,1,2:T(8,128)(2,1)S(1)} collective-permute-done((bf16[64,2,2,128]{3,0,1,2:T(8,128)(2,1)S(1)}, bf16[64,2,2,128]{3,0,1,2:T(8,128)(2,1)S(1)}, u32[]{:S(2)}, u32[]{:S(2)}) %collective-permute-start.12) | collective-permute-done | bytes 65568 | tf_op jit(solution)/shard_map/ppermute | solution.py:47
  158.8 1.6 pad_maximum_fusion
  160.4 2.2 %collective-permute-done.13 = bf16[2,64,2,2,128]{4,1,2,3,0:T(8,128)(2,1)S(1)} collective-permute-done((bf16[2,64,2,2,128]{4,1,2,3,0:T(8,128)(2,1)S(1)}, bf16[2,64,2,2,128]{4,1,2,3,0:T(8,128)(2,1)S(1)}, u32[]{:S(2)}, u32[]{:S(2)}) %collective-permute-start.13) | collective-permute-done | bytes 131104 | tf_op jit(solution)/shard_map/ppermute | solution.py:47
  163.3 4.6 %collective-permute-done.14 = bf16[2,2,64,2,2,128]{5,2,3,4,1,0:T(8,128)(2,1)S(1)} collective-permute-done((bf16[2,2,64,2,2,128]{5,2,3,4,1,0:T(8,128)(2,1)S(1)}, bf16[2,2,64,2,2,128]{5,2,3,4,1,0:T(8,128)(2,1)S(1)}, u32[]{:S(2)}, u32[]{:S(2)}) %collective-permute-start.14) | collective-permute-done | bytes 262176 | tf_op jit(solution)/shard_map/ppermute | solution.py:47
  168.1 3.8 %collective-permute-start.15 = (bf16[2,2,2,64,2,2,128]{6,3,4,5,1,0,2:T(8,128)(2,1)S(1)}, bf16[2,2,2,64,2,2,128]{6,3,4,5,1,0,2:T(8,128)(2,1)S(1)}, u32[]{:S(2)}, u32[]{:S(2)}) collective-permute-start(bf16[2,2,2,64,2,2,128]{6,3,4,5,1,0,2:T(8,128)(2,1)S(1)} %pad_maximum_fusion.22), channel_id=1, source_target_pairs={{0,16},{16,0},{32,48},{48,32},{64,80},{80,64},{96,112},{112,96},{1... | collective-permute-start | bytes 1572872 | tf_op jit(solution)/shard_map/ppermute | solution.py:47
  172.3 1.3 slice.126
  176.0 1.5 copy-done.10
  177.5 1.3 fusion.51
  178.8 1.3 fusion.50
  180.1 1.3 fusion.16
  181.6 2.4 %fusion.17 = f32[2,256,128]{1,2,0:T(8,128)S(1)} fusion(f32[2,128,256]{2,1,0:T(8,128)S(1)} %fusion.50, bf16[1,1024,2,256]{3,2,1,0:T(2,128)(2,1)S(1)} %copy-done.8, f32[2,1024]{1,0:T(2,128)S(1)} %copy-done.26, f32[2,1024]{1,0:T(2,128)S(1)} %copy-done.27, bf16[2,2,1024,128]{3,2,1,0:T(8,128)(2,1)} %bitcast.259), kind=kOutput, calls=%fused_computation.33 | convolution fusion | flops 135856128 | bytes 2637824 | tf_op jit(solution)/shard_map/pjh,jpu->jhu/dot_general | solution.py:142
  184.1 2.7 %fusion.56 = f32[2,512,128]{2,1,0:T(8,128)} fusion(f32[2,512,128]{2,1,0:T(8,128)S(1)} %copy-done.6, f32[2,513,129]{2,1,0:T(8,128)} %get-tuple-element.21, f32[2,513,129]{2,1,0:T(8,128)S(1)} %get-tuple-element.20, f32[1,512,128]{2,1,0:T(8,128)S(1)} %bitcast.255, f32[1,512,128]{2,1,0:T(8,128)S(1)} %bitcast.254), kind=kLoop, calls=%fused_computation.87 | loop fusion | flops 917504 | bytes 3670016 | tf_op jit(solution)/shard_map/sub | solution.py:172
  (148 shorter events, 23.8 us)
Async XLA Ops:
  0.6 78.9 %copy-start = (bf16[8,128,128]{2,1,0:T(8,128)(2,1)S(1)}, bf16[8,128,128]{2,1,0:T(8,128)(2,1)}, u32[]{:S(2)}) copy-start(bf16[8,128,128]{2,1,0:T(8,128)(2,1)} %param.16) | copy-start | bytes 786436
  0.7 2.8 %copy-start.4 = (f32[2,512,128]{2,1,0:T(8,128)S(1)}, f32[2,512,128]{2,1,0:T(8,128)}, u32[]{:S(2)}) copy-start(f32[2,512,128]{2,1,0:T(8,128)} %param.10) | copy-start | bytes 1572868
  3.4 1.0 copy-start.9
  3.5 3.5 %copy-start.7 = (bf16[1,1024,2,256]{3,2,1,0:T(2,128)(2,1)}, bf16[1,1024,2,256]{3,2,1,0:T(2,128)(2,1)S(1)}, u32[]{:S(2)}) copy-start(bf16[1,1024,2,256]{3,2,1,0:T(2,128)(2,1)S(1)} %get-tuple-element.28) | copy-start | bytes 3145732
  11.9 5.7 %collective-permute-start = (f32[2,2,2,2,64,2,128]{6,4,5,3,2,1,0:T(8,128)}, f32[2,2,2,2,64,2,128]{6,4,5,3,2,1,0:T(8,128)S(1)}, u32[]{:S(2)}, u32[]{:S(2)}) collective-permute-start(f32[2,2,2,2,64,2,128]{6,4,5,3,2,1,0:T(8,128)} %bitcast.234), channel_id=1, source_target_pairs={{0,16},{16,0},{32,48},{48,32},{64,80},{80,64},{96,112},{112,96},{1... | collective-permute-start | bytes 3145736 | tf_op jit(solution)/shard_map/ppermute | solution.py:36
  20.1 13.2 %collective-permute-start.1 = (f32[2,2,2,64,2,128]{5,3,4,2,1,0:T(8,128)S(1)}, f32[2,2,2,64,2,128]{5,3,4,2,1,0:T(8,128)S(1)}, u32[]{:S(2)}, u32[]{:S(2)}) collective-permute-start(f32[2,2,2,64,2,128]{5,3,4,2,1,0:T(8,128)S(1)} %dynamic-slice_bitcast_fusion), channel_id=1, source_target_pairs={{0,128},{16,144},{32,160},{48,176},{64,192},{80,208},{96,224},{112... | collective-permute-start | bytes 1572872 | tf_op jit(solution)/shard_map/ppermute | solution.py:36
  33.4 6.7 %collective-permute-start.2 = (f32[2,2,64,2,128]{4,2,3,1,0:T(8,128)S(1)}, f32[2,2,64,2,128]{4,2,3,1,0:T(8,128)S(1)}, u32[]{:S(2)}, u32[]{:S(2)}) collective-permute-start(f32[2,2,64,2,128]{4,2,3,1,0:T(8,128)S(1)} %dynamic-slice_bitcast_fusion.1), channel_id=1, source_target_pairs={{0,32},{16,48},{32,0},{48,16},{64,96},{80,112},{96,64},{112,80},{1... | collective-permute-start | bytes 786440 | tf_op jit(solution)/shard_map/ppermute | solution.py:36
  40.1 22.9 %copy-start.22 = (s32[32,1,6]{0,1,2:T(1,128)S(1)}, s32[32,1,6]{0,1,2:T(1,128)}, u32[]{:S(2)}) copy-start(s32[32,1,6]{0,1,2:T(1,128)} %param.17) | copy-start | bytes 2308
  40.1 22.9 %copy-start.23 = (s32[32,1,6]{0,1,2:T(1,128)S(1)}, s32[32,1,6]{0,1,2:T(1,128)}, u32[]{:S(2)}) copy-start(s32[32,1,6]{0,1,2:T(1,128)} %param.18) | copy-start | bytes 2308
  40.2 5.4 %collective-permute-start.3 = (f32[2,64,2,128]{3,1,0,2:T(8,128)S(1)}, f32[2,64,2,128]{3,1,0,2:T(8,128)S(1)}, u32[]{:S(2)}, u32[]{:S(2)}) collective-permute-start(f32[2,64,2,128]{3,1,0,2:T(8,128)S(1)} %bitcast.261), channel_id=1, source_target_pairs={{0,64},{16,80},{32,96},{48,112},{64,0},{80,16},{96,32},{112,48},{1... | collective-permute-start | bytes 393224 | tf_op jit(solution)/shard_map/ppermute | solution.py:36
  45.6 7.2 %collective-permute-start.4 = (bf16[2,64,2,128]{3,1,2,0:T(8,128)(2,1)S(1)}, bf16[2,64,2,128]{3,1,2,0:T(8,128)(2,1)S(1)}, u32[]{:S(2)}, u32[]{:S(2)}) collective-permute-start(bf16[2,64,2,128]{3,1,2,0:T(8,128)(2,1)S(1)} %fusion.60), channel_id=1, source_target_pairs={{0,2},{1,3},{2,0},{3,1},{4,6},{5,7},{6,4},{7,5},{8,10},{9,11},{10,... | collective-permute-start | bytes 196616 | tf_op jit(solution)/shard_map/ppermute | solution.py:47
  52.9 7.1 %collective-permute-start.5 = (bf16[2,2,64,2,128]{4,2,3,1,0:T(8,128)(2,1)S(1)}, bf16[2,2,64,2,128]{4,2,3,1,0:T(8,128)(2,1)S(1)}, u32[]{:S(2)}, u32[]{:S(2)}) collective-permute-start(bf16[2,2,64,2,128]{4,2,3,1,0:T(8,128)(2,1)S(1)} %pad_maximum_fusion.26), channel_id=1, source_target_pairs={{0,1},{1,0},{2,3},{3,2},{4,5},{5,4},{6,7},{7,6},{8,9},{9,8},{10,11... | collective-permute-start | bytes 393224 | tf_op jit(solution)/shard_map/ppermute | solution.py:47
  55.4 13.0 %copy-start.31 = (s32[64]{0:T(128)S(1)}, s32[64]{0:T(128)}, u32[]{:S(2)}) copy-start(s32[64]{0:T(128)} %param.19) | copy-start | bytes 772
  60.0 6.8 %collective-permute-start.6 = (bf16[2,2,2,64,2,128]{5,3,4,2,1,0:T(8,128)(2,1)S(1)}, bf16[2,2,2,64,2,128]{5,3,4,2,1,0:T(8,128)(2,1)S(1)}, u32[]{:S(2)}, u32[]{:S(2)}) collective-permute-start(bf16[2,2,2,64,2,128]{5,3,4,2,1,0:T(8,128)(2,1)S(1)} %pad_maximum_fusion.23), channel_id=1, source_target_pairs={{0,8},{1,9},{2,10},{3,11},{4,12},{5,13},{6,14},{7,15},{8,0},{9,1},... | collective-permute-start | bytes 786440 | tf_op jit(solution)/shard_map/ppermute | solution.py:47
  66.9 11.6 %collective-permute-start.7 = (bf16[2,2,2,2,64,2,128]{6,4,5,3,2,1,0:T(8,128)(2,1)S(1)}, bf16[2,2,2,2,64,2,128]{6,4,5,3,2,1,0:T(8,128)(2,1)S(1)}, u32[]{:S(2)}, u32[]{:S(2)}) collective-permute-start(bf16[2,2,2,2,64,2,128]{6,4,5,3,2,1,0:T(8,128)(2,1)S(1)} %pad_maximum_fusion.20), channel_id=1, source_target_pairs={{0,4},{1,5},{2,6},{3,7},{4,0},{5,1},{6,2},{7,3},{8,12},{9,13},{10,... | collective-permute-start | bytes 1572872 | tf_op jit(solution)/shard_map/ppermute | solution.py:47
  78.7 1.0 copy-start.21
  81.3 24.8 %copy-start.15 = (f32[2,64,4,128]{3,1,0,2:T(8,128)}, f32[2,64,4,128]{3,1,0,2:T(8,128)S(1)}, u32[]{:S(2)}) copy-start(f32[2,64,4,128]{3,1,0,2:T(8,128)S(1)} %fusion.30) | copy-start | bytes 786436
  81.3 24.7 %copy-start.2 = (f32[2,2,512,128]{3,2,1,0:T(8,128)S(1)}, f32[2,2,512,128]{3,2,1,0:T(8,128)}, u32[]{:S(2)}) copy-start(f32[2,2,512,128]{3,2,1,0:T(8,128)} %param.11) | copy-start | bytes 3145732
  81.3 7.8 %collective-permute-start.8 = (bf16[4,2,64,128]{3,2,1,0:T(8,128)(2,1)S(1)}, bf16[4,2,64,128]{3,2,1,0:T(8,128)(2,1)S(1)}, u32[]{:S(2)}, u32[]{:S(2)}) collective-permute-start(bf16[4,2,64,128]{3,2,1,0:T(8,128)(2,1)S(1)} %convert_bitcast_fusion), channel_id=1, source_target_pairs={{0,2},{1,3},{2,0},{3,1},{4,6},{5,7},{6,4},{7,5},{8,10},{9,11},{10,... | collective-permute-start | bytes 393224 | tf_op jit(solution)/shard_map/ppermute | solution.py:47
  89.2 16.0 %collective-permute-start.9 = (bf16[2,4,2,64,128]{4,3,2,1,0:T(8,128)(2,1)S(1)}, bf16[2,4,2,64,128]{4,3,2,1,0:T(8,128)(2,1)S(1)}, u32[]{:S(2)}, u32[]{:S(2)}) collective-permute-start(bf16[2,4,2,64,128]{4,3,2,1,0:T(8,128)(2,1)S(1)} %pad_maximum_fusion.24), channel_id=1, source_target_pairs={{0,1},{1,0},{2,3},{3,2},{4,5},{5,4},{6,7},{7,6},{8,9},{9,8},{10,11... | collective-permute-start | bytes 786440 | tf_op jit(solution)/shard_map/ppermute | solution.py:47
  106.1 17.5 %collective-permute-start.10 = (bf16[2,2,4,2,64,128]{5,4,3,2,0,1:T(8,128)(2,1)}, bf16[2,2,4,2,64,128]{5,4,3,2,0,1:T(8,128)(2,1)S(1)}, u32[]{:S(2)}, u32[]{:S(2)}) collective-permute-start(bf16[2,2,4,2,64,128]{5,4,3,2,0,1:T(8,128)(2,1)} %pad_maximum_fusion.21), channel_id=1, source_target_pairs={{0,8},{1,9},{2,10},{3,11},{4,12},{5,13},{6,14},{7,15},{8,0},{9,1},... | collective-permute-start | bytes 1572872 | tf_op jit(solution)/shard_map/ppermute | solution.py:47
  109.6 17.8 %collective-permute-start.16 = (f32[6,512,1]{1,2,0:T(1,128)S(1)}, f32[6,512,1]{1,2,0:T(1,128)S(1)}, u32[]{:S(2)}, u32[]{:S(2)}) collective-permute-start(f32[6,512,1]{1,2,0:T(1,128)S(1)} %copy.147), channel_id=1, source_target_pairs={{0,16},{16,32},{32,48},{48,64},{64,80},{80,96},{96,112},{112,128},... | collective-permute-start | bytes 36872 | tf_op jit(solution)/shard_map/ppermute | solution.py:16
  120.9 7.0 %collective-permute-start.17 = (f32[6,512,1]{1,2,0:T(1,128)}, f32[6,512,1]{1,2,0:T(1,128)}, u32[]{:S(2)}, u32[]{:S(2)}) collective-permute-start(f32[6,512,1]{1,2,0:T(1,128)} %copy.148), channel_id=1, source_target_pairs={{16,0},{32,16},{48,32},{64,48},{80,64},{96,80},{112,96},{128,112},... | collective-permute-start | bytes 36872 | tf_op jit(solution)/shard_map/ppermute | solution.py:19
  123.6 1.9 copy-start.13
  125.5 24.2 %collective-permute-start.11 = (bf16[2,2,2,4,2,64,128]{6,5,4,3,1,2,0:T(8,128)(2,1)}, bf16[2,2,2,4,2,64,128]{6,5,4,3,1,2,0:T(8,128)(2,1)}, u32[]{:S(2)}, u32[]{:S(2)}) collective-permute-start(bf16[2,2,2,4,2,64,128]{6,5,4,3,1,2,0:T(8,128)(2,1)} %pad_maximum_fusion.18), channel_id=1, source_target_pairs={{0,4},{1,5},{2,6},{3,7},{4,0},{5,1},{6,2},{7,3},{8,12},{9,13},{10,... | collective-permute-start | bytes 3145736 | tf_op jit(solution)/shard_map/ppermute | solution.py:47
  129.1 4.1 %copy-start.30 = (s32[12]{0:T(128)S(1)}, s32[12]{0:T(128)}, u32[]{:S(2)}) copy-start(s32[12]{0:T(128)} %reshape.155) | copy-start | bytes 148
  129.2 4.7 %copy-start.24 = (s32[2,1,6]{0,1,2:T(1,128)S(1)}, s32[2,1,6]{0,1,2:T(1,128)}, u32[]{:S(2)}) copy-start(s32[2,1,6]{0,1,2:T(1,128)} %get-tuple-element.70) | copy-start | bytes 148
  130.6 5.3 %collective-permute-start.18 = (f32[6,1,130]{2,1,0:T(1,128)}, f32[6,1,130]{2,1,0:T(1,128)S(1)}, u32[]{:S(2)}, u32[]{:S(2)}) collective-permute-start(f32[6,1,130]{2,1,0:T(1,128)} %get-tuple-element.19), channel_id=1, source_target_pairs={{0,1},{1,2},{2,3},{3,4},{4,5},{5,6},{6,7},{7,8},{8,9},{9,10},{10,1... | collective-permute-start | bytes 9368 | tf_op jit(solution)/shard_map/ppermute | solution.py:16
  131.9 8.1 %collective-permute-start.19 = (f32[6,1,130]{2,1,0:T(1,128)}, f32[6,1,130]{2,1,0:T(1,128)}, u32[]{:S(2)}, u32[]{:S(2)}) collective-permute-start(f32[6,1,130]{2,1,0:T(1,128)} %get-tuple-element.18), channel_id=1, source_target_pairs={{1,0},{2,1},{3,2},{4,3},{5,4},{6,5},{7,6},{8,7},{9,8},{10,9},{11,1... | collective-permute-start | bytes 9368 | tf_op jit(solution)/shard_map/ppermute | solution.py:19
  140.0 9.7 %copy-start.12 = (bf16[1,2,2,4,2,64,128]{6,5,4,3,1,2,0:T(8,128)(2,1)S(1)}, bf16[1,2,2,4,2,64,128]{6,5,4,3,1,2,0:T(8,128)(2,1)}, u32[]{:S(2)}) copy-start(bf16[1,2,2,4,2,64,128]{6,5,4,3,1,2,0:T(8,128)(2,1)} %copy-done.11) | copy-start | bytes 1572868
  140.0 9.7 %copy-start.14 = (bf16[1,2,2,4,2,64,128]{6,5,4,3,1,2,0:T(8,128)(2,1)S(1)}, bf16[1,2,2,4,2,64,128]{6,5,4,3,1,2,0:T(8,128)(2,1)}, u32[]{:S(2)}) copy-start(bf16[1,2,2,4,2,64,128]{6,5,4,3,1,2,0:T(8,128)(2,1)} %copy-done.13) | copy-start | bytes 1572868
  151.6 1.6 copy-start.19
  152.0 3.2 %copy-start.3 = (f32[2,2,512,128]{3,2,1,0:T(8,128)S(1)}, f32[2,2,512,128]{3,2,1,0:T(8,128)}, u32[]{:S(2)}) copy-start(f32[2,2,512,128]{3,2,1,0:T(8,128)} %param.11) | copy-start | bytes 3145732
  152.0 3.2 %copy-start.5 = (f32[2,512,128]{2,1,0:T(8,128)S(1)}, f32[2,512,128]{2,1,0:T(8,128)}, u32[]{:S(2)}) copy-start(f32[2,512,128]{2,1,0:T(8,128)} %param.10) | copy-start | bytes 1572868
  152.0 3.2 %copy-start.28 = (pred[129]{0:T(512)(128)(4,1)S(1)}, pred[129]{0:T(512)(128)(4,1)}, u32[]{:S(2)}) copy-start(pred[129]{0:T(512)(128)(4,1)} %get-tuple-element.64) | copy-start | bytes 391
  153.5 5.1 %collective-permute-start.12 = (bf16[64,2,2,128]{3,0,1,2:T(8,128)(2,1)S(1)}, bf16[64,2,2,128]{3,0,1,2:T(8,128)(2,1)S(1)}, u32[]{:S(2)}, u32[]{:S(2)}) collective-permute-start(bf16[64,2,2,128]{3,0,1,2:T(8,128)(2,1)S(1)} %fusion.34), channel_id=1, source_target_pairs={{0,64},{16,80},{32,96},{48,112},{64,0},{80,16},{96,32},{112,48},{1... | collective-permute-start | bytes 196616 | tf_op jit(solution)/shard_map/ppermute | solution.py:47
  158.7 3.9 %collective-permute-start.13 = (bf16[2,64,2,2,128]{4,1,2,3,0:T(8,128)(2,1)S(1)}, bf16[2,64,2,2,128]{4,1,2,3,0:T(8,128)(2,1)S(1)}, u32[]{:S(2)}, u32[]{:S(2)}) collective-permute-start(bf16[2,64,2,2,128]{4,1,2,3,0:T(8,128)(2,1)S(1)} %pad_maximum_fusion.27), channel_id=1, source_target_pairs={{0,128},{16,144},{32,160},{48,176},{64,192},{80,208},{96,224},{112... | collective-permute-start | bytes 393224 | tf_op jit(solution)/shard_map/ppermute | solution.py:47
  162.7 5.3 %collective-permute-start.14 = (bf16[2,2,64,2,2,128]{5,2,3,4,1,0:T(8,128)(2,1)S(1)}, bf16[2,2,64,2,2,128]{5,2,3,4,1,0:T(8,128)(2,1)S(1)}, u32[]{:S(2)}, u32[]{:S(2)}) collective-permute-start(bf16[2,2,64,2,2,128]{5,2,3,4,1,0:T(8,128)(2,1)S(1)} %pad_maximum_fusion.25), channel_id=1, source_target_pairs={{0,32},{16,48},{32,0},{48,16},{64,96},{80,112},{96,64},{112,80},{1... | collective-permute-start | bytes 786440 | tf_op jit(solution)/shard_map/ppermute | solution.py:47
  168.1 7.6 %collective-permute-start.15 = (bf16[2,2,2,64,2,2,128]{6,3,4,5,1,0,2:T(8,128)(2,1)S(1)}, bf16[2,2,2,64,2,2,128]{6,3,4,5,1,0,2:T(8,128)(2,1)S(1)}, u32[]{:S(2)}, u32[]{:S(2)}) collective-permute-start(bf16[2,2,2,64,2,2,128]{6,3,4,5,1,0,2:T(8,128)(2,1)S(1)} %pad_maximum_fusion.22), channel_id=1, source_target_pairs={{0,16},{16,0},{32,48},{48,32},{64,80},{80,64},{96,112},{112,96},{1... | collective-permute-start | bytes 1572872 | tf_op jit(solution)/shard_map/ppermute | solution.py:47
  172.3 1.3 copy-start.25
  173.6 1.2 copy-start.16
  175.9 1.6 copy-start.10
  175.9 1.6 copy-start.26
  175.9 1.6 copy-start.27
  176.0 4.1 %copy-start.18 = (bf16[2,2,2,2,64,2,2,128]{7,4,3,2,1,0,6,5:T(8,128)(2,1)}, bf16[2,2,2,2,64,2,2,128]{7,4,3,2,1,0,6,5:T(8,128)(2,1)S(1)}, u32[]{:S(2)}) copy-start(bf16[2,2,2,2,64,2,2,128]{7,4,3,2,1,0,6,5:T(8,128)(2,1)S(1)} %copy.140) | copy-start | bytes 3145732
  178.8 1.4 copy-start.8
  181.6 2.5 %copy-start.6 = (f32[2,512,128]{2,1,0:T(8,128)S(1)}, f32[2,512,128]{2,1,0:T(8,128)}, u32[]{:S(2)}) copy-start(f32[2,512,128]{2,1,0:T(8,128)} %param.10) | copy-start | bytes 1572868
  184.1 2.7 %copy-start.1 = (bf16[8,128,128]{2,1,0:T(8,128)(2,1)S(1)}, bf16[8,128,128]{2,1,0:T(8,128)(2,1)}, u32[]{:S(2)}) copy-start(bf16[8,128,128]{2,1,0:T(8,128)(2,1)} %param.16) | copy-start | bytes 786436
  (4 other events, 3.4 us)

commit v12 on v11

--- a/solution.py
+++ b/solution.py
@@ -144,33 +144,36 @@
     )
     adjoint = jnp.stack([grad_re, grad_im])
     adjoint = adjoint.reshape(2, strip_rows, columns)
-    stacked = jnp.concatenate([image, tv_dual.reshape(4, strip_rows, columns)], axis=0)
-    padded = padded_2(stacked, (("az", 2), ("tile", 1)), 1)
-    image_pad = padded[:2]
-    dual_pad = padded[2:].reshape(2, 2, strip_rows + 2, columns + 2)
     total_rows = tile_count * strip_rows
     total_cols = az_count * columns
-    global_row = tile_index * strip_rows - 1 + jnp.arange(strip_rows + 1, dtype=jnp.int32)
-    global_col = az_index * columns - 1 + jnp.arange(columns + 1, dtype=jnp.int32)
-    centre = image_pad[:, : strip_rows + 1, : columns + 1]
-    grad_rows = image_pad[:, 1 : strip_rows + 2, : columns + 1] - centre
-    grad_rows = jnp.where((global_row < total_rows - 1)[None, :, None], grad_rows, 0.0)
-    grad_cols = image_pad[:, : strip_rows + 1, 1 : columns + 2] - centre
-    grad_cols = jnp.where((global_col < total_cols - 1)[None, None, :], grad_cols, 0.0)
-    moved = dual_pad[:, :, : strip_rows + 1, : columns + 1] + dual_step * jnp.stack(
-        [grad_rows, grad_cols]
-    )
+    global_row = tile_index * strip_rows + jnp.arange(strip_rows, dtype=jnp.int32)
+    global_col = az_index * columns + jnp.arange(columns, dtype=jnp.int32)
+    last_row = (global_row == total_rows - 1)[None, :, None]
+    last_col = (global_col == total_cols - 1)[None, None, :]
+    up_tile = [(i + 1, i) for i in range(tile_count - 1)]
+    up_az = [(i + 1, i) for i in range(az_count - 1)]
+    next_row = lax.ppermute(image[:, :1, :], "tile", up_tile)
+    next_col = lax.ppermute(image[:, :, :1], "az", up_az)
+    grad_rows = jnp.concatenate([image[:, 1:, :], next_row], axis=1) - image
+    grad_rows = jnp.where(last_row, 0.0, grad_rows)
+    grad_cols = jnp.concatenate([image[:, :, 1:], next_col], axis=2) - image
+    grad_cols = jnp.where(last_col, 0.0, grad_cols)
+    moved = tv_dual + dual_step * jnp.stack([grad_rows, grad_cols])
     magnitude = jnp.sqrt(jnp.sum(moved * moved, axis=(0, 1)))
-    projected = moved / jnp.maximum(1.0, magnitude / edge_limit)
-    inside = (global_row >= 0)[:, None] & (global_col >= 0)[None, :]
-    projected = jnp.where(inside[None, None], projected, 0.0)
-    rows_part = jnp.where((global_row < total_rows - 1)[None, :, None], projected[0], 0.0)
-    cols_part = jnp.where((global_col < total_cols - 1)[None, None, :], projected[1], 0.0)
+    tv_new = moved / jnp.maximum(1.0, magnitude / edge_limit)
+    rows_part = jnp.where(last_row, 0.0, tv_new[0])
+    cols_part = jnp.where(last_col, 0.0, tv_new[1])
+    down_tile = [(i, i + 1) for i in range(tile_count - 1)]
+    down_az = [(i, i + 1) for i in range(az_count - 1)]
+    prev_row = lax.ppermute(rows_part[:, -1:, :], "tile", down_tile)
+    prev_col = lax.ppermute(cols_part[:, :, -1:], "az", down_az)
     divergence = (
-        rows_part[:, 1:, 1:] - rows_part[:, :-1, 1:] + cols_part[:, 1:, 1:] - cols_part[:, 1:, :-1]
+        rows_part
+        - jnp.concatenate([prev_row, rows_part[:, :-1, :]], axis=1)
+        + cols_part
+        - jnp.concatenate([prev_col, cols_part[:, :, :-1]], axis=2)
     )
     image_new = image - primal_step * (adjoint - divergence)
-    tv_new = projected[:, :, 1:, 1:]
     return (image_new, tv_new, dual_new)
 
 

time: 188 us -> 212 us (1.13)
  starting transfers between devices: 42.4 us -> 58.6 us
  waiting for transfers between devices: 86.4 us -> 97.9 us
    ppermute x12, starting transfers between devices: 22.6 us -> 41.8 us  [doubling_gather(): got = lax.ppermute(block, axis, pairs)]
    ppermute x12, waiting for transfers between devices: 56.5 us -> 70.8 us  [doubling_gather(): got = lax.ppermute(block, axis, pairs)]
    concatenate x3 -> x0, other arithmetic: 4.73 us -> none  [the longest x2 3.03 us: padded_2(): block = jnp.concatenate([low, block, high], axis=dim)]
    ppermute x4, waiting for transfers between devices: 4.05 us -> 0.01 us  [the longest x1 0.01 us: on_device(): next_row = lax.ppermute(image[:, :1, :], 'tile', up_tile)]
    ppermute x4, starting transfers between devices: 14.7 us -> 10.9 us  [the longest x1 5.28 us: on_device(): next_col = lax.ppermute(image[:, :, :1], 'az', up_az)]
    unnamed x68 -> x50, local copies, waits for them, and re-layouts: 5.75 us -> 2.91 us
    another operation x24, other arithmetic: 4.32 us -> 7.03 us  [doubling_gather(): block = jnp.stack([low, high], axis=place)]
    add x3, other arithmetic: 1.46 us -> 3.91 us  [halving_sum(): blocks = keep + lax.ppermute(send, axis, pairs)]
  transfers between devices with their start and end apart: 20 -> 20, of which waited for: 15 -> 15; matrix products, arithmetic and copies ran while one was open for 12% -> 9% of each run, Pallas kernels for 0% -> 0%
where the time goes in v12:
time: 212 us; the launch traced here: 211 us
  waiting for transfers between devices  97.9 us (46%)
  starting transfers between devices  58.6 us (28%)
  local copies, waits for them, and re-layouts  20.9 us (10%)
  other arithmetic  19.3 us (9%)
  matrix products  13.2 us (6%)
    ppermute x12, waiting for transfers between devices, doubling_gather(): got = lax.ppermute(block, axis, pairs)  70.8 us
    ppermute x12, starting transfers between devices, doubling_gather(): got = lax.ppermute(block, axis, pairs)  41.8 us
    ppermute x4, waiting for transfers between devices, halving_sum(): blocks = keep + lax.ppermute(send, axis, pairs)  27.2 us
    another operation x24, other arithmetic, doubling_gather(): block = jnp.stack([low, high], axis=place)  7.03 us
    ppermute x4, starting transfers between devices, halving_sum(): blocks = keep + lax.ppermute(send, axis, pairs)  5.83 us
    ppermute x1, starting transfers between devices, on_device(): next_col = lax.ppermute(image[:, :, :1], 'az', up_az)  5.28 us
  transfers between devices with their start and end apart: 20, of which 15 were waited for; matrix products, arithmetic and copies ran while one was open for 9% of the time, Pallas kernels for 0%

profile of v12, /device:TPU:1, one launch (start us, length us, event | category | flops | bytes accessed | tf_op | source)
XLA Modules:
  0.0 211.2 jit_solution(13275009011533967927)
XLA Ops:
  0.6 5.3 %collective-permute-start.17 = (f32[2,512,1]{2,1,0:T(8,128)}, f32[2,512,1]{2,1,0:T(8,128)}, u32[]{:S(2)}, u32[]{:S(2)}) collective-permute-start(f32[2,512,1]{2,1,0:T(8,128)} %bitcast.239), channel_id=1, source_target_pairs={{16,0},{32,16},{48,32},{64,48},{80,64},{96,80},{112,96},{128,112},... | collective-permute-start | bytes 12296 | tf_op jit(solution)/shard_map/ppermute | solution.py:156
  6.6 1.3 collective-permute-start.16
  8.0 2.7 %fusion.70 = (bf16[1,1024,2,256]{3,2,1,0:T(2,128)(2,1)S(1)}, bf16[1,1024,2,256]{3,2,1,0:T(2,128)(2,1)S(1)}) fusion(bf16[2,1024,2,256]{3,2,1,0:T(2,128)(2,1)} %param.14), kind=kLoop, calls=%fused_computation.145 | loop fusion | bytes 4194304 | tf_op jit(solution)/shard_map/slice | solution.py:75
  12.7 2.4 %fusion.52 = (f32[1,2,512,128]{3,2,1,0:T(8,128)}, bf16[2,512,128]{2,1,0:T(8,128)(2,1)S(1)}, f32[1,2,512,128]{3,2,1,0:T(8,128)}) fusion(f32[2,512,128]{2,1,0:T(8,128)S(1)} %copy-done.1, f32[2,1,128]{2,1,0:T(1,128)S(1)} %collective-permute-done.16, f32[2,511,128]{2,1,0:T(8,128)S(1)} %slice.70, pred[512]{0:T(512)(128)(4,1)S(1)} %add_compare_fusion, ...), kind=kLoop, calls=%fused_computation.70 | loop fusion | flops 917504 | bytes 2884224 | tf_op jit(solution)/shard_map/stack | solution.py:161
  16.7 1.9 multiply_subtract_fusion
  18.6 2.5 %copy.87 = f32[1024,2,128]{2,0,1:T(8,128)} copy(f32[1024,2,128]{0,2,1:T(8,128)} %get-tuple-element.15) | data formatting | bytes 2097152 | tf_op jit(solution)/shard_map/sub | solution.py:90
  21.2 2.5 %copy.88 = f32[1024,2,128]{2,0,1:T(8,128)} copy(f32[1024,2,128]{0,2,1:T(8,128)} %get-tuple-element.16) | data formatting | bytes 2097152 | tf_op jit(solution)/shard_map/add | solution.py:91
  23.7 1.7 pad_maximum_fusion
  25.4 1.2 constant_dynamic-slice_fusion.5
  27.6 3.0 %collective-permute-done = f32[2,2,2,2,64,2,128]{6,4,5,3,2,1,0:T(8,128)} collective-permute-done((f32[2,2,2,2,64,2,128]{6,4,5,3,2,1,0:T(8,128)}, f32[2,2,2,2,64,2,128]{6,4,5,3,2,1,0:T(8,128)}, u32[]{:S(2)}, u32[]{:S(2)}) %collective-permute-start) | collective-permute-done | bytes 1048608 | tf_op jit(solution)/shard_map/ppermute | solution.py:36
  30.6 1.7 bitcast_add_fusion
  33.3 5.2 %collective-permute-start.1 = (f32[2,2,2,64,2,128]{5,3,4,2,1,0:T(8,128)S(1)}, f32[2,2,2,64,2,128]{5,3,4,2,1,0:T(8,128)}, u32[]{:S(2)}, u32[]{:S(2)}) collective-permute-start(f32[2,2,2,64,2,128]{5,3,4,2,1,0:T(8,128)S(1)} %dynamic-slice_bitcast_fusion), channel_id=1, source_target_pairs={{0,128},{16,144},{32,160},{48,176},{64,192},{80,208},{96,224},{112... | collective-permute-start | bytes 1572872 | tf_op jit(solution)/shard_map/ppermute | solution.py:36
  38.6 12.1 %collective-permute-done.1 = f32[2,2,2,64,2,128]{5,3,4,2,1,0:T(8,128)} collective-permute-done((f32[2,2,2,64,2,128]{5,3,4,2,1,0:T(8,128)S(1)}, f32[2,2,2,64,2,128]{5,3,4,2,1,0:T(8,128)}, u32[]{:S(2)}, u32[]{:S(2)}) %collective-permute-start.1) | collective-permute-done | bytes 524320 | tf_op jit(solution)/shard_map/ppermute | solution.py:36
  50.7 1.3 bitcast_add_fusion.1
  52.7 7.3 %collective-permute-done.2 = f32[2,2,64,2,128]{4,2,3,1,0:T(8,128)} collective-permute-done((f32[2,2,64,2,128]{4,2,3,1,0:T(8,128)}, f32[2,2,64,2,128]{4,2,3,1,0:T(8,128)}, u32[]{:S(2)}, u32[]{:S(2)}) %collective-permute-start.2) | collective-permute-done | bytes 262176 | tf_op jit(solution)/shard_map/ppermute | solution.py:36
  61.6 4.8 %collective-permute-done.3 = f32[2,64,2,128]{3,1,0,2:T(8,128)S(1)} collective-permute-done((f32[2,64,2,128]{3,1,0,2:T(8,128)S(1)}, f32[2,64,2,128]{3,1,0,2:T(8,128)S(1)}, u32[]{:S(2)}, u32[]{:S(2)}) %collective-permute-start.3) | collective-permute-done | bytes 131104 | tf_op jit(solution)/shard_map/ppermute | solution.py:36
  66.4 5.2 %collective-permute-start.4 = (bf16[2,64,2,128]{3,1,2,0:T(8,128)(2,1)S(1)}, bf16[2,64,2,128]{3,1,2,0:T(8,128)(2,1)S(1)}, u32[]{:S(2)}, u32[]{:S(2)}) collective-permute-start(bf16[2,64,2,128]{3,1,2,0:T(8,128)(2,1)S(1)} %fusion.60), channel_id=1, source_target_pairs={{0,2},{1,3},{2,0},{3,1},{4,6},{5,7},{6,4},{7,5},{8,10},{9,11},{10,... | collective-permute-start | bytes 196616 | tf_op jit(solution)/shard_map/ppermute | solution.py:47
  71.6 1.9 collective-permute-done.4
  73.6 4.3 %collective-permute-start.5 = (bf16[2,2,64,2,128]{4,2,3,1,0:T(8,128)(2,1)S(1)}, bf16[2,2,64,2,128]{4,2,3,1,0:T(8,128)(2,1)S(1)}, u32[]{:S(2)}, u32[]{:S(2)}) collective-permute-start(bf16[2,2,64,2,128]{4,2,3,1,0:T(8,128)(2,1)S(1)} %pad_maximum_fusion.11), channel_id=1, source_target_pairs={{0,1},{1,0},{2,3},{3,2},{4,5},{5,4},{6,7},{7,6},{8,9},{9,8},{10,11... | collective-permute-start | bytes 393224 | tf_op jit(solution)/shard_map/ppermute | solution.py:47
  77.8 4.1 %collective-permute-done.5 = bf16[2,2,64,2,128]{4,2,3,1,0:T(8,128)(2,1)S(1)} collective-permute-done((bf16[2,2,64,2,128]{4,2,3,1,0:T(8,128)(2,1)S(1)}, bf16[2,2,64,2,128]{4,2,3,1,0:T(8,128)(2,1)S(1)}, u32[]{:S(2)}, u32[]{:S(2)}) %collective-permute-start.5) | collective-permute-done | bytes 131104 | tf_op jit(solution)/shard_map/ppermute | solution.py:47
  82.0 4.4 %collective-permute-start.6 = (bf16[2,2,2,64,2,128]{5,3,4,2,1,0:T(8,128)(2,1)S(1)}, bf16[2,2,2,64,2,128]{5,3,4,2,1,0:T(8,128)(2,1)}, u32[]{:S(2)}, u32[]{:S(2)}) collective-permute-start(bf16[2,2,2,64,2,128]{5,3,4,2,1,0:T(8,128)(2,1)S(1)} %pad_maximum_fusion.8), channel_id=1, source_target_pairs={{0,8},{1,9},{2,10},{3,11},{4,12},{5,13},{6,14},{7,15},{8,0},{9,1},... | collective-permute-start | bytes 786440 | tf_op jit(solution)/shard_map/ppermute | solution.py:47
  86.5 3.8 %collective-permute-done.6 = bf16[2,2,2,64,2,128]{5,3,4,2,1,0:T(8,128)(2,1)} collective-permute-done((bf16[2,2,2,64,2,128]{5,3,4,2,1,0:T(8,128)(2,1)S(1)}, bf16[2,2,2,64,2,128]{5,3,4,2,1,0:T(8,128)(2,1)}, u32[]{:S(2)}, u32[]{:S(2)}) %collective-permute-start.6) | collective-permute-done | bytes 262176 | tf_op jit(solution)/shard_map/ppermute | solution.py:47
  91.4 1.4 collective-permute-start.7
  92.9 9.8 %collective-permute-done.7 = bf16[2,2,2,2,64,2,128]{6,4,5,3,2,1,0:T(8,128)(2,1)S(1)} collective-permute-done((bf16[2,2,2,2,64,2,128]{6,4,5,3,2,1,0:T(8,128)(2,1)S(1)}, bf16[2,2,2,2,64,2,128]{6,4,5,3,2,1,0:T(8,128)(2,1)S(1)}, u32[]{:S(2)}, u32[]{:S(2)}) %collective-permute-start.7) | collective-permute-done | bytes 524320 | tf_op jit(solution)/shard_map/ppermute | solution.py:47
  103.9 1.6 fusion.30
  105.5 1.7 collective-permute-start.8
  107.2 6.3 %collective-permute-done.8 = bf16[4,2,64,128]{3,2,1,0:T(8,128)(2,1)S(1)} collective-permute-done((bf16[4,2,64,128]{3,2,1,0:T(8,128)(2,1)S(1)}, bf16[4,2,64,128]{3,2,1,0:T(8,128)(2,1)S(1)}, u32[]{:S(2)}, u32[]{:S(2)}) %collective-permute-start.8) | collective-permute-done | bytes 131104 | tf_op jit(solution)/shard_map/ppermute | solution.py:47
  113.7 11.1 %collective-permute-done.9 = bf16[2,4,2,64,128]{4,3,2,1,0:T(8,128)(2,1)S(1)} collective-permute-done((bf16[2,4,2,64,128]{4,3,2,1,0:T(8,128)(2,1)S(1)}, bf16[2,4,2,64,128]{4,3,2,1,0:T(8,128)(2,1)S(1)}, u32[]{:S(2)}, u32[]{:S(2)}) %collective-permute-start.9) | collective-permute-done | bytes 262176 | tf_op jit(solution)/shard_map/ppermute | solution.py:47
  124.9 1.6 collective-permute-start.10
  126.5 8.0 %collective-permute-done.10 = bf16[2,2,4,2,64,128]{5,4,3,2,0,1:T(8,128)(2,1)S(1)} collective-permute-done((bf16[2,2,4,2,64,128]{5,4,3,2,0,1:T(8,128)(2,1)S(1)}, bf16[2,2,4,2,64,128]{5,4,3,2,0,1:T(8,128)(2,1)S(1)}, u32[]{:S(2)}, u32[]{:S(2)}) %collective-permute-start.10) | collective-permute-done | bytes 524320 | tf_op jit(solution)/shard_map/ppermute | solution.py:47
  137.9 1.4 gather_fusion
  139.3 17.3 %collective-permute-done.11 = bf16[2,2,2,4,2,64,128]{6,5,4,3,1,2,0:T(8,128)(2,1)} collective-permute-done((bf16[2,2,2,4,2,64,128]{6,5,4,3,1,2,0:T(8,128)(2,1)}, bf16[2,2,2,4,2,64,128]{6,5,4,3,1,2,0:T(8,128)(2,1)}, u32[]{:S(2)}, u32[]{:S(2)}) %collective-permute-start.11) | collective-permute-done | bytes 1048608 | tf_op jit(solution)/shard_map/ppermute | solution.py:47
  156.6 1.5 select_bitcast_fusion.1
  158.6 1.3 fusion.10
  160.2 15.4 %collective-permute-start.12 = (bf16[64,2,2,128]{3,0,1,2:T(8,128)(2,1)S(1)}, bf16[64,2,2,128]{3,0,1,2:T(8,128)(2,1)}, u32[]{:S(2)}, u32[]{:S(2)}) collective-permute-start(bf16[64,2,2,128]{3,0,1,2:T(8,128)(2,1)S(1)} %fusion.34), channel_id=1, source_target_pairs={{0,64},{16,80},{32,96},{48,112},{64,0},{80,16},{96,32},{112,48},{1... | collective-permute-start | bytes 196616 | tf_op jit(solution)/shard_map/ppermute | solution.py:47
  175.6 1.8 collective-permute-done.12
  178.9 4.1 %collective-permute-done.13 = bf16[2,64,2,2,128]{4,1,2,3,0:T(8,128)(2,1)} collective-permute-done((bf16[2,64,2,2,128]{4,1,2,3,0:T(8,128)(2,1)}, bf16[2,64,2,2,128]{4,1,2,3,0:T(8,128)(2,1)}, u32[]{:S(2)}, u32[]{:S(2)}) %collective-permute-start.13) | collective-permute-done | bytes 131104 | tf_op jit(solution)/shard_map/ppermute | solution.py:47
  185.0 1.6 multiply_reduce_fusion
  186.8 2.6 %collective-permute-done.14 = bf16[2,2,64,2,2,128]{5,2,3,4,1,0:T(8,128)(2,1)S(1)} collective-permute-done((bf16[2,2,64,2,2,128]{5,2,3,4,1,0:T(8,128)(2,1)S(1)}, bf16[2,2,64,2,2,128]{5,2,3,4,1,0:T(8,128)(2,1)S(1)}, u32[]{:S(2)}, u32[]{:S(2)}) %collective-permute-start.14) | collective-permute-done | bytes 262176 | tf_op jit(solution)/shard_map/ppermute | solution.py:47
  189.4 5.5 %collective-permute-start.15 = (bf16[2,2,2,64,2,2,128]{6,3,4,5,1,0,2:T(8,128)(2,1)S(1)}, bf16[2,2,2,64,2,2,128]{6,3,4,5,1,0,2:T(8,128)(2,1)S(1)}, u32[]{:S(2)}, u32[]{:S(2)}) collective-permute-start(bf16[2,2,2,64,2,2,128]{6,3,4,5,1,0,2:T(8,128)(2,1)S(1)} %pad_maximum_fusion.7), channel_id=1, source_target_pairs={{0,16},{16,0},{32,48},{48,32},{64,80},{80,64},{96,112},{112,96},{1... | collective-permute-start | bytes 1572872 | tf_op jit(solution)/shard_map/ppermute | solution.py:47
  195.3 1.1 slice.90
  196.5 3.0 %collective-permute-start.19 = (f32[2,512,1]{2,1,0:T(8,128)}, f32[2,512,1]{2,1,0:T(8,128)}, u32[]{:S(2)}, u32[]{:S(2)}) collective-permute-start(f32[2,512,1]{2,1,0:T(8,128)} %slice.90), channel_id=1, source_target_pairs={{0,16},{16,32},{32,48},{48,64},{64,80},{80,96},{96,112},{112,128},... | collective-permute-start | bytes 12296 | tf_op jit(solution)/shard_map/ppermute | solution.py:169
  199.5 1.3 collective-permute-start.18
  202.0 1.3 fusion.44
  203.3 1.3 fusion.43
  204.6 1.3 fusion.16
  206.0 1.9 fusion.17
  209.1 2.1 fusion.50
  (124 shorter events, 21.8 us)
Async XLA Ops:
  0.6 103.1 %copy-start = (bf16[8,128,128]{2,1,0:T(8,128)(2,1)S(1)}, bf16[8,128,128]{2,1,0:T(8,128)(2,1)}, u32[]{:S(2)}) copy-start(bf16[8,128,128]{2,1,0:T(8,128)(2,1)} %param.16) | copy-start | bytes 786436
  0.6 12.1 %collective-permute-start.17 = (f32[2,512,1]{2,1,0:T(8,128)}, f32[2,512,1]{2,1,0:T(8,128)}, u32[]{:S(2)}, u32[]{:S(2)}) collective-permute-start(f32[2,512,1]{2,1,0:T(8,128)} %bitcast.239), channel_id=1, source_target_pairs={{16,0},{32,16},{48,32},{64,48},{80,64},{96,80},{112,96},{128,112},... | collective-permute-start | bytes 12296 | tf_op jit(solution)/shard_map/ppermute | solution.py:156
  6.6 6.1 %collective-permute-start.16 = (f32[2,1,128]{2,1,0:T(1,128)S(1)}, f32[2,1,128]{2,1,0:T(1,128)S(1)}, u32[]{:S(2)}, u32[]{:S(2)}) collective-permute-start(f32[2,1,128]{2,1,0:T(1,128)S(1)} %slice.71), channel_id=1, source_target_pairs={{1,0},{2,1},{3,2},{4,3},{5,4},{6,5},{7,6},{8,7},{9,8},{10,9},{11,1... | collective-permute-start | bytes 3080 | tf_op jit(solution)/shard_map/ppermute | solution.py:155
  7.9 4.8 %copy-start.18 = (pred[128]{0:T(512)(128)(4,1)}, pred[128]{0:T(512)(128)(4,1)S(1)}, u32[]{:S(2)}) copy-start(pred[128]{0:T(512)(128)(4,1)S(1)} %add_compare_fusion.1) | copy-start | bytes 388
  8.0 3.7 %copy-start.1 = (f32[2,512,128]{2,1,0:T(8,128)S(1)}, f32[2,512,128]{2,1,0:T(8,128)}, u32[]{:S(2)}) copy-start(f32[2,512,128]{2,1,0:T(8,128)} %param.10) | copy-start | bytes 1572868
  11.7 3.5 %copy-start.20 = (pred[512]{0:T(512)(128)(4,1)}, pred[512]{0:T(512)(128)(4,1)S(1)}, u32[]{:S(2)}) copy-start(pred[512]{0:T(512)(128)(4,1)S(1)} %add_compare_fusion) | copy-start | bytes 1540
  27.6 3.0 %collective-permute-start = (f32[2,2,2,2,64,2,128]{6,4,5,3,2,1,0:T(8,128)}, f32[2,2,2,2,64,2,128]{6,4,5,3,2,1,0:T(8,128)}, u32[]{:S(2)}, u32[]{:S(2)}) collective-permute-start(f32[2,2,2,2,64,2,128]{6,4,5,3,2,1,0:T(8,128)} %bitcast.232), channel_id=1, source_target_pairs={{0,16},{16,0},{32,48},{48,32},{64,80},{80,64},{96,112},{112,96},{1... | collective-permute-start | bytes 3145736 | tf_op jit(solution)/shard_map/ppermute | solution.py:36
  32.3 1.0 copy-start.7
  33.3 17.3 %collective-permute-start.1 = (f32[2,2,2,64,2,128]{5,3,4,2,1,0:T(8,128)S(1)}, f32[2,2,2,64,2,128]{5,3,4,2,1,0:T(8,128)}, u32[]{:S(2)}, u32[]{:S(2)}) collective-permute-start(f32[2,2,2,64,2,128]{5,3,4,2,1,0:T(8,128)S(1)} %dynamic-slice_bitcast_fusion), channel_id=1, source_target_pairs={{0,128},{16,144},{32,160},{48,176},{64,192},{80,208},{96,224},{112... | collective-permute-start | bytes 1572872 | tf_op jit(solution)/shard_map/ppermute | solution.py:36
  51.9 34.5 %copy-start.16 = (s32[32,1,6]{0,1,2:T(1,128)S(1)}, s32[32,1,6]{0,1,2:T(1,128)}, u32[]{:S(2)}) copy-start(s32[32,1,6]{0,1,2:T(1,128)} %param.17) | copy-start | bytes 2308
  51.9 34.5 %copy-start.17 = (s32[32,1,6]{0,1,2:T(1,128)S(1)}, s32[32,1,6]{0,1,2:T(1,128)}, u32[]{:S(2)}) copy-start(s32[32,1,6]{0,1,2:T(1,128)} %param.18) | copy-start | bytes 2308
  52.7 7.3 %collective-permute-start.2 = (f32[2,2,64,2,128]{4,2,3,1,0:T(8,128)}, f32[2,2,64,2,128]{4,2,3,1,0:T(8,128)}, u32[]{:S(2)}, u32[]{:S(2)}) collective-permute-start(f32[2,2,64,2,128]{4,2,3,1,0:T(8,128)} %dynamic-slice_bitcast_fusion.1), channel_id=1, source_target_pairs={{0,32},{16,48},{32,0},{48,16},{64,96},{80,112},{96,64},{112,80},{1... | collective-permute-start | bytes 786440 | tf_op jit(solution)/shard_map/ppermute | solution.py:36
  61.0 5.4 %collective-permute-start.3 = (f32[2,64,2,128]{3,1,0,2:T(8,128)S(1)}, f32[2,64,2,128]{3,1,0,2:T(8,128)S(1)}, u32[]{:S(2)}, u32[]{:S(2)}) collective-permute-start(f32[2,64,2,128]{3,1,0,2:T(8,128)S(1)} %bitcast.258), channel_id=1, source_target_pairs={{0,64},{16,80},{32,96},{48,112},{64,0},{80,16},{96,32},{112,48},{1... | collective-permute-start | bytes 393224 | tf_op jit(solution)/shard_map/ppermute | solution.py:36
  66.4 26.5 %copy-start.22 = (s32[64]{0:T(128)S(1)}, s32[64]{0:T(128)}, u32[]{:S(2)}) copy-start(s32[64]{0:T(128)} %param.19) | copy-start | bytes 772
  66.4 7.1 %collective-permute-start.4 = (bf16[2,64,2,128]{3,1,2,0:T(8,128)(2,1)S(1)}, bf16[2,64,2,128]{3,1,2,0:T(8,128)(2,1)S(1)}, u32[]{:S(2)}, u32[]{:S(2)}) collective-permute-start(bf16[2,64,2,128]{3,1,2,0:T(8,128)(2,1)S(1)} %fusion.60), channel_id=1, source_target_pairs={{0,2},{1,3},{2,0},{3,1},{4,6},{5,7},{6,4},{7,5},{8,10},{9,11},{10,... | collective-permute-start | bytes 196616 | tf_op jit(solution)/shard_map/ppermute | solution.py:47
  73.6 8.4 %collective-permute-start.5 = (bf16[2,2,64,2,128]{4,2,3,1,0:T(8,128)(2,1)S(1)}, bf16[2,2,64,2,128]{4,2,3,1,0:T(8,128)(2,1)S(1)}, u32[]{:S(2)}, u32[]{:S(2)}) collective-permute-start(bf16[2,2,64,2,128]{4,2,3,1,0:T(8,128)(2,1)S(1)} %pad_maximum_fusion.11), channel_id=1, source_target_pairs={{0,1},{1,0},{2,3},{3,2},{4,5},{5,4},{6,7},{7,6},{8,9},{9,8},{10,11... | collective-permute-start | bytes 393224 | tf_op jit(solution)/shard_map/ppermute | solution.py:47
  82.0 8.3 %collective-permute-start.6 = (bf16[2,2,2,64,2,128]{5,3,4,2,1,0:T(8,128)(2,1)S(1)}, bf16[2,2,2,64,2,128]{5,3,4,2,1,0:T(8,128)(2,1)}, u32[]{:S(2)}, u32[]{:S(2)}) collective-permute-start(bf16[2,2,2,64,2,128]{5,3,4,2,1,0:T(8,128)(2,1)S(1)} %pad_maximum_fusion.8), channel_id=1, source_target_pairs={{0,8},{1,9},{2,10},{3,11},{4,12},{5,13},{6,14},{7,15},{8,0},{9,1},... | collective-permute-start | bytes 786440 | tf_op jit(solution)/shard_map/ppermute | solution.py:47
  91.4 11.3 %collective-permute-start.7 = (bf16[2,2,2,2,64,2,128]{6,4,5,3,2,1,0:T(8,128)(2,1)S(1)}, bf16[2,2,2,2,64,2,128]{6,4,5,3,2,1,0:T(8,128)(2,1)S(1)}, u32[]{:S(2)}, u32[]{:S(2)}) collective-permute-start(bf16[2,2,2,2,64,2,128]{6,4,5,3,2,1,0:T(8,128)(2,1)S(1)} %pad_maximum_fusion.5), channel_id=1, source_target_pairs={{0,4},{1,5},{2,6},{3,7},{4,0},{5,1},{6,2},{7,3},{8,12},{9,13},{10,... | collective-permute-start | bytes 1572872 | tf_op jit(solution)/shard_map/ppermute | solution.py:47
  102.9 1.0 copy-start.13
  102.9 1.0 copy-start.14
  105.5 29.1 %copy-start.8 = (f32[2,64,4,128]{3,1,0,2:T(8,128)}, f32[2,64,4,128]{3,1,0,2:T(8,128)S(1)}, u32[]{:S(2)}) copy-start(f32[2,64,4,128]{3,1,0,2:T(8,128)S(1)} %fusion.30) | copy-start | bytes 786436
  105.5 8.0 %collective-permute-start.8 = (bf16[4,2,64,128]{3,2,1,0:T(8,128)(2,1)S(1)}, bf16[4,2,64,128]{3,2,1,0:T(8,128)(2,1)S(1)}, u32[]{:S(2)}, u32[]{:S(2)}) collective-permute-start(bf16[4,2,64,128]{3,2,1,0:T(8,128)(2,1)S(1)} %convert_bitcast_fusion), channel_id=1, source_target_pairs={{0,2},{1,3},{2,0},{3,1},{4,6},{5,7},{6,4},{7,5},{8,10},{9,11},{10,... | collective-permute-start | bytes 393224 | tf_op jit(solution)/shard_map/ppermute | solution.py:47
  113.6 11.2 %collective-permute-start.9 = (bf16[2,4,2,64,128]{4,3,2,1,0:T(8,128)(2,1)S(1)}, bf16[2,4,2,64,128]{4,3,2,1,0:T(8,128)(2,1)S(1)}, u32[]{:S(2)}, u32[]{:S(2)}) collective-permute-start(bf16[2,4,2,64,128]{4,3,2,1,0:T(8,128)(2,1)S(1)} %pad_maximum_fusion.9), channel_id=1, source_target_pairs={{0,1},{1,0},{2,3},{3,2},{4,5},{5,4},{6,7},{7,6},{8,9},{9,8},{10,11... | collective-permute-start | bytes 786440 | tf_op jit(solution)/shard_map/ppermute | solution.py:47
  124.9 9.6 %collective-permute-start.10 = (bf16[2,2,4,2,64,128]{5,4,3,2,0,1:T(8,128)(2,1)S(1)}, bf16[2,2,4,2,64,128]{5,4,3,2,0,1:T(8,128)(2,1)S(1)}, u32[]{:S(2)}, u32[]{:S(2)}) collective-permute-start(bf16[2,2,4,2,64,128]{5,4,3,2,0,1:T(8,128)(2,1)S(1)} %pad_maximum_fusion.6), channel_id=1, source_target_pairs={{0,8},{1,9},{2,10},{3,11},{4,12},{5,13},{6,14},{7,15},{8,0},{9,1},... | collective-permute-start | bytes 1572872 | tf_op jit(solution)/shard_map/ppermute | solution.py:47
  134.6 0.8 copy-start.4
  136.5 20.1 %collective-permute-start.11 = (bf16[2,2,2,4,2,64,128]{6,5,4,3,1,2,0:T(8,128)(2,1)}, bf16[2,2,2,4,2,64,128]{6,5,4,3,1,2,0:T(8,128)(2,1)}, u32[]{:S(2)}, u32[]{:S(2)}) collective-permute-start(bf16[2,2,2,4,2,64,128]{6,5,4,3,1,2,0:T(8,128)(2,1)} %pad_maximum_fusion.3), channel_id=1, source_target_pairs={{0,4},{1,5},{2,6},{3,7},{4,0},{5,1},{6,2},{7,3},{8,12},{9,13},{10,... | collective-permute-start | bytes 3145736 | tf_op jit(solution)/shard_map/ppermute | solution.py:47
  158.6 1.3 copy-start.12
  158.6 26.4 %copy-start.5 = (f32[1,2,512,128]{3,2,1,0:T(8,128)S(1)}, f32[1,2,512,128]{3,2,1,0:T(8,128)}, u32[]{:S(2)}) copy-start(f32[1,2,512,128]{3,2,1,0:T(8,128)} %get-tuple-element.31) | copy-start | bytes 1572868
  160.1 15.5 %copy-start.15 = (bf16[64,2,2,128]{3,0,1,2:T(8,128)(2,1)}, bf16[64,2,2,128]{3,0,1,2:T(8,128)(2,1)S(1)}, u32[]{:S(2)}) copy-start(bf16[64,2,2,128]{3,0,1,2:T(8,128)(2,1)S(1)} %fusion.34) | copy-start | bytes 196612
  160.2 17.2 %collective-permute-start.12 = (bf16[64,2,2,128]{3,0,1,2:T(8,128)(2,1)S(1)}, bf16[64,2,2,128]{3,0,1,2:T(8,128)(2,1)}, u32[]{:S(2)}, u32[]{:S(2)}) collective-permute-start(bf16[64,2,2,128]{3,0,1,2:T(8,128)(2,1)S(1)} %fusion.34), channel_id=1, source_target_pairs={{0,64},{16,80},{32,96},{48,112},{64,0},{80,16},{96,32},{112,48},{1... | collective-permute-start | bytes 196616 | tf_op jit(solution)/shard_map/ppermute | solution.py:47
  178.9 4.1 %collective-permute-start.13 = (bf16[2,64,2,2,128]{4,1,2,3,0:T(8,128)(2,1)}, bf16[2,64,2,2,128]{4,1,2,3,0:T(8,128)(2,1)}, u32[]{:S(2)}, u32[]{:S(2)}) collective-permute-start(bf16[2,64,2,2,128]{4,1,2,3,0:T(8,128)(2,1)} %pad_maximum_fusion.12), channel_id=1, source_target_pairs={{0,128},{16,144},{32,160},{48,176},{64,192},{80,208},{96,224},{112... | collective-permute-start | bytes 393224 | tf_op jit(solution)/shard_map/ppermute | solution.py:47
  184.0 5.3 %collective-permute-start.14 = (bf16[2,2,64,2,2,128]{5,2,3,4,1,0:T(8,128)(2,1)S(1)}, bf16[2,2,64,2,2,128]{5,2,3,4,1,0:T(8,128)(2,1)S(1)}, u32[]{:S(2)}, u32[]{:S(2)}) collective-permute-start(bf16[2,2,64,2,2,128]{5,2,3,4,1,0:T(8,128)(2,1)S(1)} %pad_maximum_fusion.10), channel_id=1, source_target_pairs={{0,32},{16,48},{32,0},{48,16},{64,96},{80,112},{96,64},{112,80},{1... | collective-permute-start | bytes 786440 | tf_op jit(solution)/shard_map/ppermute | solution.py:47
  185.0 10.0 %copy-start.6 = (f32[1,2,512,128]{3,2,1,0:T(8,128)S(1)}, f32[1,2,512,128]{3,2,1,0:T(8,128)}, u32[]{:S(2)}) copy-start(f32[1,2,512,128]{3,2,1,0:T(8,128)} %get-tuple-element.33) | copy-start | bytes 1572868
  185.0 10.0 %copy-start.10 = (f32[2,2,512,128]{3,2,1,0:T(8,128)S(1)}, f32[2,2,512,128]{3,2,1,0:T(8,128)}, u32[]{:S(2)}) copy-start(f32[2,2,512,128]{3,2,1,0:T(8,128)} %param.11) | copy-start | bytes 3145732
  189.4 5.8 %copy-start.19 = (pred[128]{0:T(512)(128)(4,1)S(1)}, pred[128]{0:T(512)(128)(4,1)}, u32[]{:S(2)}) copy-start(pred[128]{0:T(512)(128)(4,1)} %copy-done.18) | copy-start | bytes 388
  189.4 5.8 %copy-start.21 = (pred[512]{0:T(512)(128)(4,1)S(1)}, pred[512]{0:T(512)(128)(4,1)}, u32[]{:S(2)}) copy-start(pred[512]{0:T(512)(128)(4,1)} %copy-done.20) | copy-start | bytes 1540
  189.4 12.3 %collective-permute-start.15 = (bf16[2,2,2,64,2,2,128]{6,3,4,5,1,0,2:T(8,128)(2,1)S(1)}, bf16[2,2,2,64,2,2,128]{6,3,4,5,1,0,2:T(8,128)(2,1)S(1)}, u32[]{:S(2)}, u32[]{:S(2)}) collective-permute-start(bf16[2,2,2,64,2,2,128]{6,3,4,5,1,0,2:T(8,128)(2,1)S(1)} %pad_maximum_fusion.7), channel_id=1, source_target_pairs={{0,16},{16,0},{32,48},{48,32},{64,80},{80,64},{96,112},{112,96},{1... | collective-permute-start | bytes 1572872 | tf_op jit(solution)/shard_map/ppermute | solution.py:47
  195.1 6.6 %copy-start.11 = (f32[2,2,512,128]{3,2,1,0:T(8,128)}, f32[2,2,512,128]{3,2,1,0:T(8,128)S(1)}, u32[]{:S(2)}) copy-start(f32[2,2,512,128]{3,2,1,0:T(8,128)S(1)} %broadcast_divide_fusion) | copy-start | bytes 3145732
  195.2 5.7 %copy-start.9 = (f32[2,64,4,128]{3,1,0,2:T(8,128)S(1)}, f32[2,64,4,128]{3,1,0,2:T(8,128)}, u32[]{:S(2)}) copy-start(f32[2,64,4,128]{3,1,0,2:T(8,128)} %copy-done.8) | copy-start | bytes 786436
  195.3 4.2 %copy-start.2 = (f32[2,512,128]{2,1,0:T(8,128)}, f32[2,512,128]{2,1,0:T(8,128)S(1)}, u32[]{:S(2)}) copy-start(f32[2,512,128]{2,1,0:T(8,128)S(1)} %get-tuple-element.23) | copy-start | bytes 1572868
  196.5 12.7 %collective-permute-start.19 = (f32[2,512,1]{2,1,0:T(8,128)}, f32[2,512,1]{2,1,0:T(8,128)}, u32[]{:S(2)}, u32[]{:S(2)}) collective-permute-start(f32[2,512,1]{2,1,0:T(8,128)} %slice.90), channel_id=1, source_target_pairs={{0,16},{16,32},{32,48},{48,64},{64,80},{80,96},{96,112},{112,128},... | collective-permute-start | bytes 12296 | tf_op jit(solution)/shard_map/ppermute | solution.py:169
  199.5 9.6 %collective-permute-start.18 = (f32[2,1,128]{2,1,0:T(1,128)S(1)}, f32[2,1,128]{2,1,0:T(1,128)S(1)}, u32[]{:S(2)}, u32[]{:S(2)}) collective-permute-start(f32[2,1,128]{2,1,0:T(1,128)S(1)} %slice.87), channel_id=1, source_target_pairs={{0,1},{1,2},{2,3},{3,4},{4,5},{5,6},{6,7},{7,8},{8,9},{9,10},{10,1... | collective-permute-start | bytes 3080 | tf_op jit(solution)/shard_map/ppermute | solution.py:168
  205.9 3.2 %copy-start.3 = (f32[2,512,128]{2,1,0:T(8,128)S(1)}, f32[2,512,128]{2,1,0:T(8,128)}, u32[]{:S(2)}) copy-start(f32[2,512,128]{2,1,0:T(8,128)} %copy-done.2) | copy-start | bytes 1572868

commit v13 on v12

--- a/solution.py
+++ b/solution.py
@@ -92,6 +92,7 @@
     parts = jnp.stack([real_part, imag_part], axis=0).reshape(2, az_count, -1, tiles_dev, columns)
     summed = halving_sum(jnp.moveaxis(parts, 1, 0), "az", (1, 8, 2, 4))
     projection_b = jnp.transpose(summed, (2, 1, 0, 3)).astype(jnp.bfloat16)
+    tv_image, tv_old, projection_b = lax.optimization_barrier((image, tv_dual, projection_b))
     all_proj = doubling_gather(projection_b, "tile", (2, 1, 8, 4))
     all_proj = all_proj.reshape(-1, *all_proj.shape[2:])
     phase_ids = jnp.arange(kernels.shape[0], dtype=jnp.int32)
@@ -152,13 +153,13 @@
     last_col = (global_col == total_cols - 1)[None, None, :]
     up_tile = [(i + 1, i) for i in range(tile_count - 1)]
     up_az = [(i + 1, i) for i in range(az_count - 1)]
-    next_row = lax.ppermute(image[:, :1, :], "tile", up_tile)
-    next_col = lax.ppermute(image[:, :, :1], "az", up_az)
-    grad_rows = jnp.concatenate([image[:, 1:, :], next_row], axis=1) - image
+    next_row = lax.ppermute(tv_image[:, :1, :], "tile", up_tile)
+    next_col = lax.ppermute(tv_image[:, :, :1], "az", up_az)
+    grad_rows = jnp.concatenate([tv_image[:, 1:, :], next_row], axis=1) - tv_image
     grad_rows = jnp.where(last_row, 0.0, grad_rows)
-    grad_cols = jnp.concatenate([image[:, :, 1:], next_col], axis=2) - image
+    grad_cols = jnp.concatenate([tv_image[:, :, 1:], next_col], axis=2) - tv_image
     grad_cols = jnp.where(last_col, 0.0, grad_cols)
-    moved = tv_dual + dual_step * jnp.stack([grad_rows, grad_cols])
+    moved = tv_old + dual_step * jnp.stack([grad_rows, grad_cols])
     magnitude = jnp.sqrt(jnp.sum(moved * moved, axis=(0, 1)))
     tv_new = moved / jnp.maximum(1.0, magnitude / edge_limit)
     rows_part = jnp.where(last_row, 0.0, tv_new[0])

time: 212 us -> 208 us (0.981)
  other arithmetic: 19.3 us -> 14.8 us
  starting transfers between devices: 58.6 us -> 55.6 us
    ppermute x12, starting transfers between devices: 41.8 us -> 34.7 us  [doubling_gather(): got = lax.ppermute(block, axis, pairs)]
    ppermute x1, starting transfers between devices: 1.29 us -> 5.62 us  [on_device(): prev_row = lax.ppermute(rows_part[:, -1:, :], 'tile', down_tile)]
    ppermute x2, waiting for transfers between devices: 0.01 us -> 3.98 us  [the longest x1 3.98 us: on_device(): next_col = lax.ppermute(tv_image[:, :, :1], 'az', up_az)]
    another operation x24, other arithmetic: 7.03 us -> 4.6 us  [doubling_gather(): block = jnp.stack([low, high], axis=place)]
    another operation x1, other arithmetic: 2.45 us -> 0.32 us  [on_device(): moved = tv_old + dual_step * jnp.stack([grad_rows, grad_cols])]
  transfers between devices with their start and end apart: 20 -> 20, of which waited for: 15 -> 14; matrix products, arithmetic and copies ran while one was open for 9% -> 6% of each run, Pallas kernels for 0% -> 0%
where the time goes in v13:
time: 208 us; the launch traced here: 207 us
  waiting for transfers between devices  100 us (48%)
  starting transfers between devices  55.6 us (27%)
  local copies, waits for them, and re-layouts  21.5 us (10%)
  other arithmetic  14.8 us (7%)
  matrix products  13.2 us (6%)
    ppermute x12, waiting for transfers between devices, doubling_gather(): got = lax.ppermute(block, axis, pairs)  69.8 us
    ppermute x12, starting transfers between devices, doubling_gather(): got = lax.ppermute(block, axis, pairs)  34.7 us
    ppermute x4, waiting for transfers between devices, halving_sum(): blocks = keep + lax.ppermute(send, axis, pairs)  26.5 us
    ppermute x1, starting transfers between devices, on_device(): next_col = lax.ppermute(tv_image[:, :, :1], 'az', up_az)  7.13 us
    ppermute x1, starting transfers between devices, on_device(): prev_row = lax.ppermute(rows_part[:, -1:, :], 'tile', down_tile)  5.62 us
    ppermute x4, starting transfers between devices, halving_sum(): blocks = keep + lax.ppermute(send, axis, pairs)  5.01 us
    another operation x24, other arithmetic, doubling_gather(): block = jnp.stack([low, high], axis=place)  4.6 us
  transfers between devices with their start and end apart: 20, of which 14 were waited for; matrix products, arithmetic and copies ran while one was open for 6% of the time, Pallas kernels for 0%

profile of v13, /device:TPU:1, one launch (start us, length us, event | category | flops | bytes accessed | tf_op | source)
XLA Modules:
  0.0 206.6 jit_solution(14416804438374886610)
XLA Ops:
  0.7 2.7 %fusion.70 = (bf16[1,1024,2,256]{3,2,1,0:T(2,128)(2,1)S(1)}, bf16[1,1024,2,256]{3,2,1,0:T(2,128)(2,1)S(1)}) fusion(bf16[2,1024,2,256]{3,2,1,0:T(2,128)(2,1)} %param.14), kind=kLoop, calls=%fused_computation.145 | loop fusion | bytes 4194304 | tf_op jit(solution)/shard_map/slice | solution.py:75
  5.9 1.9 multiply_subtract_fusion
  7.8 2.5 %copy.88 = f32[1024,2,128]{2,0,1:T(8,128)} copy(f32[1024,2,128]{0,2,1:T(8,128)} %get-tuple-element.22) | data formatting | bytes 2097152 | tf_op jit(solution)/shard_map/add | solution.py:91
  10.4 2.5 %copy.87 = f32[1024,2,128]{2,0,1:T(8,128)} copy(f32[1024,2,128]{0,2,1:T(8,128)} %get-tuple-element.21) | data formatting | bytes 2097152 | tf_op jit(solution)/shard_map/sub | solution.py:90
  12.9 3.1 %pad_maximum_fusion = f32[2,16,64,2,128]{4,2,1,3,0:T(8,128)} fusion(f32[1,16,64,2,128]{4,2,1,3,0:T(8,128)} %bitcast.244, f32[1,16,64,2,128]{4,2,1,3,0:T(8,128)} %bitcast.245), kind=kLoop, calls=%fused_computation.1 | loop fusion | flops 524288 | bytes 4194304 | tf_op jit(solution)/shard_map/stack | solution.py:92
  16.0 2.7 %constant_dynamic-slice_fusion.5 = (f32[2,2,2,1,2,64,2,128]{7,5,3,2,1,0,6,4:T(8,128)}, f32[2,2,2,1,2,64,2,128]{7,5,3,2,1,0,6,4:T(8,128)S(1)}) fusion(f32[2,2,2,2,2,64,2,128]{7,5,3,2,1,0,6,4:T(8,128)} %bitcast.240, s32[]{:T(128)S(6)} %select_n.316, s32[]{:T(128)S(6)} %select_n.317), kind=kLoop, calls=%fused_computation.138 | loop fusion | bytes 4194312 | tf_op jit(solution)/shard_map/jit(dynamic_index_in_dim)/dynamic_slice | solution.py:33
  19.8 3.2 %collective-permute-start = (f32[2,2,2,2,64,2,128]{6,4,5,3,2,1,0:T(8,128)}, f32[2,2,2,2,64,2,128]{6,4,5,3,2,1,0:T(8,128)}, u32[]{:S(2)}, u32[]{:S(2)}) collective-permute-start(f32[2,2,2,2,64,2,128]{6,4,5,3,2,1,0:T(8,128)} %bitcast.232), channel_id=1, source_target_pairs={{0,16},{16,0},{32,48},{48,32},{64,80},{80,64},{96,112},{112,96},{1... | collective-permute-start | bytes 3145736 | tf_op jit(solution)/shard_map/ppermute | solution.py:36
  23.0 2.6 %collective-permute-done = f32[2,2,2,2,64,2,128]{6,4,5,3,2,1,0:T(8,128)} collective-permute-done((f32[2,2,2,2,64,2,128]{6,4,5,3,2,1,0:T(8,128)}, f32[2,2,2,2,64,2,128]{6,4,5,3,2,1,0:T(8,128)}, u32[]{:S(2)}, u32[]{:S(2)}) %collective-permute-start) | collective-permute-done | bytes 1048608 | tf_op jit(solution)/shard_map/ppermute | solution.py:36
  25.7 1.7 bitcast_add_fusion
  28.5 13.2 %collective-permute-done.1 = f32[2,2,2,64,2,128]{5,3,4,2,1,0:T(8,128)} collective-permute-done((f32[2,2,2,64,2,128]{5,3,4,2,1,0:T(8,128)S(1)}, f32[2,2,2,64,2,128]{5,3,4,2,1,0:T(8,128)}, u32[]{:S(2)}, u32[]{:S(2)}) %collective-permute-start.1) | collective-permute-done | bytes 524320 | tf_op jit(solution)/shard_map/ppermute | solution.py:36
  41.7 1.3 bitcast_add_fusion.1
  43.7 6.9 %collective-permute-done.2 = f32[2,2,64,2,128]{4,2,3,1,0:T(8,128)} collective-permute-done((f32[2,2,64,2,128]{4,2,3,1,0:T(8,128)}, f32[2,2,64,2,128]{4,2,3,1,0:T(8,128)}, u32[]{:S(2)}, u32[]{:S(2)}) %collective-permute-start.2) | collective-permute-done | bytes 262176 | tf_op jit(solution)/shard_map/ppermute | solution.py:36
  51.7 1.7 collective-permute-start.3
  53.3 3.7 %collective-permute-done.3 = f32[2,64,2,128]{3,1,0,2:T(8,128)S(1)} collective-permute-done((f32[2,64,2,128]{3,1,0,2:T(8,128)S(1)}, f32[2,64,2,128]{3,1,0,2:T(8,128)S(1)}, u32[]{:S(2)}, u32[]{:S(2)}) %collective-permute-start.3) | collective-permute-done | bytes 131104 | tf_op jit(solution)/shard_map/ppermute | solution.py:36
  57.1 5.3 %collective-permute-start.4 = (bf16[2,64,2,128]{3,1,2,0:T(8,128)(2,1)S(1)}, bf16[2,64,2,128]{3,1,2,0:T(8,128)(2,1)S(1)}, u32[]{:S(2)}, u32[]{:S(2)}) collective-permute-start(bf16[2,64,2,128]{3,1,2,0:T(8,128)(2,1)S(1)} %fusion.60), channel_id=1, source_target_pairs={{0,2},{1,3},{2,0},{3,1},{4,6},{5,7},{6,4},{7,5},{8,10},{9,11},{10,... | collective-permute-start | bytes 196616 | tf_op jit(solution)/shard_map/ppermute | solution.py:47
  62.4 2.0 collective-permute-done.4
  64.3 2.5 %collective-permute-start.5 = (bf16[2,2,64,2,128]{4,2,3,1,0:T(8,128)(2,1)S(1)}, bf16[2,2,64,2,128]{4,2,3,1,0:T(8,128)(2,1)S(1)}, u32[]{:S(2)}, u32[]{:S(2)}) collective-permute-start(bf16[2,2,64,2,128]{4,2,3,1,0:T(8,128)(2,1)S(1)} %pad_maximum_fusion.11), channel_id=1, source_target_pairs={{0,1},{1,0},{2,3},{3,2},{4,5},{5,4},{6,7},{7,6},{8,9},{9,8},{10,11... | collective-permute-start | bytes 393224 | tf_op jit(solution)/shard_map/ppermute | solution.py:47
  66.9 4.5 %collective-permute-done.5 = bf16[2,2,64,2,128]{4,2,3,1,0:T(8,128)(2,1)S(1)} collective-permute-done((bf16[2,2,64,2,128]{4,2,3,1,0:T(8,128)(2,1)S(1)}, bf16[2,2,64,2,128]{4,2,3,1,0:T(8,128)(2,1)S(1)}, u32[]{:S(2)}, u32[]{:S(2)}) %collective-permute-start.5) | collective-permute-done | bytes 131104 | tf_op jit(solution)/shard_map/ppermute | solution.py:47
  71.5 3.0 %collective-permute-start.6 = (bf16[2,2,2,64,2,128]{5,3,4,2,1,0:T(8,128)(2,1)S(1)}, bf16[2,2,2,64,2,128]{5,3,4,2,1,0:T(8,128)(2,1)}, u32[]{:S(2)}, u32[]{:S(2)}) collective-permute-start(bf16[2,2,2,64,2,128]{5,3,4,2,1,0:T(8,128)(2,1)S(1)} %pad_maximum_fusion.8), channel_id=1, source_target_pairs={{0,8},{1,9},{2,10},{3,11},{4,12},{5,13},{6,14},{7,15},{8,0},{9,1},... | collective-permute-start | bytes 786440 | tf_op jit(solution)/shard_map/ppermute | solution.py:47
  74.5 3.9 %collective-permute-done.6 = bf16[2,2,2,64,2,128]{5,3,4,2,1,0:T(8,128)(2,1)} collective-permute-done((bf16[2,2,2,64,2,128]{5,3,4,2,1,0:T(8,128)(2,1)S(1)}, bf16[2,2,2,64,2,128]{5,3,4,2,1,0:T(8,128)(2,1)}, u32[]{:S(2)}, u32[]{:S(2)}) %collective-permute-start.6) | collective-permute-done | bytes 262176 | tf_op jit(solution)/shard_map/ppermute | solution.py:47
  79.5 1.4 collective-permute-start.7
  81.0 9.2 %collective-permute-done.7 = bf16[2,2,2,2,64,2,128]{6,4,5,3,2,1,0:T(8,128)(2,1)S(1)} collective-permute-done((bf16[2,2,2,2,64,2,128]{6,4,5,3,2,1,0:T(8,128)(2,1)S(1)}, bf16[2,2,2,2,64,2,128]{6,4,5,3,2,1,0:T(8,128)(2,1)S(1)}, u32[]{:S(2)}, u32[]{:S(2)}) %collective-permute-start.7) | collective-permute-done | bytes 524320 | tf_op jit(solution)/shard_map/ppermute | solution.py:47
  91.3 1.6 fusion.30
  92.9 5.0 %collective-permute-start.8 = (bf16[4,2,64,128]{3,2,1,0:T(8,128)(2,1)S(1)}, bf16[4,2,64,128]{3,2,1,0:T(8,128)(2,1)S(1)}, u32[]{:S(2)}, u32[]{:S(2)}) collective-permute-start(bf16[4,2,64,128]{3,2,1,0:T(8,128)(2,1)S(1)} %convert_bitcast_fusion), channel_id=1, source_target_pairs={{0,2},{1,3},{2,0},{3,1},{4,6},{5,7},{6,4},{7,5},{8,10},{9,11},{10,... | collective-permute-start | bytes 393224 | tf_op jit(solution)/shard_map/ppermute | solution.py:47
  97.9 2.9 %collective-permute-done.8 = bf16[4,2,64,128]{3,2,1,0:T(8,128)(2,1)S(1)} collective-permute-done((bf16[4,2,64,128]{3,2,1,0:T(8,128)(2,1)S(1)}, bf16[4,2,64,128]{3,2,1,0:T(8,128)(2,1)S(1)}, u32[]{:S(2)}, u32[]{:S(2)}) %collective-permute-start.8) | collective-permute-done | bytes 131104 | tf_op jit(solution)/shard_map/ppermute | solution.py:47
  100.9 2.4 %collective-permute-start.9 = (bf16[2,4,2,64,128]{4,3,2,1,0:T(8,128)(2,1)S(1)}, bf16[2,4,2,64,128]{4,3,2,1,0:T(8,128)(2,1)S(1)}, u32[]{:S(2)}, u32[]{:S(2)}) collective-permute-start(bf16[2,4,2,64,128]{4,3,2,1,0:T(8,128)(2,1)S(1)} %pad_maximum_fusion.9), channel_id=1, source_target_pairs={{0,1},{1,0},{2,3},{3,2},{4,5},{5,4},{6,7},{7,6},{8,9},{9,8},{10,11... | collective-permute-start | bytes 786440 | tf_op jit(solution)/shard_map/ppermute | solution.py:47
  103.3 13.6 %collective-permute-done.9 = bf16[2,4,2,64,128]{4,3,2,1,0:T(8,128)(2,1)S(1)} collective-permute-done((bf16[2,4,2,64,128]{4,3,2,1,0:T(8,128)(2,1)S(1)}, bf16[2,4,2,64,128]{4,3,2,1,0:T(8,128)(2,1)S(1)}, u32[]{:S(2)}, u32[]{:S(2)}) %collective-permute-start.9) | collective-permute-done | bytes 262176 | tf_op jit(solution)/shard_map/ppermute | solution.py:47
  117.0 11.1 %collective-permute-done.10 = bf16[2,2,4,2,64,128]{5,4,3,2,0,1:T(8,128)(2,1)S(1)} collective-permute-done((bf16[2,2,4,2,64,128]{5,4,3,2,0,1:T(8,128)(2,1)S(1)}, bf16[2,2,4,2,64,128]{5,4,3,2,0,1:T(8,128)(2,1)S(1)}, u32[]{:S(2)}, u32[]{:S(2)}) %collective-permute-start.10) | collective-permute-done | bytes 524320 | tf_op jit(solution)/shard_map/ppermute | solution.py:47
  130.1 2.1 %collective-permute-start.11 = (bf16[2,2,2,4,2,64,128]{6,5,4,3,1,2,0:T(8,128)(2,1)}, bf16[2,2,2,4,2,64,128]{6,5,4,3,1,2,0:T(8,128)(2,1)}, u32[]{:S(2)}, u32[]{:S(2)}) collective-permute-start(bf16[2,2,2,4,2,64,128]{6,5,4,3,1,2,0:T(8,128)(2,1)} %pad_maximum_fusion.3), channel_id=1, source_target_pairs={{0,4},{1,5},{2,6},{3,7},{4,0},{5,1},{6,2},{7,3},{8,12},{9,13},{10,... | collective-permute-start | bytes 3145736 | tf_op jit(solution)/shard_map/ppermute | solution.py:47
  132.4 1.4 gather_fusion
  133.9 17.6 %collective-permute-done.11 = bf16[2,2,2,4,2,64,128]{6,5,4,3,1,2,0:T(8,128)(2,1)} collective-permute-done((bf16[2,2,2,4,2,64,128]{6,5,4,3,1,2,0:T(8,128)(2,1)}, bf16[2,2,2,4,2,64,128]{6,5,4,3,1,2,0:T(8,128)(2,1)}, u32[]{:S(2)}, u32[]{:S(2)}) %collective-permute-start.11) | collective-permute-done | bytes 1048608 | tf_op jit(solution)/shard_map/ppermute | solution.py:47
  151.5 1.5 select_bitcast_fusion.1
  153.6 1.3 fusion.10
  155.1 3.0 %collective-permute-start.12 = (bf16[64,2,2,128]{3,0,1,2:T(8,128)(2,1)S(1)}, bf16[64,2,2,128]{3,0,1,2:T(8,128)(2,1)S(1)}, u32[]{:S(2)}, u32[]{:S(2)}) collective-permute-start(bf16[64,2,2,128]{3,0,1,2:T(8,128)(2,1)S(1)} %fusion.34), channel_id=1, source_target_pairs={{0,64},{16,80},{32,96},{48,112},{64,0},{80,16},{96,32},{112,48},{1... | collective-permute-start | bytes 196616 | tf_op jit(solution)/shard_map/ppermute | solution.py:47
  158.3 1.3 collective-permute-start.16
  159.6 7.1 %collective-permute-start.17 = (f32[2,512,1]{2,1,0:T(8,128)S(1)}, f32[2,512,1]{2,1,0:T(8,128)S(1)}, u32[]{:S(2)}, u32[]{:S(2)}) collective-permute-start(f32[2,512,1]{2,1,0:T(8,128)S(1)} %bitcast.239), channel_id=1, source_target_pairs={{16,0},{32,16},{48,32},{64,48},{80,64},{96,80},{112,96},{128,112},... | collective-permute-start | bytes 12296 | tf_op jit(solution)/shard_map/ppermute | solution.py:157
  166.8 3.0 %collective-permute-start.13 = (bf16[2,64,2,2,128]{4,1,2,3,0:T(8,128)(2,1)S(1)}, bf16[2,64,2,2,128]{4,1,2,3,0:T(8,128)(2,1)S(1)}, u32[]{:S(2)}, u32[]{:S(2)}) collective-permute-start(bf16[2,64,2,2,128]{4,1,2,3,0:T(8,128)(2,1)S(1)} %pad_maximum_fusion.12), channel_id=1, source_target_pairs={{0,128},{16,144},{32,160},{48,176},{64,192},{80,208},{96,224},{112... | collective-permute-start | bytes 393224 | tf_op jit(solution)/shard_map/ppermute | solution.py:47
  169.8 4.0 %collective-permute-done.17 = f32[2,512,1]{2,1,0:T(8,128)S(1)} collective-permute-done((f32[2,512,1]{2,1,0:T(8,128)S(1)}, f32[2,512,1]{2,1,0:T(8,128)S(1)}, u32[]{:S(2)}, u32[]{:S(2)}) %collective-permute-start.17) | collective-permute-done | bytes 4128 | tf_op jit(solution)/shard_map/ppermute | solution.py:157
  174.5 5.0 %collective-permute-done.14 = bf16[2,2,64,2,2,128]{5,2,3,4,1,0:T(8,128)(2,1)S(1)} collective-permute-done((bf16[2,2,64,2,2,128]{5,2,3,4,1,0:T(8,128)(2,1)S(1)}, bf16[2,2,64,2,2,128]{5,2,3,4,1,0:T(8,128)(2,1)S(1)}, u32[]{:S(2)}, u32[]{:S(2)}) %collective-permute-start.14) | collective-permute-done | bytes 262176 | tf_op jit(solution)/shard_map/ppermute | solution.py:47
  179.6 7.0 %collective-permute-start.15 = (bf16[2,2,2,64,2,2,128]{6,3,4,5,1,0,2:T(8,128)(2,1)S(1)}, bf16[2,2,2,64,2,2,128]{6,3,4,5,1,0,2:T(8,128)(2,1)S(1)}, u32[]{:S(2)}, u32[]{:S(2)}) collective-permute-start(bf16[2,2,2,64,2,2,128]{6,3,4,5,1,0,2:T(8,128)(2,1)S(1)} %pad_maximum_fusion.7), channel_id=1, source_target_pairs={{0,16},{16,0},{32,48},{48,32},{64,80},{80,64},{96,112},{112,96},{1... | collective-permute-start | bytes 1572872 | tf_op jit(solution)/shard_map/ppermute | solution.py:47
  187.7 5.6 %collective-permute-start.18 = (f32[2,1,128]{2,1,0:T(1,128)S(1)}, f32[2,1,128]{2,1,0:T(1,128)S(1)}, u32[]{:S(2)}, u32[]{:S(2)}) collective-permute-start(f32[2,1,128]{2,1,0:T(1,128)S(1)} %slice.87), channel_id=1, source_target_pairs={{0,1},{1,2},{2,3},{3,4},{4,5},{5,6},{6,7},{7,8},{8,9},{9,10},{10,1... | collective-permute-start | bytes 3080 | tf_op jit(solution)/shard_map/ppermute | solution.py:169
  194.3 1.9 collective-permute-start.19
  197.4 1.3 fusion.43
  198.7 1.3 fusion.44
  200.0 1.3 fusion.17
  201.3 2.0 fusion.16
  203.4 1.1 copy.106
  204.5 2.1 %fusion.50 = f32[2,512,128]{2,1,0:T(8,128)} fusion(f32[2,512,128]{2,1,0:T(8,128)S(1)} %copy-done.1, f32[1,512,128]{2,1,0:T(8,128)S(1)} %bitcast.251, f32[1,512,128]{2,1,0:T(8,128)S(1)} %bitcast.252, f32[2,512,128]{2,1,0:T(8,128)S(1)} %get-tuple-element.30, f32[2,512,128]{2,1,0:T(8,128)S(1)} %copy-done.3, f32[2,511,128]{2,1,0:T(8,128)S(1)} %bitcast.242, ...), kind=kLoop, calls=%fused_computation.67 | loop fusion | flops 1179648 | bytes 3670016 | tf_op jit(solution)/shard_map/sub | solution.py:177
  (111 shorter events, 16.5 us)
Async XLA Ops:
  0.6 90.5 %copy-start = (bf16[8,128,128]{2,1,0:T(8,128)(2,1)S(1)}, bf16[8,128,128]{2,1,0:T(8,128)(2,1)}, u32[]{:S(2)}) copy-start(bf16[8,128,128]{2,1,0:T(8,128)(2,1)} %param.16) | copy-start | bytes 786436
  0.7 2.8 %copy-start.1 = (f32[2,512,128]{2,1,0:T(8,128)S(1)}, f32[2,512,128]{2,1,0:T(8,128)}, u32[]{:S(2)}) copy-start(f32[2,512,128]{2,1,0:T(8,128)} %param.10) | copy-start | bytes 1572868
  19.8 5.9 %collective-permute-start = (f32[2,2,2,2,64,2,128]{6,4,5,3,2,1,0:T(8,128)}, f32[2,2,2,2,64,2,128]{6,4,5,3,2,1,0:T(8,128)}, u32[]{:S(2)}, u32[]{:S(2)}) collective-permute-start(f32[2,2,2,2,64,2,128]{6,4,5,3,2,1,0:T(8,128)} %bitcast.232), channel_id=1, source_target_pairs={{0,16},{16,0},{32,48},{48,32},{64,80},{80,64},{96,112},{112,96},{1... | collective-permute-start | bytes 3145736 | tf_op jit(solution)/shard_map/ppermute | solution.py:36
  27.3 1.0 copy-start.5
  28.4 13.3 %collective-permute-start.1 = (f32[2,2,2,64,2,128]{5,3,4,2,1,0:T(8,128)S(1)}, f32[2,2,2,64,2,128]{5,3,4,2,1,0:T(8,128)}, u32[]{:S(2)}, u32[]{:S(2)}) collective-permute-start(f32[2,2,2,64,2,128]{5,3,4,2,1,0:T(8,128)S(1)} %dynamic-slice_bitcast_fusion), channel_id=1, source_target_pairs={{0,128},{16,144},{32,160},{48,176},{64,192},{80,208},{96,224},{112... | collective-permute-start | bytes 1572872 | tf_op jit(solution)/shard_map/ppermute | solution.py:36
  43.0 31.5 %copy-start.14 = (s32[32,1,6]{0,1,2:T(1,128)S(1)}, s32[32,1,6]{0,1,2:T(1,128)}, u32[]{:S(2)}) copy-start(s32[32,1,6]{0,1,2:T(1,128)} %param.18) | copy-start | bytes 2308
  43.0 31.5 %copy-start.13 = (s32[32,1,6]{0,1,2:T(1,128)S(1)}, s32[32,1,6]{0,1,2:T(1,128)}, u32[]{:S(2)}) copy-start(s32[32,1,6]{0,1,2:T(1,128)} %param.17) | copy-start | bytes 2308
  43.7 6.9 %collective-permute-start.2 = (f32[2,2,64,2,128]{4,2,3,1,0:T(8,128)}, f32[2,2,64,2,128]{4,2,3,1,0:T(8,128)}, u32[]{:S(2)}, u32[]{:S(2)}) collective-permute-start(f32[2,2,64,2,128]{4,2,3,1,0:T(8,128)} %dynamic-slice_bitcast_fusion.1), channel_id=1, source_target_pairs={{0,32},{16,48},{32,0},{48,16},{64,96},{80,112},{96,64},{112,80},{1... | collective-permute-start | bytes 786440 | tf_op jit(solution)/shard_map/ppermute | solution.py:36
  51.7 5.4 %collective-permute-start.3 = (f32[2,64,2,128]{3,1,0,2:T(8,128)S(1)}, f32[2,64,2,128]{3,1,0,2:T(8,128)S(1)}, u32[]{:S(2)}, u32[]{:S(2)}) collective-permute-start(f32[2,64,2,128]{3,1,0,2:T(8,128)S(1)} %bitcast.258), channel_id=1, source_target_pairs={{0,64},{16,80},{32,96},{48,112},{64,0},{80,16},{96,32},{112,48},{1... | collective-permute-start | bytes 393224 | tf_op jit(solution)/shard_map/ppermute | solution.py:36
  57.1 23.9 %copy-start.15 = (s32[64]{0:T(128)S(1)}, s32[64]{0:T(128)}, u32[]{:S(2)}) copy-start(s32[64]{0:T(128)} %param.19) | copy-start | bytes 772
  57.1 7.2 %collective-permute-start.4 = (bf16[2,64,2,128]{3,1,2,0:T(8,128)(2,1)S(1)}, bf16[2,64,2,128]{3,1,2,0:T(8,128)(2,1)S(1)}, u32[]{:S(2)}, u32[]{:S(2)}) collective-permute-start(bf16[2,64,2,128]{3,1,2,0:T(8,128)(2,1)S(1)} %fusion.60), channel_id=1, source_target_pairs={{0,2},{1,3},{2,0},{3,1},{4,6},{5,7},{6,4},{7,5},{8,10},{9,11},{10,... | collective-permute-start | bytes 196616 | tf_op jit(solution)/shard_map/ppermute | solution.py:47
  64.3 7.1 %collective-permute-start.5 = (bf16[2,2,64,2,128]{4,2,3,1,0:T(8,128)(2,1)S(1)}, bf16[2,2,64,2,128]{4,2,3,1,0:T(8,128)(2,1)S(1)}, u32[]{:S(2)}, u32[]{:S(2)}) collective-permute-start(bf16[2,2,64,2,128]{4,2,3,1,0:T(8,128)(2,1)S(1)} %pad_maximum_fusion.11), channel_id=1, source_target_pairs={{0,1},{1,0},{2,3},{3,2},{4,5},{5,4},{6,7},{7,6},{8,9},{9,8},{10,11... | collective-permute-start | bytes 393224 | tf_op jit(solution)/shard_map/ppermute | solution.py:47
  71.5 6.9 %collective-permute-start.6 = (bf16[2,2,2,64,2,128]{5,3,4,2,1,0:T(8,128)(2,1)S(1)}, bf16[2,2,2,64,2,128]{5,3,4,2,1,0:T(8,128)(2,1)}, u32[]{:S(2)}, u32[]{:S(2)}) collective-permute-start(bf16[2,2,2,64,2,128]{5,3,4,2,1,0:T(8,128)(2,1)S(1)} %pad_maximum_fusion.8), channel_id=1, source_target_pairs={{0,8},{1,9},{2,10},{3,11},{4,12},{5,13},{6,14},{7,15},{8,0},{9,1},... | collective-permute-start | bytes 786440 | tf_op jit(solution)/shard_map/ppermute | solution.py:47
  79.5 10.7 %collective-permute-start.7 = (bf16[2,2,2,2,64,2,128]{6,4,5,3,2,1,0:T(8,128)(2,1)S(1)}, bf16[2,2,2,2,64,2,128]{6,4,5,3,2,1,0:T(8,128)(2,1)S(1)}, u32[]{:S(2)}, u32[]{:S(2)}) collective-permute-start(bf16[2,2,2,2,64,2,128]{6,4,5,3,2,1,0:T(8,128)(2,1)S(1)} %pad_maximum_fusion.5), channel_id=1, source_target_pairs={{0,4},{1,5},{2,6},{3,7},{4,0},{5,1},{6,2},{7,3},{8,12},{9,13},{10,... | collective-permute-start | bytes 1572872 | tf_op jit(solution)/shard_map/ppermute | solution.py:47
  90.3 1.0 copy-start.11
  90.3 1.0 copy-start.12
  92.9 35.3 %copy-start.6 = (f32[2,64,4,128]{3,1,0,2:T(8,128)}, f32[2,64,4,128]{3,1,0,2:T(8,128)S(1)}, u32[]{:S(2)}) copy-start(f32[2,64,4,128]{3,1,0,2:T(8,128)S(1)} %fusion.30) | copy-start | bytes 786436
  92.9 7.9 %collective-permute-start.8 = (bf16[4,2,64,128]{3,2,1,0:T(8,128)(2,1)S(1)}, bf16[4,2,64,128]{3,2,1,0:T(8,128)(2,1)S(1)}, u32[]{:S(2)}, u32[]{:S(2)}) collective-permute-start(bf16[4,2,64,128]{3,2,1,0:T(8,128)(2,1)S(1)} %convert_bitcast_fusion), channel_id=1, source_target_pairs={{0,2},{1,3},{2,0},{3,1},{4,6},{5,7},{6,4},{7,5},{8,10},{9,11},{10,... | collective-permute-start | bytes 393224 | tf_op jit(solution)/shard_map/ppermute | solution.py:47
  100.9 15.9 %collective-permute-start.9 = (bf16[2,4,2,64,128]{4,3,2,1,0:T(8,128)(2,1)S(1)}, bf16[2,4,2,64,128]{4,3,2,1,0:T(8,128)(2,1)S(1)}, u32[]{:S(2)}, u32[]{:S(2)}) collective-permute-start(bf16[2,4,2,64,128]{4,3,2,1,0:T(8,128)(2,1)S(1)} %pad_maximum_fusion.9), channel_id=1, source_target_pairs={{0,1},{1,0},{2,3},{3,2},{4,5},{5,4},{6,7},{7,6},{8,9},{9,8},{10,11... | collective-permute-start | bytes 786440 | tf_op jit(solution)/shard_map/ppermute | solution.py:47
  116.9 11.2 %collective-permute-start.10 = (bf16[2,2,4,2,64,128]{5,4,3,2,0,1:T(8,128)(2,1)S(1)}, bf16[2,2,4,2,64,128]{5,4,3,2,0,1:T(8,128)(2,1)S(1)}, u32[]{:S(2)}, u32[]{:S(2)}) collective-permute-start(bf16[2,2,4,2,64,128]{5,4,3,2,0,1:T(8,128)(2,1)S(1)} %pad_maximum_fusion.6), channel_id=1, source_target_pairs={{0,8},{1,9},{2,10},{3,11},{4,12},{5,13},{6,14},{7,15},{8,0},{9,1},... | collective-permute-start | bytes 1572872 | tf_op jit(solution)/shard_map/ppermute | solution.py:47
  128.2 0.8 copy-start.4
  130.1 21.5 %collective-permute-start.11 = (bf16[2,2,2,4,2,64,128]{6,5,4,3,1,2,0:T(8,128)(2,1)}, bf16[2,2,2,4,2,64,128]{6,5,4,3,1,2,0:T(8,128)(2,1)}, u32[]{:S(2)}, u32[]{:S(2)}) collective-permute-start(bf16[2,2,2,4,2,64,128]{6,5,4,3,1,2,0:T(8,128)(2,1)} %pad_maximum_fusion.3), channel_id=1, source_target_pairs={{0,4},{1,5},{2,6},{3,7},{4,0},{5,1},{6,2},{7,3},{8,12},{9,13},{10,... | collective-permute-start | bytes 3145736 | tf_op jit(solution)/shard_map/ppermute | solution.py:47
  153.5 1.3 copy-start.10
  155.1 11.7 %collective-permute-start.12 = (bf16[64,2,2,128]{3,0,1,2:T(8,128)(2,1)S(1)}, bf16[64,2,2,128]{3,0,1,2:T(8,128)(2,1)S(1)}, u32[]{:S(2)}, u32[]{:S(2)}) collective-permute-start(bf16[64,2,2,128]{3,0,1,2:T(8,128)(2,1)S(1)} %fusion.34), channel_id=1, source_target_pairs={{0,64},{16,80},{32,96},{48,112},{64,0},{80,16},{96,32},{112,48},{1... | collective-permute-start | bytes 196616 | tf_op jit(solution)/shard_map/ppermute | solution.py:47
  158.3 11.5 %collective-permute-start.16 = (f32[2,1,128]{2,1,0:T(1,128)S(1)}, f32[2,1,128]{2,1,0:T(1,128)S(1)}, u32[]{:S(2)}, u32[]{:S(2)}) collective-permute-start(f32[2,1,128]{2,1,0:T(1,128)S(1)} %slice.71), channel_id=1, source_target_pairs={{1,0},{2,1},{3,2},{4,3},{5,4},{6,5},{7,6},{8,7},{9,8},{10,9},{11,1... | collective-permute-start | bytes 3080 | tf_op jit(solution)/shard_map/ppermute | solution.py:156
  159.6 14.1 %collective-permute-start.17 = (f32[2,512,1]{2,1,0:T(8,128)S(1)}, f32[2,512,1]{2,1,0:T(8,128)S(1)}, u32[]{:S(2)}, u32[]{:S(2)}) collective-permute-start(f32[2,512,1]{2,1,0:T(8,128)S(1)} %bitcast.239), channel_id=1, source_target_pairs={{16,0},{32,16},{48,32},{64,48},{80,64},{96,80},{112,96},{128,112},... | collective-permute-start | bytes 12296 | tf_op jit(solution)/shard_map/ppermute | solution.py:157
  166.8 7.5 %copy-start.8 = (f32[2,2,512,128]{3,2,1,0:T(8,128)S(1)}, f32[2,2,512,128]{3,2,1,0:T(8,128)}, u32[]{:S(2)}) copy-start(f32[2,2,512,128]{3,2,1,0:T(8,128)} %param.11) | copy-start | bytes 3145732
  166.8 7.3 %collective-permute-start.13 = (bf16[2,64,2,2,128]{4,1,2,3,0:T(8,128)(2,1)S(1)}, bf16[2,64,2,2,128]{4,1,2,3,0:T(8,128)(2,1)S(1)}, u32[]{:S(2)}, u32[]{:S(2)}) collective-permute-start(bf16[2,64,2,2,128]{4,1,2,3,0:T(8,128)(2,1)S(1)} %pad_maximum_fusion.12), channel_id=1, source_target_pairs={{0,128},{16,144},{32,160},{48,176},{64,192},{80,208},{96,224},{112... | collective-permute-start | bytes 393224 | tf_op jit(solution)/shard_map/ppermute | solution.py:47
  174.2 5.3 %collective-permute-start.14 = (bf16[2,2,64,2,2,128]{5,2,3,4,1,0:T(8,128)(2,1)S(1)}, bf16[2,2,64,2,2,128]{5,2,3,4,1,0:T(8,128)(2,1)S(1)}, u32[]{:S(2)}, u32[]{:S(2)}) collective-permute-start(bf16[2,2,64,2,2,128]{5,2,3,4,1,0:T(8,128)(2,1)S(1)} %pad_maximum_fusion.10), channel_id=1, source_target_pairs={{0,32},{16,48},{32,0},{48,16},{64,96},{80,112},{96,64},{112,80},{1... | collective-permute-start | bytes 786440 | tf_op jit(solution)/shard_map/ppermute | solution.py:47
  179.6 17.5 %collective-permute-start.15 = (bf16[2,2,2,64,2,2,128]{6,3,4,5,1,0,2:T(8,128)(2,1)S(1)}, bf16[2,2,2,64,2,2,128]{6,3,4,5,1,0,2:T(8,128)(2,1)S(1)}, u32[]{:S(2)}, u32[]{:S(2)}) collective-permute-start(bf16[2,2,2,64,2,2,128]{6,3,4,5,1,0,2:T(8,128)(2,1)S(1)} %pad_maximum_fusion.7), channel_id=1, source_target_pairs={{0,16},{16,0},{32,48},{48,32},{64,80},{80,64},{96,112},{112,96},{1... | collective-permute-start | bytes 1572872 | tf_op jit(solution)/shard_map/ppermute | solution.py:47
  186.7 10.5 %copy-start.9 = (f32[2,2,512,128]{3,2,1,0:T(8,128)}, f32[2,2,512,128]{3,2,1,0:T(8,128)S(1)}, u32[]{:S(2)}) copy-start(f32[2,2,512,128]{3,2,1,0:T(8,128)S(1)} %broadcast_divide_fusion) | copy-start | bytes 3145732
  186.7 9.5 %copy-start.7 = (f32[2,64,4,128]{3,1,0,2:T(8,128)S(1)}, f32[2,64,4,128]{3,1,0,2:T(8,128)}, u32[]{:S(2)}) copy-start(f32[2,64,4,128]{3,1,0,2:T(8,128)} %copy-done.6) | copy-start | bytes 786436
  186.9 0.8 copy-start.2
  187.7 16.9 %collective-permute-start.18 = (f32[2,1,128]{2,1,0:T(1,128)S(1)}, f32[2,1,128]{2,1,0:T(1,128)S(1)}, u32[]{:S(2)}, u32[]{:S(2)}) collective-permute-start(f32[2,1,128]{2,1,0:T(1,128)S(1)} %slice.87), channel_id=1, source_target_pairs={{0,1},{1,2},{2,3},{3,4},{4,5},{5,6},{6,7},{7,8},{8,9},{9,10},{10,1... | collective-permute-start | bytes 3080 | tf_op jit(solution)/shard_map/ppermute | solution.py:169
  194.3 10.2 %collective-permute-start.19 = (f32[2,512,1]{2,1,0:T(8,128)}, f32[2,512,1]{2,1,0:T(8,128)}, u32[]{:S(2)}, u32[]{:S(2)}) collective-permute-start(f32[2,512,1]{2,1,0:T(8,128)} %slice.90), channel_id=1, source_target_pairs={{0,16},{16,32},{32,48},{48,64},{64,80},{80,96},{96,112},{112,128},... | collective-permute-start | bytes 12296 | tf_op jit(solution)/shard_map/ppermute | solution.py:170
  201.3 3.2 %copy-start.3 = (f32[2,512,128]{2,1,0:T(8,128)S(1)}, f32[2,512,128]{2,1,0:T(8,128)}, u32[]{:S(2)}) copy-start(f32[2,512,128]{2,1,0:T(8,128)} %copy-done.2) | copy-start | bytes 1572868

commit v14 on v11

--- a/solution.py
+++ b/solution.py
@@ -75,20 +75,20 @@
     steer_im = row_steer[1]
     col_mine = lax.dynamic_slice_in_dim(col_steer, az_index, 1, 3)[..., 0]
     image_b = image.astype(jnp.bfloat16).reshape(2, tiles_dev, tile_rows, columns)
-    part_sre = steer_re
-    part_sim = steer_im
-    weight_re = col_mine[0][..., None]
-    weight_im = col_mine[1][..., None]
-    prod_re = jnp.einsum("pjh,jhu->pju", part_sre, image_b[0], preferred_element_type=jnp.float32)
+    part_sre = jnp.transpose(steer_re, (1, 0, 2))
+    part_sim = jnp.transpose(steer_im, (1, 0, 2))
+    weight_re = col_mine[0].T[..., None]
+    weight_im = col_mine[1].T[..., None]
+    prod_re = jnp.einsum("jph,jhu->jpu", part_sre, image_b[0], preferred_element_type=jnp.float32)
     prod_re = prod_re - jnp.einsum(
-        "pjh,jhu->pju", part_sim, image_b[1], preferred_element_type=jnp.float32
+        "jph,jhu->jpu", part_sim, image_b[1], preferred_element_type=jnp.float32
     )
-    prod_im = jnp.einsum("pjh,jhu->pju", part_sre, image_b[1], preferred_element_type=jnp.float32)
+    prod_im = jnp.einsum("jph,jhu->jpu", part_sre, image_b[1], preferred_element_type=jnp.float32)
     prod_im = prod_im + jnp.einsum(
-        "pjh,jhu->pju", part_sim, image_b[0], preferred_element_type=jnp.float32
+        "jph,jhu->jpu", part_sim, image_b[0], preferred_element_type=jnp.float32
     )
-    real_part = weight_re * prod_re - weight_im * prod_im
-    imag_part = weight_re * prod_im + weight_im * prod_re
+    real_part = jnp.transpose(weight_re * prod_re - weight_im * prod_im, (1, 0, 2))
+    imag_part = jnp.transpose(weight_re * prod_im + weight_im * prod_re, (1, 0, 2))
     parts = jnp.stack([real_part, imag_part], axis=0).reshape(2, az_count, -1, tiles_dev, columns)
     summed = halving_sum(jnp.moveaxis(parts, 1, 0), "az", (1, 8, 2, 4))
     projection_b = jnp.transpose(summed, (2, 1, 0, 3)).astype(jnp.bfloat16)

time: 188 us -> 185 us (0.984)
  local copies, waits for them, and re-layouts: 22.8 us -> 20.7 us
  transfers between devices with their start and end apart: 20 -> 20, of which waited for: 15 -> 15; matrix products, arithmetic and copies ran while one was open for 12% -> 13% of each run, Pallas kernels for 0% -> 0%
where the time goes in v14:
time: 185 us
  waiting for transfers between devices  85.7 us (46%)
  starting transfers between devices  42.8 us (23%)
  local copies, waits for them, and re-layouts  20.7 us (11%)
  other arithmetic  20.4 us (11%)
  matrix products  13.7 us (7%)
    ppermute x12, waiting for transfers between devices, doubling_gather(): got = lax.ppermute(block, axis, pairs)  54.8 us
    ppermute x4, waiting for transfers between devices, halving_sum(): blocks = keep + lax.ppermute(send, axis, pairs)  26 us
    ppermute x12, starting transfers between devices, doubling_gather(): got = lax.ppermute(block, axis, pairs)  23.6 us
    ppermute x2, starting transfers between devices, padded_2(): lax.ppermute(lax.slice_in_dim(block, block.shape[dim] - width, None, axis...  10.9 us
    unnamed x68, local copies, waits for them, and re-layouts  5.67 us
    ppermute x4, starting transfers between devices, halving_sum(): blocks = keep + lax.ppermute(send, axis, pairs)  5.08 us
    ppermute x2, waiting for transfers between devices, padded_2(): lax.ppermute(lax.slice_in_dim(block, 0, width, axis=dim), axis, backward)  4.89 us
    another operation x24, other arithmetic, doubling_gather(): block = jnp.stack([low, high], axis=place)  4.32 us
  transfers between devices with their start and end apart: 20, of which 15 were waited for; matrix products, arithmetic and copies ran while one was open for 13% of the time, Pallas kernels for 0%

profile of v14, /device:TPU:1, one launch (start us, length us, event | category | flops | bytes accessed | tf_op | source)
XLA Modules:
  0.0 184.8 jit_solution(10448093874429712080)
XLA Ops:
  0.7 2.7 %fusion.90 = (bf16[1,1024,2,256]{3,2,1,0:T(2,128)(2,1)S(1)}, bf16[1,1024,2,256]{3,2,1,0:T(2,128)(2,1)S(1)}) fusion(bf16[2,1024,2,256]{3,2,1,0:T(2,128)(2,1)} %param.14), kind=kLoop, calls=%fused_computation.182 | loop fusion | bytes 4194304 | tf_op jit(solution)/shard_map/slice | solution.py:75
  4.4 1.4 fusion.51
  8.6 1.3 multiply_subtract_fusion
  11.0 3.2 %collective-permute-start = (f32[2,2,2,2,64,2,128]{6,4,2,1,0,5,3:T(8,128)}, f32[2,2,2,2,64,2,128]{6,4,2,1,0,5,3:T(8,128)}, u32[]{:S(2)}, u32[]{:S(2)}) collective-permute-start(f32[2,2,2,2,64,2,128]{6,4,2,1,0,5,3:T(8,128)} %dynamic-slice_bitcast_fusion), channel_id=1, source_target_pairs={{0,16},{16,0},{32,48},{48,32},{64,80},{80,64},{96,112},{112,96},{1... | collective-permute-start | bytes 3145736 | tf_op jit(solution)/shard_map/ppermute | solution.py:36
  14.3 2.6 %collective-permute-done = f32[2,2,2,2,64,2,128]{6,4,2,1,0,5,3:T(8,128)} collective-permute-done((f32[2,2,2,2,64,2,128]{6,4,2,1,0,5,3:T(8,128)}, f32[2,2,2,2,64,2,128]{6,4,2,1,0,5,3:T(8,128)}, u32[]{:S(2)}, u32[]{:S(2)}) %collective-permute-start) | collective-permute-done | bytes 1048608 | tf_op jit(solution)/shard_map/ppermute | solution.py:36
  16.9 1.4 bitcast_add_fusion
  18.6 13.1 %collective-permute-done.1 = f32[2,2,2,64,2,128]{5,3,2,4,0,1:T(8,128)S(1)} collective-permute-done((f32[2,2,2,64,2,128]{5,3,2,4,0,1:T(8,128)S(1)}, f32[2,2,2,64,2,128]{5,3,2,4,0,1:T(8,128)S(1)}, u32[]{:S(2)}, u32[]{:S(2)}) %collective-permute-start.1) | collective-permute-done | bytes 524320 | tf_op jit(solution)/shard_map/ppermute | solution.py:36
  31.9 6.5 %collective-permute-done.2 = f32[2,2,64,2,128]{4,2,1,3,0:T(8,128)S(1)} collective-permute-done((f32[2,2,64,2,128]{4,2,1,3,0:T(8,128)S(1)}, f32[2,2,64,2,128]{4,2,1,3,0:T(8,128)S(1)}, u32[]{:S(2)}, u32[]{:S(2)}) %collective-permute-start.2) | collective-permute-done | bytes 262176 | tf_op jit(solution)/shard_map/ppermute | solution.py:36
  38.5 1.7 collective-permute-start.3
  40.2 3.8 %collective-permute-done.3 = f32[2,64,2,128]{3,1,0,2:T(8,128)S(1)} collective-permute-done((f32[2,64,2,128]{3,1,0,2:T(8,128)S(1)}, f32[2,64,2,128]{3,1,0,2:T(8,128)S(1)}, u32[]{:S(2)}, u32[]{:S(2)}) %collective-permute-start.3) | collective-permute-done | bytes 131104 | tf_op jit(solution)/shard_map/ppermute | solution.py:36
  43.9 5.3 %collective-permute-start.4 = (bf16[2,64,2,128]{3,1,2,0:T(8,128)(2,1)S(1)}, bf16[2,64,2,128]{3,1,2,0:T(8,128)(2,1)S(1)}, u32[]{:S(2)}, u32[]{:S(2)}) collective-permute-start(bf16[2,64,2,128]{3,1,2,0:T(8,128)(2,1)S(1)} %fusion.76), channel_id=1, source_target_pairs={{0,2},{1,3},{2,0},{3,1},{4,6},{5,7},{6,4},{7,5},{8,10},{9,11},{10,... | collective-permute-start | bytes 196616 | tf_op jit(solution)/shard_map/ppermute | solution.py:47
  49.2 1.9 %collective-permute-done.4 = bf16[2,64,2,128]{3,1,2,0:T(8,128)(2,1)S(1)} collective-permute-done((bf16[2,64,2,128]{3,1,2,0:T(8,128)(2,1)S(1)}, bf16[2,64,2,128]{3,1,2,0:T(8,128)(2,1)S(1)}, u32[]{:S(2)}, u32[]{:S(2)}) %collective-permute-start.4) | collective-permute-done | bytes 65568 | tf_op jit(solution)/shard_map/ppermute | solution.py:47
  51.2 2.5 %collective-permute-start.5 = (bf16[2,2,64,2,128]{4,2,3,1,0:T(8,128)(2,1)S(1)}, bf16[2,2,64,2,128]{4,2,3,1,0:T(8,128)(2,1)S(1)}, u32[]{:S(2)}, u32[]{:S(2)}) collective-permute-start(bf16[2,2,64,2,128]{4,2,3,1,0:T(8,128)(2,1)S(1)} %pad_maximum_fusion.26), channel_id=1, source_target_pairs={{0,1},{1,0},{2,3},{3,2},{4,5},{5,4},{6,7},{7,6},{8,9},{9,8},{10,11... | collective-permute-start | bytes 393224 | tf_op jit(solution)/shard_map/ppermute | solution.py:47
  53.7 4.5 %collective-permute-done.5 = bf16[2,2,64,2,128]{4,2,3,1,0:T(8,128)(2,1)S(1)} collective-permute-done((bf16[2,2,64,2,128]{4,2,3,1,0:T(8,128)(2,1)S(1)}, bf16[2,2,64,2,128]{4,2,3,1,0:T(8,128)(2,1)S(1)}, u32[]{:S(2)}, u32[]{:S(2)}) %collective-permute-start.5) | collective-permute-done | bytes 131104 | tf_op jit(solution)/shard_map/ppermute | solution.py:47
  58.3 3.0 %collective-permute-start.6 = (bf16[2,2,2,64,2,128]{5,3,4,2,1,0:T(8,128)(2,1)S(1)}, bf16[2,2,2,64,2,128]{5,3,4,2,1,0:T(8,128)(2,1)S(1)}, u32[]{:S(2)}, u32[]{:S(2)}) collective-permute-start(bf16[2,2,2,64,2,128]{5,3,4,2,1,0:T(8,128)(2,1)S(1)} %pad_maximum_fusion.23), channel_id=1, source_target_pairs={{0,8},{1,9},{2,10},{3,11},{4,12},{5,13},{6,14},{7,15},{8,0},{9,1},... | collective-permute-start | bytes 786440 | tf_op jit(solution)/shard_map/ppermute | solution.py:47
  61.4 3.8 %collective-permute-done.6 = bf16[2,2,2,64,2,128]{5,3,4,2,1,0:T(8,128)(2,1)S(1)} collective-permute-done((bf16[2,2,2,64,2,128]{5,3,4,2,1,0:T(8,128)(2,1)S(1)}, bf16[2,2,2,64,2,128]{5,3,4,2,1,0:T(8,128)(2,1)S(1)}, u32[]{:S(2)}, u32[]{:S(2)}) %collective-permute-start.6) | collective-permute-done | bytes 262176 | tf_op jit(solution)/shard_map/ppermute | solution.py:47
  65.3 1.4 collective-permute-start.7
  66.8 10.1 %collective-permute-done.7 = bf16[2,2,2,2,64,2,128]{6,4,5,3,2,1,0:T(8,128)(2,1)S(1)} collective-permute-done((bf16[2,2,2,2,64,2,128]{6,4,5,3,2,1,0:T(8,128)(2,1)S(1)}, bf16[2,2,2,2,64,2,128]{6,4,5,3,2,1,0:T(8,128)(2,1)S(1)}, u32[]{:S(2)}, u32[]{:S(2)}) %collective-permute-start.7) | collective-permute-done | bytes 524320 | tf_op jit(solution)/shard_map/ppermute | solution.py:47
  78.0 1.6 fusion.30
  79.6 4.4 %collective-permute-start.8 = (bf16[4,2,64,128]{3,2,1,0:T(8,128)(2,1)S(1)}, bf16[4,2,64,128]{3,2,1,0:T(8,128)(2,1)S(1)}, u32[]{:S(2)}, u32[]{:S(2)}) collective-permute-start(bf16[4,2,64,128]{3,2,1,0:T(8,128)(2,1)S(1)} %convert_bitcast_fusion), channel_id=1, source_target_pairs={{0,2},{1,3},{2,0},{3,1},{4,6},{5,7},{6,4},{7,5},{8,10},{9,11},{10,... | collective-permute-start | bytes 393224 | tf_op jit(solution)/shard_map/ppermute | solution.py:47
  84.0 3.4 %collective-permute-done.8 = bf16[4,2,64,128]{3,2,1,0:T(8,128)(2,1)S(1)} collective-permute-done((bf16[4,2,64,128]{3,2,1,0:T(8,128)(2,1)S(1)}, bf16[4,2,64,128]{3,2,1,0:T(8,128)(2,1)S(1)}, u32[]{:S(2)}, u32[]{:S(2)}) %collective-permute-start.8) | collective-permute-done | bytes 131104 | tf_op jit(solution)/shard_map/ppermute | solution.py:47
  87.8 15.3 %collective-permute-done.9 = bf16[2,4,2,64,128]{4,3,2,1,0:T(8,128)(2,1)S(1)} collective-permute-done((bf16[2,4,2,64,128]{4,3,2,1,0:T(8,128)(2,1)S(1)}, bf16[2,4,2,64,128]{4,3,2,1,0:T(8,128)(2,1)S(1)}, u32[]{:S(2)}, u32[]{:S(2)}) %collective-permute-start.9) | collective-permute-done | bytes 262176 | tf_op jit(solution)/shard_map/ppermute | solution.py:47
  104.0 1.7 slice_maximum_fusion
  105.7 1.9 %copy.94 = f32[6,512,1]{1,2,0:T(1,128)S(1)} copy(f32[6,512,1]{2,1,0:T(8,128)} %get-tuple-element.25) | data formatting | bytes 24576 | tf_op jit(solution)/shard_map/slice | solution.py:17
  107.6 9.6 %collective-permute-start.16 = (f32[6,512,1]{1,2,0:T(1,128)S(1)}, f32[6,512,1]{1,2,0:T(1,128)S(1)}, u32[]{:S(2)}, u32[]{:S(2)}) collective-permute-start(f32[6,512,1]{1,2,0:T(1,128)S(1)} %copy.94), channel_id=1, source_target_pairs={{0,16},{16,32},{32,48},{48,64},{64,80},{80,96},{96,112},{112,128},... | collective-permute-start | bytes 36872 | tf_op jit(solution)/shard_map/ppermute | solution.py:16
  118.2 1.9 %collective-permute-start.17 = (f32[6,512,1]{1,2,0:T(1,128)}, f32[6,512,1]{1,2,0:T(1,128)}, u32[]{:S(2)}, u32[]{:S(2)}) collective-permute-start(f32[6,512,1]{1,2,0:T(1,128)} %copy.95), channel_id=1, source_target_pairs={{16,0},{32,16},{48,32},{64,48},{80,64},{96,80},{112,96},{128,112},... | collective-permute-start | bytes 36872 | tf_op jit(solution)/shard_map/ppermute | solution.py:19
  126.6 1.5 pad_maximum_fusion.28
  128.0 1.3 collective-permute-start.18
  129.3 1.3 collective-permute-start.19
  131.9 1.5 gather_fusion
  133.3 4.9 %collective-permute-done.19 = f32[6,1,130]{2,1,0:T(1,128)} collective-permute-done((f32[6,1,130]{2,1,0:T(1,128)}, f32[6,1,130]{2,1,0:T(1,128)}, u32[]{:S(2)}, u32[]{:S(2)}) %collective-permute-start.19) | collective-permute-done | bytes 3152 | tf_op jit(solution)/shard_map/ppermute | solution.py:19
  138.2 2.2 %fusion.42 = f32[1,2,513,129]{3,2,1,0:T(8,128)S(1)} fusion(f32[6,1,130]{2,1,0:T(1,128)} %collective-permute-done.19, f32[6,512,1]{2,1,0:T(8,128)S(1)} %copy.97, f32[6,512,1]{2,1,0:T(8,128)S(1)} %copy.96, f32[4,512,128]{2,1,0:T(8,128)} %bitcast.248, f32[2,512,128]{2,1,0:T(8,128)} %param.10, f32[6,1,130]{2,1,0:T(1,128)S(1)} %collective-permute-done.18, ...), kind=kLoop, calls=%fused_computation.57 | loop fusion | flops 1323540 | bytes 2133609 | tf_op jit(solution)/shard_map/stack | solution.py:160
  140.5 7.2 %collective-permute-done.11 = bf16[2,2,2,4,2,64,128]{6,5,4,3,1,2,0:T(8,128)(2,1)} collective-permute-done((bf16[2,2,2,4,2,64,128]{6,5,4,3,1,2,0:T(8,128)(2,1)}, bf16[2,2,2,4,2,64,128]{6,5,4,3,1,2,0:T(8,128)(2,1)}, u32[]{:S(2)}, u32[]{:S(2)}) %collective-permute-start.11) | collective-permute-done | bytes 1048608 | tf_op jit(solution)/shard_map/ppermute | solution.py:47
  147.7 1.4 select_bitcast_fusion.1
  149.9 1.3 fusion.10
  151.5 1.7 collective-permute-start.12
  153.8 2.4 %collective-permute-done.12 = bf16[64,2,2,128]{3,0,1,2:T(8,128)(2,1)S(1)} collective-permute-done((bf16[64,2,2,128]{3,0,1,2:T(8,128)(2,1)S(1)}, bf16[64,2,2,128]{3,0,1,2:T(8,128)(2,1)S(1)}, u32[]{:S(2)}, u32[]{:S(2)}) %collective-permute-start.12) | collective-permute-done | bytes 65568 | tf_op jit(solution)/shard_map/ppermute | solution.py:47
  156.3 1.6 pad_maximum_fusion
  157.9 2.2 %collective-permute-done.13 = bf16[2,64,2,2,128]{4,1,2,3,0:T(8,128)(2,1)S(1)} collective-permute-done((bf16[2,64,2,2,128]{4,1,2,3,0:T(8,128)(2,1)S(1)}, bf16[2,64,2,2,128]{4,1,2,3,0:T(8,128)(2,1)S(1)}, u32[]{:S(2)}, u32[]{:S(2)}) %collective-permute-start.13) | collective-permute-done | bytes 131104 | tf_op jit(solution)/shard_map/ppermute | solution.py:47
  161.5 3.9 %collective-permute-done.14 = bf16[2,2,64,2,2,128]{5,2,3,4,1,0:T(8,128)(2,1)S(1)} collective-permute-done((bf16[2,2,64,2,2,128]{5,2,3,4,1,0:T(8,128)(2,1)S(1)}, bf16[2,2,64,2,2,128]{5,2,3,4,1,0:T(8,128)(2,1)S(1)}, u32[]{:S(2)}, u32[]{:S(2)}) %collective-permute-start.14) | collective-permute-done | bytes 262176 | tf_op jit(solution)/shard_map/ppermute | solution.py:47
  165.6 4.2 %collective-permute-start.15 = (bf16[2,2,2,64,2,2,128]{6,3,4,5,1,0,2:T(8,128)(2,1)S(1)}, bf16[2,2,2,64,2,2,128]{6,3,4,5,1,0,2:T(8,128)(2,1)S(1)}, u32[]{:S(2)}, u32[]{:S(2)}) collective-permute-start(bf16[2,2,2,64,2,2,128]{6,3,4,5,1,0,2:T(8,128)(2,1)S(1)} %pad_maximum_fusion.22), channel_id=1, source_target_pairs={{0,16},{16,0},{32,48},{48,32},{64,80},{80,64},{96,112},{112,96},{1... | collective-permute-start | bytes 1572872 | tf_op jit(solution)/shard_map/ppermute | solution.py:47
  170.2 1.3 slice.126
  173.9 1.5 copy-done.10
  175.4 1.3 fusion.57
  176.7 1.3 fusion.59
  178.1 1.3 fusion.16
  179.6 2.4 %fusion.17 = f32[2,256,128]{1,2,0:T(8,128)S(1)} fusion(f32[2,128,256]{2,1,0:T(8,128)S(1)} %fusion.59, bf16[1,1024,2,256]{3,2,1,0:T(2,128)(2,1)S(1)} %copy-done.8, f32[2,1024]{1,0:T(2,128)S(1)} %copy-done.26, f32[2,1024]{1,0:T(2,128)S(1)} %copy-done.27, bf16[2,2,1024,128]{3,2,1,0:T(8,128)(2,1)} %bitcast.269), kind=kOutput, calls=%fused_computation.33 | convolution fusion | flops 135856128 | bytes 2637824 | tf_op jit(solution)/shard_map/pjh,jpu->jhu/dot_general | solution.py:142
  182.1 2.7 %fusion.72 = f32[2,512,128]{2,1,0:T(8,128)} fusion(f32[2,512,128]{2,1,0:T(8,128)S(1)} %copy-done.6, f32[2,513,129]{2,1,0:T(8,128)} %get-tuple-element.18, f32[2,513,129]{2,1,0:T(8,128)S(1)} %get-tuple-element.17, f32[1,512,128]{2,1,0:T(8,128)S(1)} %bitcast.265, f32[1,512,128]{2,1,0:T(8,128)S(1)} %bitcast.264), kind=kLoop, calls=%fused_computation.101 | loop fusion | flops 917504 | bytes 3670016 | tf_op jit(solution)/shard_map/sub | solution.py:172
  (145 shorter events, 23.0 us)
Async XLA Ops:
  0.6 77.2 %copy-start = (bf16[8,128,128]{2,1,0:T(8,128)(2,1)S(1)}, bf16[8,128,128]{2,1,0:T(8,128)(2,1)}, u32[]{:S(2)}) copy-start(bf16[8,128,128]{2,1,0:T(8,128)(2,1)} %param.16) | copy-start | bytes 786436
  0.7 2.8 %copy-start.4 = (f32[2,512,128]{2,1,0:T(8,128)S(1)}, f32[2,512,128]{2,1,0:T(8,128)}, u32[]{:S(2)}) copy-start(f32[2,512,128]{2,1,0:T(8,128)} %param.10) | copy-start | bytes 1572868
  3.4 1.0 copy-start.9
  3.5 4.3 %copy-start.7 = (bf16[1,1024,2,256]{3,2,1,0:T(2,128)(2,1)}, bf16[1,1024,2,256]{3,2,1,0:T(2,128)(2,1)S(1)}, u32[]{:S(2)}) copy-start(bf16[1,1024,2,256]{3,2,1,0:T(2,128)(2,1)S(1)} %get-tuple-element.23) | copy-start | bytes 3145732
  7.3 1.2 copy-start.17
  11.0 5.9 %collective-permute-start = (f32[2,2,2,2,64,2,128]{6,4,2,1,0,5,3:T(8,128)}, f32[2,2,2,2,64,2,128]{6,4,2,1,0,5,3:T(8,128)}, u32[]{:S(2)}, u32[]{:S(2)}) collective-permute-start(f32[2,2,2,2,64,2,128]{6,4,2,1,0,5,3:T(8,128)} %dynamic-slice_bitcast_fusion), channel_id=1, source_target_pairs={{0,16},{16,0},{32,48},{48,32},{64,80},{80,64},{96,112},{112,96},{1... | collective-permute-start | bytes 3145736 | tf_op jit(solution)/shard_map/ppermute | solution.py:36
  18.4 13.2 %collective-permute-start.1 = (f32[2,2,2,64,2,128]{5,3,2,4,0,1:T(8,128)S(1)}, f32[2,2,2,64,2,128]{5,3,2,4,0,1:T(8,128)S(1)}, u32[]{:S(2)}, u32[]{:S(2)}) collective-permute-start(f32[2,2,2,64,2,128]{5,3,2,4,0,1:T(8,128)S(1)} %bitcast.270), channel_id=1, source_target_pairs={{0,128},{16,144},{32,160},{48,176},{64,192},{80,208},{96,224},{112... | collective-permute-start | bytes 1572872 | tf_op jit(solution)/shard_map/ppermute | solution.py:36
  31.8 6.7 %collective-permute-start.2 = (f32[2,2,64,2,128]{4,2,1,3,0:T(8,128)S(1)}, f32[2,2,64,2,128]{4,2,1,3,0:T(8,128)S(1)}, u32[]{:S(2)}, u32[]{:S(2)}) collective-permute-start(f32[2,2,64,2,128]{4,2,1,3,0:T(8,128)S(1)} %dynamic-slice_bitcast_fusion.1), channel_id=1, source_target_pairs={{0,32},{16,48},{32,0},{48,16},{64,96},{80,112},{96,64},{112,80},{1... | collective-permute-start | bytes 786440 | tf_op jit(solution)/shard_map/ppermute | solution.py:36
  31.9 29.5 %copy-start.22 = (s32[32,1,6]{0,1,2:T(1,128)S(1)}, s32[32,1,6]{0,1,2:T(1,128)}, u32[]{:S(2)}) copy-start(s32[32,1,6]{0,1,2:T(1,128)} %param.17) | copy-start | bytes 2308
  31.9 29.4 %copy-start.23 = (s32[32,1,6]{0,1,2:T(1,128)S(1)}, s32[32,1,6]{0,1,2:T(1,128)}, u32[]{:S(2)}) copy-start(s32[32,1,6]{0,1,2:T(1,128)} %param.18) | copy-start | bytes 2308
  38.5 5.4 %collective-permute-start.3 = (f32[2,64,2,128]{3,1,0,2:T(8,128)S(1)}, f32[2,64,2,128]{3,1,0,2:T(8,128)S(1)}, u32[]{:S(2)}, u32[]{:S(2)}) collective-permute-start(f32[2,64,2,128]{3,1,0,2:T(8,128)S(1)} %dynamic-slice_bitcast_fusion.2), channel_id=1, source_target_pairs={{0,64},{16,80},{32,96},{48,112},{64,0},{80,16},{96,32},{112,48},{1... | collective-permute-start | bytes 393224 | tf_op jit(solution)/shard_map/ppermute | solution.py:36
  43.9 7.2 %collective-permute-start.4 = (bf16[2,64,2,128]{3,1,2,0:T(8,128)(2,1)S(1)}, bf16[2,64,2,128]{3,1,2,0:T(8,128)(2,1)S(1)}, u32[]{:S(2)}, u32[]{:S(2)}) collective-permute-start(bf16[2,64,2,128]{3,1,2,0:T(8,128)(2,1)S(1)} %fusion.76), channel_id=1, source_target_pairs={{0,2},{1,3},{2,0},{3,1},{4,6},{5,7},{6,4},{7,5},{8,10},{9,11},{10,... | collective-permute-start | bytes 196616 | tf_op jit(solution)/shard_map/ppermute | solution.py:47
  51.2 7.1 %collective-permute-start.5 = (bf16[2,2,64,2,128]{4,2,3,1,0:T(8,128)(2,1)S(1)}, bf16[2,2,64,2,128]{4,2,3,1,0:T(8,128)(2,1)S(1)}, u32[]{:S(2)}, u32[]{:S(2)}) collective-permute-start(bf16[2,2,64,2,128]{4,2,3,1,0:T(8,128)(2,1)S(1)} %pad_maximum_fusion.26), channel_id=1, source_target_pairs={{0,1},{1,0},{2,3},{3,2},{4,5},{5,4},{6,7},{7,6},{8,9},{9,8},{10,11... | collective-permute-start | bytes 393224 | tf_op jit(solution)/shard_map/ppermute | solution.py:47
  53.7 13.0 %copy-start.31 = (s32[64]{0:T(128)S(1)}, s32[64]{0:T(128)}, u32[]{:S(2)}) copy-start(s32[64]{0:T(128)} %param.19) | copy-start | bytes 772
  58.3 6.8 %collective-permute-start.6 = (bf16[2,2,2,64,2,128]{5,3,4,2,1,0:T(8,128)(2,1)S(1)}, bf16[2,2,2,64,2,128]{5,3,4,2,1,0:T(8,128)(2,1)S(1)}, u32[]{:S(2)}, u32[]{:S(2)}) collective-permute-start(bf16[2,2,2,64,2,128]{5,3,4,2,1,0:T(8,128)(2,1)S(1)} %pad_maximum_fusion.23), channel_id=1, source_target_pairs={{0,8},{1,9},{2,10},{3,11},{4,12},{5,13},{6,14},{7,15},{8,0},{9,1},... | collective-permute-start | bytes 786440 | tf_op jit(solution)/shard_map/ppermute | solution.py:47
  65.3 11.6 %collective-permute-start.7 = (bf16[2,2,2,2,64,2,128]{6,4,5,3,2,1,0:T(8,128)(2,1)S(1)}, bf16[2,2,2,2,64,2,128]{6,4,5,3,2,1,0:T(8,128)(2,1)S(1)}, u32[]{:S(2)}, u32[]{:S(2)}) collective-permute-start(bf16[2,2,2,2,64,2,128]{6,4,5,3,2,1,0:T(8,128)(2,1)S(1)} %pad_maximum_fusion.20), channel_id=1, source_target_pairs={{0,4},{1,5},{2,6},{3,7},{4,0},{5,1},{6,2},{7,3},{8,12},{9,13},{10,... | collective-permute-start | bytes 1572872 | tf_op jit(solution)/shard_map/ppermute | solution.py:47
  79.6 24.4 %copy-start.15 = (f32[2,64,4,128]{3,1,0,2:T(8,128)}, f32[2,64,4,128]{3,1,0,2:T(8,128)S(1)}, u32[]{:S(2)}) copy-start(f32[2,64,4,128]{3,1,0,2:T(8,128)S(1)} %fusion.30) | copy-start | bytes 786436
  79.6 24.4 %copy-start.2 = (f32[2,2,512,128]{3,2,1,0:T(8,128)S(1)}, f32[2,2,512,128]{3,2,1,0:T(8,128)}, u32[]{:S(2)}) copy-start(f32[2,2,512,128]{3,2,1,0:T(8,128)} %param.11) | copy-start | bytes 3145732
  79.6 7.8 %collective-permute-start.8 = (bf16[4,2,64,128]{3,2,1,0:T(8,128)(2,1)S(1)}, bf16[4,2,64,128]{3,2,1,0:T(8,128)(2,1)S(1)}, u32[]{:S(2)}, u32[]{:S(2)}) collective-permute-start(bf16[4,2,64,128]{3,2,1,0:T(8,128)(2,1)S(1)} %convert_bitcast_fusion), channel_id=1, source_target_pairs={{0,2},{1,3},{2,0},{3,1},{4,6},{5,7},{6,4},{7,5},{8,10},{9,11},{10,... | collective-permute-start | bytes 393224 | tf_op jit(solution)/shard_map/ppermute | solution.py:47
  87.5 15.6 %collective-permute-start.9 = (bf16[2,4,2,64,128]{4,3,2,1,0:T(8,128)(2,1)S(1)}, bf16[2,4,2,64,128]{4,3,2,1,0:T(8,128)(2,1)S(1)}, u32[]{:S(2)}, u32[]{:S(2)}) collective-permute-start(bf16[2,4,2,64,128]{4,3,2,1,0:T(8,128)(2,1)S(1)} %pad_maximum_fusion.24), channel_id=1, source_target_pairs={{0,1},{1,0},{2,3},{3,2},{4,5},{5,4},{6,7},{7,6},{8,9},{9,8},{10,11... | collective-permute-start | bytes 786440 | tf_op jit(solution)/shard_map/ppermute | solution.py:47
  104.0 16.9 %collective-permute-start.10 = (bf16[2,2,4,2,64,128]{5,4,3,2,0,1:T(8,128)(2,1)}, bf16[2,2,4,2,64,128]{5,4,3,2,0,1:T(8,128)(2,1)S(1)}, u32[]{:S(2)}, u32[]{:S(2)}) collective-permute-start(bf16[2,2,4,2,64,128]{5,4,3,2,0,1:T(8,128)(2,1)} %pad_maximum_fusion.21), channel_id=1, source_target_pairs={{0,8},{1,9},{2,10},{3,11},{4,12},{5,13},{6,14},{7,15},{8,0},{9,1},... | collective-permute-start | bytes 1572872 | tf_op jit(solution)/shard_map/ppermute | solution.py:47
  107.6 17.2 %collective-permute-start.16 = (f32[6,512,1]{1,2,0:T(1,128)S(1)}, f32[6,512,1]{1,2,0:T(1,128)S(1)}, u32[]{:S(2)}, u32[]{:S(2)}) collective-permute-start(f32[6,512,1]{1,2,0:T(1,128)S(1)} %copy.94), channel_id=1, source_target_pairs={{0,16},{16,32},{32,48},{48,64},{64,80},{80,96},{96,112},{112,128},... | collective-permute-start | bytes 36872 | tf_op jit(solution)/shard_map/ppermute | solution.py:16
  118.2 7.1 %collective-permute-start.17 = (f32[6,512,1]{1,2,0:T(1,128)}, f32[6,512,1]{1,2,0:T(1,128)}, u32[]{:S(2)}, u32[]{:S(2)}) collective-permute-start(f32[6,512,1]{1,2,0:T(1,128)} %copy.95), channel_id=1, source_target_pairs={{16,0},{32,16},{48,32},{64,48},{80,64},{96,80},{112,96},{128,112},... | collective-permute-start | bytes 36872 | tf_op jit(solution)/shard_map/ppermute | solution.py:19
  120.9 1.9 %copy-start.13 = (bf16[1,2,2,4,2,64,128]{6,5,4,3,1,2,0:T(8,128)(2,1)}, bf16[1,2,2,4,2,64,128]{6,5,4,3,1,2,0:T(8,128)(2,1)S(1)}, u32[]{:S(2)}) copy-start(bf16[1,2,2,4,2,64,128]{6,5,4,3,1,2,0:T(8,128)(2,1)S(1)} %get-tuple-element.30) | copy-start | bytes 1572868
  122.8 24.9 %collective-permute-start.11 = (bf16[2,2,2,4,2,64,128]{6,5,4,3,1,2,0:T(8,128)(2,1)}, bf16[2,2,2,4,2,64,128]{6,5,4,3,1,2,0:T(8,128)(2,1)}, u32[]{:S(2)}, u32[]{:S(2)}) collective-permute-start(bf16[2,2,2,4,2,64,128]{6,5,4,3,1,2,0:T(8,128)(2,1)} %pad_maximum_fusion.18), channel_id=1, source_target_pairs={{0,4},{1,5},{2,6},{3,7},{4,0},{5,1},{6,2},{7,3},{8,12},{9,13},{10,... | collective-permute-start | bytes 3145736 | tf_op jit(solution)/shard_map/ppermute | solution.py:47
  126.5 4.1 %copy-start.30 = (s32[12]{0:T(128)S(1)}, s32[12]{0:T(128)}, u32[]{:S(2)}) copy-start(s32[12]{0:T(128)} %reshape.151) | copy-start | bytes 148
  126.5 4.7 %copy-start.24 = (s32[2,1,6]{0,1,2:T(1,128)S(1)}, s32[2,1,6]{0,1,2:T(1,128)}, u32[]{:S(2)}) copy-start(s32[2,1,6]{0,1,2:T(1,128)} %get-tuple-element.65) | copy-start | bytes 148
  128.0 5.3 %collective-permute-start.18 = (f32[6,1,130]{2,1,0:T(1,128)}, f32[6,1,130]{2,1,0:T(1,128)S(1)}, u32[]{:S(2)}, u32[]{:S(2)}) collective-permute-start(f32[6,1,130]{2,1,0:T(1,128)} %get-tuple-element.16), channel_id=1, source_target_pairs={{0,1},{1,2},{2,3},{3,4},{4,5},{5,6},{6,7},{7,8},{8,9},{9,10},{10,1... | collective-permute-start | bytes 9368 | tf_op jit(solution)/shard_map/ppermute | solution.py:16
  129.3 8.9 %collective-permute-start.19 = (f32[6,1,130]{2,1,0:T(1,128)}, f32[6,1,130]{2,1,0:T(1,128)}, u32[]{:S(2)}, u32[]{:S(2)}) collective-permute-start(f32[6,1,130]{2,1,0:T(1,128)} %get-tuple-element.15), channel_id=1, source_target_pairs={{1,0},{2,1},{3,2},{4,3},{5,4},{6,5},{7,6},{8,7},{9,8},{10,9},{11,1... | collective-permute-start | bytes 9368 | tf_op jit(solution)/shard_map/ppermute | solution.py:19
  138.2 9.4 %copy-start.12 = (bf16[1,2,2,4,2,64,128]{6,5,4,3,1,2,0:T(8,128)(2,1)S(1)}, bf16[1,2,2,4,2,64,128]{6,5,4,3,1,2,0:T(8,128)(2,1)}, u32[]{:S(2)}) copy-start(bf16[1,2,2,4,2,64,128]{6,5,4,3,1,2,0:T(8,128)(2,1)} %copy-done.11) | copy-start | bytes 1572868
  138.2 9.4 %copy-start.14 = (bf16[1,2,2,4,2,64,128]{6,5,4,3,1,2,0:T(8,128)(2,1)S(1)}, bf16[1,2,2,4,2,64,128]{6,5,4,3,1,2,0:T(8,128)(2,1)}, u32[]{:S(2)}) copy-start(bf16[1,2,2,4,2,64,128]{6,5,4,3,1,2,0:T(8,128)(2,1)} %copy-done.13) | copy-start | bytes 1572868
  149.5 1.7 copy-start.19
  149.9 3.3 %copy-start.3 = (f32[2,2,512,128]{3,2,1,0:T(8,128)S(1)}, f32[2,2,512,128]{3,2,1,0:T(8,128)}, u32[]{:S(2)}) copy-start(f32[2,2,512,128]{3,2,1,0:T(8,128)} %param.11) | copy-start | bytes 3145732
  149.9 3.3 %copy-start.5 = (f32[2,512,128]{2,1,0:T(8,128)S(1)}, f32[2,512,128]{2,1,0:T(8,128)}, u32[]{:S(2)}) copy-start(f32[2,512,128]{2,1,0:T(8,128)} %param.10) | copy-start | bytes 1572868
  149.9 3.3 %copy-start.28 = (pred[129]{0:T(512)(128)(4,1)S(1)}, pred[129]{0:T(512)(128)(4,1)}, u32[]{:S(2)}) copy-start(pred[129]{0:T(512)(128)(4,1)} %get-tuple-element.59) | copy-start | bytes 391
  151.5 4.7 %collective-permute-start.12 = (bf16[64,2,2,128]{3,0,1,2:T(8,128)(2,1)S(1)}, bf16[64,2,2,128]{3,0,1,2:T(8,128)(2,1)S(1)}, u32[]{:S(2)}, u32[]{:S(2)}) collective-permute-start(bf16[64,2,2,128]{3,0,1,2:T(8,128)(2,1)S(1)} %fusion.34), channel_id=1, source_target_pairs={{0,64},{16,80},{32,96},{48,112},{64,0},{80,16},{96,32},{112,48},{1... | collective-permute-start | bytes 196616 | tf_op jit(solution)/shard_map/ppermute | solution.py:47
  156.2 3.9 %collective-permute-start.13 = (bf16[2,64,2,2,128]{4,1,2,3,0:T(8,128)(2,1)S(1)}, bf16[2,64,2,2,128]{4,1,2,3,0:T(8,128)(2,1)S(1)}, u32[]{:S(2)}, u32[]{:S(2)}) collective-permute-start(bf16[2,64,2,2,128]{4,1,2,3,0:T(8,128)(2,1)S(1)} %pad_maximum_fusion.27), channel_id=1, source_target_pairs={{0,128},{16,144},{32,160},{48,176},{64,192},{80,208},{96,224},{112... | collective-permute-start | bytes 393224 | tf_op jit(solution)/shard_map/ppermute | solution.py:47
  160.2 5.3 %collective-permute-start.14 = (bf16[2,2,64,2,2,128]{5,2,3,4,1,0:T(8,128)(2,1)S(1)}, bf16[2,2,64,2,2,128]{5,2,3,4,1,0:T(8,128)(2,1)S(1)}, u32[]{:S(2)}, u32[]{:S(2)}) collective-permute-start(bf16[2,2,64,2,2,128]{5,2,3,4,1,0:T(8,128)(2,1)S(1)} %pad_maximum_fusion.25), channel_id=1, source_target_pairs={{0,32},{16,48},{32,0},{48,16},{64,96},{80,112},{96,64},{112,80},{1... | collective-permute-start | bytes 786440 | tf_op jit(solution)/shard_map/ppermute | solution.py:47
  165.6 8.0 %collective-permute-start.15 = (bf16[2,2,2,64,2,2,128]{6,3,4,5,1,0,2:T(8,128)(2,1)S(1)}, bf16[2,2,2,64,2,2,128]{6,3,4,5,1,0,2:T(8,128)(2,1)S(1)}, u32[]{:S(2)}, u32[]{:S(2)}) collective-permute-start(bf16[2,2,2,64,2,2,128]{6,3,4,5,1,0,2:T(8,128)(2,1)S(1)} %pad_maximum_fusion.22), channel_id=1, source_target_pairs={{0,16},{16,0},{32,48},{48,32},{64,80},{80,64},{96,112},{112,96},{1... | collective-permute-start | bytes 1572872 | tf_op jit(solution)/shard_map/ppermute | solution.py:47
  170.2 1.3 copy-start.25
  171.5 1.2 copy-start.16
  173.8 1.6 copy-start.10
  173.8 1.6 copy-start.26
  173.8 1.6 copy-start.27
  173.9 4.1 %copy-start.18 = (bf16[2,2,2,2,64,2,2,128]{7,4,3,2,1,0,6,5:T(8,128)(2,1)}, bf16[2,2,2,2,64,2,2,128]{7,4,3,2,1,0,6,5:T(8,128)(2,1)S(1)}, u32[]{:S(2)}) copy-start(bf16[2,2,2,2,64,2,2,128]{7,4,3,2,1,0,6,5:T(8,128)(2,1)S(1)} %copy.87) | copy-start | bytes 3145732
  176.7 1.4 copy-start.8
  179.5 2.5 %copy-start.6 = (f32[2,512,128]{2,1,0:T(8,128)S(1)}, f32[2,512,128]{2,1,0:T(8,128)}, u32[]{:S(2)}) copy-start(f32[2,512,128]{2,1,0:T(8,128)} %param.10) | copy-start | bytes 1572868
  182.1 2.7 %copy-start.1 = (bf16[8,128,128]{2,1,0:T(8,128)(2,1)S(1)}, bf16[8,128,128]{2,1,0:T(8,128)(2,1)}, u32[]{:S(2)}) copy-start(bf16[8,128,128]{2,1,0:T(8,128)(2,1)} %param.16) | copy-start | bytes 786436
  (4 other events, 3.4 us)

commit v15 on v14

--- a/solution.py
+++ b/solution.py
@@ -103,8 +103,13 @@
     grouped = jnp.einsum(
         "jkq,jpcu->kqpcu", counts, all_proj, preferred_element_type=jnp.float32
     )
-    forward = jnp.einsum(
-        "kqpcu,quv->cpkv", grouped, kernels.astype(jnp.float32), precision=highest
+    grouped_hi = grouped.astype(jnp.bfloat16)
+    rest = grouped - grouped_hi.astype(jnp.float32)
+    grouped_mid = rest.astype(jnp.bfloat16)
+    grouped_lo = (rest - grouped_mid.astype(jnp.float32)).astype(jnp.bfloat16)
+    forward = sum(
+        jnp.einsum("kqpcu,quv->cpkv", piece, kernels, preferred_element_type=jnp.float32)
+        for piece in (grouped_lo, grouped_mid, grouped_hi)
     )
     kern_mine = kernels[phase_mine]
     live = (aperture == 1)[None, :, None, None]

time: 185 us -> 191 us (1.032)
  starting transfers between devices: 42.8 us -> 53 us
  waiting for transfers between devices: 85.7 us -> 75.6 us
  other arithmetic: 20.4 us -> 25 us
    ppermute x12, waiting for transfers between devices: 54.8 us -> 46.4 us  [doubling_gather(): got = lax.ppermute(block, axis, pairs)]
    ppermute x12, starting transfers between devices: 23.6 us -> 29.9 us  [doubling_gather(): got = lax.ppermute(block, axis, pairs)]
    another operation x24, other arithmetic: 4.32 us -> 8.76 us  [doubling_gather(): block = jnp.stack([low, high], axis=place)]
    ppermute x2, starting transfers between devices: 10.9 us -> 14.6 us  [padded_2(): lax.ppermute(lax.slice_in_dim(block, block.shape[dim] - width, None, axis...]
    unnamed x68 -> x71, local copies, waits for them, and re-layouts: 5.67 us -> 7.52 us
  transfers between devices with their start and end apart: 20 -> 20, of which waited for: 15 -> 15; matrix products, arithmetic and copies ran while one was open for 13% -> 12% of each run, Pallas kernels for 0% -> 0%
where the time goes in v15:
time: 191 us; the launch traced here: 190 us
  waiting for transfers between devices  75.6 us (40%)
  starting transfers between devices  53 us (28%)
  other arithmetic  25 us (13%)
  local copies, waits for them, and re-layouts  21.7 us (11%)
  matrix products  13.3 us (7%)
    ppermute x12, waiting for transfers between devices, doubling_gather(): got = lax.ppermute(block, axis, pairs)  46.4 us
    ppermute x12, starting transfers between devices, doubling_gather(): got = lax.ppermute(block, axis, pairs)  29.9 us
    ppermute x4, waiting for transfers between devices, halving_sum(): blocks = keep + lax.ppermute(send, axis, pairs)  25.9 us
    ppermute x2, starting transfers between devices, padded_2(): lax.ppermute(lax.slice_in_dim(block, block.shape[dim] - width, None, axis...  14.6 us
    another operation x24, other arithmetic, doubling_gather(): block = jnp.stack([low, high], axis=place)  8.76 us
    unnamed x71, local copies, waits for them, and re-layouts  7.52 us
    ppermute x4, starting transfers between devices, halving_sum(): blocks = keep + lax.ppermute(send, axis, pairs)  5.1 us
  transfers between devices with their start and end apart: 20, of which 15 were waited for; matrix products, arithmetic and copies ran while one was open for 12% of the time, Pallas kernels for 0%

profile of v15, /device:TPU:1, one launch (start us, length us, event | category | flops | bytes accessed | tf_op | source)
XLA Modules:
  0.0 190.1 jit_solution(4241941914382180600)
XLA Ops:
  0.7 2.7 %fusion.91 = (bf16[1,1024,2,256]{3,2,1,0:T(2,128)(2,1)S(1)}, bf16[1,1024,2,256]{3,2,1,0:T(2,128)(2,1)S(1)}) fusion(bf16[2,1024,2,256]{3,2,1,0:T(2,128)(2,1)} %param.14), kind=kLoop, calls=%fused_computation.202 | loop fusion | bytes 4194304 | tf_op jit(solution)/shard_map/slice | solution.py:75
  4.4 1.4 fusion.39
  8.6 1.3 multiply_subtract_fusion
  11.3 3.2 %collective-permute-start = (f32[2,2,2,2,64,2,128]{6,4,5,3,2,1,0:T(8,128)}, f32[2,2,2,2,64,2,128]{6,4,5,3,2,1,0:T(8,128)S(1)}, u32[]{:S(2)}, u32[]{:S(2)}) collective-permute-start(f32[2,2,2,2,64,2,128]{6,4,5,3,2,1,0:T(8,128)} %bitcast.278), channel_id=1, source_target_pairs={{0,16},{16,0},{32,48},{48,32},{64,80},{80,64},{96,112},{112,96},{1... | collective-permute-start | bytes 3145736 | tf_op jit(solution)/shard_map/ppermute | solution.py:36
  14.5 2.5 %collective-permute-done = f32[2,2,2,2,64,2,128]{6,4,5,3,2,1,0:T(8,128)S(1)} collective-permute-done((f32[2,2,2,2,64,2,128]{6,4,5,3,2,1,0:T(8,128)}, f32[2,2,2,2,64,2,128]{6,4,5,3,2,1,0:T(8,128)S(1)}, u32[]{:S(2)}, u32[]{:S(2)}) %collective-permute-start) | collective-permute-done | bytes 1048608 | tf_op jit(solution)/shard_map/ppermute | solution.py:36
  18.0 1.4 fusion.36
  19.5 13.1 %collective-permute-done.1 = f32[2,2,2,64,2,128]{5,3,4,2,1,0:T(8,128)S(1)} collective-permute-done((f32[2,2,2,64,2,128]{5,3,4,2,1,0:T(8,128)S(1)}, f32[2,2,2,64,2,128]{5,3,4,2,1,0:T(8,128)S(1)}, u32[]{:S(2)}, u32[]{:S(2)}) %collective-permute-start.1) | collective-permute-done | bytes 524320 | tf_op jit(solution)/shard_map/ppermute | solution.py:36
  32.9 6.5 %collective-permute-done.2 = f32[2,2,64,2,128]{4,2,3,1,0:T(8,128)S(1)} collective-permute-done((f32[2,2,64,2,128]{4,2,3,1,0:T(8,128)S(1)}, f32[2,2,64,2,128]{4,2,3,1,0:T(8,128)S(1)}, u32[]{:S(2)}, u32[]{:S(2)}) %collective-permute-start.2) | collective-permute-done | bytes 262176 | tf_op jit(solution)/shard_map/ppermute | solution.py:36
  39.6 1.7 collective-permute-start.3
  41.3 3.7 %collective-permute-done.3 = f32[2,64,2,128]{3,2,0,1:T(2,128)S(1)} collective-permute-done((f32[2,64,2,128]{3,2,0,1:T(2,128)S(1)}, f32[2,64,2,128]{3,2,0,1:T(2,128)S(1)}, u32[]{:S(2)}, u32[]{:S(2)}) %collective-permute-start.3) | collective-permute-done | bytes 131104 | tf_op jit(solution)/shard_map/ppermute | solution.py:36
  45.2 5.3 %collective-permute-start.4 = (bf16[2,64,2,128]{3,0,2,1:T(2,128)(2,1)S(1)}, bf16[2,64,2,128]{3,0,2,1:T(2,128)(2,1)S(1)}, u32[]{:S(2)}, u32[]{:S(2)}) collective-permute-start(bf16[2,64,2,128]{3,0,2,1:T(2,128)(2,1)S(1)} %fusion.76), channel_id=1, source_target_pairs={{0,2},{1,3},{2,0},{3,1},{4,6},{5,7},{6,4},{7,5},{8,10},{9,11},{10,... | collective-permute-start | bytes 196616 | tf_op jit(solution)/shard_map/ppermute | solution.py:47
  50.4 2.0 %collective-permute-done.4 = bf16[2,64,2,128]{3,0,2,1:T(2,128)(2,1)S(1)} collective-permute-done((bf16[2,64,2,128]{3,0,2,1:T(2,128)(2,1)S(1)}, bf16[2,64,2,128]{3,0,2,1:T(2,128)(2,1)S(1)}, u32[]{:S(2)}, u32[]{:S(2)}) %collective-permute-start.4) | collective-permute-done | bytes 65568 | tf_op jit(solution)/shard_map/ppermute | solution.py:47
  52.7 2.5 %collective-permute-start.5 = (bf16[2,2,64,2,128]{4,1,0,3,2:T(2,128)(2,1)S(1)}, bf16[2,2,64,2,128]{4,1,0,3,2:T(2,128)(2,1)S(1)}, u32[]{:S(2)}, u32[]{:S(2)}) collective-permute-start(bf16[2,2,64,2,128]{4,1,0,3,2:T(2,128)(2,1)S(1)} %pad_maximum_fusion.26), channel_id=1, source_target_pairs={{0,1},{1,0},{2,3},{3,2},{4,5},{5,4},{6,7},{7,6},{8,9},{9,8},{10,11... | collective-permute-start | bytes 393224 | tf_op jit(solution)/shard_map/ppermute | solution.py:47
  55.2 4.5 %collective-permute-done.5 = bf16[2,2,64,2,128]{4,1,0,3,2:T(2,128)(2,1)S(1)} collective-permute-done((bf16[2,2,64,2,128]{4,1,0,3,2:T(2,128)(2,1)S(1)}, bf16[2,2,64,2,128]{4,1,0,3,2:T(2,128)(2,1)S(1)}, u32[]{:S(2)}, u32[]{:S(2)}) %collective-permute-start.5) | collective-permute-done | bytes 131104 | tf_op jit(solution)/shard_map/ppermute | solution.py:47
  60.4 3.1 %collective-permute-start.6 = (bf16[2,2,2,64,2,128]{5,2,1,0,4,3:T(2,128)(2,1)S(1)}, bf16[2,2,2,64,2,128]{5,2,1,0,4,3:T(2,128)(2,1)S(1)}, u32[]{:S(2)}, u32[]{:S(2)}) collective-permute-start(bf16[2,2,2,64,2,128]{5,2,1,0,4,3:T(2,128)(2,1)S(1)} %pad_maximum_fusion.23), channel_id=1, source_target_pairs={{0,8},{1,9},{2,10},{3,11},{4,12},{5,13},{6,14},{7,15},{8,0},{9,1},... | collective-permute-start | bytes 786440 | tf_op jit(solution)/shard_map/ppermute | solution.py:47
  63.5 3.7 %collective-permute-done.6 = bf16[2,2,2,64,2,128]{5,2,1,0,4,3:T(2,128)(2,1)S(1)} collective-permute-done((bf16[2,2,2,64,2,128]{5,2,1,0,4,3:T(2,128)(2,1)S(1)}, bf16[2,2,2,64,2,128]{5,2,1,0,4,3:T(2,128)(2,1)S(1)}, u32[]{:S(2)}, u32[]{:S(2)}) %collective-permute-start.6) | collective-permute-done | bytes 262176 | tf_op jit(solution)/shard_map/ppermute | solution.py:47
  68.5 1.6 collective-permute-start.7
  70.3 8.8 %collective-permute-done.7 = bf16[2,2,2,2,64,2,128]{6,3,2,1,0,5,4:T(2,128)(2,1)S(1)} collective-permute-done((bf16[2,2,2,2,64,2,128]{6,3,2,1,0,5,4:T(2,128)(2,1)S(1)}, bf16[2,2,2,2,64,2,128]{6,3,2,1,0,5,4:T(2,128)(2,1)S(1)}, u32[]{:S(2)}, u32[]{:S(2)}) %collective-permute-start.7) | collective-permute-done | bytes 524320 | tf_op jit(solution)/shard_map/ppermute | solution.py:47
  80.2 1.4 pad_maximum_fusion.17
  83.6 5.0 %collective-permute-start.8 = (bf16[4,2,64,128]{3,2,1,0:T(8,128)(2,1)S(1)}, bf16[4,2,64,128]{3,2,1,0:T(8,128)(2,1)S(1)}, u32[]{:S(2)}, u32[]{:S(2)}) collective-permute-start(bf16[4,2,64,128]{3,2,1,0:T(8,128)(2,1)S(1)} %convert_bitcast_fusion), channel_id=1, source_target_pairs={{0,2},{1,3},{2,0},{3,1},{4,6},{5,7},{6,4},{7,5},{8,10},{9,11},{10,... | collective-permute-start | bytes 393224 | tf_op jit(solution)/shard_map/ppermute | solution.py:47
  88.7 2.8 %collective-permute-done.8 = bf16[4,2,64,128]{3,2,1,0:T(8,128)(2,1)S(1)} collective-permute-done((bf16[4,2,64,128]{3,2,1,0:T(8,128)(2,1)S(1)}, bf16[4,2,64,128]{3,2,1,0:T(8,128)(2,1)S(1)}, u32[]{:S(2)}, u32[]{:S(2)}) %collective-permute-start.8) | collective-permute-done | bytes 131104 | tf_op jit(solution)/shard_map/ppermute | solution.py:47
  92.1 11.3 %collective-permute-done.9 = bf16[2,4,2,64,128]{4,3,2,1,0:T(8,128)(2,1)S(1)} collective-permute-done((bf16[2,4,2,64,128]{4,3,2,1,0:T(8,128)(2,1)S(1)}, bf16[2,4,2,64,128]{4,3,2,1,0:T(8,128)(2,1)S(1)}, u32[]{:S(2)}, u32[]{:S(2)}) %collective-permute-start.9) | collective-permute-done | bytes 262176 | tf_op jit(solution)/shard_map/ppermute | solution.py:47
  104.2 1.5 collective-permute-start.10
  105.8 1.7 slice_maximum_fusion
  107.5 1.9 copy.118
  109.3 13.4 %collective-permute-start.16 = (f32[6,512,1]{1,2,0:T(1,128)S(1)}, f32[6,512,1]{1,2,0:T(1,128)S(1)}, u32[]{:S(2)}, u32[]{:S(2)}) collective-permute-start(f32[6,512,1]{1,2,0:T(1,128)S(1)} %copy.118), channel_id=1, source_target_pairs={{0,16},{16,32},{32,48},{48,64},{64,80},{80,96},{96,112},{112,128},... | collective-permute-start | bytes 36872 | tf_op jit(solution)/shard_map/ppermute | solution.py:16
  123.8 1.9 %collective-permute-start.17 = (f32[6,512,1]{1,2,0:T(1,128)}, f32[6,512,1]{1,2,0:T(1,128)}, u32[]{:S(2)}, u32[]{:S(2)}) collective-permute-start(f32[6,512,1]{1,2,0:T(1,128)} %copy.119), channel_id=1, source_target_pairs={{16,0},{32,16},{48,32},{64,48},{80,64},{96,80},{112,96},{128,112},... | collective-permute-start | bytes 36872 | tf_op jit(solution)/shard_map/ppermute | solution.py:19
  132.0 1.5 pad_maximum_fusion.28
  133.5 1.3 collective-permute-start.18
  134.8 1.5 collective-permute-start.19
  137.6 1.5 gather_fusion
  139.0 3.3 %collective-permute-done.19 = f32[6,1,130]{2,1,0:T(1,128)} collective-permute-done((f32[6,1,130]{2,1,0:T(1,128)}, f32[6,1,130]{2,1,0:T(1,128)}, u32[]{:S(2)}, u32[]{:S(2)}) %collective-permute-start.19) | collective-permute-done | bytes 3152 | tf_op jit(solution)/shard_map/ppermute | solution.py:19
  142.3 2.2 %fusion.31 = f32[1,2,513,129]{3,2,1,0:T(8,128)S(1)} fusion(f32[6,1,130]{2,1,0:T(1,128)} %collective-permute-done.19, f32[6,512,1]{2,1,0:T(8,128)S(1)} %copy.121, f32[6,512,1]{2,1,0:T(8,128)S(1)} %copy.120, f32[4,512,128]{2,1,0:T(8,128)} %bitcast.283, f32[2,512,128]{2,1,0:T(8,128)} %param.10, f32[6,1,130]{2,1,0:T(1,128)S(1)} %collective-permute-done.18, ...), kind=kLoop, calls=%fused_computation.63 | loop fusion | flops 1323540 | bytes 2133609 | tf_op jit(solution)/shard_map/stack | solution.py:165
  144.6 7.0 %collective-permute-done.11 = bf16[2,2,2,4,2,64,128]{6,5,4,3,1,2,0:T(8,128)(2,1)} collective-permute-done((bf16[2,2,2,4,2,64,128]{6,5,4,3,1,2,0:T(8,128)(2,1)}, bf16[2,2,2,4,2,64,128]{6,5,4,3,1,2,0:T(8,128)(2,1)}, u32[]{:S(2)}, u32[]{:S(2)}) %collective-permute-start.11) | collective-permute-done | bytes 1048608 | tf_op jit(solution)/shard_map/ppermute | solution.py:47
  151.6 1.4 select_bitcast_fusion.1
  155.4 3.4 %collective-permute-start.12 = (bf16[64,2,2,128]{3,0,1,2:T(8,128)(2,1)S(1)}, bf16[64,2,2,128]{3,0,1,2:T(8,128)(2,1)S(1)}, u32[]{:S(2)}, u32[]{:S(2)}) collective-permute-start(bf16[64,2,2,128]{3,0,1,2:T(8,128)(2,1)S(1)} %fusion.23), channel_id=1, source_target_pairs={{0,64},{16,80},{32,96},{48,112},{64,0},{80,16},{96,32},{112,48},{1... | collective-permute-start | bytes 196616 | tf_op jit(solution)/shard_map/ppermute | solution.py:47
  160.6 1.6 pad_maximum_fusion
  162.2 2.2 %collective-permute-done.13 = bf16[2,64,2,2,128]{4,1,2,3,0:T(8,128)(2,1)S(1)} collective-permute-done((bf16[2,64,2,2,128]{4,1,2,3,0:T(8,128)(2,1)S(1)}, bf16[2,64,2,2,128]{4,1,2,3,0:T(8,128)(2,1)S(1)}, u32[]{:S(2)}, u32[]{:S(2)}) %collective-permute-start.13) | collective-permute-done | bytes 131104 | tf_op jit(solution)/shard_map/ppermute | solution.py:47
  164.5 2.0 %collective-permute-start.14 = (bf16[2,2,64,2,2,128]{5,2,3,4,1,0:T(8,128)(2,1)S(1)}, bf16[2,2,64,2,2,128]{5,2,3,4,1,0:T(8,128)(2,1)S(1)}, u32[]{:S(2)}, u32[]{:S(2)}) collective-permute-start(bf16[2,2,64,2,2,128]{5,2,3,4,1,0:T(8,128)(2,1)S(1)} %pad_maximum_fusion.25), channel_id=1, source_target_pairs={{0,32},{16,48},{32,0},{48,16},{64,96},{80,112},{96,64},{112,80},{1... | collective-permute-start | bytes 786440 | tf_op jit(solution)/shard_map/ppermute | solution.py:47
  167.1 3.2 %collective-permute-done.14 = bf16[2,2,64,2,2,128]{5,2,3,4,1,0:T(8,128)(2,1)S(1)} collective-permute-done((bf16[2,2,64,2,2,128]{5,2,3,4,1,0:T(8,128)(2,1)S(1)}, bf16[2,2,64,2,2,128]{5,2,3,4,1,0:T(8,128)(2,1)S(1)}, u32[]{:S(2)}, u32[]{:S(2)}) %collective-permute-start.14) | collective-permute-done | bytes 262176 | tf_op jit(solution)/shard_map/ppermute | solution.py:47
  170.4 4.8 %collective-permute-start.15 = (bf16[2,2,2,64,2,2,128]{6,3,4,5,1,0,2:T(8,128)(2,1)S(1)}, bf16[2,2,2,64,2,2,128]{6,3,4,5,1,0,2:T(8,128)(2,1)S(1)}, u32[]{:S(2)}, u32[]{:S(2)}) collective-permute-start(bf16[2,2,2,64,2,2,128]{6,3,4,5,1,0,2:T(8,128)(2,1)S(1)} %pad_maximum_fusion.22), channel_id=1, source_target_pairs={{0,16},{16,0},{32,48},{48,32},{64,80},{80,64},{96,112},{112,96},{1... | collective-permute-start | bytes 1572872 | tf_op jit(solution)/shard_map/ppermute | solution.py:47
  175.5 1.3 slice.126
  179.3 1.5 copy-done.10
  180.7 1.3 fusion.45
  182.1 1.3 fusion.47
  183.4 1.3 fusion.12
  184.9 2.4 %fusion.13 = f32[2,256,128]{1,2,0:T(8,128)S(1)} fusion(f32[2,128,256]{2,1,0:T(8,128)S(1)} %fusion.47, bf16[1,1024,2,256]{3,2,1,0:T(2,128)(2,1)S(1)} %copy-done.8, f32[2,1024]{1,0:T(2,128)S(1)} %copy-done.25, f32[2,1024]{1,0:T(2,128)S(1)} %copy-done.26, bf16[2,2,1024,128]{3,2,1,0:T(8,128)(2,1)} %bitcast.303), kind=kOutput, calls=%fused_computation.36 | convolution fusion | flops 135856128 | bytes 2637824 | tf_op jit(solution)/shard_map/pjh,jpu->jhu/dot_general | solution.py:147
  187.4 2.7 %fusion.64 = f32[2,512,128]{2,1,0:T(8,128)} fusion(f32[2,512,128]{2,1,0:T(8,128)S(1)} %copy-done.6, f32[2,513,129]{2,1,0:T(8,128)} %get-tuple-element.18, f32[2,513,129]{2,1,0:T(8,128)S(1)} %get-tuple-element.17, f32[1,512,128]{2,1,0:T(8,128)S(1)} %bitcast.299, f32[1,512,128]{2,1,0:T(8,128)S(1)} %bitcast.298), kind=kLoop, calls=%fused_computation.112 | loop fusion | flops 917504 | bytes 3670016 | tf_op jit(solution)/shard_map/sub | solution.py:177
  (150 shorter events, 30.2 us)
Async XLA Ops:
  0.6 81.5 %copy-start = (bf16[8,128,128]{2,1,0:T(8,128)(2,1)S(1)}, bf16[8,128,128]{2,1,0:T(8,128)(2,1)}, u32[]{:S(2)}) copy-start(bf16[8,128,128]{2,1,0:T(8,128)(2,1)} %param.16) | copy-start | bytes 786436
  0.7 2.8 %copy-start.4 = (f32[2,512,128]{2,1,0:T(8,128)S(1)}, f32[2,512,128]{2,1,0:T(8,128)}, u32[]{:S(2)}) copy-start(f32[2,512,128]{2,1,0:T(8,128)} %param.10) | copy-start | bytes 1572868
  3.4 1.0 copy-start.9
  3.5 4.3 %copy-start.7 = (bf16[1,1024,2,256]{3,2,1,0:T(2,128)(2,1)}, bf16[1,1024,2,256]{3,2,1,0:T(2,128)(2,1)S(1)}, u32[]{:S(2)}) copy-start(bf16[1,1024,2,256]{3,2,1,0:T(2,128)(2,1)S(1)} %get-tuple-element.28) | copy-start | bytes 3145732
  7.3 1.2 copy-start.15
  11.3 5.7 %collective-permute-start = (f32[2,2,2,2,64,2,128]{6,4,5,3,2,1,0:T(8,128)}, f32[2,2,2,2,64,2,128]{6,4,5,3,2,1,0:T(8,128)S(1)}, u32[]{:S(2)}, u32[]{:S(2)}) collective-permute-start(f32[2,2,2,2,64,2,128]{6,4,5,3,2,1,0:T(8,128)} %bitcast.278), channel_id=1, source_target_pairs={{0,16},{16,0},{32,48},{48,32},{64,80},{80,64},{96,112},{112,96},{1... | collective-permute-start | bytes 3145736 | tf_op jit(solution)/shard_map/ppermute | solution.py:36
  19.4 13.2 %collective-permute-start.1 = (f32[2,2,2,64,2,128]{5,3,4,2,1,0:T(8,128)S(1)}, f32[2,2,2,64,2,128]{5,3,4,2,1,0:T(8,128)S(1)}, u32[]{:S(2)}, u32[]{:S(2)}) collective-permute-start(f32[2,2,2,64,2,128]{5,3,4,2,1,0:T(8,128)S(1)} %dynamic-slice_bitcast_fusion), channel_id=1, source_target_pairs={{0,128},{16,144},{32,160},{48,176},{64,192},{80,208},{96,224},{112... | collective-permute-start | bytes 1572872 | tf_op jit(solution)/shard_map/ppermute | solution.py:36
  32.7 6.7 %collective-permute-start.2 = (f32[2,2,64,2,128]{4,2,3,1,0:T(8,128)S(1)}, f32[2,2,64,2,128]{4,2,3,1,0:T(8,128)S(1)}, u32[]{:S(2)}, u32[]{:S(2)}) collective-permute-start(f32[2,2,64,2,128]{4,2,3,1,0:T(8,128)S(1)} %dynamic-slice_bitcast_fusion.1), channel_id=1, source_target_pairs={{0,32},{16,48},{32,0},{48,16},{64,96},{80,112},{96,64},{112,80},{1... | collective-permute-start | bytes 786440 | tf_op jit(solution)/shard_map/ppermute | solution.py:36
  39.5 24.0 %copy-start.21 = (s32[32,1,6]{0,1,2:T(1,128)S(1)}, s32[32,1,6]{0,1,2:T(1,128)}, u32[]{:S(2)}) copy-start(s32[32,1,6]{0,1,2:T(1,128)} %param.17) | copy-start | bytes 2308
  39.5 24.0 %copy-start.22 = (s32[32,1,6]{0,1,2:T(1,128)S(1)}, s32[32,1,6]{0,1,2:T(1,128)}, u32[]{:S(2)}) copy-start(s32[32,1,6]{0,1,2:T(1,128)} %param.18) | copy-start | bytes 2308
  39.6 5.4 %collective-permute-start.3 = (f32[2,64,2,128]{3,2,0,1:T(2,128)S(1)}, f32[2,64,2,128]{3,2,0,1:T(2,128)S(1)}, u32[]{:S(2)}, u32[]{:S(2)}) collective-permute-start(f32[2,64,2,128]{3,2,0,1:T(2,128)S(1)} %bitcast.305), channel_id=1, source_target_pairs={{0,64},{16,80},{32,96},{48,112},{64,0},{80,16},{96,32},{112,48},{1... | collective-permute-start | bytes 393224 | tf_op jit(solution)/shard_map/ppermute | solution.py:36
  45.2 7.2 %collective-permute-start.4 = (bf16[2,64,2,128]{3,0,2,1:T(2,128)(2,1)S(1)}, bf16[2,64,2,128]{3,0,2,1:T(2,128)(2,1)S(1)}, u32[]{:S(2)}, u32[]{:S(2)}) collective-permute-start(bf16[2,64,2,128]{3,0,2,1:T(2,128)(2,1)S(1)} %fusion.76), channel_id=1, source_target_pairs={{0,2},{1,3},{2,0},{3,1},{4,6},{5,7},{6,4},{7,5},{8,10},{9,11},{10,... | collective-permute-start | bytes 196616 | tf_op jit(solution)/shard_map/ppermute | solution.py:47
  52.7 7.0 %collective-permute-start.5 = (bf16[2,2,64,2,128]{4,1,0,3,2:T(2,128)(2,1)S(1)}, bf16[2,2,64,2,128]{4,1,0,3,2:T(2,128)(2,1)S(1)}, u32[]{:S(2)}, u32[]{:S(2)}) collective-permute-start(bf16[2,2,64,2,128]{4,1,0,3,2:T(2,128)(2,1)S(1)} %pad_maximum_fusion.26), channel_id=1, source_target_pairs={{0,1},{1,0},{2,3},{3,2},{4,5},{5,4},{6,7},{7,6},{8,9},{9,8},{10,11... | collective-permute-start | bytes 393224 | tf_op jit(solution)/shard_map/ppermute | solution.py:47
  55.2 15.0 %copy-start.32 = (s32[64]{0:T(128)S(1)}, s32[64]{0:T(128)}, u32[]{:S(2)}) copy-start(s32[64]{0:T(128)} %param.19) | copy-start | bytes 772
  60.4 6.8 %collective-permute-start.6 = (bf16[2,2,2,64,2,128]{5,2,1,0,4,3:T(2,128)(2,1)S(1)}, bf16[2,2,2,64,2,128]{5,2,1,0,4,3:T(2,128)(2,1)S(1)}, u32[]{:S(2)}, u32[]{:S(2)}) collective-permute-start(bf16[2,2,2,64,2,128]{5,2,1,0,4,3:T(2,128)(2,1)S(1)} %pad_maximum_fusion.23), channel_id=1, source_target_pairs={{0,8},{1,9},{2,10},{3,11},{4,12},{5,13},{6,14},{7,15},{8,0},{9,1},... | collective-permute-start | bytes 786440 | tf_op jit(solution)/shard_map/ppermute | solution.py:47
  68.5 10.5 %collective-permute-start.7 = (bf16[2,2,2,2,64,2,128]{6,3,2,1,0,5,4:T(2,128)(2,1)S(1)}, bf16[2,2,2,2,64,2,128]{6,3,2,1,0,5,4:T(2,128)(2,1)S(1)}, u32[]{:S(2)}, u32[]{:S(2)}) collective-permute-start(bf16[2,2,2,2,64,2,128]{6,3,2,1,0,5,4:T(2,128)(2,1)S(1)} %pad_maximum_fusion.20), channel_id=1, source_target_pairs={{0,4},{1,5},{2,6},{3,7},{4,0},{5,1},{6,2},{7,3},{8,12},{9,13},{10,... | collective-permute-start | bytes 1572872 | tf_op jit(solution)/shard_map/ppermute | solution.py:47
  83.6 20.6 %copy-start.16 = (f32[2,64,4,128]{3,1,0,2:T(8,128)}, f32[2,64,4,128]{3,1,0,2:T(8,128)S(1)}, u32[]{:S(2)}) copy-start(f32[2,64,4,128]{3,1,0,2:T(8,128)S(1)} %fusion.21) | copy-start | bytes 786436
  83.6 22.1 %copy-start.2 = (f32[2,2,512,128]{3,2,1,0:T(8,128)S(1)}, f32[2,2,512,128]{3,2,1,0:T(8,128)}, u32[]{:S(2)}) copy-start(f32[2,2,512,128]{3,2,1,0:T(8,128)} %param.11) | copy-start | bytes 3145732
  83.6 7.8 %collective-permute-start.8 = (bf16[4,2,64,128]{3,2,1,0:T(8,128)(2,1)S(1)}, bf16[4,2,64,128]{3,2,1,0:T(8,128)(2,1)S(1)}, u32[]{:S(2)}, u32[]{:S(2)}) collective-permute-start(bf16[4,2,64,128]{3,2,1,0:T(8,128)(2,1)S(1)} %convert_bitcast_fusion), channel_id=1, source_target_pairs={{0,2},{1,3},{2,0},{3,1},{4,6},{5,7},{6,4},{7,5},{8,10},{9,11},{10,... | collective-permute-start | bytes 393224 | tf_op jit(solution)/shard_map/ppermute | solution.py:47
  91.5 11.8 %collective-permute-start.9 = (bf16[2,4,2,64,128]{4,3,2,1,0:T(8,128)(2,1)S(1)}, bf16[2,4,2,64,128]{4,3,2,1,0:T(8,128)(2,1)S(1)}, u32[]{:S(2)}, u32[]{:S(2)}) collective-permute-start(bf16[2,4,2,64,128]{4,3,2,1,0:T(8,128)(2,1)S(1)} %pad_maximum_fusion.24), channel_id=1, source_target_pairs={{0,1},{1,0},{2,3},{3,2},{4,5},{5,4},{6,7},{7,6},{8,9},{9,8},{10,11... | collective-permute-start | bytes 786440 | tf_op jit(solution)/shard_map/ppermute | solution.py:47
  104.2 22.1 %collective-permute-start.10 = (bf16[2,2,4,2,64,128]{5,4,3,2,0,1:T(8,128)(2,1)}, bf16[2,2,4,2,64,128]{5,4,3,2,0,1:T(8,128)(2,1)S(1)}, u32[]{:S(2)}, u32[]{:S(2)}) collective-permute-start(bf16[2,2,4,2,64,128]{5,4,3,2,0,1:T(8,128)(2,1)} %pad_maximum_fusion.21), channel_id=1, source_target_pairs={{0,8},{1,9},{2,10},{3,11},{4,12},{5,13},{6,14},{7,15},{8,0},{9,1},... | collective-permute-start | bytes 1572872 | tf_op jit(solution)/shard_map/ppermute | solution.py:47
  109.3 20.9 %collective-permute-start.16 = (f32[6,512,1]{1,2,0:T(1,128)S(1)}, f32[6,512,1]{1,2,0:T(1,128)S(1)}, u32[]{:S(2)}, u32[]{:S(2)}) collective-permute-start(f32[6,512,1]{1,2,0:T(1,128)S(1)} %copy.118), channel_id=1, source_target_pairs={{0,16},{16,32},{32,48},{48,64},{64,80},{80,96},{96,112},{112,128},... | collective-permute-start | bytes 36872 | tf_op jit(solution)/shard_map/ppermute | solution.py:16
  123.8 7.0 %collective-permute-start.17 = (f32[6,512,1]{1,2,0:T(1,128)}, f32[6,512,1]{1,2,0:T(1,128)}, u32[]{:S(2)}, u32[]{:S(2)}) collective-permute-start(f32[6,512,1]{1,2,0:T(1,128)} %copy.119), channel_id=1, source_target_pairs={{16,0},{32,16},{48,32},{64,48},{80,64},{96,80},{112,96},{128,112},... | collective-permute-start | bytes 36872 | tf_op jit(solution)/shard_map/ppermute | solution.py:19
  126.5 1.8 copy-start.13
  128.3 23.3 %collective-permute-start.11 = (bf16[2,2,2,4,2,64,128]{6,5,4,3,1,2,0:T(8,128)(2,1)}, bf16[2,2,2,4,2,64,128]{6,5,4,3,1,2,0:T(8,128)(2,1)}, u32[]{:S(2)}, u32[]{:S(2)}) collective-permute-start(bf16[2,2,2,4,2,64,128]{6,5,4,3,1,2,0:T(8,128)(2,1)} %pad_maximum_fusion.18), channel_id=1, source_target_pairs={{0,4},{1,5},{2,6},{3,7},{4,0},{5,1},{6,2},{7,3},{8,12},{9,13},{10,... | collective-permute-start | bytes 3145736 | tf_op jit(solution)/shard_map/ppermute | solution.py:47
  132.0 4.3 %copy-start.29 = (s32[12]{0:T(128)S(1)}, s32[12]{0:T(128)}, u32[]{:S(2)}) copy-start(s32[12]{0:T(128)} %reshape.151) | copy-start | bytes 148
  132.0 4.9 %copy-start.23 = (s32[2,1,6]{0,1,2:T(1,128)S(1)}, s32[2,1,6]{0,1,2:T(1,128)}, u32[]{:S(2)}) copy-start(s32[2,1,6]{0,1,2:T(1,128)} %get-tuple-element.71) | copy-start | bytes 148
  133.5 5.5 %collective-permute-start.18 = (f32[6,1,130]{2,1,0:T(1,128)}, f32[6,1,130]{2,1,0:T(1,128)S(1)}, u32[]{:S(2)}, u32[]{:S(2)}) collective-permute-start(f32[6,1,130]{2,1,0:T(1,128)} %get-tuple-element.16), channel_id=1, source_target_pairs={{0,1},{1,2},{2,3},{3,4},{4,5},{5,6},{6,7},{7,8},{8,9},{9,10},{10,1... | collective-permute-start | bytes 9368 | tf_op jit(solution)/shard_map/ppermute | solution.py:16
  134.8 7.6 %collective-permute-start.19 = (f32[6,1,130]{2,1,0:T(1,128)}, f32[6,1,130]{2,1,0:T(1,128)}, u32[]{:S(2)}, u32[]{:S(2)}) collective-permute-start(f32[6,1,130]{2,1,0:T(1,128)} %get-tuple-element.15), channel_id=1, source_target_pairs={{1,0},{2,1},{3,2},{4,3},{5,4},{6,5},{7,6},{8,7},{9,8},{10,9},{11,1... | collective-permute-start | bytes 9368 | tf_op jit(solution)/shard_map/ppermute | solution.py:19
  142.3 9.3 %copy-start.12 = (bf16[1,2,2,4,2,64,128]{6,5,4,3,1,2,0:T(8,128)(2,1)S(1)}, bf16[1,2,2,4,2,64,128]{6,5,4,3,1,2,0:T(8,128)(2,1)}, u32[]{:S(2)}) copy-start(bf16[1,2,2,4,2,64,128]{6,5,4,3,1,2,0:T(8,128)(2,1)} %copy-done.11) | copy-start | bytes 1572868
  142.3 9.3 %copy-start.14 = (bf16[1,2,2,4,2,64,128]{6,5,4,3,1,2,0:T(8,128)(2,1)S(1)}, bf16[1,2,2,4,2,64,128]{6,5,4,3,1,2,0:T(8,128)(2,1)}, u32[]{:S(2)}) copy-start(bf16[1,2,2,4,2,64,128]{6,5,4,3,1,2,0:T(8,128)(2,1)} %copy-done.13) | copy-start | bytes 1572868
  153.5 1.6 copy-start.20
  153.9 5.0 %copy-start.3 = (f32[2,2,512,128]{3,2,1,0:T(8,128)S(1)}, f32[2,2,512,128]{3,2,1,0:T(8,128)}, u32[]{:S(2)}) copy-start(f32[2,2,512,128]{3,2,1,0:T(8,128)} %param.11) | copy-start | bytes 3145732
  153.9 5.0 %copy-start.5 = (f32[2,512,128]{2,1,0:T(8,128)S(1)}, f32[2,512,128]{2,1,0:T(8,128)}, u32[]{:S(2)}) copy-start(f32[2,512,128]{2,1,0:T(8,128)} %param.10) | copy-start | bytes 1572868
  153.9 5.0 %copy-start.27 = (pred[129]{0:T(512)(128)(4,1)S(1)}, pred[129]{0:T(512)(128)(4,1)}, u32[]{:S(2)}) copy-start(pred[129]{0:T(512)(128)(4,1)} %get-tuple-element.67) | copy-start | bytes 391
  155.4 5.1 %collective-permute-start.12 = (bf16[64,2,2,128]{3,0,1,2:T(8,128)(2,1)S(1)}, bf16[64,2,2,128]{3,0,1,2:T(8,128)(2,1)S(1)}, u32[]{:S(2)}, u32[]{:S(2)}) collective-permute-start(bf16[64,2,2,128]{3,0,1,2:T(8,128)(2,1)S(1)} %fusion.23), channel_id=1, source_target_pairs={{0,64},{16,80},{32,96},{48,112},{64,0},{80,16},{96,32},{112,48},{1... | collective-permute-start | bytes 196616 | tf_op jit(solution)/shard_map/ppermute | solution.py:47
  160.5 3.9 %collective-permute-start.13 = (bf16[2,64,2,2,128]{4,1,2,3,0:T(8,128)(2,1)S(1)}, bf16[2,64,2,2,128]{4,1,2,3,0:T(8,128)(2,1)S(1)}, u32[]{:S(2)}, u32[]{:S(2)}) collective-permute-start(bf16[2,64,2,2,128]{4,1,2,3,0:T(8,128)(2,1)S(1)} %pad_maximum_fusion.27), channel_id=1, source_target_pairs={{0,128},{16,144},{32,160},{48,176},{64,192},{80,208},{96,224},{112... | collective-permute-start | bytes 393224 | tf_op jit(solution)/shard_map/ppermute | solution.py:47
  164.5 5.8 %collective-permute-start.14 = (bf16[2,2,64,2,2,128]{5,2,3,4,1,0:T(8,128)(2,1)S(1)}, bf16[2,2,64,2,2,128]{5,2,3,4,1,0:T(8,128)(2,1)S(1)}, u32[]{:S(2)}, u32[]{:S(2)}) collective-permute-start(bf16[2,2,64,2,2,128]{5,2,3,4,1,0:T(8,128)(2,1)S(1)} %pad_maximum_fusion.25), channel_id=1, source_target_pairs={{0,32},{16,48},{32,0},{48,16},{64,96},{80,112},{96,64},{112,80},{1... | collective-permute-start | bytes 786440 | tf_op jit(solution)/shard_map/ppermute | solution.py:47
  170.4 8.6 %collective-permute-start.15 = (bf16[2,2,2,64,2,2,128]{6,3,4,5,1,0,2:T(8,128)(2,1)S(1)}, bf16[2,2,2,64,2,2,128]{6,3,4,5,1,0,2:T(8,128)(2,1)S(1)}, u32[]{:S(2)}, u32[]{:S(2)}) collective-permute-start(bf16[2,2,2,64,2,2,128]{6,3,4,5,1,0,2:T(8,128)(2,1)S(1)} %pad_maximum_fusion.22), channel_id=1, source_target_pairs={{0,16},{16,0},{32,48},{48,32},{64,80},{80,64},{96,112},{112,96},{1... | collective-permute-start | bytes 1572872 | tf_op jit(solution)/shard_map/ppermute | solution.py:47
  175.5 1.3 copy-start.24
  176.8 1.2 copy-start.17
  179.1 1.6 copy-start.10
  179.1 1.6 copy-start.25
  179.1 1.6 copy-start.26
  179.2 4.1 %copy-start.19 = (bf16[2,2,2,2,64,2,2,128]{7,4,3,2,1,0,6,5:T(8,128)(2,1)}, bf16[2,2,2,2,64,2,2,128]{7,4,3,2,1,0,6,5:T(8,128)(2,1)S(1)}, u32[]{:S(2)}) copy-start(bf16[2,2,2,2,64,2,2,128]{7,4,3,2,1,0,6,5:T(8,128)(2,1)S(1)} %copy.111) | copy-start | bytes 3145732
  182.0 1.4 copy-start.8
  184.9 2.5 %copy-start.6 = (f32[2,512,128]{2,1,0:T(8,128)S(1)}, f32[2,512,128]{2,1,0:T(8,128)}, u32[]{:S(2)}) copy-start(f32[2,512,128]{2,1,0:T(8,128)} %param.10) | copy-start | bytes 1572868
  187.4 2.7 %copy-start.1 = (bf16[8,128,128]{2,1,0:T(8,128)(2,1)S(1)}, bf16[8,128,128]{2,1,0:T(8,128)(2,1)}, u32[]{:S(2)}) copy-start(bf16[8,128,128]{2,1,0:T(8,128)(2,1)} %param.16) | copy-start | bytes 786436
  (5 other events, 4.4 us)

commit v16 on v14

--- a/solution.py
+++ b/solution.py
@@ -73,7 +73,8 @@
     phase_mine = lax.dynamic_slice_in_dim(phase_block, tile_index * tiles_dev, tiles_dev, 0)
     steer_re = row_steer[0]
     steer_im = row_steer[1]
-    col_mine = lax.dynamic_slice_in_dim(col_steer, az_index, 1, 3)[..., 0]
+    col_pick = jnp.arange(col_steer.shape[3], dtype=jnp.int32) == az_index
+    col_mine = jnp.sum(jnp.where(col_pick, col_steer, 0.0), axis=3)
     image_b = image.astype(jnp.bfloat16).reshape(2, tiles_dev, tile_rows, columns)
     part_sre = jnp.transpose(steer_re, (1, 0, 2))
     part_sim = jnp.transpose(steer_im, (1, 0, 2))

time: 185 us -> 184 us (level)
    unnamed x68 -> x69, local copies, waits for them, and re-layouts: 5.67 us -> 4.56 us
where the time goes in v16:
time: 184 us
  waiting for transfers between devices  85.7 us (47%)
  starting transfers between devices  42.9 us (23%)
  other arithmetic  20.5 us (11%)
  local copies, waits for them, and re-layouts  19.4 us (11%)
  matrix products  13.7 us (7%)
    ppermute x12, waiting for transfers between devices, doubling_gather(): got = lax.ppermute(block, axis, pairs)  54.9 us
    ppermute x4, waiting for transfers between devices, halving_sum(): blocks = keep + lax.ppermute(send, axis, pairs)  26 us
    ppermute x12, starting transfers between devices, doubling_gather(): got = lax.ppermute(block, axis, pairs)  23.7 us
    ppermute x2, starting transfers between devices, padded_2(): lax.ppermute(lax.slice_in_dim(block, block.shape[dim] - width, None, axis...  10.9 us
    ppermute x4, starting transfers between devices, halving_sum(): blocks = keep + lax.ppermute(send, axis, pairs)  5.1 us
    ppermute x2, waiting for transfers between devices, padded_2(): lax.ppermute(lax.slice_in_dim(block, 0, width, axis=dim), axis, backward)  4.87 us
    unnamed x69, local copies, waits for them, and re-layouts  4.56 us
    another operation x24, other arithmetic, doubling_gather(): block = jnp.stack([low, high], axis=place)  4.32 us
  transfers between devices with their start and end apart: 20, of which 15 were waited for; matrix products, arithmetic and copies ran while one was open for 13% of the time, Pallas kernels for 0%

profile of v16, /device:TPU:1, one launch (start us, length us, event | category | flops | bytes accessed | tf_op | source)
XLA Modules:
  0.0 183.8 jit_solution(3837111567429125412)
XLA Ops:
  0.7 2.8 %fusion.90 = (bf16[1,1024,2,256]{3,2,1,0:T(2,128)(2,1)S(1)}, bf16[1,1024,2,256]{3,2,1,0:T(2,128)(2,1)S(1)}) fusion(bf16[2,1024,2,256]{3,2,1,0:T(2,128)(2,1)} %param.14), kind=kLoop, calls=%fused_computation.182 | loop fusion | bytes 4194304 | tf_op jit(solution)/shard_map/slice | solution.py:75
  4.9 1.4 fusion.51
  7.6 1.3 multiply_subtract_fusion
  10.0 3.2 %collective-permute-start = (f32[2,2,2,2,64,2,128]{6,4,2,1,0,5,3:T(8,128)}, f32[2,2,2,2,64,2,128]{6,4,2,1,0,5,3:T(8,128)}, u32[]{:S(2)}, u32[]{:S(2)}) collective-permute-start(f32[2,2,2,2,64,2,128]{6,4,2,1,0,5,3:T(8,128)} %dynamic-slice_bitcast_fusion), channel_id=1, source_target_pairs={{0,16},{16,0},{32,48},{48,32},{64,80},{80,64},{96,112},{112,96},{1... | collective-permute-start | bytes 3145736 | tf_op jit(solution)/shard_map/ppermute | solution.py:36
  13.3 2.6 %collective-permute-done = f32[2,2,2,2,64,2,128]{6,4,2,1,0,5,3:T(8,128)} collective-permute-done((f32[2,2,2,2,64,2,128]{6,4,2,1,0,5,3:T(8,128)}, f32[2,2,2,2,64,2,128]{6,4,2,1,0,5,3:T(8,128)}, u32[]{:S(2)}, u32[]{:S(2)}) %collective-permute-start) | collective-permute-done | bytes 1048608 | tf_op jit(solution)/shard_map/ppermute | solution.py:36
  15.9 1.4 bitcast_add_fusion
  17.6 13.1 %collective-permute-done.1 = f32[2,2,2,64,2,128]{5,3,2,4,0,1:T(8,128)S(1)} collective-permute-done((f32[2,2,2,64,2,128]{5,3,2,4,0,1:T(8,128)S(1)}, f32[2,2,2,64,2,128]{5,3,2,4,0,1:T(8,128)S(1)}, u32[]{:S(2)}, u32[]{:S(2)}) %collective-permute-start.1) | collective-permute-done | bytes 524320 | tf_op jit(solution)/shard_map/ppermute | solution.py:36
  30.9 6.5 %collective-permute-done.2 = f32[2,2,64,2,128]{4,2,1,3,0:T(8,128)S(1)} collective-permute-done((f32[2,2,64,2,128]{4,2,1,3,0:T(8,128)S(1)}, f32[2,2,64,2,128]{4,2,1,3,0:T(8,128)S(1)}, u32[]{:S(2)}, u32[]{:S(2)}) %collective-permute-start.2) | collective-permute-done | bytes 262176 | tf_op jit(solution)/shard_map/ppermute | solution.py:36
  37.5 1.7 collective-permute-start.3
  39.2 3.7 %collective-permute-done.3 = f32[2,64,2,128]{3,1,0,2:T(8,128)S(1)} collective-permute-done((f32[2,64,2,128]{3,1,0,2:T(8,128)S(1)}, f32[2,64,2,128]{3,1,0,2:T(8,128)S(1)}, u32[]{:S(2)}, u32[]{:S(2)}) %collective-permute-start.3) | collective-permute-done | bytes 131104 | tf_op jit(solution)/shard_map/ppermute | solution.py:36
  43.0 5.3 %collective-permute-start.4 = (bf16[2,64,2,128]{3,1,2,0:T(8,128)(2,1)S(1)}, bf16[2,64,2,128]{3,1,2,0:T(8,128)(2,1)S(1)}, u32[]{:S(2)}, u32[]{:S(2)}) collective-permute-start(bf16[2,64,2,128]{3,1,2,0:T(8,128)(2,1)S(1)} %fusion.76), channel_id=1, source_target_pairs={{0,2},{1,3},{2,0},{3,1},{4,6},{5,7},{6,4},{7,5},{8,10},{9,11},{10,... | collective-permute-start | bytes 196616 | tf_op jit(solution)/shard_map/ppermute | solution.py:47
  48.2 2.0 %collective-permute-done.4 = bf16[2,64,2,128]{3,1,2,0:T(8,128)(2,1)S(1)} collective-permute-done((bf16[2,64,2,128]{3,1,2,0:T(8,128)(2,1)S(1)}, bf16[2,64,2,128]{3,1,2,0:T(8,128)(2,1)S(1)}, u32[]{:S(2)}, u32[]{:S(2)}) %collective-permute-start.4) | collective-permute-done | bytes 65568 | tf_op jit(solution)/shard_map/ppermute | solution.py:47
  50.2 2.5 %collective-permute-start.5 = (bf16[2,2,64,2,128]{4,2,3,1,0:T(8,128)(2,1)S(1)}, bf16[2,2,64,2,128]{4,2,3,1,0:T(8,128)(2,1)S(1)}, u32[]{:S(2)}, u32[]{:S(2)}) collective-permute-start(bf16[2,2,64,2,128]{4,2,3,1,0:T(8,128)(2,1)S(1)} %pad_maximum_fusion.26), channel_id=1, source_target_pairs={{0,1},{1,0},{2,3},{3,2},{4,5},{5,4},{6,7},{7,6},{8,9},{9,8},{10,11... | collective-permute-start | bytes 393224 | tf_op jit(solution)/shard_map/ppermute | solution.py:47
  52.7 4.5 %collective-permute-done.5 = bf16[2,2,64,2,128]{4,2,3,1,0:T(8,128)(2,1)S(1)} collective-permute-done((bf16[2,2,64,2,128]{4,2,3,1,0:T(8,128)(2,1)S(1)}, bf16[2,2,64,2,128]{4,2,3,1,0:T(8,128)(2,1)S(1)}, u32[]{:S(2)}, u32[]{:S(2)}) %collective-permute-start.5) | collective-permute-done | bytes 131104 | tf_op jit(solution)/shard_map/ppermute | solution.py:47
  57.3 3.0 %collective-permute-start.6 = (bf16[2,2,2,64,2,128]{5,3,4,2,1,0:T(8,128)(2,1)S(1)}, bf16[2,2,2,64,2,128]{5,3,4,2,1,0:T(8,128)(2,1)S(1)}, u32[]{:S(2)}, u32[]{:S(2)}) collective-permute-start(bf16[2,2,2,64,2,128]{5,3,4,2,1,0:T(8,128)(2,1)S(1)} %pad_maximum_fusion.23), channel_id=1, source_target_pairs={{0,8},{1,9},{2,10},{3,11},{4,12},{5,13},{6,14},{7,15},{8,0},{9,1},... | collective-permute-start | bytes 786440 | tf_op jit(solution)/shard_map/ppermute | solution.py:47
  60.4 3.8 %collective-permute-done.6 = bf16[2,2,2,64,2,128]{5,3,4,2,1,0:T(8,128)(2,1)S(1)} collective-permute-done((bf16[2,2,2,64,2,128]{5,3,4,2,1,0:T(8,128)(2,1)S(1)}, bf16[2,2,2,64,2,128]{5,3,4,2,1,0:T(8,128)(2,1)S(1)}, u32[]{:S(2)}, u32[]{:S(2)}) %collective-permute-start.6) | collective-permute-done | bytes 262176 | tf_op jit(solution)/shard_map/ppermute | solution.py:47
  64.3 1.4 collective-permute-start.7
  65.8 10.1 %collective-permute-done.7 = bf16[2,2,2,2,64,2,128]{6,4,5,3,2,1,0:T(8,128)(2,1)S(1)} collective-permute-done((bf16[2,2,2,2,64,2,128]{6,4,5,3,2,1,0:T(8,128)(2,1)S(1)}, bf16[2,2,2,2,64,2,128]{6,4,5,3,2,1,0:T(8,128)(2,1)S(1)}, u32[]{:S(2)}, u32[]{:S(2)}) %collective-permute-start.7) | collective-permute-done | bytes 524320 | tf_op jit(solution)/shard_map/ppermute | solution.py:47
  77.0 1.6 fusion.30
  78.6 4.4 %collective-permute-start.8 = (bf16[4,2,64,128]{3,2,1,0:T(8,128)(2,1)S(1)}, bf16[4,2,64,128]{3,2,1,0:T(8,128)(2,1)S(1)}, u32[]{:S(2)}, u32[]{:S(2)}) collective-permute-start(bf16[4,2,64,128]{3,2,1,0:T(8,128)(2,1)S(1)} %convert_bitcast_fusion), channel_id=1, source_target_pairs={{0,2},{1,3},{2,0},{3,1},{4,6},{5,7},{6,4},{7,5},{8,10},{9,11},{10,... | collective-permute-start | bytes 393224 | tf_op jit(solution)/shard_map/ppermute | solution.py:47
  83.0 3.4 %collective-permute-done.8 = bf16[4,2,64,128]{3,2,1,0:T(8,128)(2,1)S(1)} collective-permute-done((bf16[4,2,64,128]{3,2,1,0:T(8,128)(2,1)S(1)}, bf16[4,2,64,128]{3,2,1,0:T(8,128)(2,1)S(1)}, u32[]{:S(2)}, u32[]{:S(2)}) %collective-permute-start.8) | collective-permute-done | bytes 131104 | tf_op jit(solution)/shard_map/ppermute | solution.py:47
  86.8 15.3 %collective-permute-done.9 = bf16[2,4,2,64,128]{4,3,2,1,0:T(8,128)(2,1)S(1)} collective-permute-done((bf16[2,4,2,64,128]{4,3,2,1,0:T(8,128)(2,1)S(1)}, bf16[2,4,2,64,128]{4,3,2,1,0:T(8,128)(2,1)S(1)}, u32[]{:S(2)}, u32[]{:S(2)}) %collective-permute-start.9) | collective-permute-done | bytes 262176 | tf_op jit(solution)/shard_map/ppermute | solution.py:47
  103.0 1.7 slice_maximum_fusion
  104.7 1.9 %copy.94 = f32[6,512,1]{1,2,0:T(1,128)S(1)} copy(f32[6,512,1]{2,1,0:T(8,128)} %get-tuple-element.25) | data formatting | bytes 24576 | tf_op jit(solution)/shard_map/slice | solution.py:17
  106.6 9.6 %collective-permute-start.16 = (f32[6,512,1]{1,2,0:T(1,128)S(1)}, f32[6,512,1]{1,2,0:T(1,128)S(1)}, u32[]{:S(2)}, u32[]{:S(2)}) collective-permute-start(f32[6,512,1]{1,2,0:T(1,128)S(1)} %copy.94), channel_id=1, source_target_pairs={{0,16},{16,32},{32,48},{48,64},{64,80},{80,96},{96,112},{112,128},... | collective-permute-start | bytes 36872 | tf_op jit(solution)/shard_map/ppermute | solution.py:16
  117.2 1.9 %collective-permute-start.17 = (f32[6,512,1]{1,2,0:T(1,128)}, f32[6,512,1]{1,2,0:T(1,128)}, u32[]{:S(2)}, u32[]{:S(2)}) collective-permute-start(f32[6,512,1]{1,2,0:T(1,128)} %copy.95), channel_id=1, source_target_pairs={{16,0},{32,16},{48,32},{64,48},{80,64},{96,80},{112,96},{128,112},... | collective-permute-start | bytes 36872 | tf_op jit(solution)/shard_map/ppermute | solution.py:19
  125.4 1.5 pad_maximum_fusion.28
  126.9 1.3 collective-permute-start.18
  128.2 1.3 collective-permute-start.19
  130.8 1.5 gather_fusion
  132.3 4.9 %collective-permute-done.19 = f32[6,1,130]{2,1,0:T(1,128)} collective-permute-done((f32[6,1,130]{2,1,0:T(1,128)}, f32[6,1,130]{2,1,0:T(1,128)}, u32[]{:S(2)}, u32[]{:S(2)}) %collective-permute-start.19) | collective-permute-done | bytes 3152 | tf_op jit(solution)/shard_map/ppermute | solution.py:19
  137.1 2.2 %fusion.42 = f32[1,2,513,129]{3,2,1,0:T(8,128)S(1)} fusion(f32[6,1,130]{2,1,0:T(1,128)} %collective-permute-done.19, f32[6,512,1]{2,1,0:T(8,128)S(1)} %copy.97, f32[6,512,1]{2,1,0:T(8,128)S(1)} %copy.96, f32[4,512,128]{2,1,0:T(8,128)} %bitcast.248, f32[2,512,128]{2,1,0:T(8,128)} %param.10, f32[6,1,130]{2,1,0:T(1,128)S(1)} %collective-permute-done.18, ...), kind=kLoop, calls=%fused_computation.57 | loop fusion | flops 1323540 | bytes 2133609 | tf_op jit(solution)/shard_map/stack | solution.py:161
  139.4 7.3 %collective-permute-done.11 = bf16[2,2,2,4,2,64,128]{6,5,4,3,1,2,0:T(8,128)(2,1)} collective-permute-done((bf16[2,2,2,4,2,64,128]{6,5,4,3,1,2,0:T(8,128)(2,1)}, bf16[2,2,2,4,2,64,128]{6,5,4,3,1,2,0:T(8,128)(2,1)}, u32[]{:S(2)}, u32[]{:S(2)}) %collective-permute-start.11) | collective-permute-done | bytes 1048608 | tf_op jit(solution)/shard_map/ppermute | solution.py:47
  146.6 1.4 select_bitcast_fusion.1
  148.9 1.3 fusion.10
  150.4 1.8 collective-permute-start.12
  152.8 2.3 %collective-permute-done.12 = bf16[64,2,2,128]{3,0,1,2:T(8,128)(2,1)S(1)} collective-permute-done((bf16[64,2,2,128]{3,0,1,2:T(8,128)(2,1)S(1)}, bf16[64,2,2,128]{3,0,1,2:T(8,128)(2,1)S(1)}, u32[]{:S(2)}, u32[]{:S(2)}) %collective-permute-start.12) | collective-permute-done | bytes 65568 | tf_op jit(solution)/shard_map/ppermute | solution.py:47
  155.3 1.6 pad_maximum_fusion
  156.9 2.2 %collective-permute-done.13 = bf16[2,64,2,2,128]{4,1,2,3,0:T(8,128)(2,1)S(1)} collective-permute-done((bf16[2,64,2,2,128]{4,1,2,3,0:T(8,128)(2,1)S(1)}, bf16[2,64,2,2,128]{4,1,2,3,0:T(8,128)(2,1)S(1)}, u32[]{:S(2)}, u32[]{:S(2)}) %collective-permute-start.13) | collective-permute-done | bytes 131104 | tf_op jit(solution)/shard_map/ppermute | solution.py:47
  160.5 3.9 %collective-permute-done.14 = bf16[2,2,64,2,2,128]{5,2,3,4,1,0:T(8,128)(2,1)S(1)} collective-permute-done((bf16[2,2,64,2,2,128]{5,2,3,4,1,0:T(8,128)(2,1)S(1)}, bf16[2,2,64,2,2,128]{5,2,3,4,1,0:T(8,128)(2,1)S(1)}, u32[]{:S(2)}, u32[]{:S(2)}) %collective-permute-start.14) | collective-permute-done | bytes 262176 | tf_op jit(solution)/shard_map/ppermute | solution.py:47
  164.6 4.2 %collective-permute-start.15 = (bf16[2,2,2,64,2,2,128]{6,3,4,5,1,0,2:T(8,128)(2,1)S(1)}, bf16[2,2,2,64,2,2,128]{6,3,4,5,1,0,2:T(8,128)(2,1)S(1)}, u32[]{:S(2)}, u32[]{:S(2)}) collective-permute-start(bf16[2,2,2,64,2,2,128]{6,3,4,5,1,0,2:T(8,128)(2,1)S(1)} %pad_maximum_fusion.22), channel_id=1, source_target_pairs={{0,16},{16,0},{32,48},{48,32},{64,80},{80,64},{96,112},{112,96},{1... | collective-permute-start | bytes 1572872 | tf_op jit(solution)/shard_map/ppermute | solution.py:47
  169.2 1.3 slice.126
  172.9 1.5 copy-done.10
  174.4 1.3 fusion.57
  175.7 1.3 fusion.59
  177.1 1.3 fusion.16
  178.6 2.4 %fusion.17 = f32[2,256,128]{1,2,0:T(8,128)S(1)} fusion(f32[2,128,256]{2,1,0:T(8,128)S(1)} %fusion.59, bf16[1,1024,2,256]{3,2,1,0:T(2,128)(2,1)S(1)} %copy-done.8, f32[2,1024]{1,0:T(2,128)S(1)} %copy-done.28, f32[2,1024]{1,0:T(2,128)S(1)} %copy-done.27, bf16[2,2,1024,128]{3,2,1,0:T(8,128)(2,1)} %bitcast.269), kind=kOutput, calls=%fused_computation.33 | convolution fusion | flops 135856128 | bytes 2637824 | tf_op jit(solution)/shard_map/pjh,jpu->jhu/dot_general | solution.py:143
  181.1 2.7 %fusion.72 = f32[2,512,128]{2,1,0:T(8,128)} fusion(f32[2,512,128]{2,1,0:T(8,128)S(1)} %copy-done.6, f32[2,513,129]{2,1,0:T(8,128)} %get-tuple-element.18, f32[2,513,129]{2,1,0:T(8,128)S(1)} %get-tuple-element.17, f32[1,512,128]{2,1,0:T(8,128)S(1)} %bitcast.265, f32[1,512,128]{2,1,0:T(8,128)S(1)} %bitcast.264), kind=kLoop, calls=%fused_computation.101 | loop fusion | flops 917504 | bytes 3670016 | tf_op jit(solution)/shard_map/sub | solution.py:173
  (148 shorter events, 21.9 us)
Async XLA Ops:
  0.6 76.2 %copy-start = (bf16[8,128,128]{2,1,0:T(8,128)(2,1)S(1)}, bf16[8,128,128]{2,1,0:T(8,128)(2,1)}, u32[]{:S(2)}) copy-start(bf16[8,128,128]{2,1,0:T(8,128)(2,1)} %param.16) | copy-start | bytes 786436
  0.7 2.8 %copy-start.4 = (f32[2,512,128]{2,1,0:T(8,128)S(1)}, f32[2,512,128]{2,1,0:T(8,128)}, u32[]{:S(2)}) copy-start(f32[2,512,128]{2,1,0:T(8,128)} %param.10) | copy-start | bytes 1572868
  0.7 2.9 %copy-start.21 = (f32[2,1024,2,16]{1,3,2,0:T(8,128)S(1)}, f32[2,1024,2,16]{1,3,2,0:T(8,128)}, u32[]{:S(2)}) copy-start(f32[2,1024,2,16]{1,3,2,0:T(8,128)} %param.15) | copy-start | bytes 786436
  3.5 1.5 copy-start.9
  3.5 3.3 %copy-start.7 = (bf16[1,1024,2,256]{3,2,1,0:T(2,128)(2,1)}, bf16[1,1024,2,256]{3,2,1,0:T(2,128)(2,1)S(1)}, u32[]{:S(2)}) copy-start(bf16[1,1024,2,256]{3,2,1,0:T(2,128)(2,1)S(1)} %get-tuple-element.23) | copy-start | bytes 3145732
  6.4 1.2 copy-start.17
  10.0 5.9 %collective-permute-start = (f32[2,2,2,2,64,2,128]{6,4,2,1,0,5,3:T(8,128)}, f32[2,2,2,2,64,2,128]{6,4,2,1,0,5,3:T(8,128)}, u32[]{:S(2)}, u32[]{:S(2)}) collective-permute-start(f32[2,2,2,2,64,2,128]{6,4,2,1,0,5,3:T(8,128)} %dynamic-slice_bitcast_fusion), channel_id=1, source_target_pairs={{0,16},{16,0},{32,48},{48,32},{64,80},{80,64},{96,112},{112,96},{1... | collective-permute-start | bytes 3145736 | tf_op jit(solution)/shard_map/ppermute | solution.py:36
  17.5 13.2 %collective-permute-start.1 = (f32[2,2,2,64,2,128]{5,3,2,4,0,1:T(8,128)S(1)}, f32[2,2,2,64,2,128]{5,3,2,4,0,1:T(8,128)S(1)}, u32[]{:S(2)}, u32[]{:S(2)}) collective-permute-start(f32[2,2,2,64,2,128]{5,3,2,4,0,1:T(8,128)S(1)} %bitcast.270), channel_id=1, source_target_pairs={{0,128},{16,144},{32,160},{48,176},{64,192},{80,208},{96,224},{112... | collective-permute-start | bytes 1572872 | tf_op jit(solution)/shard_map/ppermute | solution.py:36
  30.8 6.7 %collective-permute-start.2 = (f32[2,2,64,2,128]{4,2,1,3,0:T(8,128)S(1)}, f32[2,2,64,2,128]{4,2,1,3,0:T(8,128)S(1)}, u32[]{:S(2)}, u32[]{:S(2)}) collective-permute-start(f32[2,2,64,2,128]{4,2,1,3,0:T(8,128)S(1)} %dynamic-slice_bitcast_fusion.1), channel_id=1, source_target_pairs={{0,32},{16,48},{32,0},{48,16},{64,96},{80,112},{96,64},{112,80},{1... | collective-permute-start | bytes 786440 | tf_op jit(solution)/shard_map/ppermute | solution.py:36
  30.9 29.5 %copy-start.23 = (s32[32,1,6]{0,1,2:T(1,128)S(1)}, s32[32,1,6]{0,1,2:T(1,128)}, u32[]{:S(2)}) copy-start(s32[32,1,6]{0,1,2:T(1,128)} %param.17) | copy-start | bytes 2308
  30.9 29.4 %copy-start.24 = (s32[32,1,6]{0,1,2:T(1,128)S(1)}, s32[32,1,6]{0,1,2:T(1,128)}, u32[]{:S(2)}) copy-start(s32[32,1,6]{0,1,2:T(1,128)} %param.18) | copy-start | bytes 2308
  37.5 5.4 %collective-permute-start.3 = (f32[2,64,2,128]{3,1,0,2:T(8,128)S(1)}, f32[2,64,2,128]{3,1,0,2:T(8,128)S(1)}, u32[]{:S(2)}, u32[]{:S(2)}) collective-permute-start(f32[2,64,2,128]{3,1,0,2:T(8,128)S(1)} %dynamic-slice_bitcast_fusion.2), channel_id=1, source_target_pairs={{0,64},{16,80},{32,96},{48,112},{64,0},{80,16},{96,32},{112,48},{1... | collective-permute-start | bytes 393224 | tf_op jit(solution)/shard_map/ppermute | solution.py:36
  43.0 7.2 %collective-permute-start.4 = (bf16[2,64,2,128]{3,1,2,0:T(8,128)(2,1)S(1)}, bf16[2,64,2,128]{3,1,2,0:T(8,128)(2,1)S(1)}, u32[]{:S(2)}, u32[]{:S(2)}) collective-permute-start(bf16[2,64,2,128]{3,1,2,0:T(8,128)(2,1)S(1)} %fusion.76), channel_id=1, source_target_pairs={{0,2},{1,3},{2,0},{3,1},{4,6},{5,7},{6,4},{7,5},{8,10},{9,11},{10,... | collective-permute-start | bytes 196616 | tf_op jit(solution)/shard_map/ppermute | solution.py:47
  50.2 7.1 %collective-permute-start.5 = (bf16[2,2,64,2,128]{4,2,3,1,0:T(8,128)(2,1)S(1)}, bf16[2,2,64,2,128]{4,2,3,1,0:T(8,128)(2,1)S(1)}, u32[]{:S(2)}, u32[]{:S(2)}) collective-permute-start(bf16[2,2,64,2,128]{4,2,3,1,0:T(8,128)(2,1)S(1)} %pad_maximum_fusion.26), channel_id=1, source_target_pairs={{0,1},{1,0},{2,3},{3,2},{4,5},{5,4},{6,7},{7,6},{8,9},{9,8},{10,11... | collective-permute-start | bytes 393224 | tf_op jit(solution)/shard_map/ppermute | solution.py:47
  52.7 13.0 %copy-start.32 = (s32[64]{0:T(128)S(1)}, s32[64]{0:T(128)}, u32[]{:S(2)}) copy-start(s32[64]{0:T(128)} %param.19) | copy-start | bytes 772
  57.3 6.8 %collective-permute-start.6 = (bf16[2,2,2,64,2,128]{5,3,4,2,1,0:T(8,128)(2,1)S(1)}, bf16[2,2,2,64,2,128]{5,3,4,2,1,0:T(8,128)(2,1)S(1)}, u32[]{:S(2)}, u32[]{:S(2)}) collective-permute-start(bf16[2,2,2,64,2,128]{5,3,4,2,1,0:T(8,128)(2,1)S(1)} %pad_maximum_fusion.23), channel_id=1, source_target_pairs={{0,8},{1,9},{2,10},{3,11},{4,12},{5,13},{6,14},{7,15},{8,0},{9,1},... | collective-permute-start | bytes 786440 | tf_op jit(solution)/shard_map/ppermute | solution.py:47
  64.3 11.6 %collective-permute-start.7 = (bf16[2,2,2,2,64,2,128]{6,4,5,3,2,1,0:T(8,128)(2,1)S(1)}, bf16[2,2,2,2,64,2,128]{6,4,5,3,2,1,0:T(8,128)(2,1)S(1)}, u32[]{:S(2)}, u32[]{:S(2)}) collective-permute-start(bf16[2,2,2,2,64,2,128]{6,4,5,3,2,1,0:T(8,128)(2,1)S(1)} %pad_maximum_fusion.20), channel_id=1, source_target_pairs={{0,4},{1,5},{2,6},{3,7},{4,0},{5,1},{6,2},{7,3},{8,12},{9,13},{10,... | collective-permute-start | bytes 1572872 | tf_op jit(solution)/shard_map/ppermute | solution.py:47
  78.6 24.4 %copy-start.15 = (f32[2,64,4,128]{3,1,0,2:T(8,128)}, f32[2,64,4,128]{3,1,0,2:T(8,128)S(1)}, u32[]{:S(2)}) copy-start(f32[2,64,4,128]{3,1,0,2:T(8,128)S(1)} %fusion.30) | copy-start | bytes 786436
  78.6 24.4 %copy-start.2 = (f32[2,2,512,128]{3,2,1,0:T(8,128)S(1)}, f32[2,2,512,128]{3,2,1,0:T(8,128)}, u32[]{:S(2)}) copy-start(f32[2,2,512,128]{3,2,1,0:T(8,128)} %param.11) | copy-start | bytes 3145732
  78.6 7.8 %collective-permute-start.8 = (bf16[4,2,64,128]{3,2,1,0:T(8,128)(2,1)S(1)}, bf16[4,2,64,128]{3,2,1,0:T(8,128)(2,1)S(1)}, u32[]{:S(2)}, u32[]{:S(2)}) collective-permute-start(bf16[4,2,64,128]{3,2,1,0:T(8,128)(2,1)S(1)} %convert_bitcast_fusion), channel_id=1, source_target_pairs={{0,2},{1,3},{2,0},{3,1},{4,6},{5,7},{6,4},{7,5},{8,10},{9,11},{10,... | collective-permute-start | bytes 393224 | tf_op jit(solution)/shard_map/ppermute | solution.py:47
  86.5 15.6 %collective-permute-start.9 = (bf16[2,4,2,64,128]{4,3,2,1,0:T(8,128)(2,1)S(1)}, bf16[2,4,2,64,128]{4,3,2,1,0:T(8,128)(2,1)S(1)}, u32[]{:S(2)}, u32[]{:S(2)}) collective-permute-start(bf16[2,4,2,64,128]{4,3,2,1,0:T(8,128)(2,1)S(1)} %pad_maximum_fusion.24), channel_id=1, source_target_pairs={{0,1},{1,0},{2,3},{3,2},{4,5},{5,4},{6,7},{7,6},{8,9},{9,8},{10,11... | collective-permute-start | bytes 786440 | tf_op jit(solution)/shard_map/ppermute | solution.py:47
  103.0 16.8 %collective-permute-start.10 = (bf16[2,2,4,2,64,128]{5,4,3,2,0,1:T(8,128)(2,1)}, bf16[2,2,4,2,64,128]{5,4,3,2,0,1:T(8,128)(2,1)S(1)}, u32[]{:S(2)}, u32[]{:S(2)}) collective-permute-start(bf16[2,2,4,2,64,128]{5,4,3,2,0,1:T(8,128)(2,1)} %pad_maximum_fusion.21), channel_id=1, source_target_pairs={{0,8},{1,9},{2,10},{3,11},{4,12},{5,13},{6,14},{7,15},{8,0},{9,1},... | collective-permute-start | bytes 1572872 | tf_op jit(solution)/shard_map/ppermute | solution.py:47
  106.6 17.1 %collective-permute-start.16 = (f32[6,512,1]{1,2,0:T(1,128)S(1)}, f32[6,512,1]{1,2,0:T(1,128)S(1)}, u32[]{:S(2)}, u32[]{:S(2)}) collective-permute-start(f32[6,512,1]{1,2,0:T(1,128)S(1)} %copy.94), channel_id=1, source_target_pairs={{0,16},{16,32},{32,48},{48,64},{64,80},{80,96},{96,112},{112,128},... | collective-permute-start | bytes 36872 | tf_op jit(solution)/shard_map/ppermute | solution.py:16
  117.2 7.0 %collective-permute-start.17 = (f32[6,512,1]{1,2,0:T(1,128)}, f32[6,512,1]{1,2,0:T(1,128)}, u32[]{:S(2)}, u32[]{:S(2)}) collective-permute-start(f32[6,512,1]{1,2,0:T(1,128)} %copy.95), channel_id=1, source_target_pairs={{16,0},{32,16},{48,32},{64,48},{80,64},{96,80},{112,96},{128,112},... | collective-permute-start | bytes 36872 | tf_op jit(solution)/shard_map/ppermute | solution.py:19
  119.9 1.9 %copy-start.13 = (bf16[1,2,2,4,2,64,128]{6,5,4,3,1,2,0:T(8,128)(2,1)}, bf16[1,2,2,4,2,64,128]{6,5,4,3,1,2,0:T(8,128)(2,1)S(1)}, u32[]{:S(2)}) copy-start(bf16[1,2,2,4,2,64,128]{6,5,4,3,1,2,0:T(8,128)(2,1)S(1)} %get-tuple-element.30) | copy-start | bytes 1572868
  121.8 24.9 %collective-permute-start.11 = (bf16[2,2,2,4,2,64,128]{6,5,4,3,1,2,0:T(8,128)(2,1)}, bf16[2,2,2,4,2,64,128]{6,5,4,3,1,2,0:T(8,128)(2,1)}, u32[]{:S(2)}, u32[]{:S(2)}) collective-permute-start(bf16[2,2,2,4,2,64,128]{6,5,4,3,1,2,0:T(8,128)(2,1)} %pad_maximum_fusion.18), channel_id=1, source_target_pairs={{0,4},{1,5},{2,6},{3,7},{4,0},{5,1},{6,2},{7,3},{8,12},{9,13},{10,... | collective-permute-start | bytes 3145736 | tf_op jit(solution)/shard_map/ppermute | solution.py:47
  125.4 4.1 %copy-start.31 = (s32[12]{0:T(128)S(1)}, s32[12]{0:T(128)}, u32[]{:S(2)}) copy-start(s32[12]{0:T(128)} %reshape.147) | copy-start | bytes 148
  125.4 4.7 %copy-start.25 = (s32[2,1,6]{0,1,2:T(1,128)S(1)}, s32[2,1,6]{0,1,2:T(1,128)}, u32[]{:S(2)}) copy-start(s32[2,1,6]{0,1,2:T(1,128)} %get-tuple-element.61) | copy-start | bytes 148
  126.9 5.4 %collective-permute-start.18 = (f32[6,1,130]{2,1,0:T(1,128)}, f32[6,1,130]{2,1,0:T(1,128)S(1)}, u32[]{:S(2)}, u32[]{:S(2)}) collective-permute-start(f32[6,1,130]{2,1,0:T(1,128)} %get-tuple-element.16), channel_id=1, source_target_pairs={{0,1},{1,2},{2,3},{3,4},{4,5},{5,6},{6,7},{7,8},{8,9},{9,10},{10,1... | collective-permute-start | bytes 9368 | tf_op jit(solution)/shard_map/ppermute | solution.py:16
  128.2 8.9 %collective-permute-start.19 = (f32[6,1,130]{2,1,0:T(1,128)}, f32[6,1,130]{2,1,0:T(1,128)}, u32[]{:S(2)}, u32[]{:S(2)}) collective-permute-start(f32[6,1,130]{2,1,0:T(1,128)} %get-tuple-element.15), channel_id=1, source_target_pairs={{1,0},{2,1},{3,2},{4,3},{5,4},{6,5},{7,6},{8,7},{9,8},{10,9},{11,1... | collective-permute-start | bytes 9368 | tf_op jit(solution)/shard_map/ppermute | solution.py:19
  137.1 9.5 %copy-start.12 = (bf16[1,2,2,4,2,64,128]{6,5,4,3,1,2,0:T(8,128)(2,1)S(1)}, bf16[1,2,2,4,2,64,128]{6,5,4,3,1,2,0:T(8,128)(2,1)}, u32[]{:S(2)}) copy-start(bf16[1,2,2,4,2,64,128]{6,5,4,3,1,2,0:T(8,128)(2,1)} %copy-done.11) | copy-start | bytes 1572868
  137.1 9.5 %copy-start.14 = (bf16[1,2,2,4,2,64,128]{6,5,4,3,1,2,0:T(8,128)(2,1)S(1)}, bf16[1,2,2,4,2,64,128]{6,5,4,3,1,2,0:T(8,128)(2,1)}, u32[]{:S(2)}) copy-start(bf16[1,2,2,4,2,64,128]{6,5,4,3,1,2,0:T(8,128)(2,1)} %copy-done.13) | copy-start | bytes 1572868
  148.5 1.6 copy-start.19
  148.9 3.3 %copy-start.3 = (f32[2,2,512,128]{3,2,1,0:T(8,128)S(1)}, f32[2,2,512,128]{3,2,1,0:T(8,128)}, u32[]{:S(2)}) copy-start(f32[2,2,512,128]{3,2,1,0:T(8,128)} %param.11) | copy-start | bytes 3145732
  148.9 3.3 %copy-start.5 = (f32[2,512,128]{2,1,0:T(8,128)S(1)}, f32[2,512,128]{2,1,0:T(8,128)}, u32[]{:S(2)}) copy-start(f32[2,512,128]{2,1,0:T(8,128)} %param.10) | copy-start | bytes 1572868
  148.9 3.3 %copy-start.29 = (pred[129]{0:T(512)(128)(4,1)S(1)}, pred[129]{0:T(512)(128)(4,1)}, u32[]{:S(2)}) copy-start(pred[129]{0:T(512)(128)(4,1)} %get-tuple-element.57) | copy-start | bytes 391
  150.4 4.7 %collective-permute-start.12 = (bf16[64,2,2,128]{3,0,1,2:T(8,128)(2,1)S(1)}, bf16[64,2,2,128]{3,0,1,2:T(8,128)(2,1)S(1)}, u32[]{:S(2)}, u32[]{:S(2)}) collective-permute-start(bf16[64,2,2,128]{3,0,1,2:T(8,128)(2,1)S(1)} %fusion.34), channel_id=1, source_target_pairs={{0,64},{16,80},{32,96},{48,112},{64,0},{80,16},{96,32},{112,48},{1... | collective-permute-start | bytes 196616 | tf_op jit(solution)/shard_map/ppermute | solution.py:47
  155.2 3.9 %collective-permute-start.13 = (bf16[2,64,2,2,128]{4,1,2,3,0:T(8,128)(2,1)S(1)}, bf16[2,64,2,2,128]{4,1,2,3,0:T(8,128)(2,1)S(1)}, u32[]{:S(2)}, u32[]{:S(2)}) collective-permute-start(bf16[2,64,2,2,128]{4,1,2,3,0:T(8,128)(2,1)S(1)} %pad_maximum_fusion.27), channel_id=1, source_target_pairs={{0,128},{16,144},{32,160},{48,176},{64,192},{80,208},{96,224},{112... | collective-permute-start | bytes 393224 | tf_op jit(solution)/shard_map/ppermute | solution.py:47
  159.2 5.3 %collective-permute-start.14 = (bf16[2,2,64,2,2,128]{5,2,3,4,1,0:T(8,128)(2,1)S(1)}, bf16[2,2,64,2,2,128]{5,2,3,4,1,0:T(8,128)(2,1)S(1)}, u32[]{:S(2)}, u32[]{:S(2)}) collective-permute-start(bf16[2,2,64,2,2,128]{5,2,3,4,1,0:T(8,128)(2,1)S(1)} %pad_maximum_fusion.25), channel_id=1, source_target_pairs={{0,32},{16,48},{32,0},{48,16},{64,96},{80,112},{96,64},{112,80},{1... | collective-permute-start | bytes 786440 | tf_op jit(solution)/shard_map/ppermute | solution.py:47
  164.6 8.0 %collective-permute-start.15 = (bf16[2,2,2,64,2,2,128]{6,3,4,5,1,0,2:T(8,128)(2,1)S(1)}, bf16[2,2,2,64,2,2,128]{6,3,4,5,1,0,2:T(8,128)(2,1)S(1)}, u32[]{:S(2)}, u32[]{:S(2)}) collective-permute-start(bf16[2,2,2,64,2,2,128]{6,3,4,5,1,0,2:T(8,128)(2,1)S(1)} %pad_maximum_fusion.22), channel_id=1, source_target_pairs={{0,16},{16,0},{32,48},{48,32},{64,80},{80,64},{96,112},{112,96},{1... | collective-permute-start | bytes 1572872 | tf_op jit(solution)/shard_map/ppermute | solution.py:47
  169.2 1.3 copy-start.26
  172.8 1.6 copy-start.10
  172.8 1.6 copy-start.27
  172.8 1.6 copy-start.28
  172.9 4.1 %copy-start.18 = (bf16[2,2,2,2,64,2,2,128]{7,4,3,2,1,0,6,5:T(8,128)(2,1)}, bf16[2,2,2,2,64,2,2,128]{7,4,3,2,1,0,6,5:T(8,128)(2,1)S(1)}, u32[]{:S(2)}) copy-start(bf16[2,2,2,2,64,2,2,128]{7,4,3,2,1,0,6,5:T(8,128)(2,1)S(1)} %copy.87) | copy-start | bytes 3145732
  175.7 1.4 copy-start.8
  178.5 2.5 %copy-start.6 = (f32[2,512,128]{2,1,0:T(8,128)S(1)}, f32[2,512,128]{2,1,0:T(8,128)}, u32[]{:S(2)}) copy-start(f32[2,512,128]{2,1,0:T(8,128)} %param.10) | copy-start | bytes 1572868
  181.0 2.7 %copy-start.1 = (bf16[8,128,128]{2,1,0:T(8,128)(2,1)S(1)}, bf16[8,128,128]{2,1,0:T(8,128)(2,1)}, u32[]{:S(2)}) copy-start(bf16[8,128,128]{2,1,0:T(8,128)(2,1)} %param.16) | copy-start | bytes 786436
  (5 other events, 4.6 us)
